TPU v7x, 256 devices: a whole 4x4x8 slice. The times are simulated.
256 devices in a mesh: seq: 32 (over y, x, z_hi), tp: 8 (over z_lo, core).
Axes of the slice: x: 4, y: 4, z: 8 (z_hi: 2, z_lo: 4; z = z_hi * 4 + z_lo), core: 2. Of those that a mesh axis runs over, the one named last changes fastest.
Arguments:
- conv_in: bfloat16 [8192, 16384], P('seq', 'tp'), may hold values from -6 to 6
- gate_in: bfloat16 [8192, 16384], P('seq', 'tp'), may hold values from -6 to 6
- q_proj: bfloat16 [8192, 8192], P('seq', 'tp'), may hold values from -6 to 6
- k_proj: bfloat16 [8192, 1024], P('seq', 'tp'), may hold values from -6 to 6
- v_proj: bfloat16 [8192, 1024], P('seq', 'tp'), may hold values from -6 to 6
- conv_weight: float32 [4, 16384], P(None, 'tp'), may hold values from -3 to 3
- conv_bias: float32 [16384], P('tp'), may hold values from -0.5 to 0.5
- proj_dt_weight: bfloat16 [16384, 512], P('tp'), may hold values from -0.046875 to 0.046875
- proj_bc_weight: bfloat16 [32, 16384], P(None, 'tp'), may hold values from -0.046875 to 0.046875
- dt_gain: float32 [512], replicated, may hold values from 0.1 to 1.9
- dt_weight: bfloat16 [512, 16384], P(None, 'tp'), may hold values from -0.25 to 0.25
- dt_bias: float32 [16384], P('tp'), may hold values from -5 to -2
- decay_rate: float32 [16, 16384], P(None, 'tp'), may hold values from 1e-05 to 2
- skip_weight: float32 [16384], P('tp'), may hold values from 0.5 to 1.5
Outputs:
- mamba_out: bfloat16 [8192, 16384], P('seq', 'tp')
- attn_out: bfloat16 [8192, 8192], P('seq', 'tp')
All inputs are finite; a program needn't handle non-finite values.
Results may differ from a plain program's by a relative error of at most 0.0051.
Values may be sent and summed in bfloat16 or wider, within the bound.
No kernel may reach another device: no remote copies, remote signals or barrier semaphores. Data moves between devices by JAX's collectives and lax.ppermute only.
A program may use at most 128 MiB of HBM per device.

v0:
```python
import math

import jax
import jax.numpy as jnp
from jax import lax
from jax.sharding import PartitionSpec as P

KCONV = 4
HD = 128
WINDOW = 2048


steps_per_block = 16
group_width = 256
epsilon = 1e-06


def shifted(value, axis, steps):
    count = lax.axis_size(axis)
    first, last = (max(0, -steps), min(count, count - steps))
    return lax.ppermute(value, axis, [(source, source + steps) for source in range(first, last)])


def prefix(value, axis, combine, identity):
    peers, position = (lax.axis_size(axis), lax.axis_index(axis))
    everything = jax.tree.map(lambda part: lax.all_gather(part, axis), value)
    start = jax.tree.map(
        lambda part, zero: jnp.broadcast_to(jnp.asarray(zero, part.dtype), part.shape),
        value,
        identity,
    )

    def step(k, before):
        reached = k < position
        new = combine(before, jax.tree.map(lambda part: part[k], everything))
        return jax.tree.map(lambda a, b: jnp.where(reached, a, b), new, before)

    return lax.fori_loop(0, peers, step, start)


def causal_conv(padded, conv_weight, conv_bias, length):
    summed = conv_bias[None, :] + jnp.zeros((length, padded.shape[1]), jnp.float32)
    for offset in range(KCONV):
        summed = summed + conv_weight[offset][None, :] * padded[offset : offset + length]
    return jax.nn.silu(summed).astype(jnp.bfloat16)


def rank_norm(rank_low, dt_gain):
    mean_square = jnp.mean(rank_low * rank_low, axis=-1, keepdims=True)
    return (rank_low * lax.rsqrt(mean_square + epsilon) * dt_gain[None, :]).astype(jnp.bfloat16)


def chain_combine(earlier, later_part):
    return (earlier[0] * later_part[0], later_part[0] * earlier[1] + later_part[1])


def block_states(step_group, drive_group, rate_group, input_rows, output_rows, initial):
    tokens_here, channels = step_group.shape
    state_count = rate_group.shape[0]
    blocks = tokens_here // steps_per_block
    step_blocks = step_group.reshape(blocks, steps_per_block, channels)
    drive_blocks = drive_group.reshape(blocks, steps_per_block, channels)
    input_blocks = input_rows.reshape(state_count, blocks, steps_per_block)
    output_blocks = output_rows.reshape(state_count, blocks, steps_per_block)
    hidden_state = jnp.zeros((state_count, blocks, channels), jnp.float32)
    elapsed = jnp.zeros((blocks, channels), jnp.float32)
    partial_out = []
    elapsed_all = []
    for offset in range(steps_per_block):
        elapsed = elapsed + step_blocks[:, offset]
        factor = jnp.exp(-rate_group[:, None, :] * step_blocks[None, :, offset])
        hidden_state = (
            factor * hidden_state + input_blocks[:, :, offset, None] * drive_blocks[None, :, offset]
        )
        elapsed_all.append(elapsed)
        partial_out.append(jnp.sum(output_blocks[:, :, offset, None] * hidden_state, axis=0))
    block_decay = jnp.exp(-rate_group[:, None, :] * elapsed[None])
    inclusive = lax.associative_scan(chain_combine, (block_decay, hidden_state), axis=1)
    final_decay = inclusive[0][:, -1]
    final_state = final_decay * initial + inclusive[1][:, -1]
    before_decay = jnp.concatenate(
        [jnp.ones_like(block_decay[:, :1]), inclusive[0][:, :-1]], axis=1
    )
    before_state = jnp.concatenate(
        [jnp.zeros_like(hidden_state[:, :1]), inclusive[1][:, :-1]], axis=1
    )
    entering = before_decay * initial[:, None, :] + before_state
    elapsed_stack = jnp.stack(elapsed_all, axis=1)
    carried = jnp.sum(
        output_blocks[:, :, :, None]
        * jnp.exp(-rate_group[:, None, None, :] * elapsed_stack[None])
        * entering[:, :, None, :],
        axis=0,
    )
    result = (jnp.stack(partial_out, axis=1) + carried).reshape(tokens_here, channels)
    block_starts = jnp.cumsum(elapsed, axis=0) - elapsed
    through = (elapsed_stack + block_starts[:, None, :]).reshape(tokens_here, channels)
    return (final_decay, final_state, result, through)


def per_device(
    conv_in,
    gate_in,
    q_proj,
    k_proj,
    v_proj,
    conv_weight,
    conv_bias,
    proj_dt_weight,
    proj_bc_weight,
    dt_gain,
    dt_weight,
    dt_bias,
    decay_rate,
    skip_weight,
):
    tokens_here, channels = conv_in.shape
    key_span = WINDOW // tokens_here
    conv_tail = conv_in[tokens_here - (KCONV - 1) :]
    neighbour = shifted((k_proj, v_proj, conv_tail), "seq", 1)
    key_blocks = [k_proj, neighbour[0]]
    value_blocks = [v_proj, neighbour[1]]
    for distance in range(2, key_span + 1):
        distant = shifted((k_proj, v_proj), "seq", distance)
        key_blocks.append(distant[0])
        value_blocks.append(distant[1])
    padded = jnp.concatenate([neighbour[2], conv_in], axis=0).astype(jnp.float32)
    activated = causal_conv(padded, conv_weight, conv_bias, tokens_here)
    state_parts = lax.dot_general(
        proj_bc_weight, activated, (((1,), (1,)), ((), ())), preferred_element_type=jnp.float32
    )
    rank_part = jnp.dot(activated, proj_dt_weight, preferred_element_type=jnp.float32)
    rank_low, state_in = lax.psum((rank_part, state_parts), "tp")
    rank_normed = rank_norm(rank_low, dt_gain)
    step_size = jax.nn.softplus(
        jnp.dot(rank_normed, dt_weight, preferred_element_type=jnp.float32) + dt_bias[None, :]
    )
    drive_term = step_size * activated.astype(jnp.float32)
    state_count = decay_rate.shape[0]
    input_rows = state_in[:state_count]
    output_rows = state_in[state_count:]
    group_size = min(group_width, channels)
    group_count = channels // group_size

    def by_groups(matrix):
        return matrix.reshape(matrix.shape[0], group_count, group_size).transpose(1, 0, 2)

    step_groups = by_groups(step_size)
    drive_groups = by_groups(drive_term)
    rate_groups = by_groups(decay_rate)
    zero_state = jnp.zeros((group_count, state_count, group_size), jnp.float32)
    first_pass = lax.map(
        lambda pieces: block_states(
            pieces[0], pieces[1], pieces[2], input_rows, output_rows, pieces[3]
        ),
        (step_groups, drive_groups, rate_groups, zero_state),
    )
    carried = prefix(
        (first_pass[0], first_pass[1]),
        "seq",
        chain_combine,
        (jnp.ones_like(first_pass[0]), jnp.zeros_like(first_pass[1])),
    )
    entering = carried[1]

    def adjust(pieces):
        local_out, through, rate_group, enter_group = pieces
        return local_out + jnp.sum(
            output_rows[:, :, None]
            * jnp.exp(-rate_group[:, None, :] * through[None])
            * enter_group[:, None, :],
            axis=0,
        )

    mixed = lax.map(adjust, (first_pass[2], first_pass[3], rate_groups, entering))
    mamba_sum = mixed.transpose(1, 0, 2).reshape(tokens_here, channels)
    mamba_out = (
        (mamba_sum + skip_weight[None, :] * activated.astype(jnp.float32))
        * jax.nn.silu(gate_in.astype(jnp.float32))
    ).astype(jnp.bfloat16)
    heads_here = q_proj.shape[1] // HD
    kv_here = k_proj.shape[1] // HD
    grouping = heads_here // kv_here
    keys_all = jnp.concatenate(key_blocks[::-1], axis=0).reshape(-1, kv_here, HD)
    values_all = jnp.concatenate(value_blocks[::-1], axis=0).reshape(-1, kv_here, HD)
    queries = q_proj.reshape(tokens_here, kv_here, grouping, HD)
    scores = jnp.einsum("tkgd,skd->kgts", queries, keys_all, preferred_element_type=jnp.float32) * (
        1.0 / math.sqrt(HD)
    )
    index_seq = lax.axis_index("seq")
    row_ids = jnp.arange(tokens_here, dtype=jnp.int32)[:, None]
    col_ids = jnp.arange((key_span + 1) * tokens_here, dtype=jnp.int32)[None, :]
    distance_all = WINDOW + row_ids - col_ids
    in_window = (
        (distance_all >= 0)
        & (distance_all < WINDOW)
        & (col_ids + index_seq * tokens_here >= WINDOW)
    )
    row_peak = jnp.max(jnp.where(in_window, scores, -jnp.inf), axis=-1, keepdims=True)
    weights = jnp.exp(jnp.where(in_window, scores - row_peak, -jnp.inf)).astype(jnp.bfloat16)
    summed = jnp.sum(weights.astype(jnp.float32), axis=-1)
    weighted = jnp.einsum("kgts,skd->tkgd", weights, values_all, preferred_element_type=jnp.float32)
    attn_out = (
        (weighted / summed.transpose(2, 0, 1)[..., None])
        .astype(jnp.bfloat16)
        .reshape(tokens_here, heads_here * HD)
    )
    return (mamba_out, attn_out)


def solution(mesh):
    return jax.shard_map(
        per_device,
        mesh=mesh,
        in_specs=(
            P("seq", "tp"),
            P("seq", "tp"),
            P("seq", "tp"),
            P("seq", "tp"),
            P("seq", "tp"),
            P(None, "tp"),
            P("tp"),
            P("tp", None),
            P(None, "tp"),
            P(),
            P(None, "tp"),
            P("tp"),
            P(None, "tp"),
            P("tp"),
        ),
        out_specs=(P("seq", "tp"), P("seq", "tp")),
        check_vma=False,
    )
```

profile of v0, /device:TPU:8, one launch (start us, length us, event | category | flops | bytes accessed | tf_op | source)
XLA Modules:
  0.0 640.7 jit_solution(12303717999541028721)
XLA Ops:
  8.1 9.1 %collective-permute-start = (bf16[3,2048]{1,0:T(4,128)(2,1)S(1)}, bf16[3,2048]{1,0:T(4,128)(2,1)S(1)}, u32[]{:S(2)}, u32[]{:S(2)}) collective-permute-start(bf16[3,2048]{1,0:T(4,128)(2,1)S(1)} %slice.364), channel_id=1, source_target_pairs={{0,8},{8,16},{16,24},{24,32},{32,40},{40,48},{48,56},{56,64},{64,7... | collective-permute-start | bytes 36872 | tf_op jit(solution)/shard_map/ppermute | solution.py:21
  18.2 2.8 collective-permute-done
  21.0 1.5 maximum_convert_fusion
  25.0 1.5 fusion.52
  27.1 28.5 %psum.15 = f32[32,256]{1,0:T(8,128)S(1)} all-reduce(f32[32,256]{1,0:T(8,128)S(1)} %convolution_bitcast_fusion), channel_id=1, replica_groups=mesh['seq'=32,'tp'=8] {'tp'}, use_global_device_ids=true, to_apply=%region_2.3 | all-reduce | flops 8192 | bytes 65536 | tf_op jit(solution)/shard_map/psum | solution.py:133
  55.6 42.3 %all-reduce.20.cloned.1.call-done = f32[256,512]{1,0:T(8,128)} async-done(((f32[256,512]{1,0:T(8,128)}), f32[256,512]{1,0:T(8,128)}) %all-reduce.20.cloned.1.call-update) | async-done | bytes 524304 | tf_op jit(solution)/shard_map/psum | solution.py:133
  99.1 2.8 convert_multiply_fusion.2
  101.9 2.4 bitcast_bitcast_fusion
  104.3 1.5 broadcast.108.clone.1
  105.8 1.5 broadcast.108.clone
  107.3 235.8 %while.40 = (s32[]{:T(128)}, f32[8,16,256]{2,1,0:T(8,128)}, f32[8,16,256]{2,1,0:T(8,128)}, f32[8,256,256]{2,1,0:T(8,128)}, f32[8,256,256]{2,1,0:T(8,128)}, /*ind...) while((s32[]{:T(128)}, f32[8,16,256]{2,1,0:T(8,128)}, ...), condition=%wide.region_22.23_spmd, body=%wide.region_3.22_spmd.sunk | while | flops 20303872 | bytes 26850812 | solution.py:152
  124.9 1.3 multiply_reduce_fusion.34
  154.3 1.3 multiply_reduce_fusion.34
  344.8 5.4 collective-permute-start.8
  350.1 3.4 collective-permute-start.7
  353.5 5.9 collective-permute-start.6
  359.4 4.9 collective-permute-start.5
  364.3 3.1 collective-permute-start.9
  368.8 2.0 collective-permute-done.9
  370.8 6.5 %collective-permute-start.10 = (bf16[256,128]{1,0:T(8,128)(2,1)}, bf16[256,128]{1,0:T(8,128)(2,1)S(1)}, u32[]{:S(2)}, u32[]{:S(2)}) collective-permute-start(bf16[256,128]{1,0:T(8,128)(2,1)} %param.23), channel_id=1, source_target_pairs={{0,56},{8,64},{16,72},{24,80},{32,88},{40,96},{48,104},{56,112},{6... | collective-permute-start | bytes 196616 | tf_op jit(solution)/shard_map/ppermute | solution.py:21
  377.3 4.7 collective-permute-done.10
  382.0 4.2 collective-permute-start.11
  386.2 3.2 collective-permute-done.11
  389.4 8.0 %collective-permute-start.12 = (bf16[256,128]{1,0:T(8,128)(2,1)}, bf16[256,128]{1,0:T(8,128)(2,1)S(1)}, u32[]{:S(2)}, u32[]{:S(2)}) collective-permute-start(bf16[256,128]{1,0:T(8,128)(2,1)} %param.23), channel_id=1, source_target_pairs={{0,40},{8,48},{16,56},{24,64},{32,72},{40,80},{48,88},{56,96},{64,... | collective-permute-start | bytes 196616 | tf_op jit(solution)/shard_map/ppermute | solution.py:21
  397.4 4.2 collective-permute-done.12
  401.6 3.8 collective-permute-start.13
  405.4 5.0 collective-permute-done.13
  410.4 8.1 %collective-permute-start.14 = (bf16[256,128]{1,0:T(8,128)(2,1)}, bf16[256,128]{1,0:T(8,128)(2,1)S(1)}, u32[]{:S(2)}, u32[]{:S(2)}) collective-permute-start(bf16[256,128]{1,0:T(8,128)(2,1)} %param.23), channel_id=1, source_target_pairs={{0,24},{8,32},{16,40},{24,48},{32,56},{40,64},{48,72},{56,80},{64,... | collective-permute-start | bytes 196616 | tf_op jit(solution)/shard_map/ppermute | solution.py:21
  418.6 8.9 %collective-permute-done.14 = bf16[256,128]{1,0:T(8,128)(2,1)S(1)} collective-permute-done((bf16[256,128]{1,0:T(8,128)(2,1)}, bf16[256,128]{1,0:T(8,128)(2,1)S(1)}, u32[]{:S(2)}, u32[]{:S(2)}) %collective-permute-start.14) | collective-permute-done | bytes 65568 | tf_op jit(solution)/shard_map/ppermute | solution.py:21
  427.5 4.3 collective-permute-start.15
  431.8 4.1 collective-permute-done.15
  436.0 7.1 %collective-permute-start.16 = (bf16[256,128]{1,0:T(8,128)(2,1)}, bf16[256,128]{1,0:T(8,128)(2,1)S(1)}, u32[]{:S(2)}, u32[]{:S(2)}) collective-permute-start(bf16[256,128]{1,0:T(8,128)(2,1)} %param.23), channel_id=1, source_target_pairs={{0,8},{8,16},{16,24},{24,32},{32,40},{40,48},{48,56},{56,64},{64,7... | collective-permute-start | bytes 196616 | tf_op jit(solution)/shard_map/ppermute | solution.py:21
  443.1 9.0 %collective-permute-done.16 = bf16[256,128]{1,0:T(8,128)(2,1)S(1)} collective-permute-done((bf16[256,128]{1,0:T(8,128)(2,1)}, bf16[256,128]{1,0:T(8,128)(2,1)S(1)}, u32[]{:S(2)}, u32[]{:S(2)}) %collective-permute-start.16) | collective-permute-done | bytes 65568 | tf_op jit(solution)/shard_map/ppermute | solution.py:21
  452.1 4.1 collective-permute-start.1
  456.2 2.0 collective-permute-done.1
  458.2 3.1 collective-permute-start.2
  461.4 7.8 %collective-permute-done.2 = bf16[256,128]{0,1:T(8,128)(2,1)S(1)} collective-permute-done((bf16[256,128]{0,1:T(8,128)(2,1)S(1)}, bf16[256,128]{0,1:T(8,128)(2,1)S(1)}, u32[]{:S(2)}, u32[]{:S(2)}) %collective-permute-start.2) | collective-permute-done | bytes 65568 | tf_op jit(solution)/shard_map/ppermute | solution.py:21
  469.2 2.6 collective-permute-start.3
  471.8 4.8 collective-permute-done.3
  476.7 4.2 collective-permute-start.4
  480.9 7.6 %collective-permute-done.4 = bf16[256,128]{0,1:T(8,128)(2,1)S(1)} collective-permute-done((bf16[256,128]{0,1:T(8,128)(2,1)S(1)}, bf16[256,128]{0,1:T(8,128)(2,1)S(1)}, u32[]{:S(2)}, u32[]{:S(2)}) %collective-permute-start.4) | collective-permute-done | bytes 65568 | tf_op jit(solution)/shard_map/ppermute | solution.py:21
  488.6 8.1 %fusion.9 = (f32[8,256]{1,0:T(8,128)S(1)}, f32[2304,256,8]{1,0,2:T(8,128)}) fusion(pred[256,2304]{0,1:T(8,128)(4,1)S(1)} %fusion.18, bf16[2304,128]{1,0:T(8,128)(2,1)S(1)} %constant_dynamic-update-slice_fusion.9, bf16[256,1024]{1,0:T(8,128)(2,1)S(1)} %copy-done.4), kind=kOutput, calls=%fused_computation.135 | convolution fusion | flops 1222113280 | bytes 20586496 | tf_op jit(solution)/shard_map/tkgd,skd->kgts/dot_general | solution.py:187
  496.8 10.3 %convert_reduce_fusion = f32[8,256]{1,0:T(8,128)S(1)} fusion(f32[8,256]{1,0:T(8,128)S(1)} %get-tuple-element.462, f32[2304,256,8]{1,0,2:T(8,128)} %get-tuple-element.463, pred[256,2304]{0,1:T(8,128)(4,1)S(1)} %fusion.18), kind=kLoop, calls=%fused_computation.139 | loop fusion | flops 28309504 | bytes 19480576 | tf_op jit(solution)/shard_map/reduce_sum | solution.py:201
  507.0 9.0 %divide_convert_fusion = bf16[256,1,8,128]{0,3,2,1:T(8,128)(2,1)S(1)} fusion(bf16[2304,128]{0,1:T(8,128)(2,1)S(1)} %copy-done.32, f32[256,8]{0,1:T(8,128)S(1)} %bitcast.616, f32[2304,256,8]{1,0,2:T(8,128)} %get-tuple-element.463, f32[8,256]{1,0:T(8,128)S(1)} %get-tuple-element.462, pred[256,2304]{0,1:T(8,128)(4,1)S(1)} %fusion.18), kind=kOutput, calls=%fused_computation.173 | convolution fusion | flops 1227358208 | bytes 20594688 | tf_op jit(solution)/shard_map/kgts,skd->tkgd/dot_general | solution.py:202
  517.1 53.2 %all-gather.7.cloned.1.call-done = f32[256,16,256]{2,1,0:T(8,128)} async-done(((f32[8,16,256]{2,1,0:T(8,128)}), f32[256,16,256]{2,1,0:T(8,128)}) %all-gather.7.cloned.1.call-update) | async-done | bytes 4194320 | tf_op jit(solution)/shard_map/all_gather | solution.py:26
  570.3 35.1 %while.42 = (s32[]{:T(128)}, f32[8,16,256]{2,1,0:T(8,128)S(1)}, s32[]{:T(128)}, f32[32,8,16,256]{3,2,1,0:T(8,128)}, f32[32,8,16,256]{3,2,1,0:T(8,128)}, /*index=5*/s32[]{:T(128)}, s32[]{:T(128)}) while((s32[]{:T(128)}, f32[8,16,256]{2,1,0:T(8,128)S(1)}, s32[]{:T(128)}, f32[32,8,16,256]{3,2,1,0:T(8,128)}, ...), condition=%wide.region_24.25_spmd.clone, body=%wide.region_23.24_spmd.clone.sunk | while | flops 131076 | bytes 524397 | solution.py:38
  605.6 23.8 %while.41 = (s32[]{:T(128)}, f32[8,256,256]{2,1,0:T(8,128)S(1)}, f32[8,256,256]{2,1,0:T(8,128)}, f32[16,256]{1,0:T(8,128)S(1)}, f32[8,16,256]{2,1,0:T(8,128)S(1)...) while((s32[]{:T(128)}, f32[8,256,256]{2,1,0:T(8,128)S(1)}, ...), condition=%wide.region_27.28_spmd, body=%wide.region_25.27_spmd.sunk | while | flops 4198402 | bytes 1949801 | solution.py:175
  631.4 2.8 fusion.21
  (1640 shorter events, 294.9 us)
Async XLA Ops:
  7.2 91.9 %copy-start = (bf16[512,2048]{1,0:T(8,128)(2,1)S(1)}, bf16[512,2048]{1,0:T(8,128)(2,1)}, u32[]{:S(2)}) copy-start(bf16[512,2048]{1,0:T(8,128)(2,1)} %param.30) | copy-start | bytes 6291460
  7.2 15.4 %copy-start.28 = (f32[2048]{0:T(1024)S(1)}, f32[2048]{0:T(1024)}, u32[]{:S(2)}) copy-start(f32[2048]{0:T(1024)} %param.26) | copy-start | bytes 24580
  7.2 90.7 %all-reduce.20.cloned.1.call-start = ((), (), s32[]{:S(2)}) async-start(), calls=%async_computation | async-start | bytes 1048576 | tf_op jit(solution)/shard_map/psum | solution.py:133
  8.1 12.9 %collective-permute-start = (bf16[3,2048]{1,0:T(4,128)(2,1)S(1)}, bf16[3,2048]{1,0:T(4,128)(2,1)S(1)}, u32[]{:S(2)}, u32[]{:S(2)}) collective-permute-start(bf16[3,2048]{1,0:T(4,128)(2,1)S(1)} %slice.364), channel_id=1, source_target_pairs={{0,8},{8,16},{16,24},{24,32},{32,40},{40,48},{48,56},{56,64},{64,7... | collective-permute-start | bytes 36872 | tf_op jit(solution)/shard_map/ppermute | solution.py:21
  18.2 5.7 copy-start.19
  18.2 5.7 copy-start.21
  18.2 5.7 copy-start.23
  18.2 5.7 copy-start.25
  26.5 72.6 %copy-start.34 = (f32[2048]{0:T(1024)S(1)}, f32[2048]{0:T(1024)}, u32[]{:S(2)}) copy-start(f32[2048]{0:T(1024)} %param.31) | copy-start | bytes 24580
  26.5 72.6 %copy-start.35 = (f32[512]{0:T(512)S(1)}, f32[512]{0:T(512)}, u32[]{:S(2)}) copy-start(f32[512]{0:T(512)} %param.29) | copy-start | bytes 6148
  26.5 490.6 %all-gather.5.cloned.1.call-start = ((), (), s32[]{:S(2)}) async-start(), calls=%async_computation.1 | async-start | bytes 4325376 | tf_op jit(solution)/shard_map/all_gather | solution.py:26
  120.5 5.7 copy-start.15
  120.5 5.7 copy-start.16
  150.0 5.7 copy-start.15
  150.0 5.7 copy-start.16
  179.5 5.7 copy-start.15
  179.5 5.7 copy-start.16
  209.0 5.7 copy-start.15
  209.0 5.7 copy-start.16
  238.4 5.7 copy-start.15
  238.4 5.7 copy-start.16
  267.9 5.7 copy-start.15
  267.9 5.7 copy-start.16
  297.3 5.7 copy-start.15
  297.4 5.7 copy-start.16
  326.8 5.7 copy-start.15
  326.8 5.7 copy-start.16
  343.1 113.1 %copy-start.27 = (bf16[256,128]{1,0:T(8,128)(2,1)S(1)}, bf16[256,128]{1,0:T(8,128)(2,1)}, u32[]{:S(2)}) copy-start(bf16[256,128]{1,0:T(8,128)(2,1)} %param.23) | copy-start | bytes 196612
  343.1 145.6 %copy-start.4 = (bf16[256,1024]{1,0:T(8,128)(2,1)S(1)}, bf16[256,1024]{1,0:T(8,128)(2,1)}, u32[]{:S(2)}) copy-start(bf16[256,1024]{1,0:T(8,128)(2,1)} %param.22) | copy-start | bytes 1572868
  343.1 227.2 %all-gather.7.cloned.1.call-start = ((), (), s32[]{:S(2)}) async-start(), calls=%async_computation.2 | async-start | bytes 4325376 | tf_op jit(solution)/shard_map/all_gather | solution.py:26
  344.8 143.8 %collective-permute-start.8 = (bf16[256,128]{0,1:T(8,128)(2,1)S(1)}, bf16[256,128]{0,1:T(8,128)(2,1)S(1)}, u32[]{:S(2)}, u32[]{:S(2)}) collective-permute-start(bf16[256,128]{0,1:T(8,128)(2,1)S(1)} %copy.313), channel_id=1, source_target_pairs={{0,8},{8,16},{16,24},{24,32},{32,40},{40,48},{48,56},{56,64},{64,7... | collective-permute-start | bytes 196616 | tf_op jit(solution)/shard_map/ppermute | solution.py:21
  350.1 138.4 %collective-permute-start.7 = (bf16[256,128]{0,1:T(8,128)(2,1)S(1)}, bf16[256,128]{0,1:T(8,128)(2,1)S(1)}, u32[]{:S(2)}, u32[]{:S(2)}) collective-permute-start(bf16[256,128]{0,1:T(8,128)(2,1)S(1)} %copy.313), channel_id=1, source_target_pairs={{0,16},{8,24},{16,32},{24,40},{32,48},{40,56},{48,64},{56,72},{64,... | collective-permute-start | bytes 196616 | tf_op jit(solution)/shard_map/ppermute | solution.py:21
  353.5 135.0 %collective-permute-start.6 = (bf16[256,128]{0,1:T(8,128)(2,1)S(1)}, bf16[256,128]{0,1:T(8,128)(2,1)S(1)}, u32[]{:S(2)}, u32[]{:S(2)}) collective-permute-start(bf16[256,128]{0,1:T(8,128)(2,1)S(1)} %copy.313), channel_id=1, source_target_pairs={{0,24},{8,32},{16,40},{24,48},{32,56},{40,64},{48,72},{56,80},{64,... | collective-permute-start | bytes 196616 | tf_op jit(solution)/shard_map/ppermute | solution.py:21
  359.4 129.1 %collective-permute-start.5 = (bf16[256,128]{0,1:T(8,128)(2,1)S(1)}, bf16[256,128]{0,1:T(8,128)(2,1)S(1)}, u32[]{:S(2)}, u32[]{:S(2)}) collective-permute-start(bf16[256,128]{0,1:T(8,128)(2,1)S(1)} %copy.313), channel_id=1, source_target_pairs={{0,32},{8,40},{16,48},{24,56},{32,64},{40,72},{48,80},{56,88},{64,... | collective-permute-start | bytes 196616 | tf_op jit(solution)/shard_map/ppermute | solution.py:21
  364.3 6.4 %collective-permute-start.9 = (bf16[256,128]{1,0:T(8,128)(2,1)}, bf16[256,128]{1,0:T(8,128)(2,1)S(1)}, u32[]{:S(2)}, u32[]{:S(2)}) collective-permute-start(bf16[256,128]{1,0:T(8,128)(2,1)} %param.23), channel_id=1, source_target_pairs={{0,64},{8,72},{16,80},{24,88},{32,96},{40,104},{48,112},{56,120},{... | collective-permute-start | bytes 196616 | tf_op jit(solution)/shard_map/ppermute | solution.py:21
  370.8 11.3 %collective-permute-start.10 = (bf16[256,128]{1,0:T(8,128)(2,1)}, bf16[256,128]{1,0:T(8,128)(2,1)S(1)}, u32[]{:S(2)}, u32[]{:S(2)}) collective-permute-start(bf16[256,128]{1,0:T(8,128)(2,1)} %param.23), channel_id=1, source_target_pairs={{0,56},{8,64},{16,72},{24,80},{32,88},{40,96},{48,104},{56,112},{6... | collective-permute-start | bytes 196616 | tf_op jit(solution)/shard_map/ppermute | solution.py:21
  382.0 7.4 %collective-permute-start.11 = (bf16[256,128]{1,0:T(8,128)(2,1)}, bf16[256,128]{1,0:T(8,128)(2,1)S(1)}, u32[]{:S(2)}, u32[]{:S(2)}) collective-permute-start(bf16[256,128]{1,0:T(8,128)(2,1)} %param.23), channel_id=1, source_target_pairs={{0,48},{8,56},{16,64},{24,72},{32,80},{40,88},{48,96},{56,104},{64... | collective-permute-start | bytes 196616 | tf_op jit(solution)/shard_map/ppermute | solution.py:21
  389.4 12.2 %collective-permute-start.12 = (bf16[256,128]{1,0:T(8,128)(2,1)}, bf16[256,128]{1,0:T(8,128)(2,1)S(1)}, u32[]{:S(2)}, u32[]{:S(2)}) collective-permute-start(bf16[256,128]{1,0:T(8,128)(2,1)} %param.23), channel_id=1, source_target_pairs={{0,40},{8,48},{16,56},{24,64},{32,72},{40,80},{48,88},{56,96},{64,... | collective-permute-start | bytes 196616 | tf_op jit(solution)/shard_map/ppermute | solution.py:21
  401.6 8.9 %collective-permute-start.13 = (bf16[256,128]{1,0:T(8,128)(2,1)}, bf16[256,128]{1,0:T(8,128)(2,1)S(1)}, u32[]{:S(2)}, u32[]{:S(2)}) collective-permute-start(bf16[256,128]{1,0:T(8,128)(2,1)} %param.23), channel_id=1, source_target_pairs={{0,32},{8,40},{16,48},{24,56},{32,64},{40,72},{48,80},{56,88},{64,... | collective-permute-start | bytes 196616 | tf_op jit(solution)/shard_map/ppermute | solution.py:21
  410.4 17.0 %collective-permute-start.14 = (bf16[256,128]{1,0:T(8,128)(2,1)}, bf16[256,128]{1,0:T(8,128)(2,1)S(1)}, u32[]{:S(2)}, u32[]{:S(2)}) collective-permute-start(bf16[256,128]{1,0:T(8,128)(2,1)} %param.23), channel_id=1, source_target_pairs={{0,24},{8,32},{16,40},{24,48},{32,56},{40,64},{48,72},{56,80},{64,... | collective-permute-start | bytes 196616 | tf_op jit(solution)/shard_map/ppermute | solution.py:21
  427.5 8.5 %collective-permute-start.15 = (bf16[256,128]{1,0:T(8,128)(2,1)}, bf16[256,128]{1,0:T(8,128)(2,1)S(1)}, u32[]{:S(2)}, u32[]{:S(2)}) collective-permute-start(bf16[256,128]{1,0:T(8,128)(2,1)} %param.23), channel_id=1, source_target_pairs={{0,16},{8,24},{16,32},{24,40},{32,48},{40,56},{48,64},{56,72},{64,... | collective-permute-start | bytes 196616 | tf_op jit(solution)/shard_map/ppermute | solution.py:21
  436.0 16.1 %collective-permute-start.16 = (bf16[256,128]{1,0:T(8,128)(2,1)}, bf16[256,128]{1,0:T(8,128)(2,1)S(1)}, u32[]{:S(2)}, u32[]{:S(2)}) collective-permute-start(bf16[256,128]{1,0:T(8,128)(2,1)} %param.23), channel_id=1, source_target_pairs={{0,8},{8,16},{16,24},{24,32},{32,40},{40,48},{48,56},{56,64},{64,7... | collective-permute-start | bytes 196616 | tf_op jit(solution)/shard_map/ppermute | solution.py:21
  452.1 6.1 collective-permute-start.1
  458.2 11.0 %collective-permute-start.2 = (bf16[256,128]{0,1:T(8,128)(2,1)S(1)}, bf16[256,128]{0,1:T(8,128)(2,1)S(1)}, u32[]{:S(2)}, u32[]{:S(2)}) collective-permute-start(bf16[256,128]{0,1:T(8,128)(2,1)S(1)} %copy.313), channel_id=1, source_target_pairs={{0,56},{8,64},{16,72},{24,80},{32,88},{40,96},{48,104},{56,112},{6... | collective-permute-start | bytes 196616 | tf_op jit(solution)/shard_map/ppermute | solution.py:21
  469.2 7.5 %collective-permute-start.3 = (bf16[256,128]{0,1:T(8,128)(2,1)S(1)}, bf16[256,128]{0,1:T(8,128)(2,1)S(1)}, u32[]{:S(2)}, u32[]{:S(2)}) collective-permute-start(bf16[256,128]{0,1:T(8,128)(2,1)S(1)} %copy.313), channel_id=1, source_target_pairs={{0,48},{8,56},{16,64},{24,72},{32,80},{40,88},{48,96},{56,104},{64... | collective-permute-start | bytes 196616 | tf_op jit(solution)/shard_map/ppermute | solution.py:21
  476.7 11.9 %collective-permute-start.4 = (bf16[256,128]{0,1:T(8,128)(2,1)S(1)}, bf16[256,128]{0,1:T(8,128)(2,1)S(1)}, u32[]{:S(2)}, u32[]{:S(2)}) collective-permute-start(bf16[256,128]{0,1:T(8,128)(2,1)S(1)} %copy.313), channel_id=1, source_target_pairs={{0,40},{8,48},{16,56},{24,64},{32,72},{40,80},{48,88},{56,96},{64,... | collective-permute-start | bytes 196616 | tf_op jit(solution)/shard_map/ppermute | solution.py:21
  488.6 8.1 %copy-start.31 = (bf16[2304,128]{0,1:T(8,128)(2,1)}, bf16[2304,128]{0,1:T(8,128)(2,1)S(1)}, u32[]{:S(2)}) copy-start(bf16[2304,128]{0,1:T(8,128)(2,1)S(1)} %constant_dynamic-update-slice_fusion) | copy-start | bytes 1769476
  496.8 10.3 %copy-start.32 = (bf16[2304,128]{0,1:T(8,128)(2,1)S(1)}, bf16[2304,128]{0,1:T(8,128)(2,1)}, u32[]{:S(2)}) copy-start(bf16[2304,128]{0,1:T(8,128)(2,1)} %copy-done.31) | copy-start | bytes 1769476
  (85 other events, 399.2 us)
Sparse Core Ops, SparseCore 0:
  26.7 71.2 all-reduce.19
  343.2 115.6 all-gather.4
  462.9 107.3 all-gather.6
where the time goes:
time: 645 us; the launch traced here: 641 us
  local copies, waits for them, and re-layouts  179 us (28%)
  waiting for transfers between devices  162 us (25%)
  other arithmetic  137 us (21%)
  starting transfers between devices  87.9 us (14%)
  blocking collectives  28.5 us (4%)
  matrix products  21.9 us (3%)
  between operations  14.5 us (2%)
  loops' own time  9.38 us (1%)
    ppermute x17, starting transfers between devices, shifted(): lax.ppermute(value, axis, [(source, source + steps) for source in range(f...  87.7 us
    while x584, local copies, waits for them, and re-layouts  75.7 us
    ppermute x17, waiting for transfers between devices, shifted(): lax.ppermute(value, axis, [(source, source + steps) for source in range(f...  66.2 us
    all_gather x2, waiting for transfers between devices, prefix(): everything = jax.tree.map(lambda part: lax.all_gather(part, axis), value)  53.2 us
    reduce_sum x56, other arithmetic, block_states(): jnp.sum(output_blocks[:, :, offset, None] * hidden_state, axis=0)  46.7 us
    psum x1, waiting for transfers between devices, per_device(): rank_low, state_in = lax.psum((rank_part, state_parts), 'tp')  42.3 us
    select_n x32, other arithmetic, step(): return jax.tree.map(lambda a, b: jnp.where(reached, a, b), new, before)  34.5 us
    psum x1, blocking collectives, per_device(): rank_low, state_in = lax.psum((rank_part, state_parts), 'tp')  28.5 us
  transfers between devices with their start and end apart: 20, of which 15 were waited for; matrix products, arithmetic and copies ran while one was open for 5% of the time, Pallas kernels for 0%

commit v1 on v0

v1 whole, which is shorter than its diff:
```python
import functools
import math

import jax
import jax.numpy as jnp
from jax import lax
from jax.experimental import pallas as pl
from jax.experimental.pallas import tpu as pltpu
from jax.sharding import PartitionSpec as P

KCONV = 4
HD = 128
WINDOW = 2048
SUBLANES = 8
LANE_BLOCK = 128
epsilon = 1e-06


def shifted(value, axis, steps):
    count = lax.axis_size(axis)
    first, last = (max(0, -steps), min(count, count - steps))
    return lax.ppermute(value, axis, [(source, source + steps) for source in range(first, last)])


def causal_conv(padded, conv_weight, conv_bias, length):
    summed = conv_bias[None, :] + jnp.zeros((length, padded.shape[1]), jnp.float32)
    for offset in range(KCONV):
        summed = summed + conv_weight[offset][None, :] * padded[offset : offset + length]
    return jax.nn.silu(summed).astype(jnp.bfloat16)


def rank_norm(rank_low, dt_gain):
    mean_square = jnp.mean(rank_low * rank_low, axis=-1, keepdims=True)
    return (rank_low * lax.rsqrt(mean_square + epsilon) * dt_gain[None, :]).astype(jnp.bfloat16)


def scan_kernel(with_out, bc_ref, dt_ref, dr_ref, rate_ref, h0_ref, out_ref):
    states = rate_ref.shape[0]
    tokens = dt_ref.shape[0]
    neg_rate = [-rate_ref[n] for n in range(states)]

    def body(t, hs):
        dt = dt_ref[t]
        dr = dr_ref[t]
        new = []
        acc = None
        for n in range(states):
            h = jnp.exp(neg_rate[n] * dt) * hs[n] + bc_ref[n, t] * dr
            new.append(h)
            if with_out:
                term = bc_ref[states + n, t] * h
                acc = term if acc is None else acc + term
        if with_out:
            out_ref[t] = acc
        return tuple(new)

    hs = lax.fori_loop(0, tokens, body, tuple(h0_ref[n] for n in range(states)), unroll=2)
    if not with_out:
        for n in range(states):
            out_ref[n] = hs[n]


def run_scan(bc, dt3, dr3, rate3, h0, with_out):
    tokens, sub, lanes = dt3.shape
    states = rate3.shape[0]
    blocks = lanes // LANE_BLOCK
    row_spec = pl.BlockSpec((tokens, sub, LANE_BLOCK), lambda j: (0, 0, j))
    state_spec = pl.BlockSpec((states, sub, LANE_BLOCK), lambda j: (0, 0, j))
    out_shape = (tokens, sub, lanes) if with_out else (states, sub, lanes)
    elems = tokens * states * sub * lanes
    return pl.pallas_call(
        functools.partial(scan_kernel, with_out),
        grid=(blocks,),
        in_specs=[
            pl.BlockSpec(memory_space=pltpu.SMEM),
            row_spec,
            row_spec,
            state_spec,
            state_spec,
        ],
        out_specs=row_spec if with_out else state_spec,
        out_shape=jax.ShapeDtypeStruct(out_shape, jnp.float32),
        cost_estimate=pl.CostEstimate(
            flops=(6 if with_out else 4) * elems,
            transcendentals=elems,
            bytes_accessed=4 * (3 * tokens * sub * lanes + 2 * states * sub * lanes),
        ),
    )(bc, dt3, dr3, rate3, h0)


def entering_state(step_sum, final_state, rate3):
    packed = jnp.concatenate([step_sum[None], final_state], axis=0)
    gathered = lax.all_gather(packed, "seq")
    peers = gathered.shape[0]
    me = lax.axis_index("seq")
    sums = gathered[:, 0]
    states = gathered[:, 1:]
    earlier = jnp.arange(peers) < me
    masked = jnp.where(earlier[:, None, None], sums, 0.0)
    suffix = jnp.cumsum(masked[::-1], axis=0)[::-1]
    between = jnp.concatenate([suffix[1:], jnp.zeros_like(suffix[:1])], axis=0)
    weight = jnp.where(
        earlier[:, None, None, None], jnp.exp(-rate3[None] * between[:, None]), 0.0
    )
    return jnp.sum(weight * states, axis=0)


def per_device(
    conv_in,
    gate_in,
    q_proj,
    k_proj,
    v_proj,
    conv_weight,
    conv_bias,
    proj_dt_weight,
    proj_bc_weight,
    dt_gain,
    dt_weight,
    dt_bias,
    decay_rate,
    skip_weight,
):
    tokens_here, channels = conv_in.shape
    key_span = WINDOW // tokens_here
    conv_tail = conv_in[tokens_here - (KCONV - 1) :]
    neighbour = shifted((k_proj, v_proj, conv_tail), "seq", 1)
    key_blocks = [k_proj, neighbour[0]]
    value_blocks = [v_proj, neighbour[1]]
    for distance in range(2, key_span + 1):
        distant = shifted((k_proj, v_proj), "seq", distance)
        key_blocks.append(distant[0])
        value_blocks.append(distant[1])
    padded = jnp.concatenate([neighbour[2], conv_in], axis=0).astype(jnp.float32)
    activated = causal_conv(padded, conv_weight, conv_bias, tokens_here)
    state_parts = lax.dot_general(
        proj_bc_weight, activated, (((1,), (1,)), ((), ())), preferred_element_type=jnp.float32
    )
    rank_part = jnp.dot(activated, proj_dt_weight, preferred_element_type=jnp.float32)
    rank_low, state_in = lax.psum((rank_part, state_parts), "tp")
    rank_normed = rank_norm(rank_low, dt_gain)
    step_size = jax.nn.softplus(
        jnp.dot(rank_normed, dt_weight, preferred_element_type=jnp.float32) + dt_bias[None, :]
    )
    drive_term = step_size * activated.astype(jnp.float32)
    state_count = decay_rate.shape[0]
    lanes = channels // SUBLANES
    dt3 = step_size.reshape(tokens_here, SUBLANES, lanes)
    dr3 = drive_term.reshape(tokens_here, SUBLANES, lanes)
    rate3 = decay_rate.reshape(state_count, SUBLANES, lanes)
    zero_state = jnp.zeros((state_count, SUBLANES, lanes), jnp.float32)
    local_final = run_scan(state_in, dt3, dr3, rate3, zero_state, False)
    step_sum = jnp.sum(dt3, axis=0)
    entering = entering_state(step_sum, local_final, rate3)
    mamba_sum = run_scan(state_in, dt3, dr3, rate3, entering, True).reshape(tokens_here, channels)
    mamba_out = (
        (mamba_sum + skip_weight[None, :] * activated.astype(jnp.float32))
        * jax.nn.silu(gate_in.astype(jnp.float32))
    ).astype(jnp.bfloat16)
    heads_here = q_proj.shape[1] // HD
    kv_here = k_proj.shape[1] // HD
    grouping = heads_here // kv_here
    keys_all = jnp.concatenate(key_blocks[::-1], axis=0).reshape(-1, kv_here, HD)
    values_all = jnp.concatenate(value_blocks[::-1], axis=0).reshape(-1, kv_here, HD)
    queries = q_proj.reshape(tokens_here, kv_here, grouping, HD)
    scores = jnp.einsum("tkgd,skd->kgts", queries, keys_all, preferred_element_type=jnp.float32) * (
        1.0 / math.sqrt(HD)
    )
    index_seq = lax.axis_index("seq")
    row_ids = jnp.arange(tokens_here, dtype=jnp.int32)[:, None]
    col_ids = jnp.arange((key_span + 1) * tokens_here, dtype=jnp.int32)[None, :]
    distance_all = WINDOW + row_ids - col_ids
    in_window = (
        (distance_all >= 0)
        & (distance_all < WINDOW)
        & (col_ids + index_seq * tokens_here >= WINDOW)
    )
    row_peak = jnp.max(jnp.where(in_window, scores, -jnp.inf), axis=-1, keepdims=True)
    weights = jnp.exp(jnp.where(in_window, scores - row_peak, -jnp.inf)).astype(jnp.bfloat16)
    summed = jnp.sum(weights.astype(jnp.float32), axis=-1)
    weighted = jnp.einsum("kgts,skd->tkgd", weights, values_all, preferred_element_type=jnp.float32)
    attn_out = (
        (weighted / summed.transpose(2, 0, 1)[..., None])
        .astype(jnp.bfloat16)
        .reshape(tokens_here, heads_here * HD)
    )
    return (mamba_out, attn_out)


def solution(mesh):
    return jax.shard_map(
        per_device,
        mesh=mesh,
        in_specs=(
            P("seq", "tp"),
            P("seq", "tp"),
            P("seq", "tp"),
            P("seq", "tp"),
            P("seq", "tp"),
            P(None, "tp"),
            P("tp"),
            P("tp", None),
            P(None, "tp"),
            P(),
            P(None, "tp"),
            P("tp"),
            P(None, "tp"),
            P("tp"),
        ),
        out_specs=(P("seq", "tp"), P("seq", "tp")),
        check_vma=False,
    )
```

time: 645 us -> 347 us (0.54)
  local copies, waits for them, and re-layouts: 179 us -> 25.2 us
  other arithmetic: 137 us -> 29.2 us
  waiting for transfers between devices: 162 us -> 110 us
  Pallas kernels: 0 us -> 28.4 us
  loops' own time: 9.38 us -> 0 us
    while x585 -> x0, local copies, waits for them, and re-layouts: 75.8 us -> none
    reduce_sum x72 -> x1, other arithmetic: 62.1 us -> 3.78 us  [entering_state(): return jnp.sum(weight * states, axis=0)]
    all_gather x2 -> x1, waiting for transfers between devices: 53.2 us -> 0.01 us  [entering_state(): gathered = lax.all_gather(packed, 'seq')]
    select_n x32 -> x1, other arithmetic: 34.5 us -> 1.05 us  [entering_state(): masked = jnp.where(earlier[:, None, None], sums, 0.0)]
    slice x209 -> x2, local copies, waits for them, and re-layouts: 29 us -> 0.04 us  [entering_state(): between = jnp.concatenate([suffix[1:], jnp.zeros_like(suffix[:1])], axis=0)]
    pallas_call x0 -> x2, Pallas kernels: none -> 28.4 us  [run_scan(): pl.pallas_call(functools.partial(scan_kernel, with_out), grid=(blocks,),...]
    unnamed x69 -> x64, local copies, waits for them, and re-layouts: 4.79 us -> 21.1 us
    dynamic_slice x16 -> x0, local copies, waits for them, and re-layouts: 15.6 us -> none  [per_device(): lax.map(lambda pieces: block_states(pieces[0], pieces[1], pieces[2], inpu...]
  transfers between devices with their start and end apart: 20 -> 19, of which waited for: 15 -> 14; matrix products, arithmetic and copies ran while one was open for 5% -> 13% of each run, Pallas kernels for 0% -> 0%
where the time goes in v1:
time: 347 us; the launch traced here: 344 us
  waiting for transfers between devices  110 us (32%)
  starting transfers between devices  81.5 us (23%)
  other arithmetic  29.2 us (8%)
  blocking collectives  29 us (8%)
  Pallas kernels  28.4 us (8%)
  matrix products  26 us (7%)
  local copies, waits for them, and re-layouts  25.2 us (7%)
  between operations  14.6 us (4%)
    ppermute x17, starting transfers between devices, shifted(): lax.ppermute(value, axis, [(source, source + steps) for source in range(f...  81.4 us
    ppermute x17, waiting for transfers between devices, shifted(): lax.ppermute(value, axis, [(source, source + steps) for source in range(f...  69.2 us
    psum x1, waiting for transfers between devices, per_device(): rank_low, state_in = lax.psum((rank_part, state_parts), 'tp')  41.2 us
    psum x1, blocking collectives, per_device(): rank_low, state_in = lax.psum((rank_part, state_parts), 'tp')  29 us
    pallas_call x2, Pallas kernels, run_scan(): pl.pallas_call(functools.partial(scan_kernel, with_out), grid=(blocks,),...  28.4 us
    unnamed x64, local copies, waits for them, and re-layouts  21.1 us
    dot_general x1, matrix products, per_device(): jnp.einsum('kgts,skd->tkgd', weights, values_all, preferred_element_type=...  11.3 us
    reduce_sum x1, other arithmetic, per_device(): summed = jnp.sum(weights.astype(jnp.float32), axis=-1)  10.2 us
  transfers between devices with their start and end apart: 19, of which 14 were waited for; matrix products, arithmetic and copies ran while one was open for 13% of the time, Pallas kernels for 0%

profile of v1, /device:TPU:8, one launch (start us, length us, event | category | flops | bytes accessed | tf_op | source)
XLA Modules:
  0.0 344.3 jit_solution(7766932098882746284)
XLA Ops:
  8.1 9.1 %collective-permute-start = (bf16[3,2048]{1,0:T(4,128)(2,1)S(1)}, bf16[3,2048]{1,0:T(4,128)(2,1)S(1)}, u32[]{:S(2)}, u32[]{:S(2)}) collective-permute-start(bf16[3,2048]{1,0:T(4,128)(2,1)S(1)} %slice.40), channel_id=1, source_target_pairs={{0,8},{8,16},{16,24},{24,32},{32,40},{40,48},{48,56},{56,64},{64,7... | collective-permute-start | bytes 36872 | tf_op jit(solution)/shard_map/ppermute | solution.py:22
  18.2 2.8 collective-permute-done
  21.0 1.5 maximum_convert_fusion
  25.0 1.5 fusion.38
  27.7 29.0 %psum.14.bc_ref = f32[32,256]{1,0:T(8,128)} all-reduce(f32[32,256]{1,0:T(8,128)S(1)} %convolution_bitcast_fusion), channel_id=1, replica_groups=mesh['seq'=32,'tp'=8] {'tp'}, use_global_device_ids=true, to_apply=%region_0.1 | all-reduce | flops 8192 | bytes 65536 | tf_op jit(solution)/shard_map/psum | solution.py:140
  56.7 41.2 %all-reduce.3.cloned.1.call-done = f32[256,512]{1,0:T(8,128)} async-done(((f32[256,512]{1,0:T(8,128)}), f32[256,512]{1,0:T(8,128)}) %all-reduce.3.cloned.1.call-update) | async-done | bytes 524304 | tf_op jit(solution)/shard_map/psum | solution.py:140
  99.1 4.8 %fusion.35 = (f32[2048]{0:T(1024)S(1)}, f32[256,2048]{1,0:T(8,128)}, f32[256,2048]{1,0:T(8,128)}) fusion(bf16[256,2048]{1,0:T(8,128)(2,1)S(1)} %multiply_convert_fusion, f32[2048]{0:T(1024)S(1)} %copy-done.19, bf16[512,2048]{1,0:T(8,128)(2,1)S(1)} %copy-done, f32[256,512]{1,0:T(8,128)} %all-reduce.3.cloned.1.call-done, f32[512]{0:T(512)S(1)} %copy-done.20, ...), kind=kOutput, calls=%fused_computation.76 | convolution fusion | flops 542504960 | bytes 7883776 | tf_op jit(solution)/shard_map/dot_general | solution.py:143
  103.9 4.0 %copy.46 = f32[32,8,8,256]{3,2,1,0:T(8,128)} copy(f32[32,8,8,256]{3,1,2,0:T(8,128)} %bitcast.90) | data formatting | bytes 4194304
  107.9 2.3 copy.45
  110.8 12.6 %shard_map.149 = f32[16,8,256]{2,1,0:T(8,128)} custom-call(f32[32,256]{1,0:T(8,128)} %psum.14.bc_ref, f32[256,8,256]{2,1,0:T(8,128)} %bitcast.87, f32[256,8,256]{2,1,0:T(8,128)} %bitcast.85, f32[16,8,256]{2,1,0:T(8,128)} %bitcast.93, f32[16,8,256]{2,1,0:T(8,128)} %broadcast_in_dim.56.h0_ref), custom_call_target="tpu_custom_call" | custom-call | flops 33554432 | bytes 6553600 | tf_op jit(solution)/shard_map/pallas_call | solution.py:71
  123.4 1.6 pad_maximum_fusion
  125.2 5.3 %collective-permute-start.8 = (bf16[256,128]{0,1:T(8,128)(2,1)S(1)}, bf16[256,128]{0,1:T(8,128)(2,1)}, u32[]{:S(2)}, u32[]{:S(2)}) collective-permute-start(bf16[256,128]{0,1:T(8,128)(2,1)S(1)} %copy.30), channel_id=1, source_target_pairs={{0,8},{8,16},{16,24},{24,32},{32,40},{40,48},{48,56},{56,64},{64,7... | collective-permute-start | bytes 196616 | tf_op jit(solution)/shard_map/ppermute | solution.py:22
  130.5 3.4 collective-permute-start.7
  133.9 5.9 %collective-permute-start.6 = (bf16[256,128]{0,1:T(8,128)(2,1)S(1)}, bf16[256,128]{0,1:T(8,128)(2,1)}, u32[]{:S(2)}, u32[]{:S(2)}) collective-permute-start(bf16[256,128]{0,1:T(8,128)(2,1)S(1)} %copy.30), channel_id=1, source_target_pairs={{0,24},{8,32},{16,40},{24,48},{32,56},{40,64},{48,72},{56,80},{64,... | collective-permute-start | bytes 196616 | tf_op jit(solution)/shard_map/ppermute | solution.py:22
  139.8 4.9 %collective-permute-start.5 = (bf16[256,128]{0,1:T(8,128)(2,1)S(1)}, bf16[256,128]{0,1:T(8,128)(2,1)}, u32[]{:S(2)}, u32[]{:S(2)}) collective-permute-start(bf16[256,128]{0,1:T(8,128)(2,1)S(1)} %copy.30), channel_id=1, source_target_pairs={{0,32},{8,40},{16,48},{24,56},{32,64},{40,72},{48,80},{56,88},{64,... | collective-permute-start | bytes 196616 | tf_op jit(solution)/shard_map/ppermute | solution.py:22
  144.7 3.1 collective-permute-start.9
  149.7 1.6 collective-permute-done.9
  151.3 6.6 %collective-permute-start.10 = (bf16[256,128]{1,0:T(8,128)(2,1)}, bf16[256,128]{1,0:T(8,128)(2,1)S(1)}, u32[]{:S(2)}, u32[]{:S(2)}) collective-permute-start(bf16[256,128]{1,0:T(8,128)(2,1)} %param.17), channel_id=1, source_target_pairs={{0,56},{8,64},{16,72},{24,80},{32,88},{40,96},{48,104},{56,112},{6... | collective-permute-start | bytes 196616 | tf_op jit(solution)/shard_map/ppermute | solution.py:22
  158.7 3.9 %collective-permute-done.10 = bf16[256,128]{1,0:T(8,128)(2,1)S(1)} collective-permute-done((bf16[256,128]{1,0:T(8,128)(2,1)}, bf16[256,128]{1,0:T(8,128)(2,1)S(1)}, u32[]{:S(2)}, u32[]{:S(2)}) %collective-permute-start.10) | collective-permute-done | bytes 65568 | tf_op jit(solution)/shard_map/ppermute | solution.py:22
  162.6 3.8 %collective-permute-start.11 = (bf16[256,128]{1,0:T(8,128)(2,1)}, bf16[256,128]{1,0:T(8,128)(2,1)S(1)}, u32[]{:S(2)}, u32[]{:S(2)}) collective-permute-start(bf16[256,128]{1,0:T(8,128)(2,1)} %param.17), channel_id=1, source_target_pairs={{0,48},{8,56},{16,64},{24,72},{32,80},{40,88},{48,96},{56,104},{64... | collective-permute-start | bytes 196616 | tf_op jit(solution)/shard_map/ppermute | solution.py:22
  166.4 3.4 collective-permute-done.11
  169.9 7.8 %collective-permute-start.12 = (bf16[256,128]{1,0:T(8,128)(2,1)}, bf16[256,128]{1,0:T(8,128)(2,1)S(1)}, u32[]{:S(2)}, u32[]{:S(2)}) collective-permute-start(bf16[256,128]{1,0:T(8,128)(2,1)} %param.17), channel_id=1, source_target_pairs={{0,40},{8,48},{16,56},{24,64},{32,72},{40,80},{48,88},{56,96},{64,... | collective-permute-start | bytes 196616 | tf_op jit(solution)/shard_map/ppermute | solution.py:22
  177.7 5.1 %collective-permute-done.12 = bf16[256,128]{1,0:T(8,128)(2,1)S(1)} collective-permute-done((bf16[256,128]{1,0:T(8,128)(2,1)}, bf16[256,128]{1,0:T(8,128)(2,1)S(1)}, u32[]{:S(2)}, u32[]{:S(2)}) %collective-permute-start.12) | collective-permute-done | bytes 65568 | tf_op jit(solution)/shard_map/ppermute | solution.py:22
  182.8 3.2 collective-permute-start.13
  186.0 5.6 %collective-permute-done.13 = bf16[256,128]{1,0:T(8,128)(2,1)S(1)} collective-permute-done((bf16[256,128]{1,0:T(8,128)(2,1)}, bf16[256,128]{1,0:T(8,128)(2,1)S(1)}, u32[]{:S(2)}, u32[]{:S(2)}) %collective-permute-start.13) | collective-permute-done | bytes 65568 | tf_op jit(solution)/shard_map/ppermute | solution.py:22
  191.6 7.2 %collective-permute-start.14 = (bf16[256,128]{1,0:T(8,128)(2,1)}, bf16[256,128]{1,0:T(8,128)(2,1)S(1)}, u32[]{:S(2)}, u32[]{:S(2)}) collective-permute-start(bf16[256,128]{1,0:T(8,128)(2,1)} %param.17), channel_id=1, source_target_pairs={{0,24},{8,32},{16,40},{24,48},{32,56},{40,64},{48,72},{56,80},{64,... | collective-permute-start | bytes 196616 | tf_op jit(solution)/shard_map/ppermute | solution.py:22
  198.8 9.1 %collective-permute-done.14 = bf16[256,128]{1,0:T(8,128)(2,1)S(1)} collective-permute-done((bf16[256,128]{1,0:T(8,128)(2,1)}, bf16[256,128]{1,0:T(8,128)(2,1)S(1)}, u32[]{:S(2)}, u32[]{:S(2)}) %collective-permute-start.14) | collective-permute-done | bytes 65568 | tf_op jit(solution)/shard_map/ppermute | solution.py:22
  207.9 2.6 collective-permute-start.15
  210.6 5.8 %collective-permute-done.15 = bf16[256,128]{1,0:T(8,128)(2,1)S(1)} collective-permute-done((bf16[256,128]{1,0:T(8,128)(2,1)}, bf16[256,128]{1,0:T(8,128)(2,1)S(1)}, u32[]{:S(2)}, u32[]{:S(2)}) %collective-permute-start.15) | collective-permute-done | bytes 65568 | tf_op jit(solution)/shard_map/ppermute | solution.py:22
  216.4 7.2 %collective-permute-start.16 = (bf16[256,128]{1,0:T(8,128)(2,1)}, bf16[256,128]{1,0:T(8,128)(2,1)S(1)}, u32[]{:S(2)}, u32[]{:S(2)}) collective-permute-start(bf16[256,128]{1,0:T(8,128)(2,1)} %param.17), channel_id=1, source_target_pairs={{0,8},{8,16},{16,24},{24,32},{32,40},{40,48},{48,56},{56,64},{64,7... | collective-permute-start | bytes 196616 | tf_op jit(solution)/shard_map/ppermute | solution.py:22
  223.6 8.8 %collective-permute-done.16 = bf16[256,128]{1,0:T(8,128)(2,1)S(1)} collective-permute-done((bf16[256,128]{1,0:T(8,128)(2,1)}, bf16[256,128]{1,0:T(8,128)(2,1)S(1)}, u32[]{:S(2)}, u32[]{:S(2)}) %collective-permute-start.16) | collective-permute-done | bytes 65568 | tf_op jit(solution)/shard_map/ppermute | solution.py:22
  232.4 3.4 collective-permute-start.1
  236.7 3.1 collective-permute-done.1
  239.8 2.2 collective-permute-start.2
  242.6 8.1 %collective-permute-done.2 = bf16[256,128]{0,1:T(8,128)(2,1)S(1)} collective-permute-done((bf16[256,128]{0,1:T(8,128)(2,1)S(1)}, bf16[256,128]{0,1:T(8,128)(2,1)S(1)}, u32[]{:S(2)}, u32[]{:S(2)}) %collective-permute-start.2) | collective-permute-done | bytes 65568 | tf_op jit(solution)/shard_map/ppermute | solution.py:22
  250.7 1.9 collective-permute-start.3
  253.3 4.5 %collective-permute-done.3 = bf16[256,128]{0,1:T(8,128)(2,1)S(1)} collective-permute-done((bf16[256,128]{0,1:T(8,128)(2,1)S(1)}, bf16[256,128]{0,1:T(8,128)(2,1)S(1)}, u32[]{:S(2)}, u32[]{:S(2)}) %collective-permute-start.3) | collective-permute-done | bytes 65568 | tf_op jit(solution)/shard_map/ppermute | solution.py:22
  257.8 3.9 %collective-permute-start.4 = (bf16[256,128]{0,1:T(8,128)(2,1)S(1)}, bf16[256,128]{0,1:T(8,128)(2,1)S(1)}, u32[]{:S(2)}, u32[]{:S(2)}) collective-permute-start(bf16[256,128]{0,1:T(8,128)(2,1)S(1)} %copy.30), channel_id=1, source_target_pairs={{0,40},{8,48},{16,56},{24,64},{32,72},{40,80},{48,88},{56,96},{64,... | collective-permute-start | bytes 196616 | tf_op jit(solution)/shard_map/ppermute | solution.py:22
  262.3 7.3 %collective-permute-done.4 = bf16[256,128]{0,1:T(8,128)(2,1)S(1)} collective-permute-done((bf16[256,128]{0,1:T(8,128)(2,1)S(1)}, bf16[256,128]{0,1:T(8,128)(2,1)S(1)}, u32[]{:S(2)}, u32[]{:S(2)}) %collective-permute-start.4) | collective-permute-done | bytes 65568 | tf_op jit(solution)/shard_map/ppermute | solution.py:22
  270.3 1.5 constant_dynamic-update-slice_fusion.4
  276.8 7.9 %fusion = (f32[8,256]{1,0:T(8,128)S(1)}, f32[2304,256,8]{1,0,2:T(8,128)}) fusion(pred[256,2304]{0,1:T(8,128)(4,1)S(1)} %fusion.10, bf16[2304,128]{1,0:T(8,128)(2,1)S(1)} %constant_dynamic-update-slice_fusion.9, bf16[256,1024]{1,0:T(8,128)(2,1)S(1)} %copy-done.4), kind=kOutput, calls=%fused_computation.2 | convolution fusion | flops 1222113280 | bytes 20586496 | tf_op jit(solution)/shard_map/tkgd,skd->kgts/dot_general | solution.py:166
  284.7 10.2 %convert_reduce_fusion = f32[8,256]{1,0:T(8,128)S(1)} fusion(f32[8,256]{1,0:T(8,128)S(1)} %get-tuple-element.13, f32[2304,256,8]{1,0,2:T(8,128)} %get-tuple-element.14, pred[256,2304]{0,1:T(8,128)(4,1)S(1)} %fusion.10), kind=kLoop, calls=%fused_computation.6 | loop fusion | flops 28309504 | bytes 19480576 | tf_op jit(solution)/shard_map/reduce_sum | solution.py:180
  294.9 11.3 %divide_convert_fusion = bf16[256,1,8,128]{0,3,2,1:T(8,128)(2,1)S(1)} fusion(bf16[2304,128]{0,1:T(8,128)(2,1)} %constant_dynamic-update-slice_fusion, f32[256,8]{0,1:T(8,128)S(1)} %bitcast.104, f32[2304,256,8]{1,0,2:T(8,128)} %get-tuple-element.14, f32[8,256]{1,0:T(8,128)S(1)} %get-tuple-element.13, pred[256,2304]{0,1:T(8,128)(4,1)S(1)} %fusion.10), kind=kOutput, calls=%fused_computation.40 | convolution fusion | flops 1227358208 | bytes 20594688 | tf_op jit(solution)/shard_map/kgts,skd->tkgd/dot_general | solution.py:181
  308.3 3.9 %fusion.37 = f32[32,8,256]{2,1,0:T(8,128)S(1)} fusion(f32[32,8,256]{2,1,0:T(8,128)S(1)} %rev.4), kind=kOutput, calls=%fused_computation.78 | output fusion | flops 2031616 | bytes 524288 | tf_op jit(solution)/shard_map/jit(cumsum)/reduce_window_sum | solution.py:100
  312.3 3.8 %fusion.6.h0_ref = f32[16,8,256]{2,1,0:T(8,128)} fusion(f32[32,17,8,256]{3,2,1,0:T(8,128)} %bitcast.84, f32[32,8,256]{2,1,0:T(8,128)S(1)} %concatenate.17, f32[16,8,256]{2,1,0:T(8,128)S(1)} %bitcast_negate_fusion, pred[32]{0:T(512)(128)(4,1)S(1)} %copy-done.17), kind=kLoop, calls=%fused_computation.11 | loop fusion | flops 4161536 | bytes 4718624 | tf_op jit(solution)/shard_map/reduce_sum | solution.py:105
  316.1 15.8 %shard_map.150 = f32[256,8,256]{2,1,0:T(8,128)} custom-call(f32[32,256]{1,0:T(8,128)} %psum.14.bc_ref, f32[256,8,256]{2,1,0:T(8,128)} %bitcast.88, f32[256,8,256]{2,1,0:T(8,128)} %bitcast.86, f32[16,8,256]{2,1,0:T(8,128)} %bitcast.94, f32[16,8,256]{2,1,0:T(8,128)} %fusion.6.h0_ref), custom_call_target="tpu_custom_call" | custom-call | flops 50331648 | bytes 6553600 | tf_op jit(solution)/shard_map/pallas_call | solution.py:71
  332.0 2.6 copy.48
  334.7 2.8 fusion.13
  (89 shorter events, 20.8 us)
Async XLA Ops:
  7.2 91.9 %copy-start = (bf16[512,2048]{1,0:T(8,128)(2,1)S(1)}, bf16[512,2048]{1,0:T(8,128)(2,1)}, u32[]{:S(2)}) copy-start(bf16[512,2048]{1,0:T(8,128)(2,1)} %param.24) | copy-start | bytes 6291460
  7.2 15.4 %copy-start.14 = (f32[2048]{0:T(1024)S(1)}, f32[2048]{0:T(1024)}, u32[]{:S(2)}) copy-start(f32[2048]{0:T(1024)} %param.20) | copy-start | bytes 24580
  7.2 90.7 %all-reduce.3.cloned.1.call-start = ((), (), s32[]{:S(2)}) async-start(), calls=%async_computation | async-start | bytes 1048576 | tf_op jit(solution)/shard_map/psum | solution.py:140
  8.1 12.9 %collective-permute-start = (bf16[3,2048]{1,0:T(4,128)(2,1)S(1)}, bf16[3,2048]{1,0:T(4,128)(2,1)S(1)}, u32[]{:S(2)}, u32[]{:S(2)}) collective-permute-start(bf16[3,2048]{1,0:T(4,128)(2,1)S(1)} %slice.40), channel_id=1, source_target_pairs={{0,8},{8,16},{16,24},{24,32},{32,40},{40,48},{48,56},{56,64},{64,7... | collective-permute-start | bytes 36872 | tf_op jit(solution)/shard_map/ppermute | solution.py:22
  18.2 4.4 %copy-start.9 = (f32[1,2048]{1,0:T(1,128)}, f32[1,2048]{1,0:T(1,128)S(1)}, u32[]{:S(2)}) copy-start(f32[1,2048]{1,0:T(1,128)S(1)} %get-tuple-element.10) | copy-start | bytes 24580
  18.2 4.4 %copy-start.11 = (f32[1,2048]{1,0:T(1,128)}, f32[1,2048]{1,0:T(1,128)S(1)}, u32[]{:S(2)}) copy-start(f32[1,2048]{1,0:T(1,128)S(1)} %get-tuple-element.11) | copy-start | bytes 24580
  22.6 1.4 copy-start.1
  22.6 2.4 copy-start.18
  25.0 1.6 copy-start.8
  25.0 2.3 copy-start.7
  26.5 72.5 %copy-start.19 = (f32[2048]{0:T(1024)S(1)}, f32[2048]{0:T(1024)}, u32[]{:S(2)}) copy-start(f32[2048]{0:T(1024)} %param.25) | copy-start | bytes 24580
  26.5 72.5 %copy-start.20 = (f32[512]{0:T(512)S(1)}, f32[512]{0:T(512)}, u32[]{:S(2)}) copy-start(f32[512]{0:T(512)} %param.23) | copy-start | bytes 6148
  26.5 280.7 %all-gather.3.cloned.1.call-start = ((), (), s32[]{:S(2)}) async-start(), calls=%async_computation.1 | async-start | bytes 4595712 | tf_op jit(solution)/shard_map/all_gather | solution.py:93
  103.9 4.0 %copy-start.3 = (f32[256,2048]{1,0:T(8,128)S(1)}, f32[256,2048]{1,0:T(8,128)}, u32[]{:S(2)}) copy-start(f32[256,2048]{1,0:T(8,128)} %get-tuple-element.12) | copy-start | bytes 6291460
  110.8 14.2 %copy-start.13 = (bf16[256,128]{1,0:T(8,128)(2,1)S(1)}, bf16[256,128]{1,0:T(8,128)(2,1)}, u32[]{:S(2)}) copy-start(bf16[256,128]{1,0:T(8,128)(2,1)} %param.18) | copy-start | bytes 196612
  110.8 37.1 %copy-start.6 = (f32[2,8,8,256]{3,2,1,0:T(8,128)S(1)}, f32[2,8,8,256]{3,2,1,0:T(8,128)}, u32[]{:S(2)}) copy-start(f32[2,8,8,256]{3,2,1,0:T(8,128)} %copy.47) | copy-start | bytes 393220
  123.4 153.4 %copy-start.4 = (bf16[256,1024]{1,0:T(8,128)(2,1)S(1)}, bf16[256,1024]{1,0:T(8,128)(2,1)}, u32[]{:S(2)}) copy-start(bf16[256,1024]{1,0:T(8,128)(2,1)} %param.16) | copy-start | bytes 1572868
  125.2 149.5 %collective-permute-start.8 = (bf16[256,128]{0,1:T(8,128)(2,1)S(1)}, bf16[256,128]{0,1:T(8,128)(2,1)}, u32[]{:S(2)}, u32[]{:S(2)}) collective-permute-start(bf16[256,128]{0,1:T(8,128)(2,1)S(1)} %copy.30), channel_id=1, source_target_pairs={{0,8},{8,16},{16,24},{24,32},{32,40},{40,48},{48,56},{56,64},{64,7... | collective-permute-start | bytes 196616 | tf_op jit(solution)/shard_map/ppermute | solution.py:22
  130.5 142.7 %collective-permute-start.7 = (bf16[256,128]{0,1:T(8,128)(2,1)S(1)}, bf16[256,128]{0,1:T(8,128)(2,1)}, u32[]{:S(2)}, u32[]{:S(2)}) collective-permute-start(bf16[256,128]{0,1:T(8,128)(2,1)S(1)} %copy.30), channel_id=1, source_target_pairs={{0,16},{8,24},{16,32},{24,40},{32,48},{40,56},{48,64},{56,72},{64,... | collective-permute-start | bytes 196616 | tf_op jit(solution)/shard_map/ppermute | solution.py:22
  133.9 137.8 %collective-permute-start.6 = (bf16[256,128]{0,1:T(8,128)(2,1)S(1)}, bf16[256,128]{0,1:T(8,128)(2,1)}, u32[]{:S(2)}, u32[]{:S(2)}) collective-permute-start(bf16[256,128]{0,1:T(8,128)(2,1)S(1)} %copy.30), channel_id=1, source_target_pairs={{0,24},{8,32},{16,40},{24,48},{32,56},{40,64},{48,72},{56,80},{64,... | collective-permute-start | bytes 196616 | tf_op jit(solution)/shard_map/ppermute | solution.py:22
  139.8 130.4 %collective-permute-start.5 = (bf16[256,128]{0,1:T(8,128)(2,1)S(1)}, bf16[256,128]{0,1:T(8,128)(2,1)}, u32[]{:S(2)}, u32[]{:S(2)}) collective-permute-start(bf16[256,128]{0,1:T(8,128)(2,1)S(1)} %copy.30), channel_id=1, source_target_pairs={{0,32},{8,40},{16,48},{24,56},{32,64},{40,72},{48,80},{56,88},{64,... | collective-permute-start | bytes 196616 | tf_op jit(solution)/shard_map/ppermute | solution.py:22
  144.7 6.5 %collective-permute-start.9 = (bf16[256,128]{1,0:T(8,128)(2,1)}, bf16[256,128]{1,0:T(8,128)(2,1)}, u32[]{:S(2)}, u32[]{:S(2)}) collective-permute-start(bf16[256,128]{1,0:T(8,128)(2,1)} %param.17), channel_id=1, source_target_pairs={{0,64},{8,72},{16,80},{24,88},{32,96},{40,104},{48,112},{56,120},{... | collective-permute-start | bytes 196616 | tf_op jit(solution)/shard_map/ppermute | solution.py:22
  151.3 11.3 %collective-permute-start.10 = (bf16[256,128]{1,0:T(8,128)(2,1)}, bf16[256,128]{1,0:T(8,128)(2,1)S(1)}, u32[]{:S(2)}, u32[]{:S(2)}) collective-permute-start(bf16[256,128]{1,0:T(8,128)(2,1)} %param.17), channel_id=1, source_target_pairs={{0,56},{8,64},{16,72},{24,80},{32,88},{40,96},{48,104},{56,112},{6... | collective-permute-start | bytes 196616 | tf_op jit(solution)/shard_map/ppermute | solution.py:22
  162.6 7.3 %collective-permute-start.11 = (bf16[256,128]{1,0:T(8,128)(2,1)}, bf16[256,128]{1,0:T(8,128)(2,1)S(1)}, u32[]{:S(2)}, u32[]{:S(2)}) collective-permute-start(bf16[256,128]{1,0:T(8,128)(2,1)} %param.17), channel_id=1, source_target_pairs={{0,48},{8,56},{16,64},{24,72},{32,80},{40,88},{48,96},{56,104},{64... | collective-permute-start | bytes 196616 | tf_op jit(solution)/shard_map/ppermute | solution.py:22
  169.9 13.0 %collective-permute-start.12 = (bf16[256,128]{1,0:T(8,128)(2,1)}, bf16[256,128]{1,0:T(8,128)(2,1)S(1)}, u32[]{:S(2)}, u32[]{:S(2)}) collective-permute-start(bf16[256,128]{1,0:T(8,128)(2,1)} %param.17), channel_id=1, source_target_pairs={{0,40},{8,48},{16,56},{24,64},{32,72},{40,80},{48,88},{56,96},{64,... | collective-permute-start | bytes 196616 | tf_op jit(solution)/shard_map/ppermute | solution.py:22
  182.8 8.8 %collective-permute-start.13 = (bf16[256,128]{1,0:T(8,128)(2,1)}, bf16[256,128]{1,0:T(8,128)(2,1)S(1)}, u32[]{:S(2)}, u32[]{:S(2)}) collective-permute-start(bf16[256,128]{1,0:T(8,128)(2,1)} %param.17), channel_id=1, source_target_pairs={{0,32},{8,40},{16,48},{24,56},{32,64},{40,72},{48,80},{56,88},{64,... | collective-permute-start | bytes 196616 | tf_op jit(solution)/shard_map/ppermute | solution.py:22
  191.6 16.3 %collective-permute-start.14 = (bf16[256,128]{1,0:T(8,128)(2,1)}, bf16[256,128]{1,0:T(8,128)(2,1)S(1)}, u32[]{:S(2)}, u32[]{:S(2)}) collective-permute-start(bf16[256,128]{1,0:T(8,128)(2,1)} %param.17), channel_id=1, source_target_pairs={{0,24},{8,32},{16,40},{24,48},{32,56},{40,64},{48,72},{56,80},{64,... | collective-permute-start | bytes 196616 | tf_op jit(solution)/shard_map/ppermute | solution.py:22
  207.9 8.5 %collective-permute-start.15 = (bf16[256,128]{1,0:T(8,128)(2,1)}, bf16[256,128]{1,0:T(8,128)(2,1)S(1)}, u32[]{:S(2)}, u32[]{:S(2)}) collective-permute-start(bf16[256,128]{1,0:T(8,128)(2,1)} %param.17), channel_id=1, source_target_pairs={{0,16},{8,24},{16,32},{24,40},{32,48},{40,56},{48,64},{56,72},{64,... | collective-permute-start | bytes 196616 | tf_op jit(solution)/shard_map/ppermute | solution.py:22
  216.4 16.0 %collective-permute-start.16 = (bf16[256,128]{1,0:T(8,128)(2,1)}, bf16[256,128]{1,0:T(8,128)(2,1)S(1)}, u32[]{:S(2)}, u32[]{:S(2)}) collective-permute-start(bf16[256,128]{1,0:T(8,128)(2,1)} %param.17), channel_id=1, source_target_pairs={{0,8},{8,16},{16,24},{24,32},{32,40},{40,48},{48,56},{56,64},{64,7... | collective-permute-start | bytes 196616 | tf_op jit(solution)/shard_map/ppermute | solution.py:22
  232.4 7.3 %collective-permute-start.1 = (bf16[256,128]{0,1:T(8,128)(2,1)S(1)}, bf16[256,128]{0,1:T(8,128)(2,1)S(1)}, u32[]{:S(2)}, u32[]{:S(2)}) collective-permute-start(bf16[256,128]{0,1:T(8,128)(2,1)S(1)} %copy.30), channel_id=1, source_target_pairs={{0,64},{8,72},{16,80},{24,88},{32,96},{40,104},{48,112},{56,120},{... | collective-permute-start | bytes 196616 | tf_op jit(solution)/shard_map/ppermute | solution.py:22
  239.8 11.0 %collective-permute-start.2 = (bf16[256,128]{0,1:T(8,128)(2,1)S(1)}, bf16[256,128]{0,1:T(8,128)(2,1)S(1)}, u32[]{:S(2)}, u32[]{:S(2)}) collective-permute-start(bf16[256,128]{0,1:T(8,128)(2,1)S(1)} %copy.30), channel_id=1, source_target_pairs={{0,56},{8,64},{16,72},{24,80},{32,88},{40,96},{48,104},{56,112},{6... | collective-permute-start | bytes 196616 | tf_op jit(solution)/shard_map/ppermute | solution.py:22
  250.7 7.0 %collective-permute-start.3 = (bf16[256,128]{0,1:T(8,128)(2,1)S(1)}, bf16[256,128]{0,1:T(8,128)(2,1)S(1)}, u32[]{:S(2)}, u32[]{:S(2)}) collective-permute-start(bf16[256,128]{0,1:T(8,128)(2,1)S(1)} %copy.30), channel_id=1, source_target_pairs={{0,48},{8,56},{16,64},{24,72},{32,80},{40,88},{48,96},{56,104},{64... | collective-permute-start | bytes 196616 | tf_op jit(solution)/shard_map/ppermute | solution.py:22
  257.8 11.9 %collective-permute-start.4 = (bf16[256,128]{0,1:T(8,128)(2,1)S(1)}, bf16[256,128]{0,1:T(8,128)(2,1)S(1)}, u32[]{:S(2)}, u32[]{:S(2)}) collective-permute-start(bf16[256,128]{0,1:T(8,128)(2,1)S(1)} %copy.30), channel_id=1, source_target_pairs={{0,40},{8,48},{16,56},{24,64},{32,72},{40,80},{48,88},{56,96},{64,... | collective-permute-start | bytes 196616 | tf_op jit(solution)/shard_map/ppermute | solution.py:22
  294.9 12.3 %copy-start.17 = (pred[32]{0:T(512)(128)(4,1)S(1)}, pred[32]{0:T(512)(128)(4,1)}, u32[]{:S(2)}) copy-start(pred[32]{0:T(512)(128)(4,1)} %iota_compare_fusion) | copy-start | bytes 100
  331.9 2.7 copy-start.2
  331.9 2.7 copy-start.5
  331.9 2.7 copy-start.10
  332.0 2.7 copy-start.12
  332.0 2.7 copy-start.15
  332.0 2.7 copy-start.16
Sparse Core Ops, SparseCore 0:
  26.7 71.1 all-reduce.2
  125.2 118.6 all-gather.2

commit v2 on v1

--- a/solution.py
+++ b/solution.py
@@ -88,21 +88,40 @@
     )(bc, dt3, dr3, rate3, h0)
 
 
+def compose(earlier, later, rate3):
+    decay = jnp.exp(-rate3 * later[0][None])
+    states = decay * earlier[1:] + later[1:]
+    return jnp.concatenate([(earlier[0] + later[0])[None], states], axis=0)
+
+
 def entering_state(step_sum, final_state, rate3):
-    packed = jnp.concatenate([step_sum[None], final_state], axis=0)
-    gathered = lax.all_gather(packed, "seq")
-    peers = gathered.shape[0]
-    me = lax.axis_index("seq")
-    sums = gathered[:, 0]
-    states = gathered[:, 1:]
-    earlier = jnp.arange(peers) < me
-    masked = jnp.where(earlier[:, None, None], sums, 0.0)
-    suffix = jnp.cumsum(masked[::-1], axis=0)[::-1]
-    between = jnp.concatenate([suffix[1:], jnp.zeros_like(suffix[:1])], axis=0)
-    weight = jnp.where(
-        earlier[:, None, None, None], jnp.exp(-rate3[None] * between[:, None]), 0.0
-    )
-    return jnp.sum(weight * states, axis=0)
+    local = jnp.concatenate([step_sum[None], final_state], axis=0)
+    peers = lax.axis_size("seq")
+    running = shifted(local, "seq", 1)
+    distance = 1
+    while distance < peers - 1:
+        running = compose(shifted(running, "seq", distance), running, rate3)
+        distance *= 2
+    return running[1:]
+
+
+def window_blocks(k_proj, v_proj, conv_tail, key_span):
+    tokens = k_proj.shape[0]
+    own = jnp.concatenate([k_proj, v_proj], axis=1)
+    width = own.shape[1]
+    tail = conv_tail.reshape(-1, width)
+    first = shifted(jnp.concatenate([own, tail], axis=0), "seq", 1)
+    tail_in = first[tokens:].reshape(conv_tail.shape)
+    held = [first[:tokens], own]
+    reach = 2
+    while reach * 2 <= key_span:
+        held = [shifted(jnp.concatenate(held, axis=0), "seq", reach)] + held
+        reach *= 2
+    assert reach == key_span
+    held = [shifted(own, "seq", key_span)] + held
+    window = jnp.concatenate(held, axis=0)
+    half = k_proj.shape[1]
+    return window[:, :half], window[:, half:], tail_in
 
 
 def per_device(
@@ -124,20 +143,18 @@
     tokens_here, channels = conv_in.shape
     key_span = WINDOW // tokens_here
     conv_tail = conv_in[tokens_here - (KCONV - 1) :]
-    neighbour = shifted((k_proj, v_proj, conv_tail), "seq", 1)
-    key_blocks = [k_proj, neighbour[0]]
-    value_blocks = [v_proj, neighbour[1]]
-    for distance in range(2, key_span + 1):
-        distant = shifted((k_proj, v_proj), "seq", distance)
-        key_blocks.append(distant[0])
-        value_blocks.append(distant[1])
-    padded = jnp.concatenate([neighbour[2], conv_in], axis=0).astype(jnp.float32)
+    keys_window, values_window, tail_in = window_blocks(k_proj, v_proj, conv_tail, key_span)
+    padded = jnp.concatenate([tail_in, conv_in], axis=0).astype(jnp.float32)
     activated = causal_conv(padded, conv_weight, conv_bias, tokens_here)
     state_parts = lax.dot_general(
         proj_bc_weight, activated, (((1,), (1,)), ((), ())), preferred_element_type=jnp.float32
     )
     rank_part = jnp.dot(activated, proj_dt_weight, preferred_element_type=jnp.float32)
-    rank_low, state_in = lax.psum((rank_part, state_parts), "tp")
+    rank_width = rank_part.shape[1]
+    packed = jnp.concatenate([rank_part, state_parts.reshape(-1, rank_width)], axis=0)
+    total = lax.psum(packed, "tp")
+    rank_low = total[:tokens_here]
+    state_in = total[tokens_here:].reshape(state_parts.shape)
     rank_normed = rank_norm(rank_low, dt_gain)
     step_size = jax.nn.softplus(
         jnp.dot(rank_normed, dt_weight, preferred_element_type=jnp.float32) + dt_bias[None, :]
@@ -160,8 +177,8 @@
     heads_here = q_proj.shape[1] // HD
     kv_here = k_proj.shape[1] // HD
     grouping = heads_here // kv_here
-    keys_all = jnp.concatenate(key_blocks[::-1], axis=0).reshape(-1, kv_here, HD)
-    values_all = jnp.concatenate(value_blocks[::-1], axis=0).reshape(-1, kv_here, HD)
+    keys_all = keys_window.reshape(-1, kv_here, HD)
+    values_all = values_window.reshape(-1, kv_here, HD)
     queries = q_proj.reshape(tokens_here, kv_here, grouping, HD)
     scores = jnp.einsum("tkgd,skd->kgts", queries, keys_all, preferred_element_type=jnp.float32) * (
         1.0 / math.sqrt(HD)

time: 347 us -> 243 us (0.70)
  starting transfers between devices: 81.5 us -> 36.1 us
  blocking collectives: 29 us -> 0 us
  waiting for transfers between devices: 110 us -> 88.8 us
  local copies, waits for them, and re-layouts: 25.2 us -> 19.6 us
    ppermute x17 -> x10, starting transfers between devices: 81.4 us -> 36.1 us  [shifted(): lax.ppermute(value, axis, [(source, source + steps) for source in range(f...]
    ppermute x17 -> x10, waiting for transfers between devices: 69.2 us -> 30.7 us  [shifted(): lax.ppermute(value, axis, [(source, source + steps) for source in range(f...]
    psum x1 -> x0, blocking collectives: 29 us -> none  [per_device(): rank_low, state_in = lax.psum((rank_part, state_parts), 'tp')]
    psum x1, waiting for transfers between devices: 41.2 us -> 58.1 us  [per_device(): total = lax.psum(packed, 'tp')]
    unnamed x64 -> x57, local copies, waits for them, and re-layouts: 21.1 us -> 14.9 us
    concatenate x1 -> x9, other arithmetic: 1.64 us -> 6.06 us  [the longest x2 2.5 us: window_blocks(): held = [shifted(jnp.concatenate(held, axis=0), 'seq', reach)] + held]
    another operation x1 -> x0, other arithmetic: 3.93 us -> none  [entering_state(): suffix = jnp.cumsum(masked[::-1], axis=0)[::-1]]
    reduce_sum x1 -> x0, other arithmetic: 3.78 us -> none  [entering_state(): return jnp.sum(weight * states, axis=0)]
  transfers between devices with their start and end apart: 19 -> 11, of which waited for: 14 -> 6; matrix products, arithmetic and copies ran while one was open for 13% -> 22% of each run, Pallas kernels for 0% -> 5%
where the time goes in v2:
time: 243 us; the launch traced here: 239 us
  waiting for transfers between devices  88.8 us (37%)
  starting transfers between devices  36.1 us (15%)
  Pallas kernels  28.3 us (12%)
  other arithmetic  26.7 us (11%)
  matrix products  24.8 us (10%)
  local copies, waits for them, and re-layouts  19.6 us (8%)
  between operations  14.6 us (6%)
    psum x1, waiting for transfers between devices, per_device(): total = lax.psum(packed, 'tp')  58.1 us
    ppermute x10, starting transfers between devices, shifted(): lax.ppermute(value, axis, [(source, source + steps) for source in range(f...  36.1 us
    ppermute x10, waiting for transfers between devices, shifted(): lax.ppermute(value, axis, [(source, source + steps) for source in range(f...  30.7 us
    pallas_call x2, Pallas kernels, run_scan(): pl.pallas_call(functools.partial(scan_kernel, with_out), grid=(blocks,),...  28.3 us
    unnamed x57, local copies, waits for them, and re-layouts  14.9 us
    dot_general x1, matrix products, per_device(): jnp.einsum('kgts,skd->tkgd', weights, values_all, preferred_element_type=...  11.2 us
    reduce_sum x1, other arithmetic, per_device(): summed = jnp.sum(weights.astype(jnp.float32), axis=-1)  10.2 us
    dot_general x1, matrix products, per_device(): jnp.einsum('tkgd,skd->kgts', queries, keys_all, preferred_element_type=jn...  8.14 us
  transfers between devices with their start and end apart: 11, of which 6 were waited for; matrix products, arithmetic and copies ran while one was open for 22% of the time, Pallas kernels for 5%

profile of v2, /device:TPU:8, one launch (start us, length us, event | category | flops | bytes accessed | tf_op | source)
XLA Modules:
  0.0 239.0 jit_solution(7556543732819698723)
XLA Ops:
  7.2 1.0 constant_dynamic-update-slice_fusion.1
  8.2 0.8 slice.80
  9.0 0.9 constant_dynamic-update-slice_fusion
  9.9 9.1 %collective-permute-start = (bf16[280,256]{1,0:T(8,128)(2,1)S(1)}, bf16[280,256]{1,0:T(8,128)(2,1)S(1)}, u32[]{:S(2)}, u32[]{:S(2)}) collective-permute-start(bf16[280,256]{1,0:T(8,128)(2,1)S(1)} %pad_maximum_fusion.3), channel_id=1, source_target_pairs={{0,8},{8,16},{16,24},{24,32},{32,40},{40,48},{48,56},{56,64},{64,7... | collective-permute-start | bytes 430088 | tf_op jit(solution)/shard_map/ppermute | solution.py:22
  19.0 0.9 fusion.36
  20.0 4.9 %collective-permute-done = bf16[280,256]{1,0:T(8,128)(2,1)S(1)} collective-permute-done((bf16[280,256]{1,0:T(8,128)(2,1)S(1)}, bf16[280,256]{1,0:T(8,128)(2,1)S(1)}, u32[]{:S(2)}, u32[]{:S(2)}) %collective-permute-start) | collective-permute-done | bytes 143392 | tf_op jit(solution)/shard_map/ppermute | solution.py:22
  25.0 1.5 maximum_convert_fusion
  26.6 1.3 multiply_convert_fusion
  27.9 1.0 copy-done.22
  28.9 1.5 fusion.37
  30.4 1.0 convolution_bitcast_fusion
  31.5 0.8 reshape.86
  32.2 1.9 pad_maximum_fusion
  34.2 0.7 pad_maximum_fusion.2
  34.9 1.9 collective-permute-start.8
  36.8 3.5 %collective-permute-start.7 = (bf16[256,256]{1,0:T(8,128)(2,1)S(1)}, bf16[256,256]{1,0:T(8,128)(2,1)}, u32[]{:S(2)}, u32[]{:S(2)}) collective-permute-start(bf16[256,256]{1,0:T(8,128)(2,1)S(1)} %constant_dynamic-update-slice_fusion), channel_id=1, source_target_pairs={{0,64},{8,72},{16,80},{24,88},{32,96},{40,104},{48,112},{56,120},{... | collective-permute-start | bytes 393224 | tf_op jit(solution)/shard_map/ppermute | solution.py:22
  40.3 1.6 copy.26
  42.5 4.2 %collective-permute-done.8 = bf16[512,256]{1,0:T(8,128)(2,1)} collective-permute-done((bf16[512,256]{1,0:T(8,128)(2,1)}, bf16[512,256]{1,0:T(8,128)(2,1)}, u32[]{:S(2)}, u32[]{:S(2)}) %collective-permute-start.8) | collective-permute-done | bytes 262176 | tf_op jit(solution)/shard_map/ppermute | solution.py:22
  46.7 1.8 pad_maximum_fusion.1
  48.5 1.9 collective-permute-start.9
  50.4 58.1 %all-reduce.2.cloned.1.call-done = f32[272,512]{1,0:T(8,128)} async-done(((f32[272,512]{1,0:T(8,128)}), f32[272,512]{1,0:T(8,128)}) %all-reduce.2.cloned.1.call-update) | async-done | bytes 557072 | tf_op jit(solution)/shard_map/psum | solution.py:155
  108.5 1.2 multiply_reduce_fusion
  109.7 2.9 %fusion.35 = (f32[2048]{0:T(1024)S(1)}, f32[256,2048]{1,0:T(8,128)S(1)}, f32[256,2048]{1,0:T(8,128)S(1)}) fusion(bf16[256,2048]{1,0:T(8,128)(2,1)S(1)} %multiply_convert_fusion, f32[2048]{0:T(1024)} %param.25, bf16[512,2048]{1,0:T(8,128)(2,1)S(1)} %copy-done, f32[272,512]{1,0:T(8,128)} %all-reduce.2.cloned.1.call-done, f32[512]{0:T(512)} %param.23, ...), kind=kOutput, calls=%fused_computation.83 | convolution fusion | flops 542504960 | bytes 7883776 | tf_op jit(solution)/shard_map/dot_general | solution.py:160
  112.6 2.2 copy.24
  114.8 2.3 copy.25
  118.4 12.5 %shard_map.149 = f32[16,8,256]{2,1,0:T(8,128)} custom-call(f32[32,256]{1,0:T(8,128)} %reshape.87.bc_ref, f32[256,8,256]{2,1,0:T(8,128)} %bitcast.87, f32[256,8,256]{2,1,0:T(8,128)} %bitcast.89, f32[16,8,256]{2,1,0:T(8,128)} %bitcast.85, f32[16,8,256]{2,1,0:T(8,128)} %broadcast_in_dim.13.h0_ref), custom_call_target="tpu_custom_call" | custom-call | flops 33554432 | bytes 6553600 | tf_op jit(solution)/shard_map/pallas_call | solution.py:71
  130.9 1.0 pad_maximum_fusion.4
  131.8 5.4 %collective-permute-start.1 = (f32[17,8,256]{2,1,0:T(8,128)S(1)}, f32[17,8,256]{2,1,0:T(8,128)S(1)}, u32[]{:S(2)}, u32[]{:S(2)}) collective-permute-start(f32[17,8,256]{2,1,0:T(8,128)S(1)} %pad_maximum_fusion.4), channel_id=1, source_target_pairs={{0,8},{8,16},{16,24},{24,32},{32,40},{40,48},{48,56},{56,64},{64,7... | collective-permute-start | bytes 417800 | tf_op jit(solution)/shard_map/ppermute | solution.py:22
  137.3 1.3 fusion.9
  138.6 1.0 constant_dynamic-update-slice_fusion.6
  139.6 6.6 %collective-permute-done.1 = f32[17,8,256]{2,1,0:T(8,128)S(1)} collective-permute-done((f32[17,8,256]{2,1,0:T(8,128)S(1)}, f32[17,8,256]{2,1,0:T(8,128)S(1)}, u32[]{:S(2)}, u32[]{:S(2)}) %collective-permute-start.1) | collective-permute-done | bytes 139296 | tf_op jit(solution)/shard_map/ppermute | solution.py:22
  146.2 4.0 %collective-permute-start.2 = (f32[17,8,256]{2,1,0:T(8,128)S(1)}, f32[17,8,256]{2,1,0:T(8,128)S(1)}, u32[]{:S(2)}, u32[]{:S(2)}) collective-permute-start(f32[17,8,256]{2,1,0:T(8,128)S(1)} %collective-permute-done.1), channel_id=1, source_target_pairs={{0,8},{8,16},{16,24},{24,32},{32,40},{40,48},{48,56},{56,64},{64,7... | collective-permute-start | bytes 417800 | tf_op jit(solution)/shard_map/ppermute | solution.py:22
  150.2 1.1 constant_dynamic-update-slice_fusion.5
  151.3 1.0 constant_dynamic-update-slice_fusion.4
  152.3 7.9 %collective-permute-done.2 = f32[17,8,256]{2,1,0:T(8,128)S(1)} collective-permute-done((f32[17,8,256]{2,1,0:T(8,128)S(1)}, f32[17,8,256]{2,1,0:T(8,128)S(1)}, u32[]{:S(2)}, u32[]{:S(2)}) %collective-permute-start.2) | collective-permute-done | bytes 139296 | tf_op jit(solution)/shard_map/ppermute | solution.py:22
  160.2 1.9 collective-permute-start.3
  162.2 7.0 %collective-permute-done.3 = f32[17,8,256]{2,1,0:T(8,128)S(1)} collective-permute-done((f32[17,8,256]{2,1,0:T(8,128)S(1)}, f32[17,8,256]{2,1,0:T(8,128)S(1)}, u32[]{:S(2)}, u32[]{:S(2)}) %collective-permute-start.3) | collective-permute-done | bytes 139296 | tf_op jit(solution)/shard_map/ppermute | solution.py:22
  169.3 1.9 collective-permute-start.4
  171.3 8.1 %fusion = (f32[8,256]{1,0:T(8,128)S(1)}, f32[2304,256,8]{1,0,2:T(8,128)}) fusion(pred[256,2304]{0,1:T(8,128)(4,1)S(1)} %fusion.9, bf16[2304,256]{1,0:T(8,128)(2,1)S(1)} %constant_dynamic-update-slice_fusion.7, bf16[256,1024]{1,0:T(8,128)(2,1)S(1)} %copy-done.4), kind=kOutput, calls=%fused_computation.2 | convolution fusion | flops 1222113280 | bytes 20586496 | tf_op jit(solution)/shard_map/tkgd,skd->kgts/dot_general | solution.py:183
  179.5 3.6 %collective-permute-start.5 = (f32[17,8,256]{2,1,0:T(8,128)S(1)}, f32[17,8,256]{2,1,0:T(8,128)S(1)}, u32[]{:S(2)}, u32[]{:S(2)}) collective-permute-start(f32[17,8,256]{2,1,0:T(8,128)S(1)} %pad_maximum_fusion.7), channel_id=1, source_target_pairs={{0,64},{8,72},{16,80},{24,88},{32,96},{40,104},{48,112},{56,120},{... | collective-permute-start | bytes 417800 | tf_op jit(solution)/shard_map/ppermute | solution.py:22
  183.1 10.2 %convert_reduce_fusion = f32[8,256]{1,0:T(8,128)S(1)} fusion(f32[8,256]{1,0:T(8,128)S(1)} %get-tuple-element.13, f32[2304,256,8]{1,0,2:T(8,128)} %get-tuple-element.14, pred[256,2304]{0,1:T(8,128)(4,1)S(1)} %fusion.9), kind=kLoop, calls=%fused_computation.6 | loop fusion | flops 28309504 | bytes 19480576 | tf_op jit(solution)/shard_map/reduce_sum | solution.py:197
  194.1 2.8 %collective-permute-start.6 = (f32[17,8,256]{2,1,0:T(8,128)}, f32[17,8,256]{2,1,0:T(8,128)}, u32[]{:S(2)}, u32[]{:S(2)}) collective-permute-start(f32[17,8,256]{2,1,0:T(8,128)} %pad_maximum_fusion.8), channel_id=1, source_target_pairs={{0,128},{8,136},{16,144},{24,152},{32,160},{40,168},{48,176},{56,1... | collective-permute-start | bytes 417800 | tf_op jit(solution)/shard_map/ppermute | solution.py:22
  196.9 11.2 %divide_convert_fusion = bf16[256,1,8,128]{0,3,2,1:T(8,128)(2,1)S(1)} fusion(bf16[2304,256]{1,0:T(8,128)(2,1)} %copy-done.6, f32[256,8]{0,1:T(8,128)S(1)} %bitcast.108, f32[2304,256,8]{1,0,2:T(8,128)} %get-tuple-element.14, f32[8,256]{1,0:T(8,128)S(1)} %get-tuple-element.13, pred[256,2304]{0,1:T(8,128)(4,1)S(1)} %fusion.9), kind=kOutput, calls=%fused_computation.38 | convolution fusion | flops 1227358208 | bytes 20594688 | tf_op jit(solution)/shard_map/kgts,skd->tkgd/dot_general | solution.py:198
  208.1 1.0 copy.19
  209.1 1.6 fusion.30.h0_ref
  210.7 15.8 %shard_map.150 = f32[256,8,256]{2,1,0:T(8,128)} custom-call(f32[32,256]{1,0:T(8,128)} %reshape.87.bc_ref, f32[256,8,256]{2,1,0:T(8,128)} %bitcast.88, f32[256,8,256]{2,1,0:T(8,128)} %bitcast.90, f32[16,8,256]{2,1,0:T(8,128)} %bitcast.86, f32[16,8,256]{2,1,0:T(8,128)} %fusion.30.h0_ref), custom_call_target="tpu_custom_call" | custom-call | flops 50331648 | bytes 6553600 | tf_op jit(solution)/shard_map/pallas_call | solution.py:71
  226.6 2.6 %copy.27 = f32[32,8,8,256]{3,1,2,0:T(8,128)S(1)} copy(f32[32,8,8,256]{3,2,1,0:T(8,128)} %bitcast.93) | data formatting | bytes 4194304
  229.3 2.8 %fusion.12 = bf16[256,2048]{1,0:T(8,128)(2,1)} fusion(f32[256,2048]{1,0:T(8,128)S(1)} %bitcast.84, bf16[256,2048]{1,0:T(8,128)(2,1)S(1)} %copy-done.5, f32[2048]{0:T(1024)S(1)} %copy-done.20, f32[259,2048]{1,0:T(8,128)S(1)} %copy-done.2, f32[2048]{0:T(1024)S(1)} %bitcast.105, f32[2048]{0:T(1024)S(1)} %bitcast.107, f32[2048]{0:T(1024)S(1)} %bitcast.103, ...), kind=kLoop, calls=%fused_computation.22 | loop fusion | flops 12058624 | bytes 12632064 | tf_op jit(solution)/shard_map/convert_element_type | solution.py:176
  (80 shorter events, 3.0 us)
Async XLA Ops:
  7.2 102.5 %copy-start = (bf16[512,2048]{1,0:T(8,128)(2,1)S(1)}, bf16[512,2048]{1,0:T(8,128)(2,1)}, u32[]{:S(2)}) copy-start(bf16[512,2048]{1,0:T(8,128)(2,1)} %param.24) | copy-start | bytes 6291460
  7.2 19.4 %copy-start.18 = (f32[2048]{0:T(1024)S(1)}, f32[2048]{0:T(1024)}, u32[]{:S(2)}) copy-start(f32[2048]{0:T(1024)} %param.20) | copy-start | bytes 24580
  7.2 101.3 %all-reduce.2.cloned.1.call-start = ((), (), s32[]{:S(2)}) async-start(), calls=%async_computation | async-start | bytes 1114112 | tf_op jit(solution)/shard_map/psum | solution.py:155
  9.9 15.0 %collective-permute-start = (bf16[280,256]{1,0:T(8,128)(2,1)S(1)}, bf16[280,256]{1,0:T(8,128)(2,1)S(1)}, u32[]{:S(2)}, u32[]{:S(2)}) collective-permute-start(bf16[280,256]{1,0:T(8,128)(2,1)S(1)} %pad_maximum_fusion.3), channel_id=1, source_target_pairs={{0,8},{8,16},{16,24},{24,32},{32,40},{40,48},{48,56},{56,64},{64,7... | collective-permute-start | bytes 430088 | tf_op jit(solution)/shard_map/ppermute | solution.py:22
  20.0 6.5 %copy-start.10 = (f32[1,2048]{1,0:T(1,128)}, f32[1,2048]{1,0:T(1,128)S(1)}, u32[]{:S(2)}) copy-start(f32[1,2048]{1,0:T(1,128)S(1)} %get-tuple-element.8) | copy-start | bytes 24580
  20.0 6.5 %copy-start.12 = (f32[1,2048]{1,0:T(1,128)}, f32[1,2048]{1,0:T(1,128)S(1)}, u32[]{:S(2)}) copy-start(f32[1,2048]{1,0:T(1,128)S(1)} %get-tuple-element.9) | copy-start | bytes 24580
  20.0 6.5 %copy-start.14 = (f32[1,2048]{1,0:T(1,128)}, f32[1,2048]{1,0:T(1,128)S(1)}, u32[]{:S(2)}) copy-start(f32[1,2048]{1,0:T(1,128)S(1)} %get-tuple-element.10) | copy-start | bytes 24580
  20.0 6.5 %copy-start.16 = (f32[1,2048]{1,0:T(1,128)}, f32[1,2048]{1,0:T(1,128)S(1)}, u32[]{:S(2)}) copy-start(f32[1,2048]{1,0:T(1,128)S(1)} %get-tuple-element.11) | copy-start | bytes 24580
  26.5 1.4 copy-start.1
  26.6 2.3 copy-start.22
  28.9 1.5 copy-start.9
  34.9 11.8 %collective-permute-start.8 = (bf16[512,256]{1,0:T(8,128)(2,1)}, bf16[512,256]{1,0:T(8,128)(2,1)}, u32[]{:S(2)}, u32[]{:S(2)}) collective-permute-start(bf16[512,256]{1,0:T(8,128)(2,1)} %pad_maximum_fusion.2), channel_id=1, source_target_pairs={{0,16},{8,24},{16,32},{24,40},{32,48},{40,56},{48,64},{56,72},{64,... | collective-permute-start | bytes 786440 | tf_op jit(solution)/shard_map/ppermute | solution.py:22
  36.8 101.8 %collective-permute-start.7 = (bf16[256,256]{1,0:T(8,128)(2,1)S(1)}, bf16[256,256]{1,0:T(8,128)(2,1)}, u32[]{:S(2)}, u32[]{:S(2)}) collective-permute-start(bf16[256,256]{1,0:T(8,128)(2,1)S(1)} %constant_dynamic-update-slice_fusion), channel_id=1, source_target_pairs={{0,64},{8,72},{16,80},{24,88},{32,96},{40,104},{48,112},{56,120},{... | collective-permute-start | bytes 393224 | tf_op jit(solution)/shard_map/ppermute | solution.py:22
  48.5 101.7 %collective-permute-start.9 = (bf16[1024,256]{1,0:T(8,128)(2,1)}, bf16[1024,256]{1,0:T(8,128)(2,1)}, u32[]{:S(2)}, u32[]{:S(2)}) collective-permute-start(bf16[1024,256]{1,0:T(8,128)(2,1)} %pad_maximum_fusion.1), channel_id=1, source_target_pairs={{0,32},{8,40},{16,48},{24,56},{32,64},{40,72},{48,80},{56,88},{64,... | collective-permute-start | bytes 1572872 | tf_op jit(solution)/shard_map/ppermute | solution.py:22
  114.8 2.3 slice-start
  118.4 18.9 %copy-start.21 = (s32[256]{0:T(256)S(1)}, s32[256]{0:T(256)}, u32[]{:S(2)}) copy-start(s32[256]{0:T(256)} %iota_add_fusion) | copy-start | bytes 3076
  130.9 29.3 %copy-start.3 = (f32[2,8,8,256]{3,2,1,0:T(8,128)S(1)}, f32[2,8,8,256]{3,2,1,0:T(8,128)}, u32[]{:S(2)}) copy-start(f32[2,8,8,256]{3,2,1,0:T(8,128)} %copy.26) | copy-start | bytes 393220
  130.9 31.3 %copy-start.7 = (bf16[256,128]{1,0:T(8,128)(2,1)S(1)}, bf16[256,128]{1,0:T(8,128)(2,1)}, u32[]{:S(2)}) copy-start(bf16[256,128]{1,0:T(8,128)(2,1)} %param.17) | copy-start | bytes 196612
  130.9 31.3 %copy-start.8 = (bf16[256,128]{1,0:T(8,128)(2,1)S(1)}, bf16[256,128]{1,0:T(8,128)(2,1)}, u32[]{:S(2)}) copy-start(bf16[256,128]{1,0:T(8,128)(2,1)} %param.18) | copy-start | bytes 196612
  131.8 14.4 %collective-permute-start.1 = (f32[17,8,256]{2,1,0:T(8,128)S(1)}, f32[17,8,256]{2,1,0:T(8,128)S(1)}, u32[]{:S(2)}, u32[]{:S(2)}) collective-permute-start(f32[17,8,256]{2,1,0:T(8,128)S(1)} %pad_maximum_fusion.4), channel_id=1, source_target_pairs={{0,8},{8,16},{16,24},{24,32},{32,40},{40,48},{48,56},{56,64},{64,7... | collective-permute-start | bytes 417800 | tf_op jit(solution)/shard_map/ppermute | solution.py:22
  138.6 32.7 %copy-start.4 = (bf16[256,1024]{1,0:T(8,128)(2,1)S(1)}, bf16[256,1024]{1,0:T(8,128)(2,1)}, u32[]{:S(2)}) copy-start(bf16[256,1024]{1,0:T(8,128)(2,1)} %param.16) | copy-start | bytes 1572868
  146.2 14.0 %collective-permute-start.2 = (f32[17,8,256]{2,1,0:T(8,128)S(1)}, f32[17,8,256]{2,1,0:T(8,128)S(1)}, u32[]{:S(2)}, u32[]{:S(2)}) collective-permute-start(f32[17,8,256]{2,1,0:T(8,128)S(1)} %collective-permute-done.1), channel_id=1, source_target_pairs={{0,8},{8,16},{16,24},{24,32},{32,40},{40,48},{48,56},{56,64},{64,7... | collective-permute-start | bytes 417800 | tf_op jit(solution)/shard_map/ppermute | solution.py:22
  160.2 9.1 %collective-permute-start.3 = (f32[17,8,256]{2,1,0:T(8,128)S(1)}, f32[17,8,256]{2,1,0:T(8,128)S(1)}, u32[]{:S(2)}, u32[]{:S(2)}) collective-permute-start(f32[17,8,256]{2,1,0:T(8,128)S(1)} %pad_maximum_fusion.5), channel_id=1, source_target_pairs={{0,16},{8,24},{16,32},{24,40},{32,48},{40,56},{48,64},{56,72},{64,... | collective-permute-start | bytes 417800 | tf_op jit(solution)/shard_map/ppermute | solution.py:22
  162.2 17.2 %copy-start.6 = (bf16[2304,256]{1,0:T(8,128)(2,1)}, bf16[2304,256]{1,0:T(8,128)(2,1)S(1)}, u32[]{:S(2)}) copy-start(bf16[2304,256]{1,0:T(8,128)(2,1)S(1)} %constant_dynamic-update-slice_fusion.7) | copy-start | bytes 3538948
  169.3 10.1 %collective-permute-start.4 = (f32[17,8,256]{2,1,0:T(8,128)S(1)}, f32[17,8,256]{2,1,0:T(8,128)S(1)}, u32[]{:S(2)}, u32[]{:S(2)}) collective-permute-start(f32[17,8,256]{2,1,0:T(8,128)S(1)} %pad_maximum_fusion.6), channel_id=1, source_target_pairs={{0,32},{8,40},{16,48},{24,56},{32,64},{40,72},{48,80},{56,88},{64,... | collective-permute-start | bytes 417800 | tf_op jit(solution)/shard_map/ppermute | solution.py:22
  179.5 13.8 %collective-permute-start.5 = (f32[17,8,256]{2,1,0:T(8,128)S(1)}, f32[17,8,256]{2,1,0:T(8,128)S(1)}, u32[]{:S(2)}, u32[]{:S(2)}) collective-permute-start(f32[17,8,256]{2,1,0:T(8,128)S(1)} %pad_maximum_fusion.7), channel_id=1, source_target_pairs={{0,64},{8,72},{16,80},{24,88},{32,96},{40,104},{48,112},{56,120},{... | collective-permute-start | bytes 417800 | tf_op jit(solution)/shard_map/ppermute | solution.py:22
  194.1 15.1 %collective-permute-start.6 = (f32[17,8,256]{2,1,0:T(8,128)}, f32[17,8,256]{2,1,0:T(8,128)}, u32[]{:S(2)}, u32[]{:S(2)}) collective-permute-start(f32[17,8,256]{2,1,0:T(8,128)} %pad_maximum_fusion.8), channel_id=1, source_target_pairs={{0,128},{8,136},{16,144},{24,152},{32,160},{40,168},{48,176},{56,1... | collective-permute-start | bytes 417800 | tf_op jit(solution)/shard_map/ppermute | solution.py:22
  226.6 2.7 %copy-start.2 = (f32[259,2048]{1,0:T(8,128)S(1)}, f32[259,2048]{1,0:T(8,128)}, u32[]{:S(2)}) copy-start(f32[259,2048]{1,0:T(8,128)} %copy-done.1) | copy-start | bytes 6365188
  226.6 2.7 %copy-start.5 = (bf16[256,2048]{1,0:T(8,128)(2,1)S(1)}, bf16[256,2048]{1,0:T(8,128)(2,1)}, u32[]{:S(2)}) copy-start(bf16[256,2048]{1,0:T(8,128)(2,1)} %param.15) | copy-start | bytes 3145732
  226.6 2.7 %copy-start.11 = (f32[1,2048]{1,0:T(1,128)S(1)}, f32[1,2048]{1,0:T(1,128)}, u32[]{:S(2)}) copy-start(f32[1,2048]{1,0:T(1,128)} %copy-done.10) | copy-start | bytes 24580
  226.6 2.7 %copy-start.13 = (f32[1,2048]{1,0:T(1,128)S(1)}, f32[1,2048]{1,0:T(1,128)}, u32[]{:S(2)}) copy-start(f32[1,2048]{1,0:T(1,128)} %copy-done.12) | copy-start | bytes 24580
  226.6 2.7 %copy-start.15 = (f32[1,2048]{1,0:T(1,128)S(1)}, f32[1,2048]{1,0:T(1,128)}, u32[]{:S(2)}) copy-start(f32[1,2048]{1,0:T(1,128)} %copy-done.14) | copy-start | bytes 24580
  226.6 2.7 %copy-start.17 = (f32[1,2048]{1,0:T(1,128)S(1)}, f32[1,2048]{1,0:T(1,128)}, u32[]{:S(2)}) copy-start(f32[1,2048]{1,0:T(1,128)} %copy-done.16) | copy-start | bytes 24580
  226.6 2.7 %copy-start.19 = (f32[2048]{0:T(1024)S(1)}, f32[2048]{0:T(1024)}, u32[]{:S(2)}) copy-start(f32[2048]{0:T(1024)} %param.20) | copy-start | bytes 24580
  226.6 2.7 %copy-start.20 = (f32[2048]{0:T(1024)S(1)}, f32[2048]{0:T(1024)}, u32[]{:S(2)}) copy-start(f32[2048]{0:T(1024)} %param.27) | copy-start | bytes 24580
Sparse Core Ops, SparseCore 0:
  34.3 74.1 all-reduce.1

commit v3 on v2

--- a/solution.py
+++ b/solution.py
@@ -88,6 +88,16 @@
     )(bc, dt3, dr3, rate3, h0)
 
 
+def butterfly_sum(value, axis):
+    count = lax.axis_size(axis)
+    stride = 1
+    while stride < count:
+        pairs = [(source, source ^ stride) for source in range(count)]
+        value = value + lax.ppermute(value, axis, pairs)
+        stride *= 2
+    return value
+
+
 def compose(earlier, later, rate3):
     decay = jnp.exp(-rate3 * later[0][None])
     states = decay * earlier[1:] + later[1:]
@@ -152,7 +162,7 @@
     rank_part = jnp.dot(activated, proj_dt_weight, preferred_element_type=jnp.float32)
     rank_width = rank_part.shape[1]
     packed = jnp.concatenate([rank_part, state_parts.reshape(-1, rank_width)], axis=0)
-    total = lax.psum(packed, "tp")
+    total = butterfly_sum(packed, "tp")
     rank_low = total[:tokens_here]
     state_in = total[tokens_here:].reshape(state_parts.shape)
     rank_normed = rank_norm(rank_low, dt_gain)

time: 243 us -> 202 us (0.83)
  the two profiles are of different devices: /device:TPU:8 before, /device:TPU:32 now
where the time goes in v3:
time: 202 us; the launch traced here: 201 us
  starting transfers between devices  81.9 us (41%)
  Pallas kernels  28.4 us (14%)
  matrix products  23.2 us (11%)
  other arithmetic  22.9 us (11%)
  local copies, waits for them, and re-layouts  22.1 us (11%)
  waiting for transfers between devices  21.6 us (11%)
    ppermute x10, starting transfers between devices, shifted(): lax.ppermute(value, axis, [(source, source + steps) for source in range(f...  77.2 us
    pallas_call x2, Pallas kernels, run_scan(): pl.pallas_call(functools.partial(scan_kernel, with_out), grid=(blocks,),...  28.4 us
    unnamed x49, local copies, waits for them, and re-layouts  17.5 us
    ppermute x3, waiting for transfers between devices, butterfly_sum(): value = value + lax.ppermute(value, axis, pairs)  14.5 us
    dot_general x1, matrix products, per_device(): jnp.einsum('kgts,skd->tkgd', weights, values_all, preferred_element_type=...  11.2 us
    reduce_sum x1, other arithmetic, per_device(): summed = jnp.sum(weights.astype(jnp.float32), axis=-1)  10.2 us
    dot_general x1, matrix products, per_device(): jnp.einsum('tkgd,skd->kgts', queries, keys_all, preferred_element_type=jn...  8.98 us
    ppermute x10, waiting for transfers between devices, shifted(): lax.ppermute(value, axis, [(source, source + steps) for source in range(f...  7.09 us
  transfers between devices with their start and end apart: 13, of which 7 were waited for; matrix products, arithmetic and copies ran while one was open for 26% of the time, Pallas kernels for 6%

profile of v3, /device:TPU:32, one launch (start us, length us, event | category | flops | bytes accessed | tf_op | source)
XLA Modules:
  0.0 201.3 jit_solution(13238140096335335031)
XLA Ops:
  0.7 1.0 constant_dynamic-update-slice_fusion.1
  1.7 0.8 slice.80
  2.5 0.9 constant_dynamic-update-slice_fusion
  3.3 8.2 %collective-permute-start = (bf16[280,256]{1,0:T(8,128)(2,1)S(1)}, bf16[280,256]{1,0:T(8,128)(2,1)S(1)}, u32[]{:S(2)}, u32[]{:S(2)}) collective-permute-start(bf16[280,256]{1,0:T(8,128)(2,1)S(1)} %pad_maximum_fusion.3), channel_id=1, source_target_pairs={{0,8},{8,16},{16,24},{24,32},{32,40},{40,48},{48,56},{56,64},{64,7... | collective-permute-start | bytes 430088 | tf_op jit(solution)/shard_map/ppermute | solution.py:22
  11.6 0.9 fusion.37
  12.5 2.2 %collective-permute-done = bf16[280,256]{1,0:T(8,128)(2,1)S(1)} collective-permute-done((bf16[280,256]{1,0:T(8,128)(2,1)S(1)}, bf16[280,256]{1,0:T(8,128)(2,1)S(1)}, u32[]{:S(2)}, u32[]{:S(2)}) %collective-permute-start) | collective-permute-done | bytes 143392 | tf_op jit(solution)/shard_map/ppermute | solution.py:22
  14.7 1.5 maximum_convert_fusion
  16.3 1.3 multiply_convert_fusion
  17.6 1.0 copy-done.16
  18.6 0.7 fusion.38
  20.3 1.9 collective-permute-done.1
  22.3 1.1 collective-permute-start.2
  23.4 8.5 %collective-permute-start.10 = (bf16[256,256]{1,0:T(8,128)(2,1)S(1)}, bf16[256,256]{1,0:T(8,128)(2,1)}, u32[]{:S(2)}, u32[]{:S(2)}) collective-permute-start(bf16[256,256]{1,0:T(8,128)(2,1)S(1)} %constant_dynamic-update-slice_fusion), channel_id=1, source_target_pairs={{0,64},{8,72},{16,80},{24,88},{32,96},{40,104},{48,112},{56,120},{... | collective-permute-start | bytes 393224 | tf_op jit(solution)/shard_map/ppermute | solution.py:22
  31.9 1.3 collective-permute-start.11
  33.2 3.9 %collective-permute-done.2 = f32[272,512]{1,0:T(8,128)} collective-permute-done((f32[272,512]{1,0:T(8,128)S(1)}, f32[272,512]{1,0:T(8,128)}, u32[]{:S(2)}, u32[]{:S(2)}) %collective-permute-start.2) | collective-permute-done | bytes 557088 | tf_op jit(solution)/shard_map/ppermute | solution.py:96
  37.2 1.1 add.125
  38.3 3.6 %collective-permute-start.3 = (f32[272,512]{1,0:T(8,128)S(1)}, f32[272,512]{1,0:T(8,128)S(1)}, u32[]{:S(2)}, u32[]{:S(2)}) collective-permute-start(f32[272,512]{1,0:T(8,128)S(1)} %add.125), channel_id=1, source_target_pairs={{0,4},{1,5},{2,6},{3,7},{4,0},{5,1},{6,2},{7,3},{8,12},{9,13},{10,... | collective-permute-start | bytes 1671176 | tf_op jit(solution)/shard_map/ppermute | solution.py:96
  41.9 1.3 fusion.9
  43.2 1.6 copy.26
  44.8 1.6 constant_dynamic-update-slice_fusion.6
  46.4 0.9 pad_maximum_fusion.1
  47.2 9.4 %collective-permute-start.12 = (bf16[1024,256]{1,0:T(8,128)(2,1)}, bf16[1024,256]{1,0:T(8,128)(2,1)}, u32[]{:S(2)}, u32[]{:S(2)}) collective-permute-start(bf16[1024,256]{1,0:T(8,128)(2,1)} %pad_maximum_fusion.1), channel_id=1, source_target_pairs={{0,32},{8,40},{16,48},{24,56},{32,64},{40,72},{48,80},{56,88},{64,... | collective-permute-start | bytes 1572872 | tf_op jit(solution)/shard_map/ppermute | solution.py:22
  56.6 8.6 %collective-permute-done.3 = f32[272,512]{1,0:T(8,128)S(1)} collective-permute-done((f32[272,512]{1,0:T(8,128)S(1)}, f32[272,512]{1,0:T(8,128)S(1)}, u32[]{:S(2)}, u32[]{:S(2)}) %collective-permute-start.3) | collective-permute-done | bytes 557088 | tf_op jit(solution)/shard_map/ppermute | solution.py:96
  65.5 1.9 fusion.36
  67.4 2.2 %copy.24 = f32[32,8,8,256]{3,2,1,0:T(8,128)} copy(f32[32,8,8,256]{3,1,2,0:T(8,128)S(1)} %bitcast.92) | data formatting | bytes 4194304
  69.6 2.2 %copy.25 = f32[32,8,8,256]{3,2,1,0:T(8,128)} copy(f32[32,8,8,256]{3,1,2,0:T(8,128)S(1)} %bitcast.91) | data formatting | bytes 4194304
  73.1 12.5 %shard_map.149 = f32[16,8,256]{2,1,0:T(8,128)} custom-call(f32[32,256]{1,0:T(8,128)} %reshape.87.bc_ref, f32[256,8,256]{2,1,0:T(8,128)} %bitcast.87, f32[256,8,256]{2,1,0:T(8,128)} %bitcast.89, f32[16,8,256]{2,1,0:T(8,128)} %bitcast.85, f32[16,8,256]{2,1,0:T(8,128)} %broadcast_in_dim.13.h0_ref), custom_call_target="tpu_custom_call" | custom-call | flops 33554432 | bytes 6553600 | tf_op jit(solution)/shard_map/pallas_call | solution.py:71
  85.7 1.0 pad_maximum_fusion.4
  86.7 8.3 %collective-permute-start.4 = (f32[17,8,256]{2,1,0:T(8,128)S(1)}, f32[17,8,256]{2,1,0:T(8,128)S(1)}, u32[]{:S(2)}, u32[]{:S(2)}) collective-permute-start(f32[17,8,256]{2,1,0:T(8,128)S(1)} %pad_maximum_fusion.4), channel_id=1, source_target_pairs={{0,8},{8,16},{16,24},{24,32},{32,40},{40,48},{48,56},{56,64},{64,7... | collective-permute-start | bytes 417800 | tf_op jit(solution)/shard_map/ppermute | solution.py:22
  95.0 1.9 constant_dynamic-update-slice_fusion.5
  96.9 0.7 constant_dynamic-update-slice_fusion.4
  97.6 1.5 collective-permute-done.4
  99.2 8.3 %collective-permute-start.5 = (f32[17,8,256]{2,1,0:T(8,128)S(1)}, f32[17,8,256]{2,1,0:T(8,128)S(1)}, u32[]{:S(2)}, u32[]{:S(2)}) collective-permute-start(f32[17,8,256]{2,1,0:T(8,128)S(1)} %collective-permute-done.4), channel_id=1, source_target_pairs={{0,8},{8,16},{16,24},{24,32},{32,40},{40,48},{48,56},{56,64},{64,7... | collective-permute-start | bytes 417800 | tf_op jit(solution)/shard_map/ppermute | solution.py:22
  108.1 2.1 %collective-permute-done.5 = f32[17,8,256]{2,1,0:T(8,128)S(1)} collective-permute-done((f32[17,8,256]{2,1,0:T(8,128)S(1)}, f32[17,8,256]{2,1,0:T(8,128)S(1)}, u32[]{:S(2)}, u32[]{:S(2)}) %collective-permute-start.5) | collective-permute-done | bytes 139296 | tf_op jit(solution)/shard_map/ppermute | solution.py:22
  110.2 7.7 %collective-permute-start.6 = (f32[17,8,256]{2,1,0:T(8,128)S(1)}, f32[17,8,256]{2,1,0:T(8,128)S(1)}, u32[]{:S(2)}, u32[]{:S(2)}) collective-permute-start(f32[17,8,256]{2,1,0:T(8,128)S(1)} %pad_maximum_fusion.5), channel_id=1, source_target_pairs={{0,16},{8,24},{16,32},{24,40},{32,48},{40,56},{48,64},{56,72},{64,... | collective-permute-start | bytes 417800 | tf_op jit(solution)/shard_map/ppermute | solution.py:22
  119.2 1.3 collective-permute-done.6
  120.6 5.9 %collective-permute-start.7 = (f32[17,8,256]{2,1,0:T(8,128)S(1)}, f32[17,8,256]{2,1,0:T(8,128)S(1)}, u32[]{:S(2)}, u32[]{:S(2)}) collective-permute-start(f32[17,8,256]{2,1,0:T(8,128)S(1)} %pad_maximum_fusion.6), channel_id=1, source_target_pairs={{0,32},{8,40},{16,48},{24,56},{32,64},{40,72},{48,80},{56,88},{64,... | collective-permute-start | bytes 417800 | tf_op jit(solution)/shard_map/ppermute | solution.py:22
  126.5 9.0 %fusion = (f32[8,256]{1,0:T(8,128)S(1)}, f32[2304,256,8]{1,0,2:T(8,128)}) fusion(pred[256,2304]{0,1:T(8,128)(4,1)S(1)} %fusion.9, bf16[2304,256]{1,0:T(8,128)(2,1)} %constant_dynamic-update-slice_fusion.7, bf16[256,1024]{1,0:T(8,128)(2,1)S(1)} %copy-done.7), kind=kOutput, calls=%fused_computation.2 | convolution fusion | flops 1222113280 | bytes 20586496 | tf_op jit(solution)/shard_map/tkgd,skd->kgts/dot_general | solution.py:193
  135.6 8.9 %collective-permute-start.8 = (f32[17,8,256]{2,1,0:T(8,128)S(1)}, f32[17,8,256]{2,1,0:T(8,128)S(1)}, u32[]{:S(2)}, u32[]{:S(2)}) collective-permute-start(f32[17,8,256]{2,1,0:T(8,128)S(1)} %pad_maximum_fusion.7), channel_id=1, source_target_pairs={{0,64},{8,72},{16,80},{24,88},{32,96},{40,104},{48,112},{56,120},{... | collective-permute-start | bytes 417800 | tf_op jit(solution)/shard_map/ppermute | solution.py:22
  144.5 10.2 %convert_reduce_fusion = f32[8,256]{1,0:T(8,128)S(1)} fusion(f32[8,256]{1,0:T(8,128)S(1)} %get-tuple-element.13, f32[2304,256,8]{1,0,2:T(8,128)} %get-tuple-element.14, pred[256,2304]{0,1:T(8,128)(4,1)S(1)} %fusion.9), kind=kLoop, calls=%fused_computation.6 | loop fusion | flops 28309504 | bytes 19480576 | tf_op jit(solution)/shard_map/reduce_sum | solution.py:207
  154.7 0.7 pad_maximum_fusion.8
  155.4 10.7 %collective-permute-start.9 = (f32[17,8,256]{2,1,0:T(8,128)}, f32[17,8,256]{2,1,0:T(8,128)}, u32[]{:S(2)}, u32[]{:S(2)}) collective-permute-start(f32[17,8,256]{2,1,0:T(8,128)} %pad_maximum_fusion.8), channel_id=1, source_target_pairs={{0,128},{8,136},{16,144},{24,152},{32,160},{40,168},{48,176},{56,1... | collective-permute-start | bytes 417800 | tf_op jit(solution)/shard_map/ppermute | solution.py:22
  166.1 11.2 %divide_convert_fusion = bf16[256,1,8,128]{0,3,2,1:T(8,128)(2,1)S(1)} fusion(bf16[2304,256]{1,0:T(8,128)(2,1)} %constant_dynamic-update-slice_fusion.7, f32[256,8]{0,1:T(8,128)S(1)} %bitcast.108, f32[2304,256,8]{1,0,2:T(8,128)} %get-tuple-element.14, f32[8,256]{1,0:T(8,128)S(1)} %get-tuple-element.13, pred[256,2304]{0,1:T(8,128)(4,1)S(1)} %fusion.9), kind=kOutput, calls=%fused_computation.38 | convolution fusion | flops 1227358208 | bytes 20594688 | tf_op jit(solution)/shard_map/kgts,skd->tkgd/dot_general | solution.py:208
  177.3 1.0 copy.19
  178.3 1.6 fusion.30.h0_ref
  179.9 15.9 %shard_map.150 = f32[256,8,256]{2,1,0:T(8,128)} custom-call(f32[32,256]{1,0:T(8,128)} %reshape.87.bc_ref, f32[256,8,256]{2,1,0:T(8,128)} %bitcast.88, f32[256,8,256]{2,1,0:T(8,128)} %bitcast.90, f32[16,8,256]{2,1,0:T(8,128)} %bitcast.86, f32[16,8,256]{2,1,0:T(8,128)} %fusion.30.h0_ref), custom_call_target="tpu_custom_call" | custom-call | flops 50331648 | bytes 6553600 | tf_op jit(solution)/shard_map/pallas_call | solution.py:71
  195.8 2.6 %copy.27 = f32[32,8,8,256]{3,1,2,0:T(8,128)S(1)} copy(f32[32,8,8,256]{3,2,1,0:T(8,128)} %bitcast.93) | data formatting | bytes 4194304
  198.5 2.8 %fusion.12 = bf16[256,2048]{1,0:T(8,128)(2,1)} fusion(f32[256,2048]{1,0:T(8,128)S(1)} %bitcast.84, bf16[256,2048]{1,0:T(8,128)(2,1)S(1)} %copy-done.8, f32[2048]{0:T(1024)S(1)} %copy-done.15, f32[259,2048]{1,0:T(8,128)S(1)} %copy-done.2, f32[2048]{0:T(1024)S(1)} %bitcast.105, f32[2048]{0:T(1024)S(1)} %bitcast.107, f32[2048]{0:T(1024)S(1)} %bitcast.103, ...), kind=kLoop, calls=%fused_computation.22 | loop fusion | flops 12058624 | bytes 12632064 | tf_op jit(solution)/shard_map/convert_element_type | solution.py:186
  (78 shorter events, 4.8 us)
Async XLA Ops:
  0.6 64.8 %copy-start = (bf16[512,2048]{1,0:T(8,128)(2,1)S(1)}, bf16[512,2048]{1,0:T(8,128)(2,1)}, u32[]{:S(2)}) copy-start(bf16[512,2048]{1,0:T(8,128)(2,1)} %param.24) | copy-start | bytes 6291460
  0.6 15.6 %copy-start.14 = (f32[2048]{0:T(1024)S(1)}, f32[2048]{0:T(1024)}, u32[]{:S(2)}) copy-start(f32[2048]{0:T(1024)} %param.20) | copy-start | bytes 24580
  3.3 11.3 %collective-permute-start = (bf16[280,256]{1,0:T(8,128)(2,1)S(1)}, bf16[280,256]{1,0:T(8,128)(2,1)S(1)}, u32[]{:S(2)}, u32[]{:S(2)}) collective-permute-start(bf16[280,256]{1,0:T(8,128)(2,1)S(1)} %pad_maximum_fusion.3), channel_id=1, source_target_pairs={{0,8},{8,16},{16,24},{24,32},{32,40},{40,48},{48,56},{56,64},{64,7... | collective-permute-start | bytes 430088 | tf_op jit(solution)/shard_map/ppermute | solution.py:22
  16.2 1.4 copy-start.1
  16.3 2.4 %copy-start.16 = (bf16[2048,512]{1,0:T(8,128)(2,1)S(1)}, bf16[2048,512]{1,0:T(8,128)(2,1)}, u32[]{:S(2)}) copy-start(bf16[2048,512]{1,0:T(8,128)(2,1)} %param.21) | copy-start | bytes 6291460
  18.6 1.0 copy-start.4
  18.6 1.0 copy-start.13
  20.2 2.0 %collective-permute-start.1 = (f32[272,512]{1,0:T(8,128)S(1)}, f32[272,512]{1,0:T(8,128)S(1)}, u32[]{:S(2)}, u32[]{:S(2)}) collective-permute-start(f32[272,512]{1,0:T(8,128)S(1)} %pad_maximum_fusion), channel_id=1, source_target_pairs={{0,1},{1,0},{2,3},{3,2},{4,5},{5,4},{6,7},{7,6},{8,9},{9,8},{10,11... | collective-permute-start | bytes 1671176 | tf_op jit(solution)/shard_map/ppermute | solution.py:96
  22.3 14.9 %collective-permute-start.2 = (f32[272,512]{1,0:T(8,128)S(1)}, f32[272,512]{1,0:T(8,128)}, u32[]{:S(2)}, u32[]{:S(2)}) collective-permute-start(f32[272,512]{1,0:T(8,128)S(1)} %fusion.35), channel_id=1, source_target_pairs={{0,2},{1,3},{2,0},{3,1},{4,6},{5,7},{6,4},{7,5},{8,10},{9,11},{10,... | collective-permute-start | bytes 1671176 | tf_op jit(solution)/shard_map/ppermute | solution.py:96
  23.4 21.4 %collective-permute-start.10 = (bf16[256,256]{1,0:T(8,128)(2,1)S(1)}, bf16[256,256]{1,0:T(8,128)(2,1)}, u32[]{:S(2)}, u32[]{:S(2)}) collective-permute-start(bf16[256,256]{1,0:T(8,128)(2,1)S(1)} %constant_dynamic-update-slice_fusion), channel_id=1, source_target_pairs={{0,64},{8,72},{16,80},{24,88},{32,96},{40,104},{48,112},{56,120},{... | collective-permute-start | bytes 393224 | tf_op jit(solution)/shard_map/ppermute | solution.py:22
  31.9 14.5 %collective-permute-start.11 = (bf16[512,256]{1,0:T(8,128)(2,1)S(1)}, bf16[512,256]{1,0:T(8,128)(2,1)S(1)}, u32[]{:S(2)}, u32[]{:S(2)}) collective-permute-start(bf16[512,256]{1,0:T(8,128)(2,1)S(1)} %pad_maximum_fusion.2), channel_id=1, source_target_pairs={{0,16},{8,24},{16,32},{24,40},{32,48},{40,56},{48,64},{56,72},{64,... | collective-permute-start | bytes 786440 | tf_op jit(solution)/shard_map/ppermute | solution.py:22
  38.3 27.2 %copy-start.5 = (bf16[256,2048]{1,0:T(8,128)(2,1)S(1)}, bf16[256,2048]{1,0:T(8,128)(2,1)}, u32[]{:S(2)}) copy-start(bf16[256,2048]{1,0:T(8,128)(2,1)} %copy-done.4) | copy-start | bytes 3145732
  38.3 27.2 %copy-start.17 = (f32[2048]{0:T(1024)S(1)}, f32[2048]{0:T(1024)}, u32[]{:S(2)}) copy-start(f32[2048]{0:T(1024)} %param.25) | copy-start | bytes 24580
  38.3 27.2 %copy-start.18 = (f32[512]{0:T(512)S(1)}, f32[512]{0:T(512)}, u32[]{:S(2)}) copy-start(f32[512]{0:T(512)} %param.23) | copy-start | bytes 6148
  38.3 26.9 %collective-permute-start.3 = (f32[272,512]{1,0:T(8,128)S(1)}, f32[272,512]{1,0:T(8,128)S(1)}, u32[]{:S(2)}, u32[]{:S(2)}) collective-permute-start(f32[272,512]{1,0:T(8,128)S(1)} %add.125), channel_id=1, source_target_pairs={{0,4},{1,5},{2,6},{3,7},{4,0},{5,1},{6,2},{7,3},{8,12},{9,13},{10,... | collective-permute-start | bytes 1671176 | tf_op jit(solution)/shard_map/ppermute | solution.py:96
  46.4 10.2 %copy-start.9 = (bf16[512,256]{1,0:T(8,128)(2,1)}, bf16[512,256]{1,0:T(8,128)(2,1)S(1)}, u32[]{:S(2)}) copy-start(bf16[512,256]{1,0:T(8,128)(2,1)S(1)} %collective-permute-done.11) | copy-start | bytes 786436
  47.2 47.8 %collective-permute-start.12 = (bf16[1024,256]{1,0:T(8,128)(2,1)}, bf16[1024,256]{1,0:T(8,128)(2,1)}, u32[]{:S(2)}, u32[]{:S(2)}) collective-permute-start(bf16[1024,256]{1,0:T(8,128)(2,1)} %pad_maximum_fusion.1), channel_id=1, source_target_pairs={{0,32},{8,40},{16,48},{24,56},{32,64},{40,72},{48,80},{56,88},{64,... | collective-permute-start | bytes 1572872 | tf_op jit(solution)/shard_map/ppermute | solution.py:22
  65.3 2.1 %copy-start.6 = (f32[272,512]{1,0:T(8,128)}, f32[272,512]{1,0:T(8,128)S(1)}, u32[]{:S(2)}) copy-start(f32[272,512]{1,0:T(8,128)S(1)} %add.126) | copy-start | bytes 1671172
  69.6 2.3 %slice-start = ((f32[272,512]{1,0:T(8,128)}), f32[16,512]{1,0:T(8,128)S(1)}, s32[]{:S(2)}) async-start(f32[272,512]{1,0:T(8,128)} %copy-done.6), calls=%async_computation | async-start | bytes 65536 | tf_op jit(solution)/shard_map/slice | solution.py:167
  73.1 23.8 %copy-start.10 = (bf16[512,256]{1,0:T(8,128)(2,1)S(1)}, bf16[512,256]{1,0:T(8,128)(2,1)}, u32[]{:S(2)}) copy-start(bf16[512,256]{1,0:T(8,128)(2,1)} %copy-done.9) | copy-start | bytes 786436
  85.6 24.5 %copy-start.3 = (f32[2,8,8,256]{3,2,1,0:T(8,128)S(1)}, f32[2,8,8,256]{3,2,1,0:T(8,128)}, u32[]{:S(2)}) copy-start(f32[2,8,8,256]{3,2,1,0:T(8,128)} %copy.26) | copy-start | bytes 393220
  85.7 32.3 %copy-start.11 = (bf16[256,128]{1,0:T(8,128)(2,1)S(1)}, bf16[256,128]{1,0:T(8,128)(2,1)}, u32[]{:S(2)}) copy-start(bf16[256,128]{1,0:T(8,128)(2,1)} %param.17) | copy-start | bytes 196612
  85.7 32.9 %copy-start.12 = (bf16[256,128]{1,0:T(8,128)(2,1)S(1)}, bf16[256,128]{1,0:T(8,128)(2,1)}, u32[]{:S(2)}) copy-start(bf16[256,128]{1,0:T(8,128)(2,1)} %param.18) | copy-start | bytes 196612
  85.7 40.8 %copy-start.7 = (bf16[256,1024]{1,0:T(8,128)(2,1)S(1)}, bf16[256,1024]{1,0:T(8,128)(2,1)}, u32[]{:S(2)}) copy-start(bf16[256,1024]{1,0:T(8,128)(2,1)} %param.16) | copy-start | bytes 1572868
  86.7 12.5 %collective-permute-start.4 = (f32[17,8,256]{2,1,0:T(8,128)S(1)}, f32[17,8,256]{2,1,0:T(8,128)S(1)}, u32[]{:S(2)}, u32[]{:S(2)}) collective-permute-start(f32[17,8,256]{2,1,0:T(8,128)S(1)} %pad_maximum_fusion.4), channel_id=1, source_target_pairs={{0,8},{8,16},{16,24},{24,32},{32,40},{40,48},{48,56},{56,64},{64,7... | collective-permute-start | bytes 417800 | tf_op jit(solution)/shard_map/ppermute | solution.py:22
  99.2 11.0 %collective-permute-start.5 = (f32[17,8,256]{2,1,0:T(8,128)S(1)}, f32[17,8,256]{2,1,0:T(8,128)S(1)}, u32[]{:S(2)}, u32[]{:S(2)}) collective-permute-start(f32[17,8,256]{2,1,0:T(8,128)S(1)} %collective-permute-done.4), channel_id=1, source_target_pairs={{0,8},{8,16},{16,24},{24,32},{32,40},{40,48},{48,56},{56,64},{64,7... | collective-permute-start | bytes 417800 | tf_op jit(solution)/shard_map/ppermute | solution.py:22
  110.2 10.3 %collective-permute-start.6 = (f32[17,8,256]{2,1,0:T(8,128)S(1)}, f32[17,8,256]{2,1,0:T(8,128)S(1)}, u32[]{:S(2)}, u32[]{:S(2)}) collective-permute-start(f32[17,8,256]{2,1,0:T(8,128)S(1)} %pad_maximum_fusion.5), channel_id=1, source_target_pairs={{0,16},{8,24},{16,32},{24,40},{32,48},{40,56},{48,64},{56,72},{64,... | collective-permute-start | bytes 417800 | tf_op jit(solution)/shard_map/ppermute | solution.py:22
  120.6 14.9 %collective-permute-start.7 = (f32[17,8,256]{2,1,0:T(8,128)S(1)}, f32[17,8,256]{2,1,0:T(8,128)S(1)}, u32[]{:S(2)}, u32[]{:S(2)}) collective-permute-start(f32[17,8,256]{2,1,0:T(8,128)S(1)} %pad_maximum_fusion.6), channel_id=1, source_target_pairs={{0,32},{8,40},{16,48},{24,56},{32,64},{40,72},{48,80},{56,88},{64,... | collective-permute-start | bytes 417800 | tf_op jit(solution)/shard_map/ppermute | solution.py:22
  135.6 19.1 %collective-permute-start.8 = (f32[17,8,256]{2,1,0:T(8,128)S(1)}, f32[17,8,256]{2,1,0:T(8,128)S(1)}, u32[]{:S(2)}, u32[]{:S(2)}) collective-permute-start(f32[17,8,256]{2,1,0:T(8,128)S(1)} %pad_maximum_fusion.7), channel_id=1, source_target_pairs={{0,64},{8,72},{16,80},{24,88},{32,96},{40,104},{48,112},{56,120},{... | collective-permute-start | bytes 417800 | tf_op jit(solution)/shard_map/ppermute | solution.py:22
  155.4 22.9 %collective-permute-start.9 = (f32[17,8,256]{2,1,0:T(8,128)}, f32[17,8,256]{2,1,0:T(8,128)}, u32[]{:S(2)}, u32[]{:S(2)}) collective-permute-start(f32[17,8,256]{2,1,0:T(8,128)} %pad_maximum_fusion.8), channel_id=1, source_target_pairs={{0,128},{8,136},{16,144},{24,152},{32,160},{40,168},{48,176},{56,1... | collective-permute-start | bytes 417800 | tf_op jit(solution)/shard_map/ppermute | solution.py:22
  195.8 2.6 %copy-start.2 = (f32[259,2048]{1,0:T(8,128)S(1)}, f32[259,2048]{1,0:T(8,128)}, u32[]{:S(2)}) copy-start(f32[259,2048]{1,0:T(8,128)} %copy-done.1) | copy-start | bytes 6365188
  195.8 2.7 %copy-start.8 = (bf16[256,2048]{1,0:T(8,128)(2,1)S(1)}, bf16[256,2048]{1,0:T(8,128)(2,1)}, u32[]{:S(2)}) copy-start(bf16[256,2048]{1,0:T(8,128)(2,1)} %param.15) | copy-start | bytes 3145732
  195.8 2.7 %copy-start.15 = (f32[2048]{0:T(1024)S(1)}, f32[2048]{0:T(1024)}, u32[]{:S(2)}) copy-start(f32[2048]{0:T(1024)} %param.27) | copy-start | bytes 24580

commit v4 on v3

--- a/solution.py
+++ b/solution.py
@@ -88,6 +88,45 @@
     )(bc, dt3, dr3, rate3, h0)
 
 
+def attention_kernel(base_ref, q_ref, k_ref, v_ref, o_ref):
+    scores = lax.dot_general(
+        q_ref[...], k_ref[...], (((1,), (1,)), ((), ())), preferred_element_type=jnp.float32
+    ) * (1.0 / math.sqrt(HD))
+    rows = lax.broadcasted_iota(jnp.int32, scores.shape, 0)
+    cols = lax.broadcasted_iota(jnp.int32, scores.shape, 1)
+    distance = WINDOW + rows - cols
+    in_window = (distance >= 0) & (distance < WINDOW) & (cols + base_ref[0] >= WINDOW)
+    row_peak = jnp.max(jnp.where(in_window, scores, -jnp.inf), axis=1, keepdims=True)
+    weights = jnp.exp(jnp.where(in_window, scores - row_peak, -jnp.inf)).astype(jnp.bfloat16)
+    summed = jnp.sum(weights.astype(jnp.float32), axis=1, keepdims=True)
+    weighted = jnp.dot(weights, v_ref[...], preferred_element_type=jnp.float32)
+    o_ref[...] = (weighted / summed).astype(o_ref.dtype)
+
+
+def run_attention(q_proj, window, base):
+    tokens, width = q_proj.shape
+    keys = window.shape[0]
+    heads = width // HD
+    group = heads // (window.shape[1] // (2 * HD))
+    return pl.pallas_call(
+        attention_kernel,
+        grid=(heads,),
+        in_specs=[
+            pl.BlockSpec(memory_space=pltpu.SMEM),
+            pl.BlockSpec((tokens, HD), lambda h: (0, h)),
+            pl.BlockSpec((keys, HD), lambda h: (0, h // group)),
+            pl.BlockSpec((keys, HD), lambda h: (0, window.shape[1] // (2 * HD) + h // group)),
+        ],
+        out_specs=pl.BlockSpec((tokens, HD), lambda h: (0, h)),
+        out_shape=jax.ShapeDtypeStruct((tokens, width), q_proj.dtype),
+        cost_estimate=pl.CostEstimate(
+            flops=4 * tokens * keys * HD * heads,
+            transcendentals=tokens * keys * heads,
+            bytes_accessed=2 * (2 * tokens * width + 2 * keys * window.shape[1]),
+        ),
+    )(base, q_proj, window, window)
+
+
 def butterfly_sum(value, axis):
     count = lax.axis_size(axis)
     stride = 1
@@ -129,9 +168,7 @@
         reach *= 2
     assert reach == key_span
     held = [shifted(own, "seq", key_span)] + held
-    window = jnp.concatenate(held, axis=0)
-    half = k_proj.shape[1]
-    return window[:, :half], window[:, half:], tail_in
+    return jnp.concatenate(held, axis=0), tail_in
 
 
 def per_device(
@@ -153,7 +190,7 @@
     tokens_here, channels = conv_in.shape
     key_span = WINDOW // tokens_here
     conv_tail = conv_in[tokens_here - (KCONV - 1) :]
-    keys_window, values_window, tail_in = window_blocks(k_proj, v_proj, conv_tail, key_span)
+    window, tail_in = window_blocks(k_proj, v_proj, conv_tail, key_span)
     padded = jnp.concatenate([tail_in, conv_in], axis=0).astype(jnp.float32)
     activated = causal_conv(padded, conv_weight, conv_bias, tokens_here)
     state_parts = lax.dot_general(
@@ -184,33 +221,8 @@
         (mamba_sum + skip_weight[None, :] * activated.astype(jnp.float32))
         * jax.nn.silu(gate_in.astype(jnp.float32))
     ).astype(jnp.bfloat16)
-    heads_here = q_proj.shape[1] // HD
-    kv_here = k_proj.shape[1] // HD
-    grouping = heads_here // kv_here
-    keys_all = keys_window.reshape(-1, kv_here, HD)
-    values_all = values_window.reshape(-1, kv_here, HD)
-    queries = q_proj.reshape(tokens_here, kv_here, grouping, HD)
-    scores = jnp.einsum("tkgd,skd->kgts", queries, keys_all, preferred_element_type=jnp.float32) * (
-        1.0 / math.sqrt(HD)
-    )
-    index_seq = lax.axis_index("seq")
-    row_ids = jnp.arange(tokens_here, dtype=jnp.int32)[:, None]
-    col_ids = jnp.arange((key_span + 1) * tokens_here, dtype=jnp.int32)[None, :]
-    distance_all = WINDOW + row_ids - col_ids
-    in_window = (
-        (distance_all >= 0)
-        & (distance_all < WINDOW)
-        & (col_ids + index_seq * tokens_here >= WINDOW)
-    )
-    row_peak = jnp.max(jnp.where(in_window, scores, -jnp.inf), axis=-1, keepdims=True)
-    weights = jnp.exp(jnp.where(in_window, scores - row_peak, -jnp.inf)).astype(jnp.bfloat16)
-    summed = jnp.sum(weights.astype(jnp.float32), axis=-1)
-    weighted = jnp.einsum("kgts,skd->tkgd", weights, values_all, preferred_element_type=jnp.float32)
-    attn_out = (
-        (weighted / summed.transpose(2, 0, 1)[..., None])
-        .astype(jnp.bfloat16)
-        .reshape(tokens_here, heads_here * HD)
-    )
+    base = (lax.axis_index("seq") * tokens_here).astype(jnp.int32).reshape(1)
+    attn_out = run_attention(q_proj, window, base)
     return (mamba_out, attn_out)
 
 

time: 202 us -> 197 us (0.975)
  the two profiles are of different devices: /device:TPU:32 before, /device:TPU:8 now
where the time goes in v4:
time: 197 us; the launch traced here: 196 us
  waiting for transfers between devices  77.8 us (39%)
  starting transfers between devices  44.3 us (22%)
  Pallas kernels  42.6 us (22%)
  local copies, waits for them, and re-layouts  15.3 us (8%)
  other arithmetic  9.64 us (5%)
  matrix products  5.6 us (3%)
    ppermute x10, waiting for transfers between devices, shifted(): lax.ppermute(value, axis, [(source, source + steps) for source in range(f...  41.9 us
    ppermute x10, starting transfers between devices, shifted(): lax.ppermute(value, axis, [(source, source + steps) for source in range(f...  36.6 us
    ppermute x3, waiting for transfers between devices, butterfly_sum(): value = value + lax.ppermute(value, axis, pairs)  35.8 us
    pallas_call x2, Pallas kernels, run_scan(): pl.pallas_call(functools.partial(scan_kernel, with_out), grid=(blocks,),...  28.4 us
    pallas_call x1, Pallas kernels, run_attention(): pl.pallas_call(attention_kernel, grid=(heads,), in_specs=[pl.BlockSpec(me...  14.2 us
    unnamed x52, local copies, waits for them, and re-layouts  11.2 us
    ppermute x3, starting transfers between devices, butterfly_sum(): value = value + lax.ppermute(value, axis, pairs)  7.7 us
  transfers between devices with their start and end apart: 13, of which 10 were waited for; matrix products, arithmetic and copies ran while one was open for 7% of the time, Pallas kernels for 14%

profile of v4, /device:TPU:8, one launch (start us, length us, event | category | flops | bytes accessed | tf_op | source)
XLA Modules:
  0.0 196.4 jit_solution(1507964598477960356)
XLA Ops:
  0.7 0.9 slice.74
  1.6 0.9 constant_dynamic-update-slice_fusion.1
  2.5 0.9 constant_dynamic-update-slice_fusion
  3.4 9.1 %collective-permute-start = (bf16[280,256]{1,0:T(8,128)(2,1)S(1)}, bf16[280,256]{1,0:T(8,128)(2,1)S(1)}, u32[]{:S(2)}, u32[]{:S(2)}) collective-permute-start(bf16[280,256]{1,0:T(8,128)(2,1)S(1)} %pad_maximum_fusion.3), channel_id=1, source_target_pairs={{0,8},{8,16},{16,24},{24,32},{32,40},{40,48},{48,56},{56,64},{64,7... | collective-permute-start | bytes 430088 | tf_op jit(solution)/shard_map/ppermute | solution.py:22
  12.5 0.9 fusion.18
  13.4 5.0 %collective-permute-done = bf16[280,256]{1,0:T(8,128)(2,1)S(1)} collective-permute-done((bf16[280,256]{1,0:T(8,128)(2,1)S(1)}, bf16[280,256]{1,0:T(8,128)(2,1)S(1)}, u32[]{:S(2)}, u32[]{:S(2)}) %collective-permute-start) | collective-permute-done | bytes 143392 | tf_op jit(solution)/shard_map/ppermute | solution.py:22
  18.4 0.7 copy-done.6
  19.1 1.5 maximum_convert_fusion
  20.6 1.3 multiply_convert_fusion
  22.0 0.4 convolution_bitcast_fusion
  22.5 2.3 %fusion.19 = f32[256,512]{1,0:T(8,128)S(1)} fusion(bf16[256,2048]{1,0:T(8,128)(2,1)S(1)} %multiply_convert_fusion, bf16[2048,512]{1,0:T(8,128)(2,1)} %param.21), kind=kOutput, calls=%fused_computation.63 | convolution fusion | flops 536870912 | bytes 3670016 | tf_op jit(solution)/shard_map/dot_general | solution.py:199
  24.9 1.9 collective-permute-done.1
  27.0 3.6 %collective-permute-start.2 = (f32[272,512]{1,0:T(8,128)S(1)}, f32[272,512]{1,0:T(8,128)S(1)}, u32[]{:S(2)}, u32[]{:S(2)}) collective-permute-start(f32[272,512]{1,0:T(8,128)S(1)} %fusion.16), channel_id=1, source_target_pairs={{0,2},{1,3},{2,0},{3,1},{4,6},{5,7},{6,4},{7,5},{8,10},{9,11},{10,... | collective-permute-start | bytes 1671176 | tf_op jit(solution)/shard_map/ppermute | solution.py:135
  30.6 12.9 %collective-permute-done.2 = f32[272,512]{1,0:T(8,128)S(1)} collective-permute-done((f32[272,512]{1,0:T(8,128)S(1)}, f32[272,512]{1,0:T(8,128)S(1)}, u32[]{:S(2)}, u32[]{:S(2)}) %collective-permute-start.2) | collective-permute-done | bytes 557088 | tf_op jit(solution)/shard_map/ppermute | solution.py:135
  43.6 4.0 %collective-permute-start.3 = (f32[272,512]{1,0:T(8,128)S(1)}, f32[272,512]{1,0:T(8,128)S(1)}, u32[]{:S(2)}, u32[]{:S(2)}) collective-permute-start(f32[272,512]{1,0:T(8,128)S(1)} %add.103), channel_id=1, source_target_pairs={{0,4},{1,5},{2,6},{3,7},{4,0},{5,1},{6,2},{7,3},{8,12},{9,13},{10,... | collective-permute-start | bytes 1671176 | tf_op jit(solution)/shard_map/ppermute | solution.py:135
  47.6 0.7 copy.18
  48.3 0.7 pad_maximum_fusion.2
  49.0 1.9 collective-permute-start.11
  50.9 21.0 %collective-permute-done.3 = f32[272,512]{1,0:T(8,128)S(1)} collective-permute-done((f32[272,512]{1,0:T(8,128)S(1)}, f32[272,512]{1,0:T(8,128)S(1)}, u32[]{:S(2)}, u32[]{:S(2)}) %collective-permute-start.3) | collective-permute-done | bytes 557088 | tf_op jit(solution)/shard_map/ppermute | solution.py:135
  72.0 0.8 copy-done.4
  72.9 0.6 reshape.48.bc_ref
  73.5 2.9 %fusion.17 = (f32[2048]{0:T(1024)S(1)}, f32[256,2048]{1,0:T(8,128)S(1)}, f32[256,2048]{1,0:T(8,128)S(1)}) fusion(bf16[256,2048]{1,0:T(8,128)(2,1)S(1)} %multiply_convert_fusion, f32[2048]{0:T(1024)} %param.25, bf16[512,2048]{1,0:T(8,128)(2,1)S(1)} %copy-done, f32[272,512]{1,0:T(8,128)} %copy-done.4, f32[512]{0:T(512)} %param.23, f32[256]{0:T(256)S(1)} %add_rsqrt_fusion), kind=kOutput, calls=%fused_computation.61 | convolution fusion | flops 542504960 | bytes 7883776 | tf_op jit(solution)/shard_map/dot_general | solution.py:207
  76.4 2.2 %copy.16 = f32[32,8,8,256]{3,2,1,0:T(8,128)} copy(f32[32,8,8,256]{3,1,2,0:T(8,128)S(1)} %bitcast.39) | data formatting | bytes 4194304
  78.6 2.2 %copy.17 = f32[32,8,8,256]{3,2,1,0:T(8,128)} copy(f32[32,8,8,256]{3,1,2,0:T(8,128)S(1)} %bitcast.38) | data formatting | bytes 4194304
  80.9 0.7 broadcast_in_dim.5.h0_ref
  81.6 12.5 %shard_map.149 = f32[16,8,256]{2,1,0:T(8,128)} custom-call(f32[32,256]{1,0:T(8,128)} %reshape.48.bc_ref, f32[256,8,256]{2,1,0:T(8,128)} %bitcast.34, f32[256,8,256]{2,1,0:T(8,128)} %bitcast.36, f32[16,8,256]{2,1,0:T(8,128)} %bitcast.32, f32[16,8,256]{2,1,0:T(8,128)} %broadcast_in_dim.5.h0_ref), custom_call_target="tpu_custom_call" | custom-call | flops 33554432 | bytes 6553600 | tf_op jit(solution)/shard_map/pallas_call | solution.py:71
  94.1 0.9 pad_maximum_fusion.4
  95.0 4.9 %collective-permute-start.4 = (f32[17,8,256]{2,1,0:T(8,128)S(1)}, f32[17,8,256]{2,1,0:T(8,128)S(1)}, u32[]{:S(2)}, u32[]{:S(2)}) collective-permute-start(f32[17,8,256]{2,1,0:T(8,128)S(1)} %pad_maximum_fusion.4), channel_id=1, source_target_pairs={{0,8},{8,16},{16,24},{24,32},{32,40},{40,48},{48,56},{56,64},{64,7... | collective-permute-start | bytes 417800 | tf_op jit(solution)/shard_map/ppermute | solution.py:22
  99.9 3.5 %collective-permute-start.10 = (bf16[256,256]{1,0:T(8,128)(2,1)S(1)}, bf16[256,256]{1,0:T(8,128)(2,1)S(1)}, u32[]{:S(2)}, u32[]{:S(2)}) collective-permute-start(bf16[256,256]{1,0:T(8,128)(2,1)S(1)} %constant_dynamic-update-slice_fusion), channel_id=1, source_target_pairs={{0,64},{8,72},{16,80},{24,88},{32,96},{40,104},{48,112},{56,120},{... | collective-permute-start | bytes 393224 | tf_op jit(solution)/shard_map/ppermute | solution.py:22
  103.4 7.7 %collective-permute-done.4 = f32[17,8,256]{2,1,0:T(8,128)S(1)} collective-permute-done((f32[17,8,256]{2,1,0:T(8,128)S(1)}, f32[17,8,256]{2,1,0:T(8,128)S(1)}, u32[]{:S(2)}, u32[]{:S(2)}) %collective-permute-start.4) | collective-permute-done | bytes 139296 | tf_op jit(solution)/shard_map/ppermute | solution.py:22
  111.0 1.9 collective-permute-start.5
  113.0 1.0 pad_maximum_fusion.1
  114.0 3.6 %collective-permute-start.12 = (bf16[1024,256]{1,0:T(8,128)(2,1)S(1)}, bf16[1024,256]{1,0:T(8,128)(2,1)S(1)}, u32[]{:S(2)}, u32[]{:S(2)}) collective-permute-start(bf16[1024,256]{1,0:T(8,128)(2,1)S(1)} %pad_maximum_fusion.1), channel_id=1, source_target_pairs={{0,32},{8,40},{16,48},{24,56},{32,64},{40,72},{48,80},{56,88},{64,... | collective-permute-start | bytes 1572872 | tf_op jit(solution)/shard_map/ppermute | solution.py:22
  117.6 9.9 %collective-permute-done.5 = f32[17,8,256]{2,1,0:T(8,128)S(1)} collective-permute-done((f32[17,8,256]{2,1,0:T(8,128)S(1)}, f32[17,8,256]{2,1,0:T(8,128)S(1)}, u32[]{:S(2)}, u32[]{:S(2)}) %collective-permute-start.5) | collective-permute-done | bytes 139296 | tf_op jit(solution)/shard_map/ppermute | solution.py:22
  127.6 1.9 collective-permute-start.6
  129.6 6.6 %collective-permute-done.12 = bf16[1024,256]{1,0:T(8,128)(2,1)S(1)} collective-permute-done((bf16[1024,256]{1,0:T(8,128)(2,1)S(1)}, bf16[1024,256]{1,0:T(8,128)(2,1)S(1)}, u32[]{:S(2)}, u32[]{:S(2)}) %collective-permute-start.12) | collective-permute-done | bytes 524320 | tf_op jit(solution)/shard_map/ppermute | solution.py:22
  136.2 1.0 constant_dynamic-update-slice_fusion.4
  137.2 1.5 collective-permute-done.6
  138.7 1.9 collective-permute-start.7
  140.6 7.9 %collective-permute-done.7 = f32[17,8,256]{2,1,0:T(8,128)S(1)} collective-permute-done((f32[17,8,256]{2,1,0:T(8,128)S(1)}, f32[17,8,256]{2,1,0:T(8,128)S(1)}, u32[]{:S(2)}, u32[]{:S(2)}) %collective-permute-start.7) | collective-permute-done | bytes 139296 | tf_op jit(solution)/shard_map/ppermute | solution.py:22
  148.6 3.5 %collective-permute-start.8 = (f32[17,8,256]{2,1,0:T(8,128)S(1)}, f32[17,8,256]{2,1,0:T(8,128)S(1)}, u32[]{:S(2)}, u32[]{:S(2)}) collective-permute-start(f32[17,8,256]{2,1,0:T(8,128)S(1)} %pad_maximum_fusion.7), channel_id=1, source_target_pairs={{0,64},{8,72},{16,80},{24,88},{32,96},{40,104},{48,112},{56,120},{... | collective-permute-start | bytes 417800 | tf_op jit(solution)/shard_map/ppermute | solution.py:22
  152.2 3.4 %collective-permute-done.8 = f32[17,8,256]{2,1,0:T(8,128)S(1)} collective-permute-done((f32[17,8,256]{2,1,0:T(8,128)S(1)}, f32[17,8,256]{2,1,0:T(8,128)S(1)}, u32[]{:S(2)}, u32[]{:S(2)}) %collective-permute-start.8) | collective-permute-done | bytes 139296 | tf_op jit(solution)/shard_map/ppermute | solution.py:22
  155.6 4.4 %collective-permute-start.9 = (f32[17,8,256]{2,1,0:T(8,128)S(1)}, f32[17,8,256]{2,1,0:T(8,128)S(1)}, u32[]{:S(2)}, u32[]{:S(2)}) collective-permute-start(f32[17,8,256]{2,1,0:T(8,128)S(1)} %pad_maximum_fusion.8), channel_id=1, source_target_pairs={{0,128},{8,136},{16,144},{24,152},{32,160},{40,168},{48,176},{56,1... | collective-permute-start | bytes 417800 | tf_op jit(solution)/shard_map/ppermute | solution.py:22
  160.1 14.2 %shard_map.151 = bf16[256,1024]{1,0:T(8,128)(2,1)} custom-call(s32[1]{0:T(128)} %bitcast.10.base_ref, bf16[256,1024]{1,0:T(8,128)(2,1)} %q_ref.1, bf16[2304,256]{1,0:T(8,128)(2,1)} %copy-done.19, bf16[2304,256]{1,0:T(8,128)(2,1)} %copy-done.19), custom_call_target="tpu_custom_call" | custom-call | flops 2415919104 | bytes 3407872 | tf_op jit(solution)/shard_map/pallas_call | solution.py:111
  174.3 0.7 fusion.12.h0_ref
  175.0 15.8 %shard_map.150 = f32[256,8,256]{2,1,0:T(8,128)} custom-call(f32[32,256]{1,0:T(8,128)} %reshape.48.bc_ref, f32[256,8,256]{2,1,0:T(8,128)} %bitcast.35, f32[256,8,256]{2,1,0:T(8,128)} %bitcast.37, f32[16,8,256]{2,1,0:T(8,128)} %bitcast.33, f32[16,8,256]{2,1,0:T(8,128)} %fusion.12.h0_ref), custom_call_target="tpu_custom_call" | custom-call | flops 50331648 | bytes 6553600 | tf_op jit(solution)/shard_map/pallas_call | solution.py:71
  190.9 2.6 %copy.19 = f32[32,8,8,256]{3,1,2,0:T(8,128)S(1)} copy(f32[32,8,8,256]{3,2,1,0:T(8,128)} %bitcast.40) | data formatting | bytes 4194304
  193.6 2.8 %fusion.2 = bf16[256,2048]{1,0:T(8,128)(2,1)} fusion(f32[256,2048]{1,0:T(8,128)S(1)} %bitcast.31, bf16[256,2048]{1,0:T(8,128)(2,1)S(1)} %copy-done.5, f32[2048]{0:T(1024)S(1)} %copy-done.20, f32[259,2048]{1,0:T(8,128)S(1)} %copy-done.2, f32[2048]{0:T(1024)S(1)} %bitcast.51, f32[2048]{0:T(1024)S(1)} %bitcast.53, f32[2048]{0:T(1024)S(1)} %bitcast.49, ...), kind=kLoop, calls=%fused_computation.8 | loop fusion | flops 12058624 | bytes 12632064 | tf_op jit(solution)/shard_map/convert_element_type | solution.py:223
  (75 shorter events, 1.0 us)
Async XLA Ops:
  0.6 72.9 %copy-start = (bf16[512,2048]{1,0:T(8,128)(2,1)S(1)}, bf16[512,2048]{1,0:T(8,128)(2,1)}, u32[]{:S(2)}) copy-start(bf16[512,2048]{1,0:T(8,128)(2,1)} %param.24) | copy-start | bytes 6291460
  0.6 20.0 %copy-start.17 = (f32[2048]{0:T(1024)S(1)}, f32[2048]{0:T(1024)}, u32[]{:S(2)}) copy-start(f32[2048]{0:T(1024)} %param.20) | copy-start | bytes 24580
  3.4 15.0 %collective-permute-start = (bf16[280,256]{1,0:T(8,128)(2,1)S(1)}, bf16[280,256]{1,0:T(8,128)(2,1)S(1)}, u32[]{:S(2)}, u32[]{:S(2)}) collective-permute-start(bf16[280,256]{1,0:T(8,128)(2,1)S(1)} %pad_maximum_fusion.3), channel_id=1, source_target_pairs={{0,8},{8,16},{16,24},{24,32},{32,40},{40,48},{48,56},{56,64},{64,7... | collective-permute-start | bytes 430088 | tf_op jit(solution)/shard_map/ppermute | solution.py:22
  13.4 8.6 %copy-start.13 = (f32[1,2048]{1,0:T(1,128)}, f32[1,2048]{1,0:T(1,128)S(1)}, u32[]{:S(2)}) copy-start(f32[1,2048]{1,0:T(1,128)S(1)} %get-tuple-element.8) | copy-start | bytes 24580
  13.4 8.6 %copy-start.15 = (f32[1,2048]{1,0:T(1,128)}, f32[1,2048]{1,0:T(1,128)S(1)}, u32[]{:S(2)}) copy-start(f32[1,2048]{1,0:T(1,128)S(1)} %get-tuple-element.9) | copy-start | bytes 24580
  18.4 0.7 copy-start.6
  20.6 1.4 copy-start.1
  20.6 1.4 copy-start.11
  24.8 22.8 %copy-start.12 = (f32[16,2048]{1,0:T(8,128)S(1)}, f32[16,2048]{1,0:T(8,128)}, u32[]{:S(2)}) copy-start(f32[16,2048]{1,0:T(8,128)} %param.26) | copy-start | bytes 393220
  24.8 23.5 %copy-start.7 = (bf16[280,256]{1,0:T(8,128)(2,1)S(1)}, bf16[280,256]{1,0:T(8,128)(2,1)}, u32[]{:S(2)}) copy-start(bf16[280,256]{1,0:T(8,128)(2,1)} %copy-done.6) | copy-start | bytes 430084
  24.8 2.0 %collective-permute-start.1 = (f32[272,512]{1,0:T(8,128)S(1)}, f32[272,512]{1,0:T(8,128)S(1)}, u32[]{:S(2)}, u32[]{:S(2)}) collective-permute-start(f32[272,512]{1,0:T(8,128)S(1)} %pad_maximum_fusion), channel_id=1, source_target_pairs={{0,1},{1,0},{2,3},{3,2},{4,5},{5,4},{6,7},{7,6},{8,9},{9,8},{10,11... | collective-permute-start | bytes 1671176 | tf_op jit(solution)/shard_map/ppermute | solution.py:135
  27.0 16.6 %collective-permute-start.2 = (f32[272,512]{1,0:T(8,128)S(1)}, f32[272,512]{1,0:T(8,128)S(1)}, u32[]{:S(2)}, u32[]{:S(2)}) collective-permute-start(f32[272,512]{1,0:T(8,128)S(1)} %fusion.16), channel_id=1, source_target_pairs={{0,2},{1,3},{2,0},{3,1},{4,6},{5,7},{6,4},{7,5},{8,10},{9,11},{10,... | collective-permute-start | bytes 1671176 | tf_op jit(solution)/shard_map/ppermute | solution.py:135
  43.6 28.3 %collective-permute-start.3 = (f32[272,512]{1,0:T(8,128)S(1)}, f32[272,512]{1,0:T(8,128)S(1)}, u32[]{:S(2)}, u32[]{:S(2)}) collective-permute-start(f32[272,512]{1,0:T(8,128)S(1)} %add.103), channel_id=1, source_target_pairs={{0,4},{1,5},{2,6},{3,7},{4,0},{5,1},{6,2},{7,3},{8,12},{9,13},{10,... | collective-permute-start | bytes 1671176 | tf_op jit(solution)/shard_map/ppermute | solution.py:135
  49.0 64.0 %collective-permute-start.11 = (bf16[512,256]{1,0:T(8,128)(2,1)}, bf16[512,256]{1,0:T(8,128)(2,1)}, u32[]{:S(2)}, u32[]{:S(2)}) collective-permute-start(bf16[512,256]{1,0:T(8,128)(2,1)} %pad_maximum_fusion.2), channel_id=1, source_target_pairs={{0,16},{8,24},{16,32},{24,40},{32,48},{40,56},{48,64},{56,72},{64,... | collective-permute-start | bytes 786440 | tf_op jit(solution)/shard_map/ppermute | solution.py:22
  72.0 0.8 copy-start.4
  81.6 46.0 %copy-start.3 = (f32[2,8,8,256]{3,2,1,0:T(8,128)S(1)}, f32[2,8,8,256]{3,2,1,0:T(8,128)}, u32[]{:S(2)}) copy-start(f32[2,8,8,256]{3,2,1,0:T(8,128)} %copy.18) | copy-start | bytes 393220
  95.0 16.1 %collective-permute-start.4 = (f32[17,8,256]{2,1,0:T(8,128)S(1)}, f32[17,8,256]{2,1,0:T(8,128)S(1)}, u32[]{:S(2)}, u32[]{:S(2)}) collective-permute-start(f32[17,8,256]{2,1,0:T(8,128)S(1)} %pad_maximum_fusion.4), channel_id=1, source_target_pairs={{0,8},{8,16},{16,24},{24,32},{32,40},{40,48},{48,56},{56,64},{64,7... | collective-permute-start | bytes 417800 | tf_op jit(solution)/shard_map/ppermute | solution.py:22
  99.9 13.1 %collective-permute-start.10 = (bf16[256,256]{1,0:T(8,128)(2,1)S(1)}, bf16[256,256]{1,0:T(8,128)(2,1)S(1)}, u32[]{:S(2)}, u32[]{:S(2)}) collective-permute-start(bf16[256,256]{1,0:T(8,128)(2,1)S(1)} %constant_dynamic-update-slice_fusion), channel_id=1, source_target_pairs={{0,64},{8,72},{16,80},{24,88},{32,96},{40,104},{48,112},{56,120},{... | collective-permute-start | bytes 393224 | tf_op jit(solution)/shard_map/ppermute | solution.py:22
  111.0 16.5 %collective-permute-start.5 = (f32[17,8,256]{2,1,0:T(8,128)S(1)}, f32[17,8,256]{2,1,0:T(8,128)S(1)}, u32[]{:S(2)}, u32[]{:S(2)}) collective-permute-start(f32[17,8,256]{2,1,0:T(8,128)S(1)} %collective-permute-done.4), channel_id=1, source_target_pairs={{0,8},{8,16},{16,24},{24,32},{32,40},{40,48},{48,56},{56,64},{64,7... | collective-permute-start | bytes 417800 | tf_op jit(solution)/shard_map/ppermute | solution.py:22
  113.0 27.6 %copy-start.8 = (bf16[280,256]{1,0:T(8,128)(2,1)S(1)}, bf16[280,256]{1,0:T(8,128)(2,1)}, u32[]{:S(2)}) copy-start(bf16[280,256]{1,0:T(8,128)(2,1)} %copy-done.6) | copy-start | bytes 430084
  114.0 22.1 %collective-permute-start.12 = (bf16[1024,256]{1,0:T(8,128)(2,1)S(1)}, bf16[1024,256]{1,0:T(8,128)(2,1)S(1)}, u32[]{:S(2)}, u32[]{:S(2)}) collective-permute-start(bf16[1024,256]{1,0:T(8,128)(2,1)S(1)} %pad_maximum_fusion.1), channel_id=1, source_target_pairs={{0,32},{8,40},{16,48},{24,56},{32,64},{40,72},{48,80},{56,88},{64,... | collective-permute-start | bytes 1572872 | tf_op jit(solution)/shard_map/ppermute | solution.py:22
  127.6 24.6 %copy-start.9 = (bf16[256,128]{1,0:T(8,128)(2,1)S(1)}, bf16[256,128]{1,0:T(8,128)(2,1)}, u32[]{:S(2)}) copy-start(bf16[256,128]{1,0:T(8,128)(2,1)} %param.17) | copy-start | bytes 196612
  127.6 24.6 %copy-start.10 = (bf16[256,128]{1,0:T(8,128)(2,1)S(1)}, bf16[256,128]{1,0:T(8,128)(2,1)}, u32[]{:S(2)}) copy-start(bf16[256,128]{1,0:T(8,128)(2,1)} %param.18) | copy-start | bytes 196612
  127.6 11.0 %collective-permute-start.6 = (f32[17,8,256]{2,1,0:T(8,128)S(1)}, f32[17,8,256]{2,1,0:T(8,128)S(1)}, u32[]{:S(2)}, u32[]{:S(2)}) collective-permute-start(f32[17,8,256]{2,1,0:T(8,128)S(1)} %pad_maximum_fusion.5), channel_id=1, source_target_pairs={{0,16},{8,24},{16,32},{24,40},{32,48},{40,56},{48,64},{56,72},{64,... | collective-permute-start | bytes 417800 | tf_op jit(solution)/shard_map/ppermute | solution.py:22
  138.7 9.9 %collective-permute-start.7 = (f32[17,8,256]{2,1,0:T(8,128)S(1)}, f32[17,8,256]{2,1,0:T(8,128)S(1)}, u32[]{:S(2)}, u32[]{:S(2)}) collective-permute-start(f32[17,8,256]{2,1,0:T(8,128)S(1)} %pad_maximum_fusion.6), channel_id=1, source_target_pairs={{0,32},{8,40},{16,48},{24,56},{32,64},{40,72},{48,80},{56,88},{64,... | collective-permute-start | bytes 417800 | tf_op jit(solution)/shard_map/ppermute | solution.py:22
  148.6 6.9 %collective-permute-start.8 = (f32[17,8,256]{2,1,0:T(8,128)S(1)}, f32[17,8,256]{2,1,0:T(8,128)S(1)}, u32[]{:S(2)}, u32[]{:S(2)}) collective-permute-start(f32[17,8,256]{2,1,0:T(8,128)S(1)} %pad_maximum_fusion.7), channel_id=1, source_target_pairs={{0,64},{8,72},{16,80},{24,88},{32,96},{40,104},{48,112},{56,120},{... | collective-permute-start | bytes 417800 | tf_op jit(solution)/shard_map/ppermute | solution.py:22
  152.2 7.9 %copy-start.19 = (bf16[2304,256]{1,0:T(8,128)(2,1)}, bf16[2304,256]{1,0:T(8,128)(2,1)S(1)}, u32[]{:S(2)}) copy-start(bf16[2304,256]{1,0:T(8,128)(2,1)S(1)} %constant_dynamic-update-slice_fusion.7.k_ref.v_ref) | copy-start | bytes 3538948
  155.6 18.6 %collective-permute-start.9 = (f32[17,8,256]{2,1,0:T(8,128)S(1)}, f32[17,8,256]{2,1,0:T(8,128)S(1)}, u32[]{:S(2)}, u32[]{:S(2)}) collective-permute-start(f32[17,8,256]{2,1,0:T(8,128)S(1)} %pad_maximum_fusion.8), channel_id=1, source_target_pairs={{0,128},{8,136},{16,144},{24,152},{32,160},{40,168},{48,176},{56,1... | collective-permute-start | bytes 417800 | tf_op jit(solution)/shard_map/ppermute | solution.py:22
  190.8 2.7 %copy-start.2 = (f32[259,2048]{1,0:T(8,128)S(1)}, f32[259,2048]{1,0:T(8,128)}, u32[]{:S(2)}) copy-start(f32[259,2048]{1,0:T(8,128)} %copy-done.1) | copy-start | bytes 6365188
  190.8 2.7 %copy-start.5 = (bf16[256,2048]{1,0:T(8,128)(2,1)S(1)}, bf16[256,2048]{1,0:T(8,128)(2,1)}, u32[]{:S(2)}) copy-start(bf16[256,2048]{1,0:T(8,128)(2,1)} %param.15) | copy-start | bytes 3145732
  190.8 2.7 %copy-start.14 = (f32[1,2048]{1,0:T(1,128)S(1)}, f32[1,2048]{1,0:T(1,128)}, u32[]{:S(2)}) copy-start(f32[1,2048]{1,0:T(1,128)} %copy-done.13) | copy-start | bytes 24580
  190.9 2.7 %copy-start.16 = (f32[1,2048]{1,0:T(1,128)S(1)}, f32[1,2048]{1,0:T(1,128)}, u32[]{:S(2)}) copy-start(f32[1,2048]{1,0:T(1,128)} %copy-done.15) | copy-start | bytes 24580
  190.9 2.7 %copy-start.18 = (f32[2048]{0:T(1024)S(1)}, f32[2048]{0:T(1024)}, u32[]{:S(2)}) copy-start(f32[2048]{0:T(1024)} %param.20) | copy-start | bytes 24580
  190.9 2.7 %copy-start.20 = (f32[2048]{0:T(1024)S(1)}, f32[2048]{0:T(1024)}, u32[]{:S(2)}) copy-start(f32[2048]{0:T(1024)} %param.27) | copy-start | bytes 24580

commit v5 on v4

--- a/solution.py
+++ b/solution.py
@@ -88,16 +88,20 @@
     )(bc, dt3, dr3, rate3, h0)
 
 
-def attention_kernel(base_ref, q_ref, k_ref, v_ref, o_ref):
+def attention_kernel(base_ref, q_ref, k_ref, v_ref, o_ref, bias_ref):
+    @pl.when(pl.program_id(0) == 0)
+    def _():
+        rows = lax.broadcasted_iota(jnp.int32, bias_ref.shape, 0)
+        cols = lax.broadcasted_iota(jnp.int32, bias_ref.shape, 1)
+        distance = WINDOW + rows - cols
+        in_window = (distance >= 0) & (distance < WINDOW) & (cols + base_ref[0] >= WINDOW)
+        bias_ref[...] = jnp.where(in_window, 0.0, -jnp.inf)
+
     scores = lax.dot_general(
         q_ref[...], k_ref[...], (((1,), (1,)), ((), ())), preferred_element_type=jnp.float32
-    ) * (1.0 / math.sqrt(HD))
-    rows = lax.broadcasted_iota(jnp.int32, scores.shape, 0)
-    cols = lax.broadcasted_iota(jnp.int32, scores.shape, 1)
-    distance = WINDOW + rows - cols
-    in_window = (distance >= 0) & (distance < WINDOW) & (cols + base_ref[0] >= WINDOW)
-    row_peak = jnp.max(jnp.where(in_window, scores, -jnp.inf), axis=1, keepdims=True)
-    weights = jnp.exp(jnp.where(in_window, scores - row_peak, -jnp.inf)).astype(jnp.bfloat16)
+    ) * (1.0 / math.sqrt(HD)) + bias_ref[...]
+    row_peak = jnp.max(scores, axis=1, keepdims=True)
+    weights = jnp.exp(scores - row_peak).astype(jnp.bfloat16)
     summed = jnp.sum(weights.astype(jnp.float32), axis=1, keepdims=True)
     weighted = jnp.dot(weights, v_ref[...], preferred_element_type=jnp.float32)
     o_ref[...] = (weighted / summed).astype(o_ref.dtype)
@@ -119,6 +123,7 @@
         ],
         out_specs=pl.BlockSpec((tokens, HD), lambda h: (0, h)),
         out_shape=jax.ShapeDtypeStruct((tokens, width), q_proj.dtype),
+        scratch_shapes=[pltpu.VMEM((tokens, keys), jnp.float32)],
         cost_estimate=pl.CostEstimate(
             flops=4 * tokens * keys * HD * heads,
             transcendentals=tokens * keys * heads,
@@ -143,32 +148,36 @@
     return jnp.concatenate([(earlier[0] + later[0])[None], states], axis=0)
 
 
-def entering_state(step_sum, final_state, rate3):
-    local = jnp.concatenate([step_sum[None], final_state], axis=0)
+def scan_with_window(step_sum, final_state, rate3, own, key_span):
+    rows = (final_state.shape[0] + 1) * final_state.shape[1]
+    lanes = final_state.shape[2]
+    local = jnp.concatenate([step_sum[None], final_state], axis=0).reshape(rows, lanes)
+    own = own.astype(jnp.float32)
+    tokens = own.shape[0]
     peers = lax.axis_size("seq")
-    running = shifted(local, "seq", 1)
+
+    def merge(received, running):
+        earlier = received[:rows].reshape(-1, *final_state.shape[1:])
+        later = running.reshape(-1, *final_state.shape[1:])
+        return compose(earlier, later, rate3).reshape(rows, lanes)
+
+    first = shifted(jnp.concatenate([local, own], axis=0), "seq", 1)
+    running = first[:rows]
+    held = [first[rows:]]
     distance = 1
     while distance < peers - 1:
-        running = compose(shifted(running, "seq", distance), running, rate3)
+        payload = [running]
+        if len(held) < key_span:
+            payload = payload + held[-distance:]
+        received = shifted(jnp.concatenate(payload, axis=0), "seq", distance)
+        if len(held) < key_span:
+            count = len(payload) - 1
+            held = [received[rows + i * tokens : rows + (i + 1) * tokens] for i in range(count)] + held
+        running = merge(received, running)
         distance *= 2
-    return running[1:]
-
-
-def window_blocks(k_proj, v_proj, conv_tail, key_span):
-    tokens = k_proj.shape[0]
-    own = jnp.concatenate([k_proj, v_proj], axis=1)
-    width = own.shape[1]
-    tail = conv_tail.reshape(-1, width)
-    first = shifted(jnp.concatenate([own, tail], axis=0), "seq", 1)
-    tail_in = first[tokens:].reshape(conv_tail.shape)
-    held = [first[:tokens], own]
-    reach = 2
-    while reach * 2 <= key_span:
-        held = [shifted(jnp.concatenate(held, axis=0), "seq", reach)] + held
-        reach *= 2
-    assert reach == key_span
-    held = [shifted(own, "seq", key_span)] + held
-    return jnp.concatenate(held, axis=0), tail_in
+    assert len(held) == key_span
+    window = jnp.concatenate(held + [own], axis=0).astype(jnp.bfloat16)
+    return running.reshape(-1, *final_state.shape[1:])[1:], window
 
 
 def per_device(
@@ -190,7 +199,7 @@
     tokens_here, channels = conv_in.shape
     key_span = WINDOW // tokens_here
     conv_tail = conv_in[tokens_here - (KCONV - 1) :]
-    window, tail_in = window_blocks(k_proj, v_proj, conv_tail, key_span)
+    tail_in = shifted(conv_tail, "seq", 1)
     padded = jnp.concatenate([tail_in, conv_in], axis=0).astype(jnp.float32)
     activated = causal_conv(padded, conv_weight, conv_bias, tokens_here)
     state_parts = lax.dot_general(
@@ -215,7 +224,8 @@
     zero_state = jnp.zeros((state_count, SUBLANES, lanes), jnp.float32)
     local_final = run_scan(state_in, dt3, dr3, rate3, zero_state, False)
     step_sum = jnp.sum(dt3, axis=0)
-    entering = entering_state(step_sum, local_final, rate3)
+    own_kv = jnp.concatenate([k_proj, v_proj], axis=1)
+    entering, window = scan_with_window(step_sum, local_final, rate3, own_kv, key_span)
     mamba_sum = run_scan(state_in, dt3, dr3, rate3, entering, True).reshape(tokens_here, channels)
     mamba_out = (
         (mamba_sum + skip_weight[None, :] * activated.astype(jnp.float32))

time: 197 us -> 243 us (1.23)
  waiting for transfers between devices: 77.8 us -> 130 us
  starting transfers between devices: 44.3 us -> 33 us
    ppermute x10 -> x7, waiting for transfers between devices: 41.9 us -> 91.1 us  [shifted(): lax.ppermute(value, axis, [(source, source + steps) for source in range(f...]
    ppermute x10 -> x7, starting transfers between devices: 36.6 us -> 28 us  [shifted(): lax.ppermute(value, axis, [(source, source + steps) for source in range(f...]
    ppermute x3, starting transfers between devices: 7.7 us -> 4.95 us  [butterfly_sum(): value = value + lax.ppermute(value, axis, pairs)]
    ppermute x3, waiting for transfers between devices: 35.8 us -> 38.4 us  [butterfly_sum(): value = value + lax.ppermute(value, axis, pairs)]
    unnamed x52 -> x67, local copies, waits for them, and re-layouts: 11.2 us -> 13.2 us
  transfers between devices with their start and end apart: 13 -> 10, of which waited for: 10 -> 9; matrix products, arithmetic and copies ran while one was open for 7% -> 2% of each run, Pallas kernels for 14% -> 6%
where the time goes in v5:
time: 243 us; the launch traced here: 240 us
  waiting for transfers between devices  130 us (53%)
  Pallas kernels  41.8 us (17%)
  starting transfers between devices  33 us (14%)
  local copies, waits for them, and re-layouts  16.5 us (7%)
  other arithmetic  10.8 us (4%)
  matrix products  7.62 us (3%)
    ppermute x7, waiting for transfers between devices, shifted(): lax.ppermute(value, axis, [(source, source + steps) for source in range(f...  91.1 us
    ppermute x3, waiting for transfers between devices, butterfly_sum(): value = value + lax.ppermute(value, axis, pairs)  38.4 us
    pallas_call x2, Pallas kernels, run_scan(): pl.pallas_call(functools.partial(scan_kernel, with_out), grid=(blocks,),...  28.3 us
    ppermute x7, starting transfers between devices, shifted(): lax.ppermute(value, axis, [(source, source + steps) for source in range(f...  28 us
    pallas_call x1, Pallas kernels, run_attention(): pl.pallas_call(attention_kernel, grid=(heads,), in_specs=[pl.BlockSpec(me...  13.4 us
    unnamed x67, local copies, waits for them, and re-layouts  13.2 us
    ppermute x3, starting transfers between devices, butterfly_sum(): value = value + lax.ppermute(value, axis, pairs)  4.95 us
    dot_general x1, matrix products, per_device(): jnp.dot(rank_normed, dt_weight, preferred_element_type=jnp.float32)  4.91 us
  transfers between devices with their start and end apart: 10, of which 9 were waited for; matrix products, arithmetic and copies ran while one was open for 2% of the time, Pallas kernels for 6%

profile of v5, /device:TPU:8, one launch (start us, length us, event | category | flops | bytes accessed | tf_op | source)
XLA Modules:
  0.0 240.3 jit_solution(17043069552578935477)
XLA Ops:
  0.7 0.9 slice.124
  1.6 9.1 %collective-permute-start = (bf16[3,2048]{1,0:T(4,128)(2,1)S(1)}, bf16[3,2048]{1,0:T(4,128)(2,1)S(1)}, u32[]{:S(2)}, u32[]{:S(2)}) collective-permute-start(bf16[3,2048]{1,0:T(4,128)(2,1)S(1)} %slice.124), channel_id=1, source_target_pairs={{0,8},{8,16},{16,24},{24,32},{32,40},{40,48},{48,56},{56,64},{64,7... | collective-permute-start | bytes 36872 | tf_op jit(solution)/shard_map/ppermute | solution.py:22
  10.7 0.9 fusion.25
  11.7 2.8 %collective-permute-done = bf16[3,2048]{1,0:T(4,128)(2,1)S(1)} collective-permute-done((bf16[3,2048]{1,0:T(4,128)(2,1)S(1)}, bf16[3,2048]{1,0:T(4,128)(2,1)S(1)}, u32[]{:S(2)}, u32[]{:S(2)}) %collective-permute-start) | collective-permute-done | bytes 12320 | tf_op jit(solution)/shard_map/ppermute | solution.py:22
  14.5 1.5 maximum_convert_fusion
  16.0 1.3 multiply_convert_fusion
  17.4 0.4 convolution_bitcast_fusion
  17.9 2.3 fusion.26
  20.3 0.1 collective-permute-start.1
  20.4 1.9 collective-permute-done.1
  22.3 0.1 fusion.23
  22.4 1.7 collective-permute-start.2
  24.1 13.1 %collective-permute-done.2 = f32[272,512]{1,0:T(8,128)S(1)} collective-permute-done((f32[272,512]{1,0:T(8,128)S(1)}, f32[272,512]{1,0:T(8,128)S(1)}, u32[]{:S(2)}, u32[]{:S(2)}) %collective-permute-start.2) | collective-permute-done | bytes 557088 | tf_op jit(solution)/shard_map/ppermute | solution.py:140
  37.3 3.2 %collective-permute-start.3 = (f32[272,512]{1,0:T(8,128)S(1)}, f32[272,512]{1,0:T(8,128)S(1)}, u32[]{:S(2)}, u32[]{:S(2)}) collective-permute-start(f32[272,512]{1,0:T(8,128)S(1)} %add.115), channel_id=1, source_target_pairs={{0,4},{1,5},{2,6},{3,7},{4,0},{5,1},{6,2},{7,3},{8,12},{9,13},{10,... | collective-permute-start | bytes 1671176 | tf_op jit(solution)/shard_map/ppermute | solution.py:140
  40.5 0.7 copy.18
  41.2 23.4 %collective-permute-done.3 = f32[272,512]{1,0:T(8,128)S(1)} collective-permute-done((f32[272,512]{1,0:T(8,128)S(1)}, f32[272,512]{1,0:T(8,128)S(1)}, u32[]{:S(2)}, u32[]{:S(2)}) %collective-permute-start.3) | collective-permute-done | bytes 557088 | tf_op jit(solution)/shard_map/ppermute | solution.py:140
  64.6 0.1 add.116
  64.7 0.1 multiply_reduce_fusion
  64.8 0.7 copy-done.4
  65.5 0.6 reshape.100.bc_ref
  66.1 4.9 %fusion.24 = (f32[2048]{0:T(1024)S(1)}, f32[256,2048]{1,0:T(8,128)}, f32[256,2048]{1,0:T(8,128)}) fusion(bf16[256,2048]{1,0:T(8,128)(2,1)S(1)} %multiply_convert_fusion, f32[2048]{0:T(1024)S(1)} %copy-done.27, bf16[512,2048]{1,0:T(8,128)(2,1)S(1)} %copy-done, f32[272,512]{1,0:T(8,128)} %copy-done.4, f32[512]{0:T(512)S(1)} %copy-done.28, ...), kind=kOutput, calls=%fused_computation.66 | convolution fusion | flops 542504960 | bytes 7883776 | tf_op jit(solution)/shard_map/dot_general | solution.py:216
  71.0 4.0 %copy.17 = f32[32,8,8,256]{3,2,1,0:T(8,128)} copy(f32[32,8,8,256]{3,1,2,0:T(8,128)} %bitcast.87) | data formatting | bytes 4194304
  75.0 2.3 copy.16
  77.2 0.7 broadcast_in_dim.5.h0_ref
  77.9 12.5 %shard_map.149 = f32[16,8,256]{2,1,0:T(8,128)} custom-call(f32[32,256]{1,0:T(8,128)} %reshape.100.bc_ref, f32[256,8,256]{2,1,0:T(8,128)} %bitcast.84, f32[256,8,256]{2,1,0:T(8,128)} %bitcast.82, f32[16,8,256]{2,1,0:T(8,128)} %bitcast.80, f32[16,8,256]{2,1,0:T(8,128)} %broadcast_in_dim.5.h0_ref), custom_call_target="tpu_custom_call" | custom-call | flops 33554432 | bytes 6553600 | tf_op jit(solution)/shard_map/pallas_call | solution.py:71
  90.4 0.9 maximum_bitcast_fusion
  91.4 5.4 %collective-permute-start.4 = (f32[392,256]{1,0:T(8,128)S(1)}, f32[392,256]{1,0:T(8,128)S(1)}, u32[]{:S(2)}, u32[]{:S(2)}) collective-permute-start(f32[392,256]{1,0:T(8,128)S(1)} %pad_maximum_fusion.3), channel_id=1, source_target_pairs={{0,8},{8,16},{16,24},{24,32},{32,40},{40,48},{48,56},{56,64},{64,7... | collective-permute-start | bytes 1204232 | tf_op jit(solution)/shard_map/ppermute | solution.py:22
  96.8 22.2 %collective-permute-done.4 = f32[392,256]{1,0:T(8,128)S(1)} collective-permute-done((f32[392,256]{1,0:T(8,128)S(1)}, f32[392,256]{1,0:T(8,128)S(1)}, u32[]{:S(2)}, u32[]{:S(2)}) %collective-permute-start.4) | collective-permute-done | bytes 401440 | tf_op jit(solution)/shard_map/ppermute | solution.py:22
  118.9 1.9 collective-permute-start.5
  120.9 18.1 %collective-permute-done.5 = f32[392,256]{1,0:T(8,128)S(1)} collective-permute-done((f32[392,256]{1,0:T(8,128)S(1)}, f32[392,256]{1,0:T(8,128)S(1)}, u32[]{:S(2)}, u32[]{:S(2)}) %collective-permute-start.5) | collective-permute-done | bytes 401440 | tf_op jit(solution)/shard_map/ppermute | solution.py:22
  139.1 1.9 collective-permute-start.6
  141.0 18.1 %collective-permute-done.6 = f32[648,256]{1,0:T(8,128)S(1)} collective-permute-done((f32[648,256]{1,0:T(8,128)S(1)}, f32[648,256]{1,0:T(8,128)S(1)}, u32[]{:S(2)}, u32[]{:S(2)}) %collective-permute-start.6) | collective-permute-done | bytes 663584 | tf_op jit(solution)/shard_map/ppermute | solution.py:22
  159.1 0.5 copy-done.13
  159.7 1.1 pad_maximum_fusion
  160.8 2.0 collective-permute-start.7
  162.9 29.0 %collective-permute-done.7 = f32[1160,256]{1,0:T(8,128)} collective-permute-done((f32[1160,256]{1,0:T(8,128)}, f32[1160,256]{1,0:T(8,128)}, u32[]{:S(2)}, u32[]{:S(2)}) %collective-permute-start.7) | collective-permute-done | bytes 1187872 | tf_op jit(solution)/shard_map/ppermute | solution.py:22
  191.9 0.9 fusion.18
  192.8 0.7 slice_add_fusion.1
  193.6 3.5 %collective-permute-start.8 = (f32[136,256]{1,0:T(8,128)S(1)}, f32[136,256]{1,0:T(8,128)S(1)}, u32[]{:S(2)}, u32[]{:S(2)}) collective-permute-start(f32[136,256]{1,0:T(8,128)S(1)} %maximum_bitcast_fusion.3), channel_id=1, source_target_pairs={{0,64},{8,72},{16,80},{24,88},{32,96},{40,104},{48,112},{56,120},{... | collective-permute-start | bytes 417800 | tf_op jit(solution)/shard_map/ppermute | solution.py:22
  197.1 1.3 fusion.10
  198.4 1.0 convert_dynamic-update-slice_fusion.2
  199.5 1.1 collective-permute-done.8
  200.6 4.2 %collective-permute-start.9 = (f32[136,256]{1,0:T(8,128)S(1)}, f32[136,256]{1,0:T(8,128)S(1)}, u32[]{:S(2)}, u32[]{:S(2)}) collective-permute-start(f32[136,256]{1,0:T(8,128)S(1)} %maximum_bitcast_fusion.4), channel_id=1, source_target_pairs={{0,128},{8,136},{16,144},{24,152},{32,160},{40,168},{48,176},{56,1... | collective-permute-start | bytes 417800 | tf_op jit(solution)/shard_map/ppermute | solution.py:22
  204.8 13.4 %shard_map.151 = bf16[256,1024]{1,0:T(8,128)(2,1)} custom-call(s32[1]{0:T(128)} %bitcast.20.base_ref, bf16[256,1024]{1,0:T(8,128)(2,1)} %q_ref.1, bf16[2304,256]{1,0:T(8,128)(2,1)} %copy-done.12, bf16[2304,256]{1,0:T(8,128)(2,1)} %copy-done.12), custom_call_target="tpu_custom_call" | custom-call | flops 2415919104 | bytes 3407872 | tf_op jit(solution)/shard_map/pallas_call | solution.py:115
  218.2 0.7 fusion.14.h0_ref
  218.9 15.8 %shard_map.150 = f32[256,8,256]{2,1,0:T(8,128)} custom-call(f32[32,256]{1,0:T(8,128)} %reshape.100.bc_ref, f32[256,8,256]{2,1,0:T(8,128)} %bitcast.85, f32[256,8,256]{2,1,0:T(8,128)} %bitcast.83, f32[16,8,256]{2,1,0:T(8,128)} %bitcast.81, f32[16,8,256]{2,1,0:T(8,128)} %fusion.14.h0_ref), custom_call_target="tpu_custom_call" | custom-call | flops 50331648 | bytes 6553600 | tf_op jit(solution)/shard_map/pallas_call | solution.py:71
  234.8 2.6 %copy.19 = f32[32,8,8,256]{3,1,2,0:T(8,128)S(1)} copy(f32[32,8,8,256]{3,2,1,0:T(8,128)} %bitcast.88) | data formatting | bytes 4194304
  237.5 2.8 %fusion.2 = bf16[256,2048]{1,0:T(8,128)(2,1)} fusion(f32[256,2048]{1,0:T(8,128)S(1)} %bitcast.79, bf16[256,2048]{1,0:T(8,128)(2,1)S(1)} %copy-done.7, f32[2048]{0:T(1024)S(1)} %copy-done.26, f32[259,2048]{1,0:T(8,128)S(1)} %copy-done.2, f32[2048]{0:T(1024)S(1)} %bitcast.99, f32[2048]{0:T(1024)S(1)} %bitcast.101, f32[2048]{0:T(1024)S(1)} %bitcast.97, ...), kind=kLoop, calls=%fused_computation.8 | loop fusion | flops 12058624 | bytes 12632064 | tf_op jit(solution)/shard_map/convert_element_type | solution.py:233
  (83 shorter events, 0.8 us)
Async XLA Ops:
  0.6 65.5 %copy-start = (bf16[512,2048]{1,0:T(8,128)(2,1)S(1)}, bf16[512,2048]{1,0:T(8,128)(2,1)}, u32[]{:S(2)}) copy-start(bf16[512,2048]{1,0:T(8,128)(2,1)} %param.24) | copy-start | bytes 6291460
  0.6 15.4 %copy-start.24 = (f32[2048]{0:T(1024)S(1)}, f32[2048]{0:T(1024)}, u32[]{:S(2)}) copy-start(f32[2048]{0:T(1024)} %param.20) | copy-start | bytes 24580
  1.6 12.9 %collective-permute-start = (bf16[3,2048]{1,0:T(4,128)(2,1)S(1)}, bf16[3,2048]{1,0:T(4,128)(2,1)S(1)}, u32[]{:S(2)}, u32[]{:S(2)}) collective-permute-start(bf16[3,2048]{1,0:T(4,128)(2,1)S(1)} %slice.124), channel_id=1, source_target_pairs={{0,8},{8,16},{16,24},{24,32},{32,40},{40,48},{48,56},{56,64},{64,7... | collective-permute-start | bytes 36872 | tf_op jit(solution)/shard_map/ppermute | solution.py:22
  11.6 5.7 %copy-start.16 = (f32[1,2048]{1,0:T(1,128)}, f32[1,2048]{1,0:T(1,128)S(1)}, u32[]{:S(2)}) copy-start(f32[1,2048]{1,0:T(1,128)S(1)} %get-tuple-element.6) | copy-start | bytes 24580
  11.6 5.7 %copy-start.18 = (f32[1,2048]{1,0:T(1,128)}, f32[1,2048]{1,0:T(1,128)S(1)}, u32[]{:S(2)}) copy-start(f32[1,2048]{1,0:T(1,128)S(1)} %get-tuple-element.7) | copy-start | bytes 24580
  11.7 5.7 %copy-start.20 = (f32[1,2048]{1,0:T(1,128)}, f32[1,2048]{1,0:T(1,128)S(1)}, u32[]{:S(2)}) copy-start(f32[1,2048]{1,0:T(1,128)S(1)} %get-tuple-element.8) | copy-start | bytes 24580
  11.7 5.7 %copy-start.22 = (f32[1,2048]{1,0:T(1,128)}, f32[1,2048]{1,0:T(1,128)S(1)}, u32[]{:S(2)}) copy-start(f32[1,2048]{1,0:T(1,128)S(1)} %get-tuple-element.9) | copy-start | bytes 24580
  16.0 1.4 copy-start.1
  16.0 1.4 copy-start.14
  20.2 20.3 %copy-start.15 = (f32[16,2048]{1,0:T(8,128)S(1)}, f32[16,2048]{1,0:T(8,128)}, u32[]{:S(2)}) copy-start(f32[16,2048]{1,0:T(8,128)} %param.26) | copy-start | bytes 393220
  20.2 21.0 %copy-start.8 = (bf16[256,128]{1,0:T(8,128)(2,1)S(1)}, bf16[256,128]{1,0:T(8,128)(2,1)}, u32[]{:S(2)}) copy-start(bf16[256,128]{1,0:T(8,128)(2,1)} %param.17) | copy-start | bytes 196612
  20.2 21.0 %copy-start.10 = (bf16[256,128]{1,0:T(8,128)(2,1)S(1)}, bf16[256,128]{1,0:T(8,128)(2,1)}, u32[]{:S(2)}) copy-start(bf16[256,128]{1,0:T(8,128)(2,1)} %param.18) | copy-start | bytes 196612
  20.3 2.0 collective-permute-start.1
  22.4 43.7 %copy-start.27 = (f32[2048]{0:T(1024)S(1)}, f32[2048]{0:T(1024)}, u32[]{:S(2)}) copy-start(f32[2048]{0:T(1024)} %param.25) | copy-start | bytes 24580
  22.4 43.7 %copy-start.28 = (f32[512]{0:T(512)S(1)}, f32[512]{0:T(512)}, u32[]{:S(2)}) copy-start(f32[512]{0:T(512)} %param.23) | copy-start | bytes 6148
  22.4 14.8 %collective-permute-start.2 = (f32[272,512]{1,0:T(8,128)S(1)}, f32[272,512]{1,0:T(8,128)S(1)}, u32[]{:S(2)}, u32[]{:S(2)}) collective-permute-start(f32[272,512]{1,0:T(8,128)S(1)} %fusion.23), channel_id=1, source_target_pairs={{0,2},{1,3},{2,0},{3,1},{4,6},{5,7},{6,4},{7,5},{8,10},{9,11},{10,... | collective-permute-start | bytes 1671176 | tf_op jit(solution)/shard_map/ppermute | solution.py:140
  37.3 27.3 %collective-permute-start.3 = (f32[272,512]{1,0:T(8,128)S(1)}, f32[272,512]{1,0:T(8,128)S(1)}, u32[]{:S(2)}, u32[]{:S(2)}) collective-permute-start(f32[272,512]{1,0:T(8,128)S(1)} %add.115), channel_id=1, source_target_pairs={{0,4},{1,5},{2,6},{3,7},{4,0},{5,1},{6,2},{7,3},{8,12},{9,13},{10,... | collective-permute-start | bytes 1671176 | tf_op jit(solution)/shard_map/ppermute | solution.py:140
  64.7 0.8 copy-start.4
  71.0 4.0 %copy-start.5 = (f32[256,2048]{1,0:T(8,128)S(1)}, f32[256,2048]{1,0:T(8,128)}, u32[]{:S(2)}) copy-start(f32[256,2048]{1,0:T(8,128)} %get-tuple-element.10) | copy-start | bytes 6291460
  77.9 61.0 %copy-start.3 = (f32[2,8,8,256]{3,2,1,0:T(8,128)S(1)}, f32[2,8,8,256]{3,2,1,0:T(8,128)}, u32[]{:S(2)}) copy-start(f32[2,8,8,256]{3,2,1,0:T(8,128)} %copy.18) | copy-start | bytes 393220
  91.4 27.5 %collective-permute-start.4 = (f32[392,256]{1,0:T(8,128)S(1)}, f32[392,256]{1,0:T(8,128)S(1)}, u32[]{:S(2)}, u32[]{:S(2)}) collective-permute-start(f32[392,256]{1,0:T(8,128)S(1)} %pad_maximum_fusion.3), channel_id=1, source_target_pairs={{0,8},{8,16},{16,24},{24,32},{32,40},{40,48},{48,56},{56,64},{64,7... | collective-permute-start | bytes 1204232 | tf_op jit(solution)/shard_map/ppermute | solution.py:22
  118.9 20.0 %collective-permute-start.5 = (f32[392,256]{1,0:T(8,128)S(1)}, f32[392,256]{1,0:T(8,128)S(1)}, u32[]{:S(2)}, u32[]{:S(2)}) collective-permute-start(f32[392,256]{1,0:T(8,128)S(1)} %collective-permute-done.4), channel_id=1, source_target_pairs={{0,8},{8,16},{16,24},{24,32},{32,40},{40,48},{48,56},{56,64},{64,7... | collective-permute-start | bytes 1204232 | tf_op jit(solution)/shard_map/ppermute | solution.py:22
  138.9 20.2 %copy-start.6 = (f32[392,256]{1,0:T(8,128)}, f32[392,256]{1,0:T(8,128)S(1)}, u32[]{:S(2)}) copy-start(f32[392,256]{1,0:T(8,128)S(1)} %collective-permute-done.5) | copy-start | bytes 1204228
  139.1 20.0 %collective-permute-start.6 = (f32[648,256]{1,0:T(8,128)S(1)}, f32[648,256]{1,0:T(8,128)S(1)}, u32[]{:S(2)}, u32[]{:S(2)}) collective-permute-start(f32[648,256]{1,0:T(8,128)S(1)} %pad_maximum_fusion.1), channel_id=1, source_target_pairs={{0,16},{8,24},{16,32},{24,40},{32,48},{40,56},{48,64},{56,72},{64,... | collective-permute-start | bytes 1990664 | tf_op jit(solution)/shard_map/ppermute | solution.py:22
  159.1 0.6 copy-start.13
  159.7 39.7 %copy-start.9 = (bf16[256,128]{1,0:T(8,128)(2,1)S(1)}, bf16[256,128]{1,0:T(8,128)(2,1)}, u32[]{:S(2)}) copy-start(bf16[256,128]{1,0:T(8,128)(2,1)} %param.17) | copy-start | bytes 196612
  160.8 38.6 %copy-start.11 = (bf16[256,128]{1,0:T(8,128)(2,1)S(1)}, bf16[256,128]{1,0:T(8,128)(2,1)}, u32[]{:S(2)}) copy-start(bf16[256,128]{1,0:T(8,128)(2,1)} %param.18) | copy-start | bytes 196612
  160.8 31.0 %collective-permute-start.7 = (f32[1160,256]{1,0:T(8,128)}, f32[1160,256]{1,0:T(8,128)}, u32[]{:S(2)}, u32[]{:S(2)}) collective-permute-start(f32[1160,256]{1,0:T(8,128)} %pad_maximum_fusion), channel_id=1, source_target_pairs={{0,32},{8,40},{16,48},{24,56},{32,64},{40,72},{48,80},{56,88},{64,... | collective-permute-start | bytes 3563528 | tf_op jit(solution)/shard_map/ppermute | solution.py:22
  193.6 6.9 %collective-permute-start.8 = (f32[136,256]{1,0:T(8,128)S(1)}, f32[136,256]{1,0:T(8,128)S(1)}, u32[]{:S(2)}, u32[]{:S(2)}) collective-permute-start(f32[136,256]{1,0:T(8,128)S(1)} %maximum_bitcast_fusion.3), channel_id=1, source_target_pairs={{0,64},{8,72},{16,80},{24,88},{32,96},{40,104},{48,112},{56,120},{... | collective-permute-start | bytes 417800 | tf_op jit(solution)/shard_map/ppermute | solution.py:22
  199.5 1.1 copy-start.12
  200.6 17.6 %collective-permute-start.9 = (f32[136,256]{1,0:T(8,128)S(1)}, f32[136,256]{1,0:T(8,128)S(1)}, u32[]{:S(2)}, u32[]{:S(2)}) collective-permute-start(f32[136,256]{1,0:T(8,128)S(1)} %maximum_bitcast_fusion.4), channel_id=1, source_target_pairs={{0,128},{8,136},{16,144},{24,152},{32,160},{40,168},{48,176},{56,1... | collective-permute-start | bytes 417800 | tf_op jit(solution)/shard_map/ppermute | solution.py:22
  234.8 2.7 %copy-start.2 = (f32[259,2048]{1,0:T(8,128)S(1)}, f32[259,2048]{1,0:T(8,128)}, u32[]{:S(2)}) copy-start(f32[259,2048]{1,0:T(8,128)} %copy-done.1) | copy-start | bytes 6365188
  234.8 2.7 %copy-start.7 = (bf16[256,2048]{1,0:T(8,128)(2,1)S(1)}, bf16[256,2048]{1,0:T(8,128)(2,1)}, u32[]{:S(2)}) copy-start(bf16[256,2048]{1,0:T(8,128)(2,1)} %param.15) | copy-start | bytes 3145732
  234.8 2.7 %copy-start.17 = (f32[1,2048]{1,0:T(1,128)S(1)}, f32[1,2048]{1,0:T(1,128)}, u32[]{:S(2)}) copy-start(f32[1,2048]{1,0:T(1,128)} %copy-done.16) | copy-start | bytes 24580
  234.8 2.7 %copy-start.19 = (f32[1,2048]{1,0:T(1,128)S(1)}, f32[1,2048]{1,0:T(1,128)}, u32[]{:S(2)}) copy-start(f32[1,2048]{1,0:T(1,128)} %copy-done.18) | copy-start | bytes 24580
  234.8 2.7 %copy-start.21 = (f32[1,2048]{1,0:T(1,128)S(1)}, f32[1,2048]{1,0:T(1,128)}, u32[]{:S(2)}) copy-start(f32[1,2048]{1,0:T(1,128)} %copy-done.20) | copy-start | bytes 24580
  234.8 2.7 %copy-start.23 = (f32[1,2048]{1,0:T(1,128)S(1)}, f32[1,2048]{1,0:T(1,128)}, u32[]{:S(2)}) copy-start(f32[1,2048]{1,0:T(1,128)} %copy-done.22) | copy-start | bytes 24580
  234.8 2.7 %copy-start.25 = (f32[2048]{0:T(1024)S(1)}, f32[2048]{0:T(1024)}, u32[]{:S(2)}) copy-start(f32[2048]{0:T(1024)} %param.20) | copy-start | bytes 24580
  234.8 2.7 %copy-start.26 = (f32[2048]{0:T(1024)S(1)}, f32[2048]{0:T(1024)}, u32[]{:S(2)}) copy-start(f32[2048]{0:T(1024)} %param.27) | copy-start | bytes 24580

commit v6 on v4

--- a/solution.py
+++ b/solution.py
@@ -88,16 +88,20 @@
     )(bc, dt3, dr3, rate3, h0)
 
 
-def attention_kernel(base_ref, q_ref, k_ref, v_ref, o_ref):
+def attention_kernel(base_ref, q_ref, k_ref, v_ref, o_ref, bias_ref):
+    @pl.when(pl.program_id(0) == 0)
+    def _():
+        rows = lax.broadcasted_iota(jnp.int32, bias_ref.shape, 0)
+        cols = lax.broadcasted_iota(jnp.int32, bias_ref.shape, 1)
+        distance = WINDOW + rows - cols
+        in_window = (distance >= 0) & (distance < WINDOW) & (cols + base_ref[0] >= WINDOW)
+        bias_ref[...] = jnp.where(in_window, 0.0, -jnp.inf)
+
     scores = lax.dot_general(
         q_ref[...], k_ref[...], (((1,), (1,)), ((), ())), preferred_element_type=jnp.float32
-    ) * (1.0 / math.sqrt(HD))
-    rows = lax.broadcasted_iota(jnp.int32, scores.shape, 0)
-    cols = lax.broadcasted_iota(jnp.int32, scores.shape, 1)
-    distance = WINDOW + rows - cols
-    in_window = (distance >= 0) & (distance < WINDOW) & (cols + base_ref[0] >= WINDOW)
-    row_peak = jnp.max(jnp.where(in_window, scores, -jnp.inf), axis=1, keepdims=True)
-    weights = jnp.exp(jnp.where(in_window, scores - row_peak, -jnp.inf)).astype(jnp.bfloat16)
+    ) * (1.0 / math.sqrt(HD)) + bias_ref[...]
+    row_peak = jnp.max(scores, axis=1, keepdims=True)
+    weights = jnp.exp(scores - row_peak).astype(jnp.bfloat16)
     summed = jnp.sum(weights.astype(jnp.float32), axis=1, keepdims=True)
     weighted = jnp.dot(weights, v_ref[...], preferred_element_type=jnp.float32)
     o_ref[...] = (weighted / summed).astype(o_ref.dtype)
@@ -119,6 +123,7 @@
         ],
         out_specs=pl.BlockSpec((tokens, HD), lambda h: (0, h)),
         out_shape=jax.ShapeDtypeStruct((tokens, width), q_proj.dtype),
+        scratch_shapes=[pltpu.VMEM((tokens, keys), jnp.float32)],
         cost_estimate=pl.CostEstimate(
             flops=4 * tokens * keys * HD * heads,
             transcendentals=tokens * keys * heads,
@@ -127,14 +132,24 @@
     )(base, q_proj, window, window)
 
 
-def butterfly_sum(value, axis):
-    count = lax.axis_size(axis)
-    stride = 1
-    while stride < count:
-        pairs = [(source, source ^ stride) for source in range(count)]
+def butterfly_sum(value, axis, first, last):
+    stride = first
+    while stride < last:
+        pairs = [(source, source ^ stride) for source in range(lax.axis_size(axis))]
         value = value + lax.ppermute(value, axis, pairs)
         stride *= 2
     return value
+
+
+def chip_first_sum(value, axis):
+    count = lax.axis_size(axis)
+    value = butterfly_sum(value, axis, 1, 2)
+    half = value.shape[0] // 2
+    core = lax.axis_index(axis) % 2
+    mine = jnp.where(core == 0, value[:half], value[half:])
+    mine = butterfly_sum(mine, axis, 2, count)
+    other = lax.ppermute(mine, axis, [(source, source ^ 1) for source in range(count)])
+    return jnp.where(core == 0, jnp.concatenate([mine, other]), jnp.concatenate([other, mine]))
 
 
 def compose(earlier, later, rate3):
@@ -199,7 +214,7 @@
     rank_part = jnp.dot(activated, proj_dt_weight, preferred_element_type=jnp.float32)
     rank_width = rank_part.shape[1]
     packed = jnp.concatenate([rank_part, state_parts.reshape(-1, rank_width)], axis=0)
-    total = butterfly_sum(packed, "tp")
+    total = chip_first_sum(packed, "tp")
     rank_low = total[:tokens_here]
     state_in = total[tokens_here:].reshape(state_parts.shape)
     rank_normed = rank_norm(rank_low, dt_gain)

time: 197 us -> 188 us (0.954)
  waiting for transfers between devices: 77.8 us -> 61.1 us
  other arithmetic: 9.64 us -> 13.3 us
  starting transfers between devices: 44.3 us -> 47.6 us
    ppermute x3, waiting for transfers between devices: 35.8 us -> 21.6 us  [butterfly_sum(): value = value + lax.ppermute(value, axis, pairs)]
    ppermute x10, starting transfers between devices: 36.6 us -> 39.9 us  [shifted(): lax.ppermute(value, axis, [(source, source + steps) for source in range(f...]
    ppermute x10, waiting for transfers between devices: 41.9 us -> 39.5 us  [shifted(): lax.ppermute(value, axis, [(source, source + steps) for source in range(f...]
    unnamed x52 -> x58, local copies, waits for them, and re-layouts: 11.2 us -> 10.7 us
  transfers between devices with their start and end apart: 13 -> 14, of which waited for: 10 -> 10; matrix products, arithmetic and copies ran while one was open for 7% -> 10% of each run, Pallas kernels for 14% -> 14%
where the time goes in v6:
time: 188 us
  waiting for transfers between devices  61.1 us (32%)
  starting transfers between devices  47.6 us (25%)
  Pallas kernels  41.8 us (22%)
  local copies, waits for them, and re-layouts  16.2 us (9%)
  other arithmetic  13.3 us (7%)
  matrix products  6.24 us (3%)
    ppermute x10, starting transfers between devices, shifted(): lax.ppermute(value, axis, [(source, source + steps) for source in range(f...  39.9 us
    ppermute x10, waiting for transfers between devices, shifted(): lax.ppermute(value, axis, [(source, source + steps) for source in range(f...  39.5 us
    pallas_call x2, Pallas kernels, run_scan(): pl.pallas_call(functools.partial(scan_kernel, with_out), grid=(blocks,),...  28.4 us
    ppermute x3, waiting for transfers between devices, butterfly_sum(): value = value + lax.ppermute(value, axis, pairs)  21.6 us
    pallas_call x1, Pallas kernels, run_attention(): pl.pallas_call(attention_kernel, grid=(heads,), in_specs=[pl.BlockSpec(me...  13.4 us
    unnamed x58, local copies, waits for them, and re-layouts  10.7 us
    ppermute x3, starting transfers between devices, butterfly_sum(): value = value + lax.ppermute(value, axis, pairs)  7.6 us
  transfers between devices with their start and end apart: 14, of which 10 were waited for; matrix products, arithmetic and copies ran while one was open for 10% of the time, Pallas kernels for 14%

profile of v6, /device:TPU:8, one launch (start us, length us, event | category | flops | bytes accessed | tf_op | source)
XLA Modules:
  0.0 187.5 jit_solution(9252220444174031257)
XLA Ops:
  0.7 0.9 slice.80
  1.6 0.9 constant_dynamic-update-slice_fusion.1
  2.5 0.9 constant_dynamic-update-slice_fusion
  3.4 9.1 %collective-permute-start = (bf16[280,256]{1,0:T(8,128)(2,1)S(1)}, bf16[280,256]{1,0:T(8,128)(2,1)S(1)}, u32[]{:S(2)}, u32[]{:S(2)}) collective-permute-start(bf16[280,256]{1,0:T(8,128)(2,1)S(1)} %pad_maximum_fusion.3), channel_id=1, source_target_pairs={{0,8},{8,16},{16,24},{24,32},{32,40},{40,48},{48,56},{56,64},{64,7... | collective-permute-start | bytes 430088 | tf_op jit(solution)/shard_map/ppermute | solution.py:22
  12.5 0.9 fusion.18
  13.4 4.9 %collective-permute-done = bf16[280,256]{1,0:T(8,128)(2,1)S(1)} collective-permute-done((bf16[280,256]{1,0:T(8,128)(2,1)S(1)}, bf16[280,256]{1,0:T(8,128)(2,1)S(1)}, u32[]{:S(2)}, u32[]{:S(2)}) %collective-permute-start) | collective-permute-done | bytes 143392 | tf_op jit(solution)/shard_map/ppermute | solution.py:22
  18.4 1.5 maximum_convert_fusion
  20.0 1.3 multiply_convert_fusion
  21.8 2.3 %fusion.19 = f32[256,512]{1,0:T(8,128)S(1)} fusion(bf16[256,2048]{1,0:T(8,128)(2,1)S(1)} %multiply_convert_fusion, bf16[2048,512]{1,0:T(8,128)(2,1)} %param.21), kind=kOutput, calls=%fused_computation.65 | convolution fusion | flops 536870912 | bytes 3670016 | tf_op jit(solution)/shard_map/dot_general | solution.py:214
  24.2 0.8 copy-done.5
  24.9 0.8 pad_maximum_fusion
  25.8 2.3 %collective-permute-done.1 = f32[272,512]{1,0:T(8,128)} collective-permute-done((f32[272,512]{1,0:T(8,128)}, f32[272,512]{1,0:T(8,128)}, u32[]{:S(2)}, u32[]{:S(2)}) %collective-permute-start.1) | collective-permute-done | bytes 557088 | tf_op jit(solution)/shard_map/ppermute | solution.py:139
  28.1 1.3 fusion.16
  29.4 3.6 %collective-permute-start.2 = (f32[136,512]{1,0:T(8,128)S(1)}, f32[136,512]{1,0:T(8,128)S(1)}, u32[]{:S(2)}, u32[]{:S(2)}) collective-permute-start(f32[136,512]{1,0:T(8,128)S(1)} %slice_select_fusion), channel_id=1, source_target_pairs={{0,2},{1,3},{2,0},{3,1},{4,6},{5,7},{6,4},{7,5},{8,10},{9,11},{10,... | collective-permute-start | bytes 835592 | tf_op jit(solution)/shard_map/ppermute | solution.py:139
  33.0 7.0 %collective-permute-done.2 = f32[136,512]{1,0:T(8,128)S(1)} collective-permute-done((f32[136,512]{1,0:T(8,128)S(1)}, f32[136,512]{1,0:T(8,128)S(1)}, u32[]{:S(2)}, u32[]{:S(2)}) %collective-permute-start.2) | collective-permute-done | bytes 278560 | tf_op jit(solution)/shard_map/ppermute | solution.py:139
  40.1 4.0 %collective-permute-start.3 = (f32[136,512]{1,0:T(8,128)S(1)}, f32[136,512]{1,0:T(8,128)S(1)}, u32[]{:S(2)}, u32[]{:S(2)}) collective-permute-start(f32[136,512]{1,0:T(8,128)S(1)} %fusion.25), channel_id=1, source_target_pairs={{0,4},{1,5},{2,6},{3,7},{4,0},{5,1},{6,2},{7,3},{8,12},{9,13},{10,... | collective-permute-start | bytes 835592 | tf_op jit(solution)/shard_map/ppermute | solution.py:139
  44.1 12.4 %collective-permute-done.3 = f32[136,512]{1,0:T(8,128)S(1)} collective-permute-done((f32[136,512]{1,0:T(8,128)S(1)}, f32[136,512]{1,0:T(8,128)S(1)}, u32[]{:S(2)}, u32[]{:S(2)}) %collective-permute-start.3) | collective-permute-done | bytes 278560 | tf_op jit(solution)/shard_map/ppermute | solution.py:139
  56.6 0.7 copy.18
  57.3 0.7 pad_maximum_fusion.2
  58.0 1.9 %collective-permute-start.12 = (bf16[512,256]{1,0:T(8,128)(2,1)}, bf16[512,256]{1,0:T(8,128)(2,1)}, u32[]{:S(2)}, u32[]{:S(2)}) collective-permute-start(bf16[512,256]{1,0:T(8,128)(2,1)} %pad_maximum_fusion.2), channel_id=1, source_target_pairs={{0,16},{8,24},{16,32},{24,40},{32,48},{40,56},{48,64},{56,72},{64,... | collective-permute-start | bytes 786440 | tf_op jit(solution)/shard_map/ppermute | solution.py:22
  60.9 1.4 reshape.48.bc_ref
  62.3 3.5 %fusion.17 = (f32[2048]{0:T(1024)}, f32[256,2048]{1,0:T(8,128)S(1)}, f32[256,2048]{1,0:T(8,128)S(1)}) fusion(bf16[256,2048]{1,0:T(8,128)(2,1)S(1)} %multiply_convert_fusion, f32[2048]{0:T(1024)} %param.25, bf16[512,2048]{1,0:T(8,128)(2,1)S(1)} %copy-done, f32[272,512]{1,0:T(8,128)} %copy-done.4, f32[512]{0:T(512)} %param.23, f32[256]{0:T(256)S(1)} %add_rsqrt_fusion), kind=kOutput, calls=%fused_computation.63 | convolution fusion | flops 542504960 | bytes 7883776 | tf_op jit(solution)/shard_map/dot_general | solution.py:222
  65.8 2.2 %copy.16 = f32[32,8,8,256]{3,2,1,0:T(8,128)} copy(f32[32,8,8,256]{3,1,2,0:T(8,128)S(1)} %bitcast.39) | data formatting | bytes 4194304
  68.0 2.3 %copy.17 = f32[32,8,8,256]{3,2,1,0:T(8,128)} copy(f32[32,8,8,256]{3,1,2,0:T(8,128)S(1)} %bitcast.38) | data formatting | bytes 4194304
  71.0 12.5 %shard_map.149 = f32[16,8,256]{2,1,0:T(8,128)} custom-call(f32[32,256]{1,0:T(8,128)} %reshape.48.bc_ref, f32[256,8,256]{2,1,0:T(8,128)} %bitcast.34, f32[256,8,256]{2,1,0:T(8,128)} %bitcast.36, f32[16,8,256]{2,1,0:T(8,128)} %bitcast.32, f32[16,8,256]{2,1,0:T(8,128)} %broadcast_in_dim.5.h0_ref), custom_call_target="tpu_custom_call" | custom-call | flops 33554432 | bytes 6553600 | tf_op jit(solution)/shard_map/pallas_call | solution.py:71
  83.5 0.9 pad_maximum_fusion.4
  84.4 6.4 %collective-permute-start.5 = (f32[17,8,256]{2,1,0:T(8,128)S(1)}, f32[17,8,256]{2,1,0:T(8,128)}, u32[]{:S(2)}, u32[]{:S(2)}) collective-permute-start(f32[17,8,256]{2,1,0:T(8,128)S(1)} %pad_maximum_fusion.4), channel_id=1, source_target_pairs={{0,8},{8,16},{16,24},{24,32},{32,40},{40,48},{48,56},{56,64},{64,7... | collective-permute-start | bytes 417800 | tf_op jit(solution)/shard_map/ppermute | solution.py:22
  90.8 3.5 %collective-permute-start.11 = (bf16[256,256]{1,0:T(8,128)(2,1)S(1)}, bf16[256,256]{1,0:T(8,128)(2,1)S(1)}, u32[]{:S(2)}, u32[]{:S(2)}) collective-permute-start(bf16[256,256]{1,0:T(8,128)(2,1)S(1)} %constant_dynamic-update-slice_fusion), channel_id=1, source_target_pairs={{0,64},{8,72},{16,80},{24,88},{32,96},{40,104},{48,112},{56,120},{... | collective-permute-start | bytes 393224 | tf_op jit(solution)/shard_map/ppermute | solution.py:22
  94.3 8.0 %collective-permute-done.5 = f32[17,8,256]{2,1,0:T(8,128)} collective-permute-done((f32[17,8,256]{2,1,0:T(8,128)S(1)}, f32[17,8,256]{2,1,0:T(8,128)}, u32[]{:S(2)}, u32[]{:S(2)}) %collective-permute-start.5) | collective-permute-done | bytes 139296 | tf_op jit(solution)/shard_map/ppermute | solution.py:22
  102.3 1.9 %collective-permute-start.6 = (f32[17,8,256]{2,1,0:T(8,128)}, f32[17,8,256]{2,1,0:T(8,128)S(1)}, u32[]{:S(2)}, u32[]{:S(2)}) collective-permute-start(f32[17,8,256]{2,1,0:T(8,128)} %collective-permute-done.5), channel_id=1, source_target_pairs={{0,8},{8,16},{16,24},{24,32},{32,40},{40,48},{48,56},{56,64},{64,7... | collective-permute-start | bytes 417800 | tf_op jit(solution)/shard_map/ppermute | solution.py:22
  104.2 1.0 pad_maximum_fusion.1
  105.2 5.9 %collective-permute-start.13 = (bf16[1024,256]{1,0:T(8,128)(2,1)S(1)}, bf16[1024,256]{1,0:T(8,128)(2,1)S(1)}, u32[]{:S(2)}, u32[]{:S(2)}) collective-permute-start(bf16[1024,256]{1,0:T(8,128)(2,1)S(1)} %pad_maximum_fusion.1), channel_id=1, source_target_pairs={{0,32},{8,40},{16,48},{24,56},{32,64},{40,72},{48,80},{56,88},{64,... | collective-permute-start | bytes 1572872 | tf_op jit(solution)/shard_map/ppermute | solution.py:22
  111.1 7.3 %collective-permute-done.6 = f32[17,8,256]{2,1,0:T(8,128)S(1)} collective-permute-done((f32[17,8,256]{2,1,0:T(8,128)}, f32[17,8,256]{2,1,0:T(8,128)S(1)}, u32[]{:S(2)}, u32[]{:S(2)}) %collective-permute-start.6) | collective-permute-done | bytes 139296 | tf_op jit(solution)/shard_map/ppermute | solution.py:22
  118.5 0.7 slice_add_fusion.4
  119.2 1.0 slice_add_fusion
  120.2 1.9 %collective-permute-start.7 = (f32[17,8,256]{2,1,0:T(8,128)S(1)}, f32[17,8,256]{2,1,0:T(8,128)S(1)}, u32[]{:S(2)}, u32[]{:S(2)}) collective-permute-start(f32[17,8,256]{2,1,0:T(8,128)S(1)} %pad_maximum_fusion.5), channel_id=1, source_target_pairs={{0,16},{8,24},{16,32},{24,40},{32,48},{40,56},{48,64},{56,72},{64,... | collective-permute-start | bytes 417800 | tf_op jit(solution)/shard_map/ppermute | solution.py:22
  122.1 6.1 %collective-permute-done.13 = bf16[1024,256]{1,0:T(8,128)(2,1)S(1)} collective-permute-done((bf16[1024,256]{1,0:T(8,128)(2,1)S(1)}, bf16[1024,256]{1,0:T(8,128)(2,1)S(1)}, u32[]{:S(2)}, u32[]{:S(2)}) %collective-permute-start.13) | collective-permute-done | bytes 524320 | tf_op jit(solution)/shard_map/ppermute | solution.py:22
  128.2 1.0 constant_dynamic-update-slice_fusion.4
  129.2 1.8 collective-permute-done.7
  131.1 1.9 %collective-permute-start.8 = (f32[17,8,256]{2,1,0:T(8,128)S(1)}, f32[17,8,256]{2,1,0:T(8,128)S(1)}, u32[]{:S(2)}, u32[]{:S(2)}) collective-permute-start(f32[17,8,256]{2,1,0:T(8,128)S(1)} %pad_maximum_fusion.6), channel_id=1, source_target_pairs={{0,32},{8,40},{16,48},{24,56},{32,64},{40,72},{48,80},{56,88},{64,... | collective-permute-start | bytes 417800 | tf_op jit(solution)/shard_map/ppermute | solution.py:22
  133.0 7.9 %collective-permute-done.8 = f32[17,8,256]{2,1,0:T(8,128)S(1)} collective-permute-done((f32[17,8,256]{2,1,0:T(8,128)S(1)}, f32[17,8,256]{2,1,0:T(8,128)S(1)}, u32[]{:S(2)}, u32[]{:S(2)}) %collective-permute-start.8) | collective-permute-done | bytes 139296 | tf_op jit(solution)/shard_map/ppermute | solution.py:22
  141.0 3.5 %collective-permute-start.9 = (f32[17,8,256]{2,1,0:T(8,128)S(1)}, f32[17,8,256]{2,1,0:T(8,128)S(1)}, u32[]{:S(2)}, u32[]{:S(2)}) collective-permute-start(f32[17,8,256]{2,1,0:T(8,128)S(1)} %pad_maximum_fusion.7), channel_id=1, source_target_pairs={{0,64},{8,72},{16,80},{24,88},{32,96},{40,104},{48,112},{56,120},{... | collective-permute-start | bytes 417800 | tf_op jit(solution)/shard_map/ppermute | solution.py:22
  144.6 3.4 %collective-permute-done.9 = f32[17,8,256]{2,1,0:T(8,128)S(1)} collective-permute-done((f32[17,8,256]{2,1,0:T(8,128)S(1)}, f32[17,8,256]{2,1,0:T(8,128)S(1)}, u32[]{:S(2)}, u32[]{:S(2)}) %collective-permute-start.9) | collective-permute-done | bytes 139296 | tf_op jit(solution)/shard_map/ppermute | solution.py:22
  148.1 3.9 %collective-permute-start.10 = (f32[17,8,256]{2,1,0:T(8,128)S(1)}, f32[17,8,256]{2,1,0:T(8,128)S(1)}, u32[]{:S(2)}, u32[]{:S(2)}) collective-permute-start(f32[17,8,256]{2,1,0:T(8,128)S(1)} %pad_maximum_fusion.8), channel_id=1, source_target_pairs={{0,128},{8,136},{16,144},{24,152},{32,160},{40,168},{48,176},{56,1... | collective-permute-start | bytes 417800 | tf_op jit(solution)/shard_map/ppermute | solution.py:22
  152.0 13.4 %shard_map.151 = bf16[256,1024]{1,0:T(8,128)(2,1)} custom-call(s32[1]{0:T(128)} %bitcast.10.base_ref, bf16[256,1024]{1,0:T(8,128)(2,1)} %q_ref.1, bf16[2304,256]{1,0:T(8,128)(2,1)} %copy-done.21, bf16[2304,256]{1,0:T(8,128)(2,1)} %copy-done.21), custom_call_target="tpu_custom_call" | custom-call | flops 2415919104 | bytes 3407872 | tf_op jit(solution)/shard_map/pallas_call | solution.py:115
  166.1 15.8 %shard_map.150 = f32[256,8,256]{2,1,0:T(8,128)} custom-call(f32[32,256]{1,0:T(8,128)} %reshape.48.bc_ref, f32[256,8,256]{2,1,0:T(8,128)} %bitcast.35, f32[256,8,256]{2,1,0:T(8,128)} %bitcast.37, f32[16,8,256]{2,1,0:T(8,128)} %bitcast.33, f32[16,8,256]{2,1,0:T(8,128)} %fusion.12.h0_ref), custom_call_target="tpu_custom_call" | custom-call | flops 50331648 | bytes 6553600 | tf_op jit(solution)/shard_map/pallas_call | solution.py:71
  182.0 2.6 %copy.19 = f32[32,8,8,256]{3,1,2,0:T(8,128)S(1)} copy(f32[32,8,8,256]{3,2,1,0:T(8,128)} %bitcast.40) | data formatting | bytes 4194304
  184.7 2.8 %fusion.2 = bf16[256,2048]{1,0:T(8,128)(2,1)} fusion(f32[256,2048]{1,0:T(8,128)S(1)} %bitcast.31, bf16[256,2048]{1,0:T(8,128)(2,1)S(1)} %copy-done.6, f32[2048]{0:T(1024)S(1)} %copy-done.22, f32[259,2048]{1,0:T(8,128)S(1)} %copy-done.2, f32[2048]{0:T(1024)S(1)} %bitcast.51, f32[2048]{0:T(1024)S(1)} %bitcast.53, f32[2048]{0:T(1024)S(1)} %bitcast.49, ...), kind=kLoop, calls=%fused_computation.8 | loop fusion | flops 12058624 | bytes 12632064 | tf_op jit(solution)/shard_map/convert_element_type | solution.py:238
  (85 shorter events, 3.5 us)
Async XLA Ops:
  0.6 61.7 %copy-start = (bf16[512,2048]{1,0:T(8,128)(2,1)S(1)}, bf16[512,2048]{1,0:T(8,128)(2,1)}, u32[]{:S(2)}) copy-start(bf16[512,2048]{1,0:T(8,128)(2,1)} %param.24) | copy-start | bytes 6291460
  0.6 19.3 %copy-start.19 = (f32[2048]{0:T(1024)S(1)}, f32[2048]{0:T(1024)}, u32[]{:S(2)}) copy-start(f32[2048]{0:T(1024)} %param.20) | copy-start | bytes 24580
  3.4 15.0 %collective-permute-start = (bf16[280,256]{1,0:T(8,128)(2,1)S(1)}, bf16[280,256]{1,0:T(8,128)(2,1)S(1)}, u32[]{:S(2)}, u32[]{:S(2)}) collective-permute-start(bf16[280,256]{1,0:T(8,128)(2,1)S(1)} %pad_maximum_fusion.3), channel_id=1, source_target_pairs={{0,8},{8,16},{16,24},{24,32},{32,40},{40,48},{48,56},{56,64},{64,7... | collective-permute-start | bytes 430088 | tf_op jit(solution)/shard_map/ppermute | solution.py:22
  13.4 7.9 %copy-start.11 = (f32[1,2048]{1,0:T(1,128)}, f32[1,2048]{1,0:T(1,128)S(1)}, u32[]{:S(2)}) copy-start(f32[1,2048]{1,0:T(1,128)S(1)} %get-tuple-element.6) | copy-start | bytes 24580
  13.4 7.9 %copy-start.13 = (f32[1,2048]{1,0:T(1,128)}, f32[1,2048]{1,0:T(1,128)S(1)}, u32[]{:S(2)}) copy-start(f32[1,2048]{1,0:T(1,128)S(1)} %get-tuple-element.7) | copy-start | bytes 24580
  13.4 7.9 %copy-start.15 = (f32[1,2048]{1,0:T(1,128)}, f32[1,2048]{1,0:T(1,128)S(1)}, u32[]{:S(2)}) copy-start(f32[1,2048]{1,0:T(1,128)S(1)} %get-tuple-element.8) | copy-start | bytes 24580
  13.4 7.9 %copy-start.17 = (f32[1,2048]{1,0:T(1,128)}, f32[1,2048]{1,0:T(1,128)S(1)}, u32[]{:S(2)}) copy-start(f32[1,2048]{1,0:T(1,128)S(1)} %get-tuple-element.9) | copy-start | bytes 24580
  19.9 1.4 copy-start.1
  20.0 1.4 copy-start.9
  24.1 0.8 copy-start.5
  25.8 2.3 %collective-permute-start.1 = (f32[272,512]{1,0:T(8,128)}, f32[272,512]{1,0:T(8,128)}, u32[]{:S(2)}, u32[]{:S(2)}) collective-permute-start(f32[272,512]{1,0:T(8,128)} %pad_maximum_fusion), channel_id=1, source_target_pairs={{0,1},{1,0},{2,3},{3,2},{4,5},{5,4},{6,7},{7,6},{8,9},{9,8},{10,11... | collective-permute-start | bytes 1671176 | tf_op jit(solution)/shard_map/ppermute | solution.py:139
  25.8 30.8 %copy-start.10 = (f32[16,2048]{1,0:T(8,128)S(1)}, f32[16,2048]{1,0:T(8,128)}, u32[]{:S(2)}) copy-start(f32[16,2048]{1,0:T(8,128)} %param.26) | copy-start | bytes 393220
  29.4 10.6 %collective-permute-start.2 = (f32[136,512]{1,0:T(8,128)S(1)}, f32[136,512]{1,0:T(8,128)S(1)}, u32[]{:S(2)}, u32[]{:S(2)}) collective-permute-start(f32[136,512]{1,0:T(8,128)S(1)} %slice_select_fusion), channel_id=1, source_target_pairs={{0,2},{1,3},{2,0},{3,1},{4,6},{5,7},{6,4},{7,5},{8,10},{9,11},{10,... | collective-permute-start | bytes 835592 | tf_op jit(solution)/shard_map/ppermute | solution.py:139
  40.1 16.4 %collective-permute-start.3 = (f32[136,512]{1,0:T(8,128)S(1)}, f32[136,512]{1,0:T(8,128)S(1)}, u32[]{:S(2)}, u32[]{:S(2)}) collective-permute-start(f32[136,512]{1,0:T(8,128)S(1)} %fusion.25), channel_id=1, source_target_pairs={{0,4},{1,5},{2,6},{3,7},{4,0},{5,1},{6,2},{7,3},{8,12},{9,13},{10,... | collective-permute-start | bytes 835592 | tf_op jit(solution)/shard_map/ppermute | solution.py:139
  56.5 3.5 %collective-permute-start.4 = (f32[136,512]{1,0:T(8,128)S(1)}, f32[136,512]{1,0:T(8,128)S(1)}, u32[]{:S(2)}, u32[]{:S(2)}) collective-permute-start(f32[136,512]{1,0:T(8,128)S(1)} %add.109), channel_id=1, source_target_pairs={{0,1},{1,0},{2,3},{3,2},{4,5},{5,4},{6,7},{7,6},{8,9},{9,8},{10,11... | collective-permute-start | bytes 835592 | tf_op jit(solution)/shard_map/ppermute | solution.py:151
  58.0 46.2 %collective-permute-start.12 = (bf16[512,256]{1,0:T(8,128)(2,1)}, bf16[512,256]{1,0:T(8,128)(2,1)}, u32[]{:S(2)}, u32[]{:S(2)}) collective-permute-start(bf16[512,256]{1,0:T(8,128)(2,1)} %pad_maximum_fusion.2), channel_id=1, source_target_pairs={{0,16},{8,24},{16,32},{24,40},{32,48},{40,56},{48,64},{56,72},{64,... | collective-permute-start | bytes 786440 | tf_op jit(solution)/shard_map/ppermute | solution.py:22
  60.0 0.8 copy-start.4
  68.0 2.3 %copy-start.23 = (f32[2048]{0:T(1024)S(1)}, f32[2048]{0:T(1024)}, u32[]{:S(2)}) copy-start(f32[2048]{0:T(1024)} %get-tuple-element.2) | copy-start | bytes 24580
  71.0 48.2 %copy-start.3 = (f32[2,8,8,256]{3,2,1,0:T(8,128)S(1)}, f32[2,8,8,256]{3,2,1,0:T(8,128)}, u32[]{:S(2)}) copy-start(f32[2,8,8,256]{3,2,1,0:T(8,128)} %copy.18) | copy-start | bytes 393220
  84.4 17.8 %collective-permute-start.5 = (f32[17,8,256]{2,1,0:T(8,128)S(1)}, f32[17,8,256]{2,1,0:T(8,128)}, u32[]{:S(2)}, u32[]{:S(2)}) collective-permute-start(f32[17,8,256]{2,1,0:T(8,128)S(1)} %pad_maximum_fusion.4), channel_id=1, source_target_pairs={{0,8},{8,16},{16,24},{24,32},{32,40},{40,48},{48,56},{56,64},{64,7... | collective-permute-start | bytes 417800 | tf_op jit(solution)/shard_map/ppermute | solution.py:22
  90.8 13.4 %collective-permute-start.11 = (bf16[256,256]{1,0:T(8,128)(2,1)S(1)}, bf16[256,256]{1,0:T(8,128)(2,1)S(1)}, u32[]{:S(2)}, u32[]{:S(2)}) collective-permute-start(bf16[256,256]{1,0:T(8,128)(2,1)S(1)} %constant_dynamic-update-slice_fusion), channel_id=1, source_target_pairs={{0,64},{8,72},{16,80},{24,88},{32,96},{40,104},{48,112},{56,120},{... | collective-permute-start | bytes 393224 | tf_op jit(solution)/shard_map/ppermute | solution.py:22
  102.3 16.2 %collective-permute-start.6 = (f32[17,8,256]{2,1,0:T(8,128)}, f32[17,8,256]{2,1,0:T(8,128)S(1)}, u32[]{:S(2)}, u32[]{:S(2)}) collective-permute-start(f32[17,8,256]{2,1,0:T(8,128)} %collective-permute-done.5), channel_id=1, source_target_pairs={{0,8},{8,16},{16,24},{24,32},{32,40},{40,48},{48,56},{56,64},{64,7... | collective-permute-start | bytes 417800 | tf_op jit(solution)/shard_map/ppermute | solution.py:22
  105.2 23.0 %collective-permute-start.13 = (bf16[1024,256]{1,0:T(8,128)(2,1)S(1)}, bf16[1024,256]{1,0:T(8,128)(2,1)S(1)}, u32[]{:S(2)}, u32[]{:S(2)}) collective-permute-start(bf16[1024,256]{1,0:T(8,128)(2,1)S(1)} %pad_maximum_fusion.1), channel_id=1, source_target_pairs={{0,32},{8,40},{16,48},{24,56},{32,64},{40,72},{48,80},{56,88},{64,... | collective-permute-start | bytes 1572872 | tf_op jit(solution)/shard_map/ppermute | solution.py:22
  119.2 25.4 %copy-start.7 = (bf16[256,128]{1,0:T(8,128)(2,1)S(1)}, bf16[256,128]{1,0:T(8,128)(2,1)}, u32[]{:S(2)}) copy-start(bf16[256,128]{1,0:T(8,128)(2,1)} %param.17) | copy-start | bytes 196612
  119.2 25.4 %copy-start.8 = (bf16[256,128]{1,0:T(8,128)(2,1)S(1)}, bf16[256,128]{1,0:T(8,128)(2,1)}, u32[]{:S(2)}) copy-start(bf16[256,128]{1,0:T(8,128)(2,1)} %param.18) | copy-start | bytes 196612
  120.2 10.9 %collective-permute-start.7 = (f32[17,8,256]{2,1,0:T(8,128)S(1)}, f32[17,8,256]{2,1,0:T(8,128)S(1)}, u32[]{:S(2)}, u32[]{:S(2)}) collective-permute-start(f32[17,8,256]{2,1,0:T(8,128)S(1)} %pad_maximum_fusion.5), channel_id=1, source_target_pairs={{0,16},{8,24},{16,32},{24,40},{32,48},{40,56},{48,64},{56,72},{64,... | collective-permute-start | bytes 417800 | tf_op jit(solution)/shard_map/ppermute | solution.py:22
  131.1 9.9 %collective-permute-start.8 = (f32[17,8,256]{2,1,0:T(8,128)S(1)}, f32[17,8,256]{2,1,0:T(8,128)S(1)}, u32[]{:S(2)}, u32[]{:S(2)}) collective-permute-start(f32[17,8,256]{2,1,0:T(8,128)S(1)} %pad_maximum_fusion.6), channel_id=1, source_target_pairs={{0,32},{8,40},{16,48},{24,56},{32,64},{40,72},{48,80},{56,88},{64,... | collective-permute-start | bytes 417800 | tf_op jit(solution)/shard_map/ppermute | solution.py:22
  141.0 6.9 %collective-permute-start.9 = (f32[17,8,256]{2,1,0:T(8,128)S(1)}, f32[17,8,256]{2,1,0:T(8,128)S(1)}, u32[]{:S(2)}, u32[]{:S(2)}) collective-permute-start(f32[17,8,256]{2,1,0:T(8,128)S(1)} %pad_maximum_fusion.7), channel_id=1, source_target_pairs={{0,64},{8,72},{16,80},{24,88},{32,96},{40,104},{48,112},{56,120},{... | collective-permute-start | bytes 417800 | tf_op jit(solution)/shard_map/ppermute | solution.py:22
  144.6 7.4 %copy-start.21 = (bf16[2304,256]{1,0:T(8,128)(2,1)}, bf16[2304,256]{1,0:T(8,128)(2,1)S(1)}, u32[]{:S(2)}) copy-start(bf16[2304,256]{1,0:T(8,128)(2,1)S(1)} %constant_dynamic-update-slice_fusion.7.k_ref.v_ref) | copy-start | bytes 3538948
  148.1 17.4 %collective-permute-start.10 = (f32[17,8,256]{2,1,0:T(8,128)S(1)}, f32[17,8,256]{2,1,0:T(8,128)S(1)}, u32[]{:S(2)}, u32[]{:S(2)}) collective-permute-start(f32[17,8,256]{2,1,0:T(8,128)S(1)} %pad_maximum_fusion.8), channel_id=1, source_target_pairs={{0,128},{8,136},{16,144},{24,152},{32,160},{40,168},{48,176},{56,1... | collective-permute-start | bytes 417800 | tf_op jit(solution)/shard_map/ppermute | solution.py:22
  182.0 2.7 %copy-start.2 = (f32[259,2048]{1,0:T(8,128)S(1)}, f32[259,2048]{1,0:T(8,128)}, u32[]{:S(2)}) copy-start(f32[259,2048]{1,0:T(8,128)} %copy-done.1) | copy-start | bytes 6365188
  182.0 2.7 %copy-start.6 = (bf16[256,2048]{1,0:T(8,128)(2,1)S(1)}, bf16[256,2048]{1,0:T(8,128)(2,1)}, u32[]{:S(2)}) copy-start(bf16[256,2048]{1,0:T(8,128)(2,1)} %param.15) | copy-start | bytes 3145732
  182.0 2.7 %copy-start.12 = (f32[1,2048]{1,0:T(1,128)S(1)}, f32[1,2048]{1,0:T(1,128)}, u32[]{:S(2)}) copy-start(f32[1,2048]{1,0:T(1,128)} %copy-done.11) | copy-start | bytes 24580
  182.0 2.7 %copy-start.14 = (f32[1,2048]{1,0:T(1,128)S(1)}, f32[1,2048]{1,0:T(1,128)}, u32[]{:S(2)}) copy-start(f32[1,2048]{1,0:T(1,128)} %copy-done.13) | copy-start | bytes 24580
  182.0 2.7 %copy-start.16 = (f32[1,2048]{1,0:T(1,128)S(1)}, f32[1,2048]{1,0:T(1,128)}, u32[]{:S(2)}) copy-start(f32[1,2048]{1,0:T(1,128)} %copy-done.15) | copy-start | bytes 24580
  182.0 2.7 %copy-start.18 = (f32[1,2048]{1,0:T(1,128)S(1)}, f32[1,2048]{1,0:T(1,128)}, u32[]{:S(2)}) copy-start(f32[1,2048]{1,0:T(1,128)} %copy-done.17) | copy-start | bytes 24580
  182.0 2.7 %copy-start.20 = (f32[2048]{0:T(1024)S(1)}, f32[2048]{0:T(1024)}, u32[]{:S(2)}) copy-start(f32[2048]{0:T(1024)} %param.20) | copy-start | bytes 24580
  182.0 2.7 %copy-start.22 = (f32[2048]{0:T(1024)S(1)}, f32[2048]{0:T(1024)}, u32[]{:S(2)}) copy-start(f32[2048]{0:T(1024)} %param.27) | copy-start | bytes 24580

commit v7 on v6

--- a/solution.py
+++ b/solution.py
@@ -141,15 +141,19 @@
     return value
 
 
-def chip_first_sum(value, axis):
+def chip_first_sum(value, axis, attend):
     count = lax.axis_size(axis)
     value = butterfly_sum(value, axis, 1, 2)
     half = value.shape[0] // 2
     core = lax.axis_index(axis) % 2
     mine = jnp.where(core == 0, value[:half], value[half:])
-    mine = butterfly_sum(mine, axis, 2, count)
+    mine = butterfly_sum(mine, axis, 2, 4)
+    mine, attended = attend(mine)
+    mine = butterfly_sum(mine, axis, 4, count)
+    mine, attended = lax.optimization_barrier((mine, attended))
     other = lax.ppermute(mine, axis, [(source, source ^ 1) for source in range(count)])
-    return jnp.where(core == 0, jnp.concatenate([mine, other]), jnp.concatenate([other, mine]))
+    both = jnp.where(core == 0, jnp.concatenate([mine, other]), jnp.concatenate([other, mine]))
+    return both, attended
 
 
 def compose(earlier, later, rate3):
@@ -214,7 +218,13 @@
     rank_part = jnp.dot(activated, proj_dt_weight, preferred_element_type=jnp.float32)
     rank_width = rank_part.shape[1]
     packed = jnp.concatenate([rank_part, state_parts.reshape(-1, rank_width)], axis=0)
-    total = chip_first_sum(packed, "tp")
+    base = (lax.axis_index("seq") * tokens_here).astype(jnp.int32).reshape(1)
+
+    def attend(partial):
+        partial, ready = lax.optimization_barrier((partial, window))
+        return partial, run_attention(q_proj, ready, base)
+
+    total, attn_out = chip_first_sum(packed, "tp", attend)
     rank_low = total[:tokens_here]
     state_in = total[tokens_here:].reshape(state_parts.shape)
     rank_normed = rank_norm(rank_low, dt_gain)
@@ -236,8 +246,6 @@
         (mamba_sum + skip_weight[None, :] * activated.astype(jnp.float32))
         * jax.nn.silu(gate_in.astype(jnp.float32))
     ).astype(jnp.bfloat16)
-    base = (lax.axis_index("seq") * tokens_here).astype(jnp.int32).reshape(1)
-    attn_out = run_attention(q_proj, window, base)
     return (mamba_out, attn_out)
 
 

time: 188 us -> 197 us (1.048)
  the two profiles are of different devices: /device:TPU:8 before, /device:TPU:56 now
where the time goes in v7:
time: 197 us; the launch traced here: 196 us
  waiting for transfers between devices  89.4 us (45%)
  Pallas kernels  41.8 us (21%)
  starting transfers between devices  28.1 us (14%)
  local copies, waits for them, and re-layouts  17.3 us (9%)
  other arithmetic  12.6 us (6%)
  matrix products  5.6 us (3%)
    ppermute x10, waiting for transfers between devices, shifted(): lax.ppermute(value, axis, [(source, source + steps) for source in range(f...  88.6 us
    pallas_call x2, Pallas kernels, run_scan(): pl.pallas_call(functools.partial(scan_kernel, with_out), grid=(blocks,),...  28.4 us
    ppermute x10, starting transfers between devices, shifted(): lax.ppermute(value, axis, [(source, source + steps) for source in range(f...  24.6 us
    pallas_call x1, Pallas kernels, run_attention(): pl.pallas_call(attention_kernel, grid=(heads,), in_specs=[pl.BlockSpec(me...  13.4 us
    unnamed x58, local copies, waits for them, and re-layouts  13.2 us
  transfers between devices with their start and end apart: 14, of which 10 were waited for; matrix products, arithmetic and copies ran while one was open for 3% of the time, Pallas kernels for 7%

profile of v7, /device:TPU:56, one launch (start us, length us, event | category | flops | bytes accessed | tf_op | source)
XLA Modules:
  0.0 196.1 jit_solution(14690950638757678717)
XLA Ops:
  0.7 0.9 slice.80
  1.6 0.9 constant_dynamic-update-slice_fusion.1
  2.5 0.9 constant_dynamic-update-slice_fusion
  3.4 8.2 %collective-permute-start = (bf16[280,256]{1,0:T(8,128)(2,1)S(1)}, bf16[280,256]{1,0:T(8,128)(2,1)S(1)}, u32[]{:S(2)}, u32[]{:S(2)}) collective-permute-start(bf16[280,256]{1,0:T(8,128)(2,1)S(1)} %pad_maximum_fusion.3), channel_id=1, source_target_pairs={{0,8},{8,16},{16,24},{24,32},{32,40},{40,48},{48,56},{56,64},{64,7... | collective-permute-start | bytes 430088 | tf_op jit(solution)/shard_map/ppermute | solution.py:22
  11.6 0.9 fusion.18
  12.5 7.8 %collective-permute-done = bf16[280,256]{1,0:T(8,128)(2,1)S(1)} collective-permute-done((bf16[280,256]{1,0:T(8,128)(2,1)S(1)}, bf16[280,256]{1,0:T(8,128)(2,1)S(1)}, u32[]{:S(2)}, u32[]{:S(2)}) %collective-permute-start) | collective-permute-done | bytes 143392 | tf_op jit(solution)/shard_map/ppermute | solution.py:22
  20.3 1.5 maximum_convert_fusion
  21.9 1.3 multiply_convert_fusion
  23.7 2.3 %fusion.19 = f32[256,512]{1,0:T(8,128)S(1)} fusion(bf16[256,2048]{1,0:T(8,128)(2,1)S(1)} %multiply_convert_fusion, bf16[2048,512]{1,0:T(8,128)(2,1)} %param.21), kind=kOutput, calls=%fused_computation.65 | convolution fusion | flops 536870912 | bytes 3670016 | tf_op jit(solution)/shard_map/dot_general | solution.py:218
  26.1 0.8 copy-done.5
  26.8 0.8 pad_maximum_fusion
  27.7 0.7 pad_maximum_fusion.2
  28.4 1.9 collective-permute-start.4
  30.3 1.3 collective-permute-start.3
  31.6 9.9 %collective-permute-done.4 = bf16[512,256]{1,0:T(8,128)(2,1)} collective-permute-done((bf16[512,256]{1,0:T(8,128)(2,1)}, bf16[512,256]{1,0:T(8,128)(2,1)}, u32[]{:S(2)}, u32[]{:S(2)}) %collective-permute-start.4) | collective-permute-done | bytes 262176 | tf_op jit(solution)/shard_map/ppermute | solution.py:22
  41.5 1.0 pad_maximum_fusion.1
  42.5 1.9 collective-permute-start.5
  44.5 0.9 constant_dynamic-update-slice_fusion.6
  45.4 1.3 fusion.16
  46.9 13.4 %collective-permute-done.5 = bf16[1024,256]{1,0:T(8,128)(2,1)S(1)} collective-permute-done((bf16[1024,256]{1,0:T(8,128)(2,1)S(1)}, bf16[1024,256]{1,0:T(8,128)(2,1)S(1)}, u32[]{:S(2)}, u32[]{:S(2)}) %collective-permute-start.5) | collective-permute-done | bytes 524320 | tf_op jit(solution)/shard_map/ppermute | solution.py:22
  60.4 1.0 constant_dynamic-update-slice_fusion.4
  61.5 0.9 copy-done.22
  62.5 3.3 %collective-permute-start.6 = (f32[136,512]{1,0:T(8,128)S(1)}, f32[136,512]{1,0:T(8,128)}, u32[]{:S(2)}, u32[]{:S(2)}) collective-permute-start(f32[136,512]{1,0:T(8,128)S(1)} %fusion.25), channel_id=1, source_target_pairs={{0,4},{1,5},{2,6},{3,7},{4,0},{5,1},{6,2},{7,3},{8,12},{9,13},{10,... | collective-permute-start | bytes 835592 | tf_op jit(solution)/shard_map/ppermute | solution.py:139
  65.8 13.4 %shard_map.149 = bf16[256,1024]{1,0:T(8,128)(2,1)} custom-call(s32[1]{0:T(128)} %bitcast.5.base_ref, bf16[256,1024]{1,0:T(8,128)(2,1)} %q_ref.1, bf16[2304,256]{1,0:T(8,128)(2,1)} %copy-done.22, bf16[2304,256]{1,0:T(8,128)(2,1)} %copy-done.22), custom_call_target="tpu_custom_call" | custom-call | flops 2415919104 | bytes 3407872 | tf_op jit(solution)/shard_map/pallas_call | solution.py:115
  79.2 1.0 add.109
  80.3 0.7 copy.18
  81.0 0.8 collective-permute-done.7
  81.9 0.8 copy-done.4
  83.4 2.9 %fusion.17 = (f32[2048]{0:T(1024)S(1)}, f32[256,2048]{1,0:T(8,128)S(1)}, f32[256,2048]{1,0:T(8,128)S(1)}) fusion(bf16[256,2048]{1,0:T(8,128)(2,1)S(1)} %multiply_convert_fusion, f32[2048]{0:T(1024)} %param.25, bf16[512,2048]{1,0:T(8,128)(2,1)S(1)} %copy-done, f32[272,512]{1,0:T(8,128)} %copy-done.4, f32[512]{0:T(512)} %param.23, f32[256]{0:T(256)S(1)} %add_rsqrt_fusion), kind=kOutput, calls=%fused_computation.63 | convolution fusion | flops 542504960 | bytes 7883776 | tf_op jit(solution)/shard_map/dot_general | solution.py:232
  86.3 2.2 %copy.16 = f32[32,8,8,256]{3,2,1,0:T(8,128)} copy(f32[32,8,8,256]{3,1,2,0:T(8,128)S(1)} %bitcast.39) | data formatting | bytes 4194304
  88.5 2.3 %copy.17 = f32[32,8,8,256]{3,2,1,0:T(8,128)} copy(f32[32,8,8,256]{3,1,2,0:T(8,128)S(1)} %bitcast.38) | data formatting | bytes 4194304
  91.5 12.5 %shard_map.150 = f32[16,8,256]{2,1,0:T(8,128)} custom-call(f32[32,256]{1,0:T(8,128)} %reshape.49.bc_ref, f32[256,8,256]{2,1,0:T(8,128)} %bitcast.34, f32[256,8,256]{2,1,0:T(8,128)} %bitcast.36, f32[16,8,256]{2,1,0:T(8,128)} %bitcast.32, f32[16,8,256]{2,1,0:T(8,128)} %broadcast_in_dim.5.h0_ref), custom_call_target="tpu_custom_call" | custom-call | flops 33554432 | bytes 6553600 | tf_op jit(solution)/shard_map/pallas_call | solution.py:71
  104.0 0.9 pad_maximum_fusion.4
  104.9 2.9 %collective-permute-start.8 = (f32[17,8,256]{2,1,0:T(8,128)S(1)}, f32[17,8,256]{2,1,0:T(8,128)S(1)}, u32[]{:S(2)}, u32[]{:S(2)}) collective-permute-start(f32[17,8,256]{2,1,0:T(8,128)S(1)} %pad_maximum_fusion.4), channel_id=1, source_target_pairs={{0,8},{8,16},{16,24},{24,32},{32,40},{40,48},{48,56},{56,64},{64,7... | collective-permute-start | bytes 417800 | tf_op jit(solution)/shard_map/ppermute | solution.py:22
  107.9 14.6 %collective-permute-done.8 = f32[17,8,256]{2,1,0:T(8,128)S(1)} collective-permute-done((f32[17,8,256]{2,1,0:T(8,128)S(1)}, f32[17,8,256]{2,1,0:T(8,128)S(1)}, u32[]{:S(2)}, u32[]{:S(2)}) %collective-permute-start.8) | collective-permute-done | bytes 139296 | tf_op jit(solution)/shard_map/ppermute | solution.py:22
  122.4 1.9 collective-permute-start.9
  124.3 15.0 %collective-permute-done.9 = f32[17,8,256]{2,1,0:T(8,128)S(1)} collective-permute-done((f32[17,8,256]{2,1,0:T(8,128)S(1)}, f32[17,8,256]{2,1,0:T(8,128)S(1)}, u32[]{:S(2)}, u32[]{:S(2)}) %collective-permute-start.9) | collective-permute-done | bytes 139296 | tf_op jit(solution)/shard_map/ppermute | solution.py:22
  139.5 1.9 collective-permute-start.10
  141.4 7.7 %collective-permute-done.10 = f32[17,8,256]{2,1,0:T(8,128)S(1)} collective-permute-done((f32[17,8,256]{2,1,0:T(8,128)S(1)}, f32[17,8,256]{2,1,0:T(8,128)S(1)}, u32[]{:S(2)}, u32[]{:S(2)}) %collective-permute-start.10) | collective-permute-done | bytes 139296 | tf_op jit(solution)/shard_map/ppermute | solution.py:22
  149.1 1.9 collective-permute-start.11
  151.0 7.4 %collective-permute-done.11 = f32[17,8,256]{2,1,0:T(8,128)S(1)} collective-permute-done((f32[17,8,256]{2,1,0:T(8,128)S(1)}, f32[17,8,256]{2,1,0:T(8,128)S(1)}, u32[]{:S(2)}, u32[]{:S(2)}) %collective-permute-start.11) | collective-permute-done | bytes 139296 | tf_op jit(solution)/shard_map/ppermute | solution.py:22
  158.5 1.3 collective-permute-start.12
  159.8 5.6 %collective-permute-done.12 = f32[17,8,256]{2,1,0:T(8,128)S(1)} collective-permute-done((f32[17,8,256]{2,1,0:T(8,128)S(1)}, f32[17,8,256]{2,1,0:T(8,128)S(1)}, u32[]{:S(2)}, u32[]{:S(2)}) %collective-permute-start.12) | collective-permute-done | bytes 139296 | tf_op jit(solution)/shard_map/ppermute | solution.py:22
  165.6 1.3 collective-permute-start.13
  166.9 7.2 %collective-permute-done.13 = f32[17,8,256]{2,1,0:T(8,128)S(1)} collective-permute-done((f32[17,8,256]{2,1,0:T(8,128)S(1)}, f32[17,8,256]{2,1,0:T(8,128)S(1)}, u32[]{:S(2)}, u32[]{:S(2)}) %collective-permute-start.13) | collective-permute-done | bytes 139296 | tf_op jit(solution)/shard_map/ppermute | solution.py:22
  174.7 15.8 %shard_map.151 = f32[256,8,256]{2,1,0:T(8,128)} custom-call(f32[32,256]{1,0:T(8,128)} %reshape.49.bc_ref, f32[256,8,256]{2,1,0:T(8,128)} %bitcast.35, f32[256,8,256]{2,1,0:T(8,128)} %bitcast.37, f32[16,8,256]{2,1,0:T(8,128)} %bitcast.33, f32[16,8,256]{2,1,0:T(8,128)} %fusion.12.h0_ref), custom_call_target="tpu_custom_call" | custom-call | flops 50331648 | bytes 6553600 | tf_op jit(solution)/shard_map/pallas_call | solution.py:71
  190.6 2.6 %copy.19 = f32[32,8,8,256]{3,1,2,0:T(8,128)S(1)} copy(f32[32,8,8,256]{3,2,1,0:T(8,128)} %bitcast.40) | data formatting | bytes 4194304
  193.3 2.8 %fusion.2 = bf16[256,2048]{1,0:T(8,128)(2,1)} fusion(f32[256,2048]{1,0:T(8,128)S(1)} %bitcast.31, bf16[256,2048]{1,0:T(8,128)(2,1)S(1)} %copy-done.6, f32[2048]{0:T(1024)S(1)} %copy-done.23, f32[259,2048]{1,0:T(8,128)S(1)} %copy-done.2, f32[2048]{0:T(1024)S(1)} %bitcast.51, f32[2048]{0:T(1024)S(1)} %bitcast.53, f32[2048]{0:T(1024)S(1)} %bitcast.49, ...), kind=kLoop, calls=%fused_computation.8 | loop fusion | flops 12058624 | bytes 12632064 | tf_op jit(solution)/shard_map/convert_element_type | solution.py:248
  (85 shorter events, 3.4 us)
Async XLA Ops:
  0.6 82.8 %copy-start = (bf16[512,2048]{1,0:T(8,128)(2,1)S(1)}, bf16[512,2048]{1,0:T(8,128)(2,1)}, u32[]{:S(2)}) copy-start(bf16[512,2048]{1,0:T(8,128)(2,1)} %param.24) | copy-start | bytes 6291460
  0.6 21.2 %copy-start.20 = (f32[2048]{0:T(1024)S(1)}, f32[2048]{0:T(1024)}, u32[]{:S(2)}) copy-start(f32[2048]{0:T(1024)} %param.20) | copy-start | bytes 24580
  3.4 17.0 %collective-permute-start = (bf16[280,256]{1,0:T(8,128)(2,1)S(1)}, bf16[280,256]{1,0:T(8,128)(2,1)S(1)}, u32[]{:S(2)}, u32[]{:S(2)}) collective-permute-start(bf16[280,256]{1,0:T(8,128)(2,1)S(1)} %pad_maximum_fusion.3), channel_id=1, source_target_pairs={{0,8},{8,16},{16,24},{24,32},{32,40},{40,48},{48,56},{56,64},{64,7... | collective-permute-start | bytes 430088 | tf_op jit(solution)/shard_map/ppermute | solution.py:22
  12.5 10.7 %copy-start.12 = (f32[1,2048]{1,0:T(1,128)}, f32[1,2048]{1,0:T(1,128)S(1)}, u32[]{:S(2)}) copy-start(f32[1,2048]{1,0:T(1,128)S(1)} %get-tuple-element.14) | copy-start | bytes 24580
  12.5 10.7 %copy-start.14 = (f32[1,2048]{1,0:T(1,128)}, f32[1,2048]{1,0:T(1,128)S(1)}, u32[]{:S(2)}) copy-start(f32[1,2048]{1,0:T(1,128)S(1)} %get-tuple-element.15) | copy-start | bytes 24580
  12.5 10.7 %copy-start.16 = (f32[1,2048]{1,0:T(1,128)}, f32[1,2048]{1,0:T(1,128)S(1)}, u32[]{:S(2)}) copy-start(f32[1,2048]{1,0:T(1,128)S(1)} %get-tuple-element.16) | copy-start | bytes 24580
  12.5 10.7 %copy-start.18 = (f32[1,2048]{1,0:T(1,128)}, f32[1,2048]{1,0:T(1,128)S(1)}, u32[]{:S(2)}) copy-start(f32[1,2048]{1,0:T(1,128)S(1)} %get-tuple-element.17) | copy-start | bytes 24580
  21.9 1.4 copy-start.1
  21.9 1.4 copy-start.10
  23.7 4.0 %copy-start.7 = (f32[16,512]{1,0:T(8,128)}, f32[16,512]{1,0:T(8,128)S(1)}, u32[]{:S(2)}) copy-start(f32[16,512]{1,0:T(8,128)S(1)} %reshape.47) | copy-start | bytes 98308
  26.0 0.8 copy-start.5
  27.7 17.7 %collective-permute-start.1 = (f32[272,512]{1,0:T(8,128)}, f32[272,512]{1,0:T(8,128)}, u32[]{:S(2)}, u32[]{:S(2)}) collective-permute-start(f32[272,512]{1,0:T(8,128)} %pad_maximum_fusion), channel_id=1, source_target_pairs={{0,1},{1,0},{2,3},{3,2},{4,5},{5,4},{6,7},{7,6},{8,9},{9,8},{10,11... | collective-permute-start | bytes 1671176 | tf_op jit(solution)/shard_map/ppermute | solution.py:139
  28.4 13.1 %collective-permute-start.4 = (bf16[512,256]{1,0:T(8,128)(2,1)}, bf16[512,256]{1,0:T(8,128)(2,1)}, u32[]{:S(2)}, u32[]{:S(2)}) collective-permute-start(bf16[512,256]{1,0:T(8,128)(2,1)} %pad_maximum_fusion.2), channel_id=1, source_target_pairs={{0,16},{8,24},{16,32},{24,40},{32,48},{40,56},{48,64},{56,72},{64,... | collective-permute-start | bytes 786440 | tf_op jit(solution)/shard_map/ppermute | solution.py:22
  30.3 14.1 %collective-permute-start.3 = (bf16[256,256]{1,0:T(8,128)(2,1)S(1)}, bf16[256,256]{1,0:T(8,128)(2,1)}, u32[]{:S(2)}, u32[]{:S(2)}) collective-permute-start(bf16[256,256]{1,0:T(8,128)(2,1)S(1)} %constant_dynamic-update-slice_fusion), channel_id=1, source_target_pairs={{0,64},{8,72},{16,80},{24,88},{32,96},{40,104},{48,112},{56,120},{... | collective-permute-start | bytes 393224 | tf_op jit(solution)/shard_map/ppermute | solution.py:22
  42.5 17.8 %collective-permute-start.5 = (bf16[1024,256]{1,0:T(8,128)(2,1)S(1)}, bf16[1024,256]{1,0:T(8,128)(2,1)S(1)}, u32[]{:S(2)}, u32[]{:S(2)}) collective-permute-start(bf16[1024,256]{1,0:T(8,128)(2,1)S(1)} %pad_maximum_fusion.1), channel_id=1, source_target_pairs={{0,32},{8,40},{16,48},{24,56},{32,64},{40,72},{48,80},{56,88},{64,... | collective-permute-start | bytes 1572872 | tf_op jit(solution)/shard_map/ppermute | solution.py:22
  45.4 16.0 %copy-start.8 = (bf16[256,128]{1,0:T(8,128)(2,1)S(1)}, bf16[256,128]{1,0:T(8,128)(2,1)}, u32[]{:S(2)}) copy-start(bf16[256,128]{1,0:T(8,128)(2,1)} %param.17) | copy-start | bytes 196612
  45.4 16.0 %copy-start.9 = (bf16[256,128]{1,0:T(8,128)(2,1)S(1)}, bf16[256,128]{1,0:T(8,128)(2,1)}, u32[]{:S(2)}) copy-start(bf16[256,128]{1,0:T(8,128)(2,1)} %param.18) | copy-start | bytes 196612
  46.8 14.6 %collective-permute-start.2 = (f32[136,512]{1,0:T(8,128)S(1)}, f32[136,512]{1,0:T(8,128)S(1)}, u32[]{:S(2)}, u32[]{:S(2)}) collective-permute-start(f32[136,512]{1,0:T(8,128)S(1)} %slice_select_fusion), channel_id=1, source_target_pairs={{0,2},{1,3},{2,0},{3,1},{4,6},{5,7},{6,4},{7,5},{8,10},{9,11},{10,... | collective-permute-start | bytes 835592 | tf_op jit(solution)/shard_map/ppermute | solution.py:139
  61.4 1.0 copy-start.22
  62.5 16.7 %collective-permute-start.6 = (f32[136,512]{1,0:T(8,128)S(1)}, f32[136,512]{1,0:T(8,128)}, u32[]{:S(2)}, u32[]{:S(2)}) collective-permute-start(f32[136,512]{1,0:T(8,128)S(1)} %fusion.25), channel_id=1, source_target_pairs={{0,4},{1,5},{2,6},{3,7},{4,0},{5,1},{6,2},{7,3},{8,12},{9,13},{10,... | collective-permute-start | bytes 835592 | tf_op jit(solution)/shard_map/ppermute | solution.py:139
  65.8 14.5 %copy-start.11 = (f32[16,2048]{1,0:T(8,128)S(1)}, f32[16,2048]{1,0:T(8,128)}, u32[]{:S(2)}) copy-start(f32[16,2048]{1,0:T(8,128)} %param.26) | copy-start | bytes 393220
  80.2 1.6 collective-permute-start.7
  81.9 0.8 copy-start.4
  91.5 47.9 %copy-start.3 = (f32[2,8,8,256]{3,2,1,0:T(8,128)S(1)}, f32[2,8,8,256]{3,2,1,0:T(8,128)}, u32[]{:S(2)}) copy-start(f32[2,8,8,256]{3,2,1,0:T(8,128)} %copy.18) | copy-start | bytes 393220
  104.9 17.5 %collective-permute-start.8 = (f32[17,8,256]{2,1,0:T(8,128)S(1)}, f32[17,8,256]{2,1,0:T(8,128)S(1)}, u32[]{:S(2)}, u32[]{:S(2)}) collective-permute-start(f32[17,8,256]{2,1,0:T(8,128)S(1)} %pad_maximum_fusion.4), channel_id=1, source_target_pairs={{0,8},{8,16},{16,24},{24,32},{32,40},{40,48},{48,56},{56,64},{64,7... | collective-permute-start | bytes 417800 | tf_op jit(solution)/shard_map/ppermute | solution.py:22
  122.4 17.0 %collective-permute-start.9 = (f32[17,8,256]{2,1,0:T(8,128)S(1)}, f32[17,8,256]{2,1,0:T(8,128)S(1)}, u32[]{:S(2)}, u32[]{:S(2)}) collective-permute-start(f32[17,8,256]{2,1,0:T(8,128)S(1)} %collective-permute-done.8), channel_id=1, source_target_pairs={{0,8},{8,16},{16,24},{24,32},{32,40},{40,48},{48,56},{56,64},{64,7... | collective-permute-start | bytes 417800 | tf_op jit(solution)/shard_map/ppermute | solution.py:22
  139.5 9.6 %collective-permute-start.10 = (f32[17,8,256]{2,1,0:T(8,128)S(1)}, f32[17,8,256]{2,1,0:T(8,128)S(1)}, u32[]{:S(2)}, u32[]{:S(2)}) collective-permute-start(f32[17,8,256]{2,1,0:T(8,128)S(1)} %pad_maximum_fusion.5), channel_id=1, source_target_pairs={{0,16},{8,24},{16,32},{24,40},{32,48},{40,56},{48,64},{56,72},{64,... | collective-permute-start | bytes 417800 | tf_op jit(solution)/shard_map/ppermute | solution.py:22
  149.1 9.4 %collective-permute-start.11 = (f32[17,8,256]{2,1,0:T(8,128)S(1)}, f32[17,8,256]{2,1,0:T(8,128)S(1)}, u32[]{:S(2)}, u32[]{:S(2)}) collective-permute-start(f32[17,8,256]{2,1,0:T(8,128)S(1)} %pad_maximum_fusion.6), channel_id=1, source_target_pairs={{0,32},{8,40},{16,48},{24,56},{32,64},{40,72},{48,80},{56,88},{64,... | collective-permute-start | bytes 417800 | tf_op jit(solution)/shard_map/ppermute | solution.py:22
  158.5 6.9 %collective-permute-start.12 = (f32[17,8,256]{2,1,0:T(8,128)S(1)}, f32[17,8,256]{2,1,0:T(8,128)S(1)}, u32[]{:S(2)}, u32[]{:S(2)}) collective-permute-start(f32[17,8,256]{2,1,0:T(8,128)S(1)} %pad_maximum_fusion.7), channel_id=1, source_target_pairs={{0,64},{8,72},{16,80},{24,88},{32,96},{40,104},{48,112},{56,120},{... | collective-permute-start | bytes 417800 | tf_op jit(solution)/shard_map/ppermute | solution.py:22
  165.6 8.5 %collective-permute-start.13 = (f32[17,8,256]{2,1,0:T(8,128)S(1)}, f32[17,8,256]{2,1,0:T(8,128)S(1)}, u32[]{:S(2)}, u32[]{:S(2)}) collective-permute-start(f32[17,8,256]{2,1,0:T(8,128)S(1)} %pad_maximum_fusion.8), channel_id=1, source_target_pairs={{0,128},{8,136},{16,144},{24,152},{32,160},{40,168},{48,176},{56,1... | collective-permute-start | bytes 417800 | tf_op jit(solution)/shard_map/ppermute | solution.py:22
  190.5 2.7 %copy-start.2 = (f32[259,2048]{1,0:T(8,128)S(1)}, f32[259,2048]{1,0:T(8,128)}, u32[]{:S(2)}) copy-start(f32[259,2048]{1,0:T(8,128)} %copy-done.1) | copy-start | bytes 6365188
  190.5 2.7 %copy-start.6 = (bf16[256,2048]{1,0:T(8,128)(2,1)S(1)}, bf16[256,2048]{1,0:T(8,128)(2,1)}, u32[]{:S(2)}) copy-start(bf16[256,2048]{1,0:T(8,128)(2,1)} %param.15) | copy-start | bytes 3145732
  190.5 2.7 %copy-start.13 = (f32[1,2048]{1,0:T(1,128)S(1)}, f32[1,2048]{1,0:T(1,128)}, u32[]{:S(2)}) copy-start(f32[1,2048]{1,0:T(1,128)} %copy-done.12) | copy-start | bytes 24580
  190.6 2.7 %copy-start.15 = (f32[1,2048]{1,0:T(1,128)S(1)}, f32[1,2048]{1,0:T(1,128)}, u32[]{:S(2)}) copy-start(f32[1,2048]{1,0:T(1,128)} %copy-done.14) | copy-start | bytes 24580
  190.6 2.7 %copy-start.17 = (f32[1,2048]{1,0:T(1,128)S(1)}, f32[1,2048]{1,0:T(1,128)}, u32[]{:S(2)}) copy-start(f32[1,2048]{1,0:T(1,128)} %copy-done.16) | copy-start | bytes 24580
  190.6 2.7 %copy-start.19 = (f32[1,2048]{1,0:T(1,128)S(1)}, f32[1,2048]{1,0:T(1,128)}, u32[]{:S(2)}) copy-start(f32[1,2048]{1,0:T(1,128)} %copy-done.18) | copy-start | bytes 24580
  190.6 2.7 %copy-start.21 = (f32[2048]{0:T(1024)S(1)}, f32[2048]{0:T(1024)}, u32[]{:S(2)}) copy-start(f32[2048]{0:T(1024)} %param.20) | copy-start | bytes 24580
  190.6 2.7 %copy-start.23 = (f32[2048]{0:T(1024)S(1)}, f32[2048]{0:T(1024)}, u32[]{:S(2)}) copy-start(f32[2048]{0:T(1024)} %param.27) | copy-start | bytes 24580

commit v8 on v6

--- a/solution.py
+++ b/solution.py
@@ -159,14 +159,17 @@
 
 
 def entering_state(step_sum, final_state, rate3):
-    local = jnp.concatenate([step_sum[None], final_state], axis=0)
+    inclusive = jnp.concatenate([step_sum[None], final_state], axis=0)
+    exclusive = None
     peers = lax.axis_size("seq")
-    running = shifted(local, "seq", 1)
     distance = 1
-    while distance < peers - 1:
-        running = compose(shifted(running, "seq", distance), running, rate3)
+    while distance < peers:
+        received = shifted(inclusive, "seq", distance)
+        exclusive = received if exclusive is None else compose(received, exclusive, rate3)
+        if distance * 2 < peers:
+            inclusive = compose(received, inclusive, rate3)
         distance *= 2
-    return running[1:]
+    return exclusive[1:]
 
 
 def window_blocks(k_proj, v_proj, conv_tail, key_span):

time: 188 us -> 182 us (0.968)
  waiting for transfers between devices: 61.1 us -> 48.6 us
  local copies, waits for them, and re-layouts: 16.2 us -> 22.4 us
  starting transfers between devices: 47.6 us -> 43.4 us
    ppermute x10 -> x9, waiting for transfers between devices: 39.5 us -> 27 us  [shifted(): lax.ppermute(value, axis, [(source, source + steps) for source in range(f...]
    unnamed x58, local copies, waits for them, and re-layouts: 10.7 us -> 17.7 us
    ppermute x10 -> x9, starting transfers between devices: 39.9 us -> 35.8 us  [shifted(): lax.ppermute(value, axis, [(source, source + steps) for source in range(f...]
  transfers between devices with their start and end apart: 14 -> 13, of which waited for: 10 -> 8; matrix products, arithmetic and copies ran while one was open for 10% -> 15% of each run, Pallas kernels for 14% -> 14%
where the time goes in v8:
time: 182 us; the launch traced here: 180 us
  waiting for transfers between devices  48.6 us (27%)
  starting transfers between devices  43.4 us (24%)
  Pallas kernels  41.8 us (23%)
  local copies, waits for them, and re-layouts  22.4 us (12%)
  other arithmetic  14.7 us (8%)
  matrix products  7.92 us (4%)
    ppermute x9, starting transfers between devices, shifted(): lax.ppermute(value, axis, [(source, source + steps) for source in range(f...  35.8 us
    pallas_call x2, Pallas kernels, run_scan(): pl.pallas_call(functools.partial(scan_kernel, with_out), grid=(blocks,),...  28.3 us
    ppermute x9, waiting for transfers between devices, shifted(): lax.ppermute(value, axis, [(source, source + steps) for source in range(f...  27 us
    ppermute x3, waiting for transfers between devices, butterfly_sum(): value = value + lax.ppermute(value, axis, pairs)  21.6 us
    unnamed x58, local copies, waits for them, and re-layouts  17.7 us
    pallas_call x1, Pallas kernels, run_attention(): pl.pallas_call(attention_kernel, grid=(heads,), in_specs=[pl.BlockSpec(me...  13.4 us
    ppermute x3, starting transfers between devices, butterfly_sum(): value = value + lax.ppermute(value, axis, pairs)  7.6 us
    dot_general x1, matrix products, per_device(): jnp.dot(rank_normed, dt_weight, preferred_element_type=jnp.float32)  5.19 us
  transfers between devices with their start and end apart: 13, of which 8 were waited for; matrix products, arithmetic and copies ran while one was open for 15% of the time, Pallas kernels for 14%

profile of v8, /device:TPU:8, one launch (start us, length us, event | category | flops | bytes accessed | tf_op | source)
XLA Modules:
  0.0 180.0 jit_solution(10726342419103546455)
XLA Ops:
  0.7 0.9 slice.82
  1.6 0.9 constant_dynamic-update-slice_fusion.1
  2.5 0.9 constant_dynamic-update-slice_fusion
  3.4 9.1 %collective-permute-start = (bf16[280,256]{1,0:T(8,128)(2,1)S(1)}, bf16[280,256]{1,0:T(8,128)(2,1)S(1)}, u32[]{:S(2)}, u32[]{:S(2)}) collective-permute-start(bf16[280,256]{1,0:T(8,128)(2,1)S(1)} %pad_maximum_fusion.3), channel_id=1, source_target_pairs={{0,8},{8,16},{16,24},{24,32},{32,40},{40,48},{48,56},{56,64},{64,7... | collective-permute-start | bytes 430088 | tf_op jit(solution)/shard_map/ppermute | solution.py:22
  12.5 0.9 fusion.17
  13.4 4.9 %collective-permute-done = bf16[280,256]{1,0:T(8,128)(2,1)S(1)} collective-permute-done((bf16[280,256]{1,0:T(8,128)(2,1)S(1)}, bf16[280,256]{1,0:T(8,128)(2,1)S(1)}, u32[]{:S(2)}, u32[]{:S(2)}) %collective-permute-start) | collective-permute-done | bytes 143392 | tf_op jit(solution)/shard_map/ppermute | solution.py:22
  18.4 1.5 maximum_convert_fusion
  20.0 1.3 multiply_convert_fusion
  21.8 2.3 %fusion.18 = f32[256,512]{1,0:T(8,128)S(1)} fusion(bf16[256,2048]{1,0:T(8,128)(2,1)S(1)} %multiply_convert_fusion, bf16[2048,512]{1,0:T(8,128)(2,1)} %param.21), kind=kOutput, calls=%fused_computation.66 | convolution fusion | flops 536870912 | bytes 3670016 | tf_op jit(solution)/shard_map/dot_general | solution.py:217
  24.2 0.8 copy-done.4
  24.9 0.8 pad_maximum_fusion
  25.8 2.3 %collective-permute-done.1 = f32[272,512]{1,0:T(8,128)} collective-permute-done((f32[272,512]{1,0:T(8,128)}, f32[272,512]{1,0:T(8,128)}, u32[]{:S(2)}, u32[]{:S(2)}) %collective-permute-start.1) | collective-permute-done | bytes 557088 | tf_op jit(solution)/shard_map/ppermute | solution.py:139
  28.1 1.3 fusion.15
  29.4 3.6 %collective-permute-start.2 = (f32[136,512]{1,0:T(8,128)S(1)}, f32[136,512]{1,0:T(8,128)S(1)}, u32[]{:S(2)}, u32[]{:S(2)}) collective-permute-start(f32[136,512]{1,0:T(8,128)S(1)} %slice_select_fusion), channel_id=1, source_target_pairs={{0,2},{1,3},{2,0},{3,1},{4,6},{5,7},{6,4},{7,5},{8,10},{9,11},{10,... | collective-permute-start | bytes 835592 | tf_op jit(solution)/shard_map/ppermute | solution.py:139
  33.1 7.0 %collective-permute-done.2 = f32[136,512]{1,0:T(8,128)S(1)} collective-permute-done((f32[136,512]{1,0:T(8,128)S(1)}, f32[136,512]{1,0:T(8,128)S(1)}, u32[]{:S(2)}, u32[]{:S(2)}) %collective-permute-start.2) | collective-permute-done | bytes 278560 | tf_op jit(solution)/shard_map/ppermute | solution.py:139
  40.1 4.0 %collective-permute-start.3 = (f32[136,512]{1,0:T(8,128)S(1)}, f32[136,512]{1,0:T(8,128)S(1)}, u32[]{:S(2)}, u32[]{:S(2)}) collective-permute-start(f32[136,512]{1,0:T(8,128)S(1)} %fusion.24), channel_id=1, source_target_pairs={{0,4},{1,5},{2,6},{3,7},{4,0},{5,1},{6,2},{7,3},{8,12},{9,13},{10,... | collective-permute-start | bytes 835592 | tf_op jit(solution)/shard_map/ppermute | solution.py:139
  44.1 12.4 %collective-permute-done.3 = f32[136,512]{1,0:T(8,128)S(1)} collective-permute-done((f32[136,512]{1,0:T(8,128)S(1)}, f32[136,512]{1,0:T(8,128)S(1)}, u32[]{:S(2)}, u32[]{:S(2)}) %collective-permute-start.3) | collective-permute-done | bytes 278560 | tf_op jit(solution)/shard_map/ppermute | solution.py:139
  56.4 0.7 add.133
  57.2 3.5 %collective-permute-start.10 = (bf16[256,256]{1,0:T(8,128)(2,1)S(1)}, bf16[256,256]{1,0:T(8,128)(2,1)}, u32[]{:S(2)}, u32[]{:S(2)}) collective-permute-start(bf16[256,256]{1,0:T(8,128)(2,1)S(1)} %constant_dynamic-update-slice_fusion), channel_id=1, source_target_pairs={{0,64},{8,72},{16,80},{24,88},{32,96},{40,104},{48,112},{56,120},{... | collective-permute-start | bytes 393224 | tf_op jit(solution)/shard_map/ppermute | solution.py:22
  60.7 0.7 copy.18
  61.4 0.7 pad_maximum_fusion.2
  62.1 1.9 %collective-permute-start.11 = (bf16[512,256]{1,0:T(8,128)(2,1)}, bf16[512,256]{1,0:T(8,128)(2,1)}, u32[]{:S(2)}, u32[]{:S(2)}) collective-permute-start(bf16[512,256]{1,0:T(8,128)(2,1)} %pad_maximum_fusion.2), channel_id=1, source_target_pairs={{0,16},{8,24},{16,32},{24,40},{32,48},{40,56},{48,64},{56,72},{64,... | collective-permute-start | bytes 786440 | tf_op jit(solution)/shard_map/ppermute | solution.py:22
  64.1 1.3 maximum_select_fusion
  65.5 5.2 %fusion.16 = (f32[2048]{0:T(1024)}, f32[256,2048]{1,0:T(8,128)}, f32[256,2048]{1,0:T(8,128)}) fusion(bf16[256,2048]{1,0:T(8,128)(2,1)S(1)} %multiply_convert_fusion, f32[2048]{0:T(1024)} %param.25, bf16[512,2048]{1,0:T(8,128)(2,1)S(1)} %copy-done, f32[272,512]{1,0:T(8,128)S(1)} %maximum_select_fusion, f32[512]{0:T(512)S(1)} %copy-done.23, ...), kind=kOutput, calls=%fused_computation.64 | convolution fusion | flops 542504960 | bytes 7883776 | tf_op jit(solution)/shard_map/dot_general | solution.py:225
  71.3 3.9 %copy.16 = f32[32,8,8,256]{3,2,1,0:T(8,128)} copy(f32[32,8,8,256]{3,1,2,0:T(8,128)} %bitcast.44) | data formatting | bytes 4194304
  75.3 2.3 %copy.17 = f32[32,8,8,256]{3,2,1,0:T(8,128)} copy(f32[32,8,8,256]{3,1,2,0:T(8,128)S(1)} %bitcast.43) | data formatting | bytes 4194304
  78.2 12.5 %shard_map.149 = f32[16,8,256]{2,1,0:T(8,128)} custom-call(f32[32,256]{1,0:T(8,128)} %reshape.57.bc_ref, f32[256,8,256]{2,1,0:T(8,128)} %bitcast.39, f32[256,8,256]{2,1,0:T(8,128)} %bitcast.41, f32[16,8,256]{2,1,0:T(8,128)} %bitcast.37, f32[16,8,256]{2,1,0:T(8,128)} %broadcast_in_dim.5.h0_ref), custom_call_target="tpu_custom_call" | custom-call | flops 33554432 | bytes 6553600 | tf_op jit(solution)/shard_map/pallas_call | solution.py:71
  90.7 0.9 pad_maximum_fusion.4
  91.7 6.4 %collective-permute-start.5 = (f32[17,8,256]{2,1,0:T(8,128)S(1)}, f32[17,8,256]{2,1,0:T(8,128)S(1)}, u32[]{:S(2)}, u32[]{:S(2)}) collective-permute-start(f32[17,8,256]{2,1,0:T(8,128)S(1)} %pad_maximum_fusion.4), channel_id=1, source_target_pairs={{0,8},{8,16},{16,24},{24,32},{32,40},{40,48},{48,56},{56,64},{64,7... | collective-permute-start | bytes 417800 | tf_op jit(solution)/shard_map/ppermute | solution.py:22
  98.0 1.6 constant_dynamic-update-slice_fusion.6
  99.6 1.0 pad_maximum_fusion.1
  100.6 4.8 %collective-permute-start.12 = (bf16[1024,256]{1,0:T(8,128)(2,1)S(1)}, bf16[1024,256]{1,0:T(8,128)(2,1)}, u32[]{:S(2)}, u32[]{:S(2)}) collective-permute-start(bf16[1024,256]{1,0:T(8,128)(2,1)S(1)} %pad_maximum_fusion.1), channel_id=1, source_target_pairs={{0,32},{8,40},{16,48},{24,56},{32,64},{40,72},{48,80},{56,88},{64,... | collective-permute-start | bytes 1572872 | tf_op jit(solution)/shard_map/ppermute | solution.py:22
  105.4 3.8 %collective-permute-done.5 = f32[17,8,256]{2,1,0:T(8,128)S(1)} collective-permute-done((f32[17,8,256]{2,1,0:T(8,128)S(1)}, f32[17,8,256]{2,1,0:T(8,128)S(1)}, u32[]{:S(2)}, u32[]{:S(2)}) %collective-permute-start.5) | collective-permute-done | bytes 139296 | tf_op jit(solution)/shard_map/ppermute | solution.py:22
  109.2 1.0 multiply_add_fusion.3
  110.2 1.9 %collective-permute-start.6 = (f32[17,8,256]{2,1,0:T(8,128)S(1)}, f32[17,8,256]{2,1,0:T(8,128)S(1)}, u32[]{:S(2)}, u32[]{:S(2)}) collective-permute-start(f32[17,8,256]{2,1,0:T(8,128)S(1)} %pad_maximum_fusion.5), channel_id=1, source_target_pairs={{0,16},{8,24},{16,32},{24,40},{32,48},{40,56},{48,64},{56,72},{64,... | collective-permute-start | bytes 417800 | tf_op jit(solution)/shard_map/ppermute | solution.py:22
  112.2 9.0 %collective-permute-done.12 = bf16[1024,256]{1,0:T(8,128)(2,1)} collective-permute-done((bf16[1024,256]{1,0:T(8,128)(2,1)S(1)}, bf16[1024,256]{1,0:T(8,128)(2,1)}, u32[]{:S(2)}, u32[]{:S(2)}) %collective-permute-start.12) | collective-permute-done | bytes 524320 | tf_op jit(solution)/shard_map/ppermute | solution.py:22
  121.2 1.9 %constant_dynamic-update-slice_fusion.5 = bf16[2304,256]{1,0:T(8,128)(2,1)} fusion(bf16[2304,256]{1,0:T(8,128)(2,1)} %constant_dynamic-update-slice_fusion.6, bf16[1024,256]{1,0:T(8,128)(2,1)} %collective-permute-done.12), kind=kLoop, calls=%fused_computation.49 | loop fusion | bytes 1048576
  123.1 1.7 constant_dynamic-update-slice_fusion.4
  124.8 2.6 %collective-permute-start.7 = (f32[17,8,256]{2,1,0:T(8,128)S(1)}, f32[17,8,256]{2,1,0:T(8,128)S(1)}, u32[]{:S(2)}, u32[]{:S(2)}) collective-permute-start(f32[17,8,256]{2,1,0:T(8,128)S(1)} %pad_maximum_fusion.6), channel_id=1, source_target_pairs={{0,32},{8,40},{16,48},{24,56},{32,64},{40,72},{48,80},{56,88},{64,... | collective-permute-start | bytes 417800 | tf_op jit(solution)/shard_map/ppermute | solution.py:22
  128.0 6.6 %collective-permute-done.7 = f32[17,8,256]{2,1,0:T(8,128)S(1)} collective-permute-done((f32[17,8,256]{2,1,0:T(8,128)S(1)}, f32[17,8,256]{2,1,0:T(8,128)S(1)}, u32[]{:S(2)}, u32[]{:S(2)}) %collective-permute-start.7) | collective-permute-done | bytes 139296 | tf_op jit(solution)/shard_map/ppermute | solution.py:22
  134.7 3.0 %collective-permute-start.8 = (f32[17,8,256]{2,1,0:T(8,128)S(1)}, f32[17,8,256]{2,1,0:T(8,128)S(1)}, u32[]{:S(2)}, u32[]{:S(2)}) collective-permute-start(f32[17,8,256]{2,1,0:T(8,128)S(1)} %pad_maximum_fusion.7), channel_id=1, source_target_pairs={{0,64},{8,72},{16,80},{24,88},{32,96},{40,104},{48,112},{56,120},{... | collective-permute-start | bytes 417800 | tf_op jit(solution)/shard_map/ppermute | solution.py:22
  139.0 2.6 %collective-permute-done.8 = f32[17,8,256]{2,1,0:T(8,128)S(1)} collective-permute-done((f32[17,8,256]{2,1,0:T(8,128)S(1)}, f32[17,8,256]{2,1,0:T(8,128)S(1)}, u32[]{:S(2)}, u32[]{:S(2)}) %collective-permute-start.8) | collective-permute-done | bytes 139296 | tf_op jit(solution)/shard_map/ppermute | solution.py:22
  141.7 2.7 %collective-permute-start.9 = (f32[17,8,256]{2,1,0:T(8,128)S(1)}, f32[17,8,256]{2,1,0:T(8,128)S(1)}, u32[]{:S(2)}, u32[]{:S(2)}) collective-permute-start(f32[17,8,256]{2,1,0:T(8,128)S(1)} %pad_maximum_fusion.8), channel_id=1, source_target_pairs={{0,128},{8,136},{16,144},{24,152},{32,160},{40,168},{48,176},{56,1... | collective-permute-start | bytes 417800 | tf_op jit(solution)/shard_map/ppermute | solution.py:22
  144.4 13.4 %shard_map.151 = bf16[256,1024]{1,0:T(8,128)(2,1)} custom-call(s32[1]{0:T(128)} %bitcast.12.base_ref, bf16[256,1024]{1,0:T(8,128)(2,1)} %q_ref.1, bf16[2304,256]{1,0:T(8,128)(2,1)} %constant_dynamic-update-slice_fusion.7.k_ref.v_ref, bf16[2304,256]{1,0:T(8,128)(2,1)} %constant_dynamic-update-slice_fusion.7.k_ref.v_ref), custom_call_target="tpu_custom_call" | custom-call | flops 2415919104 | bytes 3407872 | tf_op jit(solution)/shard_map/pallas_call | solution.py:115
  157.8 0.8 fusion.12.h0_ref
  158.5 15.8 %shard_map.150 = f32[256,8,256]{2,1,0:T(8,128)} custom-call(f32[32,256]{1,0:T(8,128)} %reshape.57.bc_ref, f32[256,8,256]{2,1,0:T(8,128)} %bitcast.40, f32[256,8,256]{2,1,0:T(8,128)} %bitcast.42, f32[16,8,256]{2,1,0:T(8,128)} %bitcast.38, f32[16,8,256]{2,1,0:T(8,128)} %fusion.12.h0_ref), custom_call_target="tpu_custom_call" | custom-call | flops 50331648 | bytes 6553600 | tf_op jit(solution)/shard_map/pallas_call | solution.py:71
  174.5 2.6 %copy.19 = f32[32,8,8,256]{3,1,2,0:T(8,128)S(1)} copy(f32[32,8,8,256]{3,2,1,0:T(8,128)} %bitcast.45) | data formatting | bytes 4194304
  177.2 2.8 %fusion.2 = bf16[256,2048]{1,0:T(8,128)(2,1)} fusion(f32[256,2048]{1,0:T(8,128)S(1)} %bitcast.36, bf16[256,2048]{1,0:T(8,128)(2,1)S(1)} %copy-done.6, f32[2048]{0:T(1024)S(1)} %copy-done.22, f32[259,2048]{1,0:T(8,128)S(1)} %copy-done.2, f32[2048]{0:T(1024)S(1)} %bitcast.55, f32[2048]{0:T(1024)S(1)} %bitcast.57, f32[2048]{0:T(1024)S(1)} %bitcast.53, ...), kind=kLoop, calls=%fused_computation.8 | loop fusion | flops 12058624 | bytes 12632064 | tf_op jit(solution)/shard_map/convert_element_type | solution.py:241
  (84 shorter events, 4.3 us)
Async XLA Ops:
  0.6 64.9 %copy-start = (bf16[512,2048]{1,0:T(8,128)(2,1)S(1)}, bf16[512,2048]{1,0:T(8,128)(2,1)}, u32[]{:S(2)}) copy-start(bf16[512,2048]{1,0:T(8,128)(2,1)} %param.24) | copy-start | bytes 6291460
  0.6 19.3 %copy-start.20 = (f32[2048]{0:T(1024)S(1)}, f32[2048]{0:T(1024)}, u32[]{:S(2)}) copy-start(f32[2048]{0:T(1024)} %param.20) | copy-start | bytes 24580
  3.4 15.0 %collective-permute-start = (bf16[280,256]{1,0:T(8,128)(2,1)S(1)}, bf16[280,256]{1,0:T(8,128)(2,1)S(1)}, u32[]{:S(2)}, u32[]{:S(2)}) collective-permute-start(bf16[280,256]{1,0:T(8,128)(2,1)S(1)} %pad_maximum_fusion.3), channel_id=1, source_target_pairs={{0,8},{8,16},{16,24},{24,32},{32,40},{40,48},{48,56},{56,64},{64,7... | collective-permute-start | bytes 430088 | tf_op jit(solution)/shard_map/ppermute | solution.py:22
  13.4 7.9 %copy-start.11 = (f32[1,2048]{1,0:T(1,128)}, f32[1,2048]{1,0:T(1,128)S(1)}, u32[]{:S(2)}) copy-start(f32[1,2048]{1,0:T(1,128)S(1)} %get-tuple-element.9) | copy-start | bytes 24580
  13.4 7.9 %copy-start.13 = (f32[1,2048]{1,0:T(1,128)}, f32[1,2048]{1,0:T(1,128)S(1)}, u32[]{:S(2)}) copy-start(f32[1,2048]{1,0:T(1,128)S(1)} %get-tuple-element.10) | copy-start | bytes 24580
  13.4 7.9 %copy-start.15 = (f32[1,2048]{1,0:T(1,128)}, f32[1,2048]{1,0:T(1,128)S(1)}, u32[]{:S(2)}) copy-start(f32[1,2048]{1,0:T(1,128)S(1)} %get-tuple-element.11) | copy-start | bytes 24580
  13.4 7.9 %copy-start.17 = (f32[1,2048]{1,0:T(1,128)}, f32[1,2048]{1,0:T(1,128)S(1)}, u32[]{:S(2)}) copy-start(f32[1,2048]{1,0:T(1,128)S(1)} %get-tuple-element.12) | copy-start | bytes 24580
  19.9 1.4 copy-start.1
  20.0 1.4 copy-start.9
  24.1 0.8 copy-start.4
  25.8 2.3 %collective-permute-start.1 = (f32[272,512]{1,0:T(8,128)}, f32[272,512]{1,0:T(8,128)}, u32[]{:S(2)}, u32[]{:S(2)}) collective-permute-start(f32[272,512]{1,0:T(8,128)} %pad_maximum_fusion), channel_id=1, source_target_pairs={{0,1},{1,0},{2,3},{3,2},{4,5},{5,4},{6,7},{7,6},{8,9},{9,8},{10,11... | collective-permute-start | bytes 1671176 | tf_op jit(solution)/shard_map/ppermute | solution.py:139
  25.8 34.9 %copy-start.10 = (f32[16,2048]{1,0:T(8,128)S(1)}, f32[16,2048]{1,0:T(8,128)}, u32[]{:S(2)}) copy-start(f32[16,2048]{1,0:T(8,128)} %param.26) | copy-start | bytes 393220
  29.4 36.1 %copy-start.23 = (f32[512]{0:T(512)S(1)}, f32[512]{0:T(512)}, u32[]{:S(2)}) copy-start(f32[512]{0:T(512)} %param.23) | copy-start | bytes 6148
  29.4 10.6 %collective-permute-start.2 = (f32[136,512]{1,0:T(8,128)S(1)}, f32[136,512]{1,0:T(8,128)S(1)}, u32[]{:S(2)}, u32[]{:S(2)}) collective-permute-start(f32[136,512]{1,0:T(8,128)S(1)} %slice_select_fusion), channel_id=1, source_target_pairs={{0,2},{1,3},{2,0},{3,1},{4,6},{5,7},{6,4},{7,5},{8,10},{9,11},{10,... | collective-permute-start | bytes 835592 | tf_op jit(solution)/shard_map/ppermute | solution.py:139
  40.1 16.4 %collective-permute-start.3 = (f32[136,512]{1,0:T(8,128)S(1)}, f32[136,512]{1,0:T(8,128)S(1)}, u32[]{:S(2)}, u32[]{:S(2)}) collective-permute-start(f32[136,512]{1,0:T(8,128)S(1)} %fusion.24), channel_id=1, source_target_pairs={{0,4},{1,5},{2,6},{3,7},{4,0},{5,1},{6,2},{7,3},{8,12},{9,13},{10,... | collective-permute-start | bytes 835592 | tf_op jit(solution)/shard_map/ppermute | solution.py:139
  57.2 6.9 %collective-permute-start.4 = (f32[136,512]{1,0:T(8,128)}, f32[136,512]{1,0:T(8,128)}, u32[]{:S(2)}, u32[]{:S(2)}) collective-permute-start(f32[136,512]{1,0:T(8,128)} %add.133), channel_id=1, source_target_pairs={{0,1},{1,0},{2,3},{3,2},{4,5},{5,4},{6,7},{7,6},{8,9},{9,8},{10,11... | collective-permute-start | bytes 835592 | tf_op jit(solution)/shard_map/ppermute | solution.py:151
  57.2 40.8 %collective-permute-start.10 = (bf16[256,256]{1,0:T(8,128)(2,1)S(1)}, bf16[256,256]{1,0:T(8,128)(2,1)}, u32[]{:S(2)}, u32[]{:S(2)}) collective-permute-start(bf16[256,256]{1,0:T(8,128)(2,1)S(1)} %constant_dynamic-update-slice_fusion), channel_id=1, source_target_pairs={{0,64},{8,72},{16,80},{24,88},{32,96},{40,104},{48,112},{56,120},{... | collective-permute-start | bytes 393224 | tf_op jit(solution)/shard_map/ppermute | solution.py:22
  62.1 37.5 %collective-permute-start.11 = (bf16[512,256]{1,0:T(8,128)(2,1)}, bf16[512,256]{1,0:T(8,128)(2,1)}, u32[]{:S(2)}, u32[]{:S(2)}) collective-permute-start(bf16[512,256]{1,0:T(8,128)(2,1)} %pad_maximum_fusion.2), channel_id=1, source_target_pairs={{0,16},{8,24},{16,32},{24,40},{32,48},{40,56},{48,64},{56,72},{64,... | collective-permute-start | bytes 786440 | tf_op jit(solution)/shard_map/ppermute | solution.py:22
  71.3 4.0 %copy-start.5 = (f32[256,2048]{1,0:T(8,128)S(1)}, f32[256,2048]{1,0:T(8,128)}, u32[]{:S(2)}) copy-start(f32[256,2048]{1,0:T(8,128)} %get-tuple-element.3) | copy-start | bytes 6291460
  75.3 2.3 %copy-start.19 = (f32[2048]{0:T(1024)S(1)}, f32[2048]{0:T(1024)}, u32[]{:S(2)}) copy-start(f32[2048]{0:T(1024)} %get-tuple-element.2) | copy-start | bytes 24580
  78.2 31.0 %copy-start.3 = (f32[2,8,8,256]{3,2,1,0:T(8,128)S(1)}, f32[2,8,8,256]{3,2,1,0:T(8,128)}, u32[]{:S(2)}) copy-start(f32[2,8,8,256]{3,2,1,0:T(8,128)} %copy.18) | copy-start | bytes 393220
  91.7 17.6 %collective-permute-start.5 = (f32[17,8,256]{2,1,0:T(8,128)S(1)}, f32[17,8,256]{2,1,0:T(8,128)S(1)}, u32[]{:S(2)}, u32[]{:S(2)}) collective-permute-start(f32[17,8,256]{2,1,0:T(8,128)S(1)} %pad_maximum_fusion.4), channel_id=1, source_target_pairs={{0,8},{8,16},{16,24},{24,32},{32,40},{40,48},{48,56},{56,64},{64,7... | collective-permute-start | bytes 417800 | tf_op jit(solution)/shard_map/ppermute | solution.py:22
  100.6 20.6 %collective-permute-start.12 = (bf16[1024,256]{1,0:T(8,128)(2,1)S(1)}, bf16[1024,256]{1,0:T(8,128)(2,1)}, u32[]{:S(2)}, u32[]{:S(2)}) collective-permute-start(bf16[1024,256]{1,0:T(8,128)(2,1)S(1)} %pad_maximum_fusion.1), channel_id=1, source_target_pairs={{0,32},{8,40},{16,48},{24,56},{32,64},{40,72},{48,80},{56,88},{64,... | collective-permute-start | bytes 1572872 | tf_op jit(solution)/shard_map/ppermute | solution.py:22
  109.2 28.5 %copy-start.7 = (bf16[256,128]{1,0:T(8,128)(2,1)S(1)}, bf16[256,128]{1,0:T(8,128)(2,1)}, u32[]{:S(2)}) copy-start(bf16[256,128]{1,0:T(8,128)(2,1)} %param.17) | copy-start | bytes 196612
  109.2 29.1 %copy-start.8 = (bf16[256,128]{1,0:T(8,128)(2,1)S(1)}, bf16[256,128]{1,0:T(8,128)(2,1)}, u32[]{:S(2)}) copy-start(bf16[256,128]{1,0:T(8,128)(2,1)} %param.18) | copy-start | bytes 196612
  110.2 14.5 %collective-permute-start.6 = (f32[17,8,256]{2,1,0:T(8,128)S(1)}, f32[17,8,256]{2,1,0:T(8,128)S(1)}, u32[]{:S(2)}, u32[]{:S(2)}) collective-permute-start(f32[17,8,256]{2,1,0:T(8,128)S(1)} %pad_maximum_fusion.5), channel_id=1, source_target_pairs={{0,16},{8,24},{16,32},{24,40},{32,48},{40,56},{48,64},{56,72},{64,... | collective-permute-start | bytes 417800 | tf_op jit(solution)/shard_map/ppermute | solution.py:22
  124.8 9.8 %collective-permute-start.7 = (f32[17,8,256]{2,1,0:T(8,128)S(1)}, f32[17,8,256]{2,1,0:T(8,128)S(1)}, u32[]{:S(2)}, u32[]{:S(2)}) collective-permute-start(f32[17,8,256]{2,1,0:T(8,128)S(1)} %pad_maximum_fusion.6), channel_id=1, source_target_pairs={{0,32},{8,40},{16,48},{24,56},{32,64},{40,72},{48,80},{56,88},{64,... | collective-permute-start | bytes 417800 | tf_op jit(solution)/shard_map/ppermute | solution.py:22
  134.7 6.9 %collective-permute-start.8 = (f32[17,8,256]{2,1,0:T(8,128)S(1)}, f32[17,8,256]{2,1,0:T(8,128)S(1)}, u32[]{:S(2)}, u32[]{:S(2)}) collective-permute-start(f32[17,8,256]{2,1,0:T(8,128)S(1)} %pad_maximum_fusion.7), channel_id=1, source_target_pairs={{0,64},{8,72},{16,80},{24,88},{32,96},{40,104},{48,112},{56,120},{... | collective-permute-start | bytes 417800 | tf_op jit(solution)/shard_map/ppermute | solution.py:22
  141.7 16.1 %collective-permute-start.9 = (f32[17,8,256]{2,1,0:T(8,128)S(1)}, f32[17,8,256]{2,1,0:T(8,128)S(1)}, u32[]{:S(2)}, u32[]{:S(2)}) collective-permute-start(f32[17,8,256]{2,1,0:T(8,128)S(1)} %pad_maximum_fusion.8), channel_id=1, source_target_pairs={{0,128},{8,136},{16,144},{24,152},{32,160},{40,168},{48,176},{56,1... | collective-permute-start | bytes 417800 | tf_op jit(solution)/shard_map/ppermute | solution.py:22
  174.4 2.7 %copy-start.2 = (f32[259,2048]{1,0:T(8,128)S(1)}, f32[259,2048]{1,0:T(8,128)}, u32[]{:S(2)}) copy-start(f32[259,2048]{1,0:T(8,128)} %copy-done.1) | copy-start | bytes 6365188
  174.4 2.7 %copy-start.6 = (bf16[256,2048]{1,0:T(8,128)(2,1)S(1)}, bf16[256,2048]{1,0:T(8,128)(2,1)}, u32[]{:S(2)}) copy-start(bf16[256,2048]{1,0:T(8,128)(2,1)} %param.15) | copy-start | bytes 3145732
  174.4 2.7 %copy-start.12 = (f32[1,2048]{1,0:T(1,128)S(1)}, f32[1,2048]{1,0:T(1,128)}, u32[]{:S(2)}) copy-start(f32[1,2048]{1,0:T(1,128)} %copy-done.11) | copy-start | bytes 24580
  174.4 2.7 %copy-start.14 = (f32[1,2048]{1,0:T(1,128)S(1)}, f32[1,2048]{1,0:T(1,128)}, u32[]{:S(2)}) copy-start(f32[1,2048]{1,0:T(1,128)} %copy-done.13) | copy-start | bytes 24580
  174.4 2.7 %copy-start.16 = (f32[1,2048]{1,0:T(1,128)S(1)}, f32[1,2048]{1,0:T(1,128)}, u32[]{:S(2)}) copy-start(f32[1,2048]{1,0:T(1,128)} %copy-done.15) | copy-start | bytes 24580
  174.4 2.7 %copy-start.18 = (f32[1,2048]{1,0:T(1,128)S(1)}, f32[1,2048]{1,0:T(1,128)}, u32[]{:S(2)}) copy-start(f32[1,2048]{1,0:T(1,128)} %copy-done.17) | copy-start | bytes 24580
  174.4 2.7 %copy-start.21 = (f32[2048]{0:T(1024)S(1)}, f32[2048]{0:T(1024)}, u32[]{:S(2)}) copy-start(f32[2048]{0:T(1024)} %param.20) | copy-start | bytes 24580
  174.4 2.7 %copy-start.22 = (f32[2048]{0:T(1024)S(1)}, f32[2048]{0:T(1024)}, u32[]{:S(2)}) copy-start(f32[2048]{0:T(1024)} %param.27) | copy-start | bytes 24580

commit v9 on v8

--- a/solution.py
+++ b/solution.py
@@ -221,24 +221,29 @@
     rank_low = total[:tokens_here]
     state_in = total[tokens_here:].reshape(state_parts.shape)
     rank_normed = rank_norm(rank_low, dt_gain)
-    step_size = jax.nn.softplus(
-        jnp.dot(rank_normed, dt_weight, preferred_element_type=jnp.float32) + dt_bias[None, :]
-    )
-    drive_term = step_size * activated.astype(jnp.float32)
     state_count = decay_rate.shape[0]
     lanes = channels // SUBLANES
-    dt3 = step_size.reshape(tokens_here, SUBLANES, lanes)
-    dr3 = drive_term.reshape(tokens_here, SUBLANES, lanes)
-    rate3 = decay_rate.reshape(state_count, SUBLANES, lanes)
+
+    def cube(matrix):
+        return matrix.reshape(matrix.shape[:-1] + (SUBLANES, lanes))
+
+    act3 = cube(activated).astype(jnp.float32)
+    dt3 = jax.nn.softplus(
+        jnp.einsum("tr,rsl->tsl", rank_normed, cube(dt_weight), preferred_element_type=jnp.float32)
+        + cube(dt_bias)[None]
+    )
+    dr3 = dt3 * act3
+    rate3 = cube(decay_rate)
     zero_state = jnp.zeros((state_count, SUBLANES, lanes), jnp.float32)
     local_final = run_scan(state_in, dt3, dr3, rate3, zero_state, False)
     step_sum = jnp.sum(dt3, axis=0)
     entering = entering_state(step_sum, local_final, rate3)
-    mamba_sum = run_scan(state_in, dt3, dr3, rate3, entering, True).reshape(tokens_here, channels)
+    mamba_sum = run_scan(state_in, dt3, dr3, rate3, entering, True)
     mamba_out = (
-        (mamba_sum + skip_weight[None, :] * activated.astype(jnp.float32))
-        * jax.nn.silu(gate_in.astype(jnp.float32))
-    ).astype(jnp.bfloat16)
+        ((mamba_sum + cube(skip_weight)[None] * act3) * jax.nn.silu(cube(gate_in).astype(jnp.float32)))
+        .astype(jnp.bfloat16)
+        .reshape(tokens_here, channels)
+    )
     base = (lax.axis_index("seq") * tokens_here).astype(jnp.int32).reshape(1)
     attn_out = run_attention(q_proj, window, base)
     return (mamba_out, attn_out)

time: 182 us -> 179 us (0.984)
  local copies, waits for them, and re-layouts: 22.4 us -> 16 us
  matrix products: 7.92 us -> 2.67 us
  waiting for transfers between devices: 48.6 us -> 53.3 us
  other arithmetic: 14.7 us -> 18.2 us
    unnamed x58 -> x42, local copies, waits for them, and re-layouts: 17.7 us -> 9.43 us
    ppermute x9, waiting for transfers between devices: 27 us -> 31.6 us  [shifted(): lax.ppermute(value, axis, [(source, source + steps) for source in range(f...]
    dot_general x1, matrix products: 5.19 us -> 0.76 us  [per_device(): jnp.einsum('tr,rsl->tsl', rank_normed, cube(dt_weight), preferred_element...]
    reduce_sum x0 -> x1, other arithmetic: none -> 1.9 us  [per_device(): step_sum = jnp.sum(dt3, axis=0)]
    mul x0 -> x1, other arithmetic: none -> 1.85 us  [per_device(): dr3 = dt3 * act3]
  transfers between devices with their start and end apart: 13 -> 13, of which waited for: 8 -> 9; matrix products, arithmetic and copies ran while one was open for 15% -> 11% of each run, Pallas kernels for 14% -> 15%
where the time goes in v9:
time: 179 us; the launch traced here: 177 us
  waiting for transfers between devices  53.3 us (30%)
  starting transfers between devices  44 us (25%)
  Pallas kernels  41.8 us (23%)
  other arithmetic  18.2 us (10%)
  local copies, waits for them, and re-layouts  16 us (9%)
  matrix products  2.67 us (1%)
    ppermute x9, starting transfers between devices, shifted(): lax.ppermute(value, axis, [(source, source + steps) for source in range(f...  36.3 us
    ppermute x9, waiting for transfers between devices, shifted(): lax.ppermute(value, axis, [(source, source + steps) for source in range(f...  31.6 us
    pallas_call x2, Pallas kernels, run_scan(): pl.pallas_call(functools.partial(scan_kernel, with_out), grid=(blocks,),...  28.4 us
    ppermute x3, waiting for transfers between devices, butterfly_sum(): value = value + lax.ppermute(value, axis, pairs)  21.6 us
    pallas_call x1, Pallas kernels, run_attention(): pl.pallas_call(attention_kernel, grid=(heads,), in_specs=[pl.BlockSpec(me...  13.4 us
    unnamed x42, local copies, waits for them, and re-layouts  9.43 us
    ppermute x3, starting transfers between devices, butterfly_sum(): value = value + lax.ppermute(value, axis, pairs)  7.61 us
  transfers between devices with their start and end apart: 13, of which 9 were waited for; matrix products, arithmetic and copies ran while one was open for 11% of the time, Pallas kernels for 15%

profile of v9, /device:TPU:8, one launch (start us, length us, event | category | flops | bytes accessed | tf_op | source)
XLA Modules:
  0.0 177.0 jit_solution(1742217412846679616)
XLA Ops:
  0.7 1.0 constant_dynamic-update-slice_fusion.1
  1.7 0.8 slice.82
  2.5 0.9 constant_dynamic-update-slice_fusion
  3.3 9.1 %collective-permute-start = (bf16[280,256]{1,0:T(8,128)(2,1)S(1)}, bf16[280,256]{1,0:T(8,128)(2,1)S(1)}, u32[]{:S(2)}, u32[]{:S(2)}) collective-permute-start(bf16[280,256]{1,0:T(8,128)(2,1)S(1)} %pad_maximum_fusion.3), channel_id=1, source_target_pairs={{0,8},{8,16},{16,24},{24,32},{32,40},{40,48},{48,56},{56,64},{64,7... | collective-permute-start | bytes 430088 | tf_op jit(solution)/shard_map/ppermute | solution.py:22
  12.5 0.9 fusion.22
  13.4 5.0 %collective-permute-done = bf16[280,256]{1,0:T(8,128)(2,1)S(1)} collective-permute-done((bf16[280,256]{1,0:T(8,128)(2,1)S(1)}, bf16[280,256]{1,0:T(8,128)(2,1)S(1)}, u32[]{:S(2)}, u32[]{:S(2)}) %collective-permute-start) | collective-permute-done | bytes 143392 | tf_op jit(solution)/shard_map/ppermute | solution.py:22
  19.1 1.5 maximum_convert_fusion
  20.6 1.3 multiply_convert_fusion
  22.0 1.5 fusion.23
  23.9 1.9 %pad_maximum_fusion = f32[272,512]{1,0:T(8,128)} fusion(f32[16,512]{1,0:T(8,128)S(1)} %reshape.53, f32[256,512]{1,0:T(8,128)} %fusion.23), kind=kLoop, calls=%fused_computation.26 | loop fusion | flops 139264 | bytes 1114112 | tf_op jit(solution)/shard_map/concatenate | solution.py:219
  25.8 2.3 %collective-permute-done.1 = f32[272,512]{1,0:T(8,128)} collective-permute-done((f32[272,512]{1,0:T(8,128)}, f32[272,512]{1,0:T(8,128)}, u32[]{:S(2)}, u32[]{:S(2)}) %collective-permute-start.1) | collective-permute-done | bytes 557088 | tf_op jit(solution)/shard_map/ppermute | solution.py:139
  28.1 1.3 fusion.20
  29.4 3.6 %collective-permute-start.2 = (f32[136,512]{1,0:T(8,128)S(1)}, f32[136,512]{1,0:T(8,128)S(1)}, u32[]{:S(2)}, u32[]{:S(2)}) collective-permute-start(f32[136,512]{1,0:T(8,128)S(1)} %slice_select_fusion), channel_id=1, source_target_pairs={{0,2},{1,3},{2,0},{3,1},{4,6},{5,7},{6,4},{7,5},{8,10},{9,11},{10,... | collective-permute-start | bytes 835592 | tf_op jit(solution)/shard_map/ppermute | solution.py:139
  33.1 7.0 %collective-permute-done.2 = f32[136,512]{1,0:T(8,128)S(1)} collective-permute-done((f32[136,512]{1,0:T(8,128)S(1)}, f32[136,512]{1,0:T(8,128)S(1)}, u32[]{:S(2)}, u32[]{:S(2)}) %collective-permute-start.2) | collective-permute-done | bytes 278560 | tf_op jit(solution)/shard_map/ppermute | solution.py:139
  40.1 4.0 %collective-permute-start.3 = (f32[136,512]{1,0:T(8,128)S(1)}, f32[136,512]{1,0:T(8,128)S(1)}, u32[]{:S(2)}, u32[]{:S(2)}) collective-permute-start(f32[136,512]{1,0:T(8,128)S(1)} %fusion.28), channel_id=1, source_target_pairs={{0,4},{1,5},{2,6},{3,7},{4,0},{5,1},{6,2},{7,3},{8,12},{9,13},{10,... | collective-permute-start | bytes 835592 | tf_op jit(solution)/shard_map/ppermute | solution.py:139
  44.1 12.4 %collective-permute-done.3 = f32[136,512]{1,0:T(8,128)S(1)} collective-permute-done((f32[136,512]{1,0:T(8,128)S(1)}, f32[136,512]{1,0:T(8,128)S(1)}, u32[]{:S(2)}, u32[]{:S(2)}) %collective-permute-start.3) | collective-permute-done | bytes 278560 | tf_op jit(solution)/shard_map/ppermute | solution.py:139
  56.6 3.5 %collective-permute-start.10 = (bf16[256,256]{1,0:T(8,128)(2,1)S(1)}, bf16[256,256]{1,0:T(8,128)(2,1)}, u32[]{:S(2)}, u32[]{:S(2)}) collective-permute-start(bf16[256,256]{1,0:T(8,128)(2,1)S(1)} %constant_dynamic-update-slice_fusion), channel_id=1, source_target_pairs={{0,64},{8,72},{16,80},{24,88},{32,96},{40,104},{48,112},{56,120},{... | collective-permute-start | bytes 393224 | tf_op jit(solution)/shard_map/ppermute | solution.py:22
  60.1 1.3 add.139
  61.4 1.6 copy.20
  63.0 2.8 %copy.21 = f32[32,8,8,256]{3,2,1,0:T(8,128)} copy(bf16[32,8,8,256]{3,1,2,0:T(8,128)(2,1)} %bitcast.73) | data formatting | bytes 3145728
  65.8 1.3 mul.238
  67.3 0.7 copy-done.6
  68.0 0.8 pad_maximum_fusion.2
  68.8 1.9 %collective-permute-start.11 = (bf16[512,256]{1,0:T(8,128)(2,1)}, bf16[512,256]{1,0:T(8,128)(2,1)S(1)}, u32[]{:S(2)}, u32[]{:S(2)}) collective-permute-start(bf16[512,256]{1,0:T(8,128)(2,1)} %pad_maximum_fusion.2), channel_id=1, source_target_pairs={{0,16},{8,24},{16,32},{24,40},{32,48},{40,56},{48,64},{56,72},{64,... | collective-permute-start | bytes 786440 | tf_op jit(solution)/shard_map/ppermute | solution.py:22
  70.7 1.1 maximum_select_fusion
  72.0 0.8 fusion.5
  72.7 1.9 %fusion.21 = (f32[8,256]{1,0:T(8,128)S(1)}, f32[256,8,256]{2,1,0:T(8,128)S(1)}) fusion(f32[8,256]{1,0:T(8,128)S(1)} %copy-done.11, f32[256,8,256]{2,0,1:T(8,128)S(1)} %fusion.5), kind=kLoop, calls=%fused_computation.68 | loop fusion | flops 4192256 | bytes 4210688 | tf_op jit(solution)/shard_map/reduce_sum | solution.py:239
  74.7 1.8 %bitcast_multiply_fusion.2.dr_ref = f32[256,8,256]{2,1,0:T(8,128)} fusion(f32[256,8,256]{2,1,0:T(8,128)S(1)} %get-tuple-element.3.dt_ref, f32[32,8,8,256]{3,2,1,0:T(8,128)S(1)} %copy.19), kind=kLoop, calls=%fused_computation.8 | loop fusion | flops 524288 | bytes 6291456 | tf_op jit(solution)/shard_map/mul | solution.py:235
  77.9 12.5 %shard_map.149 = f32[16,8,256]{2,1,0:T(8,128)} custom-call(f32[32,256]{1,0:T(8,128)} %reshape.54.bc_ref, f32[256,8,256]{2,1,0:T(8,128)} %copy-done.2, f32[256,8,256]{2,1,0:T(8,128)} %bitcast_multiply_fusion.2.dr_ref, f32[16,8,256]{2,1,0:T(8,128)} %bitcast.69, f32[16,8,256]{2,1,0:T(8,128)} %broadcast_in_dim.5.h0_ref), custom_call_target="tpu_custom_call" | custom-call | flops 33554432 | bytes 6553600 | tf_op jit(solution)/shard_map/pallas_call | solution.py:71
  90.5 0.9 pad_maximum_fusion.4
  91.4 6.4 %collective-permute-start.5 = (f32[17,8,256]{2,1,0:T(8,128)S(1)}, f32[17,8,256]{2,1,0:T(8,128)S(1)}, u32[]{:S(2)}, u32[]{:S(2)}) collective-permute-start(f32[17,8,256]{2,1,0:T(8,128)S(1)} %pad_maximum_fusion.4), channel_id=1, source_target_pairs={{0,8},{8,16},{16,24},{24,32},{32,40},{40,48},{48,56},{56,64},{64,7... | collective-permute-start | bytes 417800 | tf_op jit(solution)/shard_map/ppermute | solution.py:22
  97.7 0.9 constant_dynamic-update-slice_fusion.6
  98.7 4.8 %collective-permute-start.12 = (bf16[1024,256]{1,0:T(8,128)(2,1)S(1)}, bf16[1024,256]{1,0:T(8,128)(2,1)S(1)}, u32[]{:S(2)}, u32[]{:S(2)}) collective-permute-start(bf16[1024,256]{1,0:T(8,128)(2,1)S(1)} %pad_maximum_fusion.1), channel_id=1, source_target_pairs={{0,32},{8,40},{16,48},{24,56},{32,64},{40,72},{48,80},{56,88},{64,... | collective-permute-start | bytes 1572872 | tf_op jit(solution)/shard_map/ppermute | solution.py:22
  103.5 6.0 %collective-permute-done.5 = f32[17,8,256]{2,1,0:T(8,128)S(1)} collective-permute-done((f32[17,8,256]{2,1,0:T(8,128)S(1)}, f32[17,8,256]{2,1,0:T(8,128)S(1)}, u32[]{:S(2)}, u32[]{:S(2)}) %collective-permute-start.5) | collective-permute-done | bytes 139296 | tf_op jit(solution)/shard_map/ppermute | solution.py:22
  109.5 1.0 multiply_add_fusion.3
  110.5 1.9 %collective-permute-start.6 = (f32[17,8,256]{2,1,0:T(8,128)S(1)}, f32[17,8,256]{2,1,0:T(8,128)S(1)}, u32[]{:S(2)}, u32[]{:S(2)}) collective-permute-start(f32[17,8,256]{2,1,0:T(8,128)S(1)} %pad_maximum_fusion.5), channel_id=1, source_target_pairs={{0,16},{8,24},{16,32},{24,40},{32,48},{40,56},{48,64},{56,72},{64,... | collective-permute-start | bytes 417800 | tf_op jit(solution)/shard_map/ppermute | solution.py:22
  112.5 8.3 %collective-permute-done.12 = bf16[1024,256]{1,0:T(8,128)(2,1)S(1)} collective-permute-done((bf16[1024,256]{1,0:T(8,128)(2,1)S(1)}, bf16[1024,256]{1,0:T(8,128)(2,1)S(1)}, u32[]{:S(2)}, u32[]{:S(2)}) %collective-permute-start.12) | collective-permute-done | bytes 524320 | tf_op jit(solution)/shard_map/ppermute | solution.py:22
  120.8 1.6 collective-permute-done.6
  122.4 2.7 %collective-permute-start.7 = (f32[17,8,256]{2,1,0:T(8,128)S(1)}, f32[17,8,256]{2,1,0:T(8,128)S(1)}, u32[]{:S(2)}, u32[]{:S(2)}) collective-permute-start(f32[17,8,256]{2,1,0:T(8,128)S(1)} %pad_maximum_fusion.6), channel_id=1, source_target_pairs={{0,32},{8,40},{16,48},{24,56},{32,64},{40,72},{48,80},{56,88},{64,... | collective-permute-start | bytes 417800 | tf_op jit(solution)/shard_map/ppermute | solution.py:22
  125.2 7.2 %collective-permute-done.7 = f32[17,8,256]{2,1,0:T(8,128)S(1)} collective-permute-done((f32[17,8,256]{2,1,0:T(8,128)S(1)}, f32[17,8,256]{2,1,0:T(8,128)S(1)}, u32[]{:S(2)}, u32[]{:S(2)}) %collective-permute-start.7) | collective-permute-done | bytes 139296 | tf_op jit(solution)/shard_map/ppermute | solution.py:22
  132.4 3.2 %collective-permute-start.8 = (f32[17,8,256]{2,1,0:T(8,128)S(1)}, f32[17,8,256]{2,1,0:T(8,128)S(1)}, u32[]{:S(2)}, u32[]{:S(2)}) collective-permute-start(f32[17,8,256]{2,1,0:T(8,128)S(1)} %pad_maximum_fusion.7), channel_id=1, source_target_pairs={{0,64},{8,72},{16,80},{24,88},{32,96},{40,104},{48,112},{56,120},{... | collective-permute-start | bytes 417800 | tf_op jit(solution)/shard_map/ppermute | solution.py:22
  135.7 3.7 %collective-permute-done.8 = f32[17,8,256]{2,1,0:T(8,128)S(1)} collective-permute-done((f32[17,8,256]{2,1,0:T(8,128)S(1)}, f32[17,8,256]{2,1,0:T(8,128)S(1)}, u32[]{:S(2)}, u32[]{:S(2)}) %collective-permute-start.8) | collective-permute-done | bytes 139296 | tf_op jit(solution)/shard_map/ppermute | solution.py:22
  139.4 2.8 %collective-permute-start.9 = (f32[17,8,256]{2,1,0:T(8,128)S(1)}, f32[17,8,256]{2,1,0:T(8,128)S(1)}, u32[]{:S(2)}, u32[]{:S(2)}) collective-permute-start(f32[17,8,256]{2,1,0:T(8,128)S(1)} %pad_maximum_fusion.8), channel_id=1, source_target_pairs={{0,128},{8,136},{16,144},{24,152},{32,160},{40,168},{48,176},{56,1... | collective-permute-start | bytes 417800 | tf_op jit(solution)/shard_map/ppermute | solution.py:22
  142.2 13.4 %shard_map.151 = bf16[256,1024]{1,0:T(8,128)(2,1)} custom-call(s32[1]{0:T(128)} %bitcast.14.base_ref, bf16[256,1024]{1,0:T(8,128)(2,1)} %q_ref.1, bf16[2304,256]{1,0:T(8,128)(2,1)} %copy-done.13, bf16[2304,256]{1,0:T(8,128)(2,1)} %copy-done.13), custom_call_target="tpu_custom_call" | custom-call | flops 2415919104 | bytes 3407872 | tf_op jit(solution)/shard_map/pallas_call | solution.py:115
  155.7 0.8 fusion.17.h0_ref
  156.4 15.8 %shard_map.150 = f32[256,8,256]{2,1,0:T(8,128)} custom-call(f32[32,256]{1,0:T(8,128)} %reshape.54.bc_ref, f32[256,8,256]{2,1,0:T(8,128)} %copy-done.2, f32[256,8,256]{2,1,0:T(8,128)} %bitcast_multiply_fusion.2.dr_ref, f32[16,8,256]{2,1,0:T(8,128)} %bitcast.70, f32[16,8,256]{2,1,0:T(8,128)} %fusion.17.h0_ref), custom_call_target="tpu_custom_call" | custom-call | flops 50331648 | bytes 6553600 | tf_op jit(solution)/shard_map/pallas_call | solution.py:71
  172.3 3.4 %fusion.12 = bf16[256,8,256]{2,1,0:T(8,128)(2,1)S(1)} fusion(f32[32,8,8,256]{3,2,1,0:T(8,128)} %copy.21, f32[256,8,256]{2,1,0:T(8,128)} %shard_map.150, f32[32,8,8,256]{3,2,1,0:T(8,128)} %copy-done.1, f32[8,256]{1,0:T(8,128)S(1)} %copy-done.12), kind=kLoop, calls=%fused_computation.23 | loop fusion | flops 4194304 | bytes 7348224 | tf_op jit(solution)/shard_map/convert_element_type | solution.py:244
  175.7 1.3 copy.22
  (70 shorter events, 3.6 us)
Async XLA Ops:
  0.6 21.3 %copy-start = (bf16[2048,512]{1,0:T(8,128)(2,1)S(1)}, bf16[2048,512]{1,0:T(8,128)(2,1)}, u32[]{:S(2)}) copy-start(bf16[2048,512]{1,0:T(8,128)(2,1)} %param.21) | copy-start | bytes 6291460
  0.6 19.9 %copy-start.14 = (f32[2048]{0:T(1024)S(1)}, f32[2048]{0:T(1024)}, u32[]{:S(2)}) copy-start(f32[2048]{0:T(1024)} %param.20) | copy-start | bytes 24580
  3.3 15.0 %collective-permute-start = (bf16[280,256]{1,0:T(8,128)(2,1)S(1)}, bf16[280,256]{1,0:T(8,128)(2,1)S(1)}, u32[]{:S(2)}, u32[]{:S(2)}) collective-permute-start(bf16[280,256]{1,0:T(8,128)(2,1)S(1)} %pad_maximum_fusion.3), channel_id=1, source_target_pairs={{0,8},{8,16},{16,24},{24,32},{32,40},{40,48},{48,56},{56,64},{64,7... | collective-permute-start | bytes 430088 | tf_op jit(solution)/shard_map/ppermute | solution.py:22
  18.4 0.7 copy-start.5
  21.9 1.5 copy-start.10
  25.8 2.3 %collective-permute-start.1 = (f32[272,512]{1,0:T(8,128)}, f32[272,512]{1,0:T(8,128)}, u32[]{:S(2)}, u32[]{:S(2)}) collective-permute-start(f32[272,512]{1,0:T(8,128)} %pad_maximum_fusion), channel_id=1, source_target_pairs={{0,1},{1,0},{2,3},{3,2},{4,5},{5,4},{6,7},{7,6},{8,9},{9,8},{10,11... | collective-permute-start | bytes 1671176 | tf_op jit(solution)/shard_map/ppermute | solution.py:139
  29.4 10.6 %collective-permute-start.2 = (f32[136,512]{1,0:T(8,128)S(1)}, f32[136,512]{1,0:T(8,128)S(1)}, u32[]{:S(2)}, u32[]{:S(2)}) collective-permute-start(f32[136,512]{1,0:T(8,128)S(1)} %slice_select_fusion), channel_id=1, source_target_pairs={{0,2},{1,3},{2,0},{3,1},{4,6},{5,7},{6,4},{7,5},{8,10},{9,11},{10,... | collective-permute-start | bytes 835592 | tf_op jit(solution)/shard_map/ppermute | solution.py:139
  40.1 16.4 %collective-permute-start.3 = (f32[136,512]{1,0:T(8,128)S(1)}, f32[136,512]{1,0:T(8,128)S(1)}, u32[]{:S(2)}, u32[]{:S(2)}) collective-permute-start(f32[136,512]{1,0:T(8,128)S(1)} %fusion.28), channel_id=1, source_target_pairs={{0,4},{1,5},{2,6},{3,7},{4,0},{5,1},{6,2},{7,3},{8,12},{9,13},{10,... | collective-permute-start | bytes 835592 | tf_op jit(solution)/shard_map/ppermute | solution.py:139
  56.5 14.2 %collective-permute-start.4 = (f32[136,512]{1,0:T(8,128)S(1)}, f32[136,512]{1,0:T(8,128)}, u32[]{:S(2)}, u32[]{:S(2)}) collective-permute-start(f32[136,512]{1,0:T(8,128)S(1)} %add.136), channel_id=1, source_target_pairs={{0,1},{1,0},{2,3},{3,2},{4,5},{5,4},{6,7},{7,6},{8,9},{9,8},{10,11... | collective-permute-start | bytes 835592 | tf_op jit(solution)/shard_map/ppermute | solution.py:151
  56.6 41.1 %collective-permute-start.10 = (bf16[256,256]{1,0:T(8,128)(2,1)S(1)}, bf16[256,256]{1,0:T(8,128)(2,1)}, u32[]{:S(2)}, u32[]{:S(2)}) collective-permute-start(bf16[256,256]{1,0:T(8,128)(2,1)S(1)} %constant_dynamic-update-slice_fusion), channel_id=1, source_target_pairs={{0,64},{8,72},{16,80},{24,88},{32,96},{40,104},{48,112},{56,120},{... | collective-permute-start | bytes 393224 | tf_op jit(solution)/shard_map/ppermute | solution.py:22
  67.1 0.9 copy-start.6
  67.1 4.9 %copy-start.4 = (bf16[512,2048]{1,0:T(8,128)(2,1)S(1)}, bf16[512,2048]{1,0:T(8,128)(2,1)}, u32[]{:S(2)}) copy-start(bf16[512,2048]{1,0:T(8,128)(2,1)} %param.24) | copy-start | bytes 6291460
  67.1 4.9 %copy-start.15 = (f32[512]{0:T(512)S(1)}, f32[512]{0:T(512)}, u32[]{:S(2)}) copy-start(f32[512]{0:T(512)} %param.23) | copy-start | bytes 6148
  68.0 6.7 %copy-start.1 = (f32[32,8,8,256]{3,2,1,0:T(8,128)}, f32[32,8,8,256]{3,2,1,0:T(8,128)S(1)}, u32[]{:S(2)}) copy-start(f32[32,8,8,256]{3,2,1,0:T(8,128)S(1)} %copy.19) | copy-start | bytes 6291460
  68.8 29.9 %collective-permute-start.11 = (bf16[512,256]{1,0:T(8,128)(2,1)}, bf16[512,256]{1,0:T(8,128)(2,1)S(1)}, u32[]{:S(2)}, u32[]{:S(2)}) collective-permute-start(bf16[512,256]{1,0:T(8,128)(2,1)} %pad_maximum_fusion.2), channel_id=1, source_target_pairs={{0,16},{8,24},{16,32},{24,40},{32,48},{40,56},{48,64},{56,72},{64,... | collective-permute-start | bytes 786440 | tf_op jit(solution)/shard_map/ppermute | solution.py:22
  71.9 0.8 copy-start.11
  74.6 2.0 %copy-start.2 = (f32[256,8,256]{2,1,0:T(8,128)}, f32[256,8,256]{2,1,0:T(8,128)S(1)}, u32[]{:S(2)}) copy-start(f32[256,8,256]{2,1,0:T(8,128)S(1)} %get-tuple-element.3.dt_ref) | copy-start | bytes 6291460
  77.9 31.6 %copy-start.3 = (f32[2,8,8,256]{3,2,1,0:T(8,128)S(1)}, f32[2,8,8,256]{3,2,1,0:T(8,128)}, u32[]{:S(2)}) copy-start(f32[2,8,8,256]{3,2,1,0:T(8,128)} %copy.20) | copy-start | bytes 393220
  91.4 18.1 %collective-permute-start.5 = (f32[17,8,256]{2,1,0:T(8,128)S(1)}, f32[17,8,256]{2,1,0:T(8,128)S(1)}, u32[]{:S(2)}, u32[]{:S(2)}) collective-permute-start(f32[17,8,256]{2,1,0:T(8,128)S(1)} %pad_maximum_fusion.4), channel_id=1, source_target_pairs={{0,8},{8,16},{16,24},{24,32},{32,40},{40,48},{48,56},{56,64},{64,7... | collective-permute-start | bytes 417800 | tf_op jit(solution)/shard_map/ppermute | solution.py:22
  98.7 26.5 %copy-start.7 = (bf16[280,256]{1,0:T(8,128)(2,1)S(1)}, bf16[280,256]{1,0:T(8,128)(2,1)}, u32[]{:S(2)}) copy-start(bf16[280,256]{1,0:T(8,128)(2,1)} %copy-done.5) | copy-start | bytes 430084
  98.7 22.0 %collective-permute-start.12 = (bf16[1024,256]{1,0:T(8,128)(2,1)S(1)}, bf16[1024,256]{1,0:T(8,128)(2,1)S(1)}, u32[]{:S(2)}, u32[]{:S(2)}) collective-permute-start(bf16[1024,256]{1,0:T(8,128)(2,1)S(1)} %pad_maximum_fusion.1), channel_id=1, source_target_pairs={{0,32},{8,40},{16,48},{24,56},{32,64},{40,72},{48,80},{56,88},{64,... | collective-permute-start | bytes 1572872 | tf_op jit(solution)/shard_map/ppermute | solution.py:22
  109.5 26.1 %copy-start.8 = (bf16[256,128]{1,0:T(8,128)(2,1)S(1)}, bf16[256,128]{1,0:T(8,128)(2,1)}, u32[]{:S(2)}) copy-start(bf16[256,128]{1,0:T(8,128)(2,1)} %param.17) | copy-start | bytes 196612
  109.5 26.1 %copy-start.9 = (bf16[256,128]{1,0:T(8,128)(2,1)S(1)}, bf16[256,128]{1,0:T(8,128)(2,1)}, u32[]{:S(2)}) copy-start(bf16[256,128]{1,0:T(8,128)(2,1)} %param.18) | copy-start | bytes 196612
  110.5 11.8 %collective-permute-start.6 = (f32[17,8,256]{2,1,0:T(8,128)S(1)}, f32[17,8,256]{2,1,0:T(8,128)S(1)}, u32[]{:S(2)}, u32[]{:S(2)}) collective-permute-start(f32[17,8,256]{2,1,0:T(8,128)S(1)} %pad_maximum_fusion.5), channel_id=1, source_target_pairs={{0,16},{8,24},{16,32},{24,40},{32,48},{40,56},{48,64},{56,72},{64,... | collective-permute-start | bytes 417800 | tf_op jit(solution)/shard_map/ppermute | solution.py:22
  122.4 9.9 %collective-permute-start.7 = (f32[17,8,256]{2,1,0:T(8,128)S(1)}, f32[17,8,256]{2,1,0:T(8,128)S(1)}, u32[]{:S(2)}, u32[]{:S(2)}) collective-permute-start(f32[17,8,256]{2,1,0:T(8,128)S(1)} %pad_maximum_fusion.6), channel_id=1, source_target_pairs={{0,32},{8,40},{16,48},{24,56},{32,64},{40,72},{48,80},{56,88},{64,... | collective-permute-start | bytes 417800 | tf_op jit(solution)/shard_map/ppermute | solution.py:22
  132.4 6.9 %collective-permute-start.8 = (f32[17,8,256]{2,1,0:T(8,128)S(1)}, f32[17,8,256]{2,1,0:T(8,128)S(1)}, u32[]{:S(2)}, u32[]{:S(2)}) collective-permute-start(f32[17,8,256]{2,1,0:T(8,128)S(1)} %pad_maximum_fusion.7), channel_id=1, source_target_pairs={{0,64},{8,72},{16,80},{24,88},{32,96},{40,104},{48,112},{56,120},{... | collective-permute-start | bytes 417800 | tf_op jit(solution)/shard_map/ppermute | solution.py:22
  135.7 6.6 %copy-start.13 = (bf16[2304,256]{1,0:T(8,128)(2,1)}, bf16[2304,256]{1,0:T(8,128)(2,1)S(1)}, u32[]{:S(2)}) copy-start(bf16[2304,256]{1,0:T(8,128)(2,1)S(1)} %constant_dynamic-update-slice_fusion.7.k_ref.v_ref) | copy-start | bytes 3538948
  139.4 16.3 %collective-permute-start.9 = (f32[17,8,256]{2,1,0:T(8,128)S(1)}, f32[17,8,256]{2,1,0:T(8,128)S(1)}, u32[]{:S(2)}, u32[]{:S(2)}) collective-permute-start(f32[17,8,256]{2,1,0:T(8,128)S(1)} %pad_maximum_fusion.8), channel_id=1, source_target_pairs={{0,128},{8,136},{16,144},{24,152},{32,160},{40,168},{48,176},{56,1... | collective-permute-start | bytes 417800 | tf_op jit(solution)/shard_map/ppermute | solution.py:22
  156.4 15.8 %copy-start.12 = (f32[8,256]{1,0:T(8,128)S(1)}, f32[8,256]{1,0:T(8,128)}, u32[]{:S(2)}) copy-start(f32[8,256]{1,0:T(8,128)} %mul.238) | copy-start | bytes 24580

commit v10 on v9

--- a/solution.py
+++ b/solution.py
@@ -102,7 +102,8 @@
     ) * (1.0 / math.sqrt(HD)) + bias_ref[...]
     row_peak = jnp.max(scores, axis=1, keepdims=True)
     weights = jnp.exp(scores - row_peak).astype(jnp.bfloat16)
-    summed = jnp.sum(weights.astype(jnp.float32), axis=1, keepdims=True)
+    ones = jnp.ones(v_ref.shape, v_ref.dtype)
+    summed = jnp.dot(weights, ones, preferred_element_type=jnp.float32)
     weighted = jnp.dot(weights, v_ref[...], preferred_element_type=jnp.float32)
     o_ref[...] = (weighted / summed).astype(o_ref.dtype)
 
@@ -217,17 +218,19 @@
     rank_part = jnp.dot(activated, proj_dt_weight, preferred_element_type=jnp.float32)
     rank_width = rank_part.shape[1]
     packed = jnp.concatenate([rank_part, state_parts.reshape(-1, rank_width)], axis=0)
+    lanes = channels // SUBLANES
+
+    def cube(matrix):
+        return matrix.reshape(matrix.shape[:-1] + (SUBLANES, lanes))
+
+    act3 = cube(activated).astype(jnp.float32)
+    gate3 = jax.nn.silu(cube(gate_in).astype(jnp.float32))
     total = chip_first_sum(packed, "tp")
+    total, window, act3, gate3 = lax.optimization_barrier((total, window, act3, gate3))
     rank_low = total[:tokens_here]
     state_in = total[tokens_here:].reshape(state_parts.shape)
     rank_normed = rank_norm(rank_low, dt_gain)
     state_count = decay_rate.shape[0]
-    lanes = channels // SUBLANES
-
-    def cube(matrix):
-        return matrix.reshape(matrix.shape[:-1] + (SUBLANES, lanes))
-
-    act3 = cube(activated).astype(jnp.float32)
     dt3 = jax.nn.softplus(
         jnp.einsum("tr,rsl->tsl", rank_normed, cube(dt_weight), preferred_element_type=jnp.float32)
         + cube(dt_bias)[None]
@@ -240,7 +243,7 @@
     entering = entering_state(step_sum, local_final, rate3)
     mamba_sum = run_scan(state_in, dt3, dr3, rate3, entering, True)
     mamba_out = (
-        ((mamba_sum + cube(skip_weight)[None] * act3) * jax.nn.silu(cube(gate_in).astype(jnp.float32)))
+        ((mamba_sum + cube(skip_weight)[None] * act3) * gate3)
         .astype(jnp.bfloat16)
         .reshape(tokens_here, channels)
     )

time: 179 us -> 180 us (level)
  other arithmetic: 18.2 us -> 21.3 us
  starting transfers between devices: 44 us -> 41.1 us
  waiting for transfers between devices: 53.3 us -> 51.2 us
    ppermute x3, waiting for transfers between devices: 21.6 us -> 10.2 us  [butterfly_sum(): value = value + lax.ppermute(value, axis, pairs)]
    ppermute x9, waiting for transfers between devices: 31.6 us -> 39.6 us  [shifted(): lax.ppermute(value, axis, [(source, source + steps) for source in range(f...]
    ppermute x9, starting transfers between devices: 36.3 us -> 33.5 us  [shifted(): lax.ppermute(value, axis, [(source, source + steps) for source in range(f...]
    mul x0 -> x1, other arithmetic: none -> 1.91 us  [per_device(): gate3 = jax.nn.silu(cube(gate_in).astype(jnp.float32))]
    unnamed x42 -> x54, local copies, waits for them, and re-layouts: 9.43 us -> 10.8 us
  transfers between devices with their start and end apart: 13 -> 13, of which waited for: 9 -> 9; matrix products, arithmetic and copies ran while one was open for 11% -> 10% of each run, Pallas kernels for 15% -> 7%
where the time goes in v10:
time: 180 us; the launch traced here: 178 us
  waiting for transfers between devices  51.2 us (28%)
  Pallas kernels  41.5 us (23%)
  starting transfers between devices  41.1 us (23%)
  other arithmetic  21.3 us (12%)
  local copies, waits for them, and re-layouts  17.5 us (10%)
  matrix products  4.09 us (2%)
    ppermute x9, waiting for transfers between devices, shifted(): lax.ppermute(value, axis, [(source, source + steps) for source in range(f...  39.6 us
    ppermute x9, starting transfers between devices, shifted(): lax.ppermute(value, axis, [(source, source + steps) for source in range(f...  33.5 us
    pallas_call x2, Pallas kernels, run_scan(): pl.pallas_call(functools.partial(scan_kernel, with_out), grid=(blocks,),...  28.4 us
    pallas_call x1, Pallas kernels, run_attention(): pl.pallas_call(attention_kernel, grid=(heads,), in_specs=[pl.BlockSpec(me...  13.2 us
    unnamed x54, local copies, waits for them, and re-layouts  10.8 us
    ppermute x3, waiting for transfers between devices, butterfly_sum(): value = value + lax.ppermute(value, axis, pairs)  10.2 us
    ppermute x3, starting transfers between devices, butterfly_sum(): value = value + lax.ppermute(value, axis, pairs)  7.52 us
  transfers between devices with their start and end apart: 13, of which 9 were waited for; matrix products, arithmetic and copies ran while one was open for 10% of the time, Pallas kernels for 7%

profile of v10, /device:TPU:8, one launch (start us, length us, event | category | flops | bytes accessed | tf_op | source)
XLA Modules:
  0.0 177.9 jit_solution(4822808435661721105)
XLA Ops:
  0.6 0.9 slice.82
  1.6 0.9 constant_dynamic-update-slice_fusion.1
  2.5 0.9 constant_dynamic-update-slice_fusion
  3.3 9.1 %collective-permute-start = (bf16[280,256]{1,0:T(8,128)(2,1)S(1)}, bf16[280,256]{1,0:T(8,128)(2,1)S(1)}, u32[]{:S(2)}, u32[]{:S(2)}) collective-permute-start(bf16[280,256]{1,0:T(8,128)(2,1)S(1)} %pad_maximum_fusion.3), channel_id=1, source_target_pairs={{0,8},{8,16},{16,24},{24,32},{32,40},{40,48},{48,56},{56,64},{64,7... | collective-permute-start | bytes 430088 | tf_op jit(solution)/shard_map/ppermute | solution.py:22
  12.4 1.5 fusion.19
  14.0 4.4 %collective-permute-done = bf16[280,256]{1,0:T(8,128)(2,1)S(1)} collective-permute-done((bf16[280,256]{1,0:T(8,128)(2,1)S(1)}, bf16[280,256]{1,0:T(8,128)(2,1)S(1)}, u32[]{:S(2)}, u32[]{:S(2)}) %collective-permute-start) | collective-permute-done | bytes 143392 | tf_op jit(solution)/shard_map/ppermute | solution.py:22
  18.4 1.6 maximum_convert_fusion
  20.1 1.3 multiply_convert_fusion.1
  21.4 1.0 convolution_bitcast_fusion
  24.7 0.8 pad_maximum_fusion
  26.3 1.9 %collective-permute-start.6 = (bf16[512,256]{1,0:T(8,128)(2,1)}, bf16[512,256]{1,0:T(8,128)(2,1)}, u32[]{:S(2)}, u32[]{:S(2)}) collective-permute-start(bf16[512,256]{1,0:T(8,128)(2,1)} %pad_maximum_fusion.2), channel_id=1, source_target_pairs={{0,16},{8,24},{16,32},{24,40},{32,48},{40,56},{48,64},{56,72},{64,... | collective-permute-start | bytes 786440 | tf_op jit(solution)/shard_map/ppermute | solution.py:22
  28.2 3.5 %collective-permute-start.5 = (bf16[256,256]{1,0:T(8,128)(2,1)S(1)}, bf16[256,256]{1,0:T(8,128)(2,1)}, u32[]{:S(2)}, u32[]{:S(2)}) collective-permute-start(bf16[256,256]{1,0:T(8,128)(2,1)S(1)} %constant_dynamic-update-slice_fusion), channel_id=1, source_target_pairs={{0,64},{8,72},{16,80},{24,88},{32,96},{40,104},{48,112},{56,120},{... | collective-permute-start | bytes 393224 | tf_op jit(solution)/shard_map/ppermute | solution.py:22
  31.8 1.5 copy.20
  33.3 6.2 %collective-permute-done.6 = bf16[512,256]{1,0:T(8,128)(2,1)} collective-permute-done((bf16[512,256]{1,0:T(8,128)(2,1)}, bf16[512,256]{1,0:T(8,128)(2,1)}, u32[]{:S(2)}, u32[]{:S(2)}) %collective-permute-start.6) | collective-permute-done | bytes 262176 | tf_op jit(solution)/shard_map/ppermute | solution.py:22
  39.5 1.8 %pad_maximum_fusion.1 = bf16[1024,256]{1,0:T(8,128)(2,1)} fusion(bf16[256,256]{1,0:T(8,128)(2,1)S(1)} %constant_dynamic-update-slice_fusion, bf16[256,256]{1,0:T(8,128)(2,1)S(1)} %slice.112, bf16[512,256]{1,0:T(8,128)(2,1)} %collective-permute-done.6), kind=kLoop, calls=%fused_computation.24 | loop fusion | flops 1572864 | bytes 1048576 | tf_op jit(solution)/shard_map/concatenate | solution.py:186
  41.3 1.9 %collective-permute-start.7 = (bf16[1024,256]{1,0:T(8,128)(2,1)}, bf16[1024,256]{1,0:T(8,128)(2,1)}, u32[]{:S(2)}, u32[]{:S(2)}) collective-permute-start(bf16[1024,256]{1,0:T(8,128)(2,1)} %pad_maximum_fusion.1), channel_id=1, source_target_pairs={{0,32},{8,40},{16,48},{24,56},{32,64},{40,72},{48,80},{56,88},{64,... | collective-permute-start | bytes 1572872 | tf_op jit(solution)/shard_map/ppermute | solution.py:22
  43.2 1.1 fusion.17
  45.9 3.5 %collective-permute-start.2 = (f32[136,512]{1,0:T(8,128)}, f32[136,512]{1,0:T(8,128)}, u32[]{:S(2)}, u32[]{:S(2)}) collective-permute-start(f32[136,512]{1,0:T(8,128)} %slice_select_fusion), channel_id=1, source_target_pairs={{0,2},{1,3},{2,0},{3,1},{4,6},{5,7},{6,4},{7,5},{8,10},{9,11},{10,... | collective-permute-start | bytes 835592 | tf_op jit(solution)/shard_map/ppermute | solution.py:140
  49.4 1.9 %bitcast_multiply_fusion = f32[256,8,256]{2,1,0:T(8,128)} fusion(f32[32,8,8,256]{3,2,1,0:T(8,128)S(1)} %copy.20), kind=kLoop, calls=%fused_computation.1 | loop fusion | flops 2097152 | bytes 4194304 | tf_op jit(solution)/shard_map/jit(silu)/mul | solution.py:227
  51.4 1.3 add.140
  53.3 2.9 %collective-permute-done.2 = f32[136,512]{1,0:T(8,128)} collective-permute-done((f32[136,512]{1,0:T(8,128)}, f32[136,512]{1,0:T(8,128)}, u32[]{:S(2)}, u32[]{:S(2)}) %collective-permute-start.2) | collective-permute-done | bytes 278560 | tf_op jit(solution)/shard_map/ppermute | solution.py:140
  56.2 1.2 fusion.25
  57.4 4.0 %collective-permute-start.3 = (f32[136,512]{1,0:T(8,128)S(1)}, f32[136,512]{1,0:T(8,128)S(1)}, u32[]{:S(2)}, u32[]{:S(2)}) collective-permute-start(f32[136,512]{1,0:T(8,128)S(1)} %fusion.25), channel_id=1, source_target_pairs={{0,4},{1,5},{2,6},{3,7},{4,0},{5,1},{6,2},{7,3},{8,12},{9,13},{10,... | collective-permute-start | bytes 835592 | tf_op jit(solution)/shard_map/ppermute | solution.py:140
  61.4 0.9 constant_dynamic-update-slice_fusion.6
  62.3 1.6 copy.19
  63.9 1.1 constant_dynamic-update-slice_fusion.5
  65.0 1.0 constant_dynamic-update-slice_fusion.4
  66.0 7.3 %collective-permute-done.3 = f32[136,512]{1,0:T(8,128)S(1)} collective-permute-done((f32[136,512]{1,0:T(8,128)S(1)}, f32[136,512]{1,0:T(8,128)S(1)}, u32[]{:S(2)}, u32[]{:S(2)}) %collective-permute-start.3) | collective-permute-done | bytes 278560 | tf_op jit(solution)/shard_map/ppermute | solution.py:140
  73.5 1.4 collective-permute-done.4
  75.8 2.4 %fusion.3 = f32[256,8,256]{2,0,1:T(8,128)S(1)} fusion(bf16[64,8,8,256]{3,2,1,0:T(8,128)(2,1)} %bitcast.62, f32[272,512]{1,0:T(8,128)S(1)} %maximum_select_fusion, f32[512]{0:T(512)S(1)} %copy-done.21, f32[256]{0:T(256)S(1)} %add_rsqrt_fusion), kind=kOutput, calls=%fused_computation.6 | convolution fusion | flops 537264128 | bytes 4721664 | tf_op jit(solution)/shard_map/tr,rsl->tsl/dot_general | solution.py:235
  78.1 1.9 %fusion.18 = (f32[8,256]{1,0:T(8,128)S(1)}, f32[256,8,256]{2,1,0:T(8,128)S(1)}) fusion(f32[8,256]{1,0:T(8,128)S(1)} %copy-done.13, f32[256,8,256]{2,0,1:T(8,128)S(1)} %fusion.3), kind=kLoop, calls=%fused_computation.64 | loop fusion | flops 4192256 | bytes 4210688 | tf_op jit(solution)/shard_map/reduce_sum | solution.py:242
  80.0 1.8 %mul.207.dr_ref = f32[256,8,256]{2,1,0:T(8,128)} multiply(f32[256,8,256]{2,1,0:T(8,128)S(1)} %get-tuple-element.11.dt_ref, f32[256,8,256]{2,1,0:T(8,128)S(1)} %bitcast.57) | non-fusion elementwise | flops 524288 | bytes 6291456 | tf_op jit(solution)/shard_map/mul | solution.py:238
  82.8 12.5 %shard_map.149 = f32[16,8,256]{2,1,0:T(8,128)} custom-call(f32[32,256]{1,0:T(8,128)} %reshape.54.bc_ref, f32[256,8,256]{2,1,0:T(8,128)} %copy-done.2, f32[256,8,256]{2,1,0:T(8,128)} %mul.207.dr_ref, f32[16,8,256]{2,1,0:T(8,128)} %bitcast.59, f32[16,8,256]{2,1,0:T(8,128)} %broadcast_in_dim.5.h0_ref), custom_call_target="tpu_custom_call" | custom-call | flops 33554432 | bytes 6553600 | tf_op jit(solution)/shard_map/pallas_call | solution.py:71
  95.3 0.9 pad_maximum_fusion.4
  96.2 5.4 %collective-permute-start.8 = (f32[17,8,256]{2,1,0:T(8,128)S(1)}, f32[17,8,256]{2,1,0:T(8,128)S(1)}, u32[]{:S(2)}, u32[]{:S(2)}) collective-permute-start(f32[17,8,256]{2,1,0:T(8,128)S(1)} %pad_maximum_fusion.4), channel_id=1, source_target_pairs={{0,8},{8,16},{16,24},{24,32},{32,40},{40,48},{48,56},{56,64},{64,7... | collective-permute-start | bytes 417800 | tf_op jit(solution)/shard_map/ppermute | solution.py:22
  101.6 10.5 %collective-permute-done.8 = f32[17,8,256]{2,1,0:T(8,128)S(1)} collective-permute-done((f32[17,8,256]{2,1,0:T(8,128)S(1)}, f32[17,8,256]{2,1,0:T(8,128)S(1)}, u32[]{:S(2)}, u32[]{:S(2)}) %collective-permute-start.8) | collective-permute-done | bytes 139296 | tf_op jit(solution)/shard_map/ppermute | solution.py:22
  112.1 0.9 multiply_add_fusion.3
  113.1 1.9 %collective-permute-start.9 = (f32[17,8,256]{2,1,0:T(8,128)S(1)}, f32[17,8,256]{2,1,0:T(8,128)S(1)}, u32[]{:S(2)}, u32[]{:S(2)}) collective-permute-start(f32[17,8,256]{2,1,0:T(8,128)S(1)} %pad_maximum_fusion.5), channel_id=1, source_target_pairs={{0,16},{8,24},{16,32},{24,40},{32,48},{40,56},{48,64},{56,72},{64,... | collective-permute-start | bytes 417800 | tf_op jit(solution)/shard_map/ppermute | solution.py:22
  115.0 7.7 %collective-permute-done.9 = f32[17,8,256]{2,1,0:T(8,128)S(1)} collective-permute-done((f32[17,8,256]{2,1,0:T(8,128)S(1)}, f32[17,8,256]{2,1,0:T(8,128)S(1)}, u32[]{:S(2)}, u32[]{:S(2)}) %collective-permute-start.9) | collective-permute-done | bytes 139296 | tf_op jit(solution)/shard_map/ppermute | solution.py:22
  122.8 1.9 %collective-permute-start.10 = (f32[17,8,256]{2,1,0:T(8,128)S(1)}, f32[17,8,256]{2,1,0:T(8,128)S(1)}, u32[]{:S(2)}, u32[]{:S(2)}) collective-permute-start(f32[17,8,256]{2,1,0:T(8,128)S(1)} %pad_maximum_fusion.6), channel_id=1, source_target_pairs={{0,32},{8,40},{16,48},{24,56},{32,64},{40,72},{48,80},{56,88},{64,... | collective-permute-start | bytes 417800 | tf_op jit(solution)/shard_map/ppermute | solution.py:22
  124.7 7.4 %collective-permute-done.10 = f32[17,8,256]{2,1,0:T(8,128)S(1)} collective-permute-done((f32[17,8,256]{2,1,0:T(8,128)S(1)}, f32[17,8,256]{2,1,0:T(8,128)S(1)}, u32[]{:S(2)}, u32[]{:S(2)}) %collective-permute-start.10) | collective-permute-done | bytes 139296 | tf_op jit(solution)/shard_map/ppermute | solution.py:22
  132.2 3.5 %collective-permute-start.11 = (f32[17,8,256]{2,1,0:T(8,128)S(1)}, f32[17,8,256]{2,1,0:T(8,128)S(1)}, u32[]{:S(2)}, u32[]{:S(2)}) collective-permute-start(f32[17,8,256]{2,1,0:T(8,128)S(1)} %pad_maximum_fusion.7), channel_id=1, source_target_pairs={{0,64},{8,72},{16,80},{24,88},{32,96},{40,104},{48,112},{56,120},{... | collective-permute-start | bytes 417800 | tf_op jit(solution)/shard_map/ppermute | solution.py:22
  135.7 3.4 %collective-permute-done.11 = f32[17,8,256]{2,1,0:T(8,128)S(1)} collective-permute-done((f32[17,8,256]{2,1,0:T(8,128)S(1)}, f32[17,8,256]{2,1,0:T(8,128)S(1)}, u32[]{:S(2)}, u32[]{:S(2)}) %collective-permute-start.11) | collective-permute-done | bytes 139296 | tf_op jit(solution)/shard_map/ppermute | solution.py:22
  139.2 4.4 %collective-permute-start.12 = (f32[17,8,256]{2,1,0:T(8,128)S(1)}, f32[17,8,256]{2,1,0:T(8,128)S(1)}, u32[]{:S(2)}, u32[]{:S(2)}) collective-permute-start(f32[17,8,256]{2,1,0:T(8,128)S(1)} %pad_maximum_fusion.8), channel_id=1, source_target_pairs={{0,128},{8,136},{16,144},{24,152},{32,160},{40,168},{48,176},{56,1... | collective-permute-start | bytes 417800 | tf_op jit(solution)/shard_map/ppermute | solution.py:22
  143.6 13.2 %shard_map.151 = bf16[256,1024]{1,0:T(8,128)(2,1)} custom-call(s32[1]{0:T(128)} %bitcast.14.base_ref, bf16[256,1024]{1,0:T(8,128)(2,1)} %q_ref.1, bf16[2304,256]{1,0:T(8,128)(2,1)} %copy-done.18, bf16[2304,256]{1,0:T(8,128)(2,1)} %copy-done.18), custom_call_target="tpu_custom_call" | custom-call | flops 2415919104 | bytes 3407872 | tf_op jit(solution)/shard_map/pallas_call | solution.py:116
  157.5 15.8 %shard_map.150 = f32[256,8,256]{2,1,0:T(8,128)} custom-call(f32[32,256]{1,0:T(8,128)} %reshape.54.bc_ref, f32[256,8,256]{2,1,0:T(8,128)} %copy-done.2, f32[256,8,256]{2,1,0:T(8,128)} %mul.207.dr_ref, f32[16,8,256]{2,1,0:T(8,128)} %bitcast.60, f32[16,8,256]{2,1,0:T(8,128)} %fusion.14.h0_ref), custom_call_target="tpu_custom_call" | custom-call | flops 50331648 | bytes 6553600 | tf_op jit(solution)/shard_map/pallas_call | solution.py:71
  173.4 3.3 %multiply_convert_fusion = bf16[256,8,256]{2,1,0:T(8,128)(2,1)S(1)} fusion(f32[256,8,256]{2,1,0:T(8,128)} %bitcast_multiply_fusion, f32[256,8,256]{2,1,0:T(8,128)} %shard_map.150, f32[256,8,256]{2,1,0:T(8,128)} %bitcast.56, f32[8,256]{1,0:T(8,128)S(1)} %mul.239), kind=kLoop, calls=%fused_computation.18 | loop fusion | flops 2097152 | bytes 7348224 | tf_op jit(solution)/shard_map/convert_element_type | solution.py:247
  176.6 1.3 copy.22
  (83 shorter events, 8.2 us)
Async XLA Ops:
  0.6 22.6 %copy-start = (bf16[2048,512]{1,0:T(8,128)(2,1)S(1)}, bf16[2048,512]{1,0:T(8,128)(2,1)}, u32[]{:S(2)}) copy-start(bf16[2048,512]{1,0:T(8,128)(2,1)} %param.21) | copy-start | bytes 6291460
  3.3 15.0 %collective-permute-start = (bf16[280,256]{1,0:T(8,128)(2,1)S(1)}, bf16[280,256]{1,0:T(8,128)(2,1)S(1)}, u32[]{:S(2)}, u32[]{:S(2)}) collective-permute-start(bf16[280,256]{1,0:T(8,128)(2,1)S(1)} %pad_maximum_fusion.3), channel_id=1, source_target_pairs={{0,8},{8,16},{16,24},{24,32},{32,40},{40,48},{48,56},{56,64},{64,7... | collective-permute-start | bytes 430088 | tf_op jit(solution)/shard_map/ppermute | solution.py:22
  18.4 1.6 copy-start.14
  18.4 1.6 copy-start.15
  18.4 1.6 copy-start.16
  18.4 1.6 copy-start.17
  18.4 1.6 copy-start.20
  20.0 1.4 copy-start.11
  23.2 2.4 %copy-start.7 = (f32[16,512]{1,0:T(8,128)}, f32[16,512]{1,0:T(8,128)S(1)}, u32[]{:S(2)}) copy-start(f32[16,512]{1,0:T(8,128)S(1)} %reshape.53) | copy-start | bytes 98308
  23.9 0.8 copy-start.5
  25.6 17.6 %collective-permute-start.1 = (f32[272,512]{1,0:T(8,128)}, f32[272,512]{1,0:T(8,128)}, u32[]{:S(2)}, u32[]{:S(2)}) collective-permute-start(f32[272,512]{1,0:T(8,128)} %pad_maximum_fusion), channel_id=1, source_target_pairs={{0,1},{1,0},{2,3},{3,2},{4,5},{5,4},{6,7},{7,6},{8,9},{9,8},{10,11... | collective-permute-start | bytes 1671176 | tf_op jit(solution)/shard_map/ppermute | solution.py:140
  26.3 13.1 %collective-permute-start.6 = (bf16[512,256]{1,0:T(8,128)(2,1)}, bf16[512,256]{1,0:T(8,128)(2,1)}, u32[]{:S(2)}, u32[]{:S(2)}) collective-permute-start(bf16[512,256]{1,0:T(8,128)(2,1)} %pad_maximum_fusion.2), channel_id=1, source_target_pairs={{0,16},{8,24},{16,32},{24,40},{32,48},{40,56},{48,64},{56,72},{64,... | collective-permute-start | bytes 786440 | tf_op jit(solution)/shard_map/ppermute | solution.py:22
  28.2 33.2 %collective-permute-start.5 = (bf16[256,256]{1,0:T(8,128)(2,1)S(1)}, bf16[256,256]{1,0:T(8,128)(2,1)}, u32[]{:S(2)}, u32[]{:S(2)}) collective-permute-start(bf16[256,256]{1,0:T(8,128)(2,1)S(1)} %constant_dynamic-update-slice_fusion), channel_id=1, source_target_pairs={{0,64},{8,72},{16,80},{24,88},{32,96},{40,104},{48,112},{56,120},{... | collective-permute-start | bytes 393224 | tf_op jit(solution)/shard_map/ppermute | solution.py:22
  31.7 11.4 %copy-start.6 = (f32[256,512]{1,0:T(8,128)S(1)}, f32[256,512]{1,0:T(8,128)}, u32[]{:S(2)}) copy-start(f32[256,512]{1,0:T(8,128)} %copy-done.5) | copy-start | bytes 1572868
  31.8 11.4 %copy-start.8 = (f32[16,512]{1,0:T(8,128)S(1)}, f32[16,512]{1,0:T(8,128)}, u32[]{:S(2)}) copy-start(f32[16,512]{1,0:T(8,128)} %copy-done.7) | copy-start | bytes 98308
  41.3 22.6 %collective-permute-start.7 = (bf16[1024,256]{1,0:T(8,128)(2,1)}, bf16[1024,256]{1,0:T(8,128)(2,1)}, u32[]{:S(2)}, u32[]{:S(2)}) collective-permute-start(bf16[1024,256]{1,0:T(8,128)(2,1)} %pad_maximum_fusion.1), channel_id=1, source_target_pairs={{0,32},{8,40},{16,48},{24,56},{32,64},{40,72},{48,80},{56,88},{64,... | collective-permute-start | bytes 1572872 | tf_op jit(solution)/shard_map/ppermute | solution.py:22
  44.3 0.8 copy-start.3
  45.9 6.7 %copy-start.12 = (f32[16,2048]{1,0:T(8,128)S(1)}, f32[16,2048]{1,0:T(8,128)}, u32[]{:S(2)}) copy-start(f32[16,2048]{1,0:T(8,128)} %param.26) | copy-start | bytes 393220
  45.9 10.3 %collective-permute-start.2 = (f32[136,512]{1,0:T(8,128)}, f32[136,512]{1,0:T(8,128)}, u32[]{:S(2)}, u32[]{:S(2)}) collective-permute-start(f32[136,512]{1,0:T(8,128)} %slice_select_fusion), channel_id=1, source_target_pairs={{0,2},{1,3},{2,0},{3,1},{4,6},{5,7},{6,4},{7,5},{8,10},{9,11},{10,... | collective-permute-start | bytes 835592 | tf_op jit(solution)/shard_map/ppermute | solution.py:140
  57.4 15.8 %collective-permute-start.3 = (f32[136,512]{1,0:T(8,128)S(1)}, f32[136,512]{1,0:T(8,128)S(1)}, u32[]{:S(2)}, u32[]{:S(2)}) collective-permute-start(f32[136,512]{1,0:T(8,128)S(1)} %fusion.25), channel_id=1, source_target_pairs={{0,4},{1,5},{2,6},{3,7},{4,0},{5,1},{6,2},{7,3},{8,12},{9,13},{10,... | collective-permute-start | bytes 835592 | tf_op jit(solution)/shard_map/ppermute | solution.py:140
  63.9 9.5 %copy-start.9 = (bf16[256,128]{1,0:T(8,128)(2,1)S(1)}, bf16[256,128]{1,0:T(8,128)(2,1)}, u32[]{:S(2)}) copy-start(bf16[256,128]{1,0:T(8,128)(2,1)} %param.17) | copy-start | bytes 196612
  63.9 9.6 %copy-start.10 = (bf16[256,128]{1,0:T(8,128)(2,1)S(1)}, bf16[256,128]{1,0:T(8,128)(2,1)}, u32[]{:S(2)}) copy-start(bf16[256,128]{1,0:T(8,128)(2,1)} %param.18) | copy-start | bytes 196612
  63.9 11.9 %copy-start.21 = (f32[512]{0:T(512)S(1)}, f32[512]{0:T(512)}, u32[]{:S(2)}) copy-start(f32[512]{0:T(512)} %param.23) | copy-start | bytes 6148
  73.3 1.6 collective-permute-start.4
  73.5 1.5 copy-start.18
  75.8 2.4 %copy-start.13 = (f32[8,256]{1,0:T(8,128)S(1)}, f32[8,256]{1,0:T(8,128)}, u32[]{:S(2)}) copy-start(f32[8,256]{1,0:T(8,128)} %add.140) | copy-start | bytes 24580
  78.1 1.9 %copy-start.1 = (f32[32,8,8,256]{3,2,1,0:T(8,128)S(1)}, f32[32,8,8,256]{3,2,1,0:T(8,128)}, u32[]{:S(2)}) copy-start(f32[32,8,8,256]{3,2,1,0:T(8,128)} %copy.19) | copy-start | bytes 6291460
  80.0 2.1 %copy-start.2 = (f32[256,8,256]{2,1,0:T(8,128)}, f32[256,8,256]{2,1,0:T(8,128)S(1)}, u32[]{:S(2)}) copy-start(f32[256,8,256]{2,1,0:T(8,128)S(1)} %get-tuple-element.11.dt_ref) | copy-start | bytes 6291460
  82.7 29.4 %copy-start.4 = (f32[2,8,8,256]{3,2,1,0:T(8,128)S(1)}, f32[2,8,8,256]{3,2,1,0:T(8,128)}, u32[]{:S(2)}) copy-start(f32[2,8,8,256]{3,2,1,0:T(8,128)} %copy.21) | copy-start | bytes 393220
  95.3 40.4 %copy-start.19 = (f32[2048]{0:T(1024)S(1)}, f32[2048]{0:T(1024)}, u32[]{:S(2)}) copy-start(f32[2048]{0:T(1024)} %param.27) | copy-start | bytes 24580
  96.2 15.9 %collective-permute-start.8 = (f32[17,8,256]{2,1,0:T(8,128)S(1)}, f32[17,8,256]{2,1,0:T(8,128)S(1)}, u32[]{:S(2)}, u32[]{:S(2)}) collective-permute-start(f32[17,8,256]{2,1,0:T(8,128)S(1)} %pad_maximum_fusion.4), channel_id=1, source_target_pairs={{0,8},{8,16},{16,24},{24,32},{32,40},{40,48},{48,56},{56,64},{64,7... | collective-permute-start | bytes 417800 | tf_op jit(solution)/shard_map/ppermute | solution.py:22
  113.1 9.6 %collective-permute-start.9 = (f32[17,8,256]{2,1,0:T(8,128)S(1)}, f32[17,8,256]{2,1,0:T(8,128)S(1)}, u32[]{:S(2)}, u32[]{:S(2)}) collective-permute-start(f32[17,8,256]{2,1,0:T(8,128)S(1)} %pad_maximum_fusion.5), channel_id=1, source_target_pairs={{0,16},{8,24},{16,32},{24,40},{32,48},{40,56},{48,64},{56,72},{64,... | collective-permute-start | bytes 417800 | tf_op jit(solution)/shard_map/ppermute | solution.py:22
  122.8 9.4 %collective-permute-start.10 = (f32[17,8,256]{2,1,0:T(8,128)S(1)}, f32[17,8,256]{2,1,0:T(8,128)S(1)}, u32[]{:S(2)}, u32[]{:S(2)}) collective-permute-start(f32[17,8,256]{2,1,0:T(8,128)S(1)} %pad_maximum_fusion.6), channel_id=1, source_target_pairs={{0,32},{8,40},{16,48},{24,56},{32,64},{40,72},{48,80},{56,88},{64,... | collective-permute-start | bytes 417800 | tf_op jit(solution)/shard_map/ppermute | solution.py:22
  132.2 6.9 %collective-permute-start.11 = (f32[17,8,256]{2,1,0:T(8,128)S(1)}, f32[17,8,256]{2,1,0:T(8,128)S(1)}, u32[]{:S(2)}, u32[]{:S(2)}) collective-permute-start(f32[17,8,256]{2,1,0:T(8,128)S(1)} %pad_maximum_fusion.7), channel_id=1, source_target_pairs={{0,64},{8,72},{16,80},{24,88},{32,96},{40,104},{48,112},{56,120},{... | collective-permute-start | bytes 417800 | tf_op jit(solution)/shard_map/ppermute | solution.py:22
  139.2 17.6 %collective-permute-start.12 = (f32[17,8,256]{2,1,0:T(8,128)S(1)}, f32[17,8,256]{2,1,0:T(8,128)S(1)}, u32[]{:S(2)}, u32[]{:S(2)}) collective-permute-start(f32[17,8,256]{2,1,0:T(8,128)S(1)} %pad_maximum_fusion.8), channel_id=1, source_target_pairs={{0,128},{8,136},{16,144},{24,152},{32,160},{40,168},{48,176},{56,1... | collective-permute-start | bytes 417800 | tf_op jit(solution)/shard_map/ppermute | solution.py:22

commit v11 on v9

--- a/solution.py
+++ b/solution.py
@@ -41,7 +41,7 @@
 
     def body(t, hs):
         dt = dt_ref[t]
-        dr = dr_ref[t]
+        dr = dt * dr_ref[t]
         new = []
         acc = None
         for n in range(states):
@@ -97,8 +97,8 @@
         in_window = (distance >= 0) & (distance < WINDOW) & (cols + base_ref[0] >= WINDOW)
         bias_ref[...] = jnp.where(in_window, 0.0, -jnp.inf)
 
-    scores = lax.dot_general(
-        q_ref[...], k_ref[...], (((1,), (1,)), ((), ())), preferred_element_type=jnp.float32
+    scores = jnp.dot(
+        q_ref[...], k_ref[...], preferred_element_type=jnp.float32
     ) * (1.0 / math.sqrt(HD)) + bias_ref[...]
     row_peak = jnp.max(scores, axis=1, keepdims=True)
     weights = jnp.exp(scores - row_peak).astype(jnp.bfloat16)
@@ -118,7 +118,7 @@
         in_specs=[
             pl.BlockSpec(memory_space=pltpu.SMEM),
             pl.BlockSpec((tokens, HD), lambda h: (0, h)),
-            pl.BlockSpec((keys, HD), lambda h: (0, h // group)),
+            pl.BlockSpec((HD, keys), lambda h: (h // group, 0)),
             pl.BlockSpec((keys, HD), lambda h: (0, window.shape[1] // (2 * HD) + h // group)),
         ],
         out_specs=pl.BlockSpec((tokens, HD), lambda h: (0, h)),
@@ -129,7 +129,7 @@
             transcendentals=tokens * keys * heads,
             bytes_accessed=2 * (2 * tokens * width + 2 * keys * window.shape[1]),
         ),
-    )(base, q_proj, window, window)
+    )(base, q_proj, window[:, : width // group].T, window)
 
 
 def butterfly_sum(value, axis, first, last):
@@ -232,13 +232,12 @@
         jnp.einsum("tr,rsl->tsl", rank_normed, cube(dt_weight), preferred_element_type=jnp.float32)
         + cube(dt_bias)[None]
     )
-    dr3 = dt3 * act3
     rate3 = cube(decay_rate)
     zero_state = jnp.zeros((state_count, SUBLANES, lanes), jnp.float32)
-    local_final = run_scan(state_in, dt3, dr3, rate3, zero_state, False)
+    local_final = run_scan(state_in, dt3, act3, rate3, zero_state, False)
     step_sum = jnp.sum(dt3, axis=0)
     entering = entering_state(step_sum, local_final, rate3)
-    mamba_sum = run_scan(state_in, dt3, dr3, rate3, entering, True)
+    mamba_sum = run_scan(state_in, dt3, act3, rate3, entering, True)
     mamba_out = (
         ((mamba_sum + cube(skip_weight)[None] * act3) * jax.nn.silu(cube(gate_in).astype(jnp.float32)))
         .astype(jnp.bfloat16)

time: 179 us -> 181 us (1.011)
  waiting for transfers between devices: 53.3 us -> 41.7 us
  local copies, waits for them, and re-layouts: 16 us -> 24.8 us
  other arithmetic: 18.2 us -> 22.1 us
  matrix products: 2.67 us -> 4.67 us
    ppermute x3, waiting for transfers between devices: 21.6 us -> 15.5 us  [butterfly_sum(): value = value + lax.ppermute(value, axis, pairs)]
    ppermute x9, waiting for transfers between devices: 31.6 us -> 26.2 us  [shifted(): lax.ppermute(value, axis, [(source, source + steps) for source in range(f...]
    unnamed x42 -> x30, local copies, waits for them, and re-layouts: 9.43 us -> 14.7 us
    reduce_sum x1, other arithmetic: 1.9 us -> 4.83 us  [per_device(): step_sum = jnp.sum(dt3, axis=0)]
    transpose x0 -> x2, local copies, waits for them, and re-layouts: none -> 2.17 us  [run_attention(): window[:, :width // group]]
    mul x1 -> x0, other arithmetic: 1.85 us -> none  [per_device(): dr3 = dt3 * act3]
  transfers between devices with their start and end apart: 13 -> 13, of which waited for: 9 -> 8; matrix products, arithmetic and copies ran while one was open for 11% -> 18% of each run, Pallas kernels for 15% -> 14%
where the time goes in v11:
time: 181 us; the launch traced here: 180 us
  starting transfers between devices  43.8 us (24%)
  Pallas kernels  41.8 us (23%)
  waiting for transfers between devices  41.7 us (23%)
  local copies, waits for them, and re-layouts  24.8 us (14%)
  other arithmetic  22.1 us (12%)
  matrix products  4.67 us (3%)
    ppermute x9, starting transfers between devices, shifted(): lax.ppermute(value, axis, [(source, source + steps) for source in range(f...  36.2 us
    pallas_call x2, Pallas kernels, run_scan(): pl.pallas_call(functools.partial(scan_kernel, with_out), grid=(blocks,),...  28.5 us
    ppermute x9, waiting for transfers between devices, shifted(): lax.ppermute(value, axis, [(source, source + steps) for source in range(f...  26.2 us
    ppermute x3, waiting for transfers between devices, butterfly_sum(): value = value + lax.ppermute(value, axis, pairs)  15.5 us
    unnamed x30, local copies, waits for them, and re-layouts  14.7 us
    pallas_call x1, Pallas kernels, run_attention(): pl.pallas_call(attention_kernel, grid=(heads,), in_specs=[pl.BlockSpec(me...  13.3 us
    ppermute x3, starting transfers between devices, butterfly_sum(): value = value + lax.ppermute(value, axis, pairs)  7.61 us
    reduce_sum x1, other arithmetic, per_device(): step_sum = jnp.sum(dt3, axis=0)  4.83 us
  transfers between devices with their start and end apart: 13, of which 8 were waited for; matrix products, arithmetic and copies ran while one was open for 18% of the time, Pallas kernels for 14%

profile of v11, /device:TPU:8, one launch (start us, length us, event | category | flops | bytes accessed | tf_op | source)
XLA Modules:
  0.0 179.8 jit_solution(16500082673309927964)
XLA Ops:
  0.7 1.0 constant_dynamic-update-slice_fusion.1
  3.3 9.1 %collective-permute-start = (bf16[280,256]{1,0:T(8,128)(2,1)S(1)}, bf16[280,256]{1,0:T(8,128)(2,1)S(1)}, u32[]{:S(2)}, u32[]{:S(2)}) collective-permute-start(bf16[280,256]{1,0:T(8,128)(2,1)S(1)} %pad_maximum_fusion.3), channel_id=1, source_target_pairs={{0,8},{8,16},{16,24},{24,32},{32,40},{40,48},{48,56},{56,64},{64,7... | collective-permute-start | bytes 430088 | tf_op jit(solution)/shard_map/ppermute | solution.py:22
  12.5 0.9 fusion.21
  13.4 5.0 %collective-permute-done = bf16[280,256]{1,0:T(8,128)(2,1)S(1)} collective-permute-done((bf16[280,256]{1,0:T(8,128)(2,1)S(1)}, bf16[280,256]{1,0:T(8,128)(2,1)S(1)}, u32[]{:S(2)}, u32[]{:S(2)}) %collective-permute-start) | collective-permute-done | bytes 143392 | tf_op jit(solution)/shard_map/ppermute | solution.py:22
  18.4 1.5 maximum_convert_fusion
  19.9 1.3 multiply_convert_fusion
  21.3 1.5 fusion.22
  22.8 1.0 convolution_bitcast_fusion
  24.6 1.9 %pad_maximum_fusion = f32[272,512]{1,0:T(8,128)} fusion(f32[16,512]{1,0:T(8,128)S(1)} %reshape.53, f32[256,512]{1,0:T(8,128)} %fusion.22), kind=kLoop, calls=%fused_computation.24 | loop fusion | flops 139264 | bytes 1114112 | tf_op jit(solution)/shard_map/concatenate | solution.py:219
  26.5 2.3 %collective-permute-done.1 = f32[272,512]{1,0:T(8,128)} collective-permute-done((f32[272,512]{1,0:T(8,128)}, f32[272,512]{1,0:T(8,128)}, u32[]{:S(2)}, u32[]{:S(2)}) %collective-permute-start.1) | collective-permute-done | bytes 557088 | tf_op jit(solution)/shard_map/ppermute | solution.py:139
  28.8 1.3 fusion.19
  30.1 3.6 %collective-permute-start.2 = (f32[136,512]{1,0:T(8,128)S(1)}, f32[136,512]{1,0:T(8,128)S(1)}, u32[]{:S(2)}, u32[]{:S(2)}) collective-permute-start(f32[136,512]{1,0:T(8,128)S(1)} %slice_select_fusion), channel_id=1, source_target_pairs={{0,2},{1,3},{2,0},{3,1},{4,6},{5,7},{6,4},{7,5},{8,10},{9,11},{10,... | collective-permute-start | bytes 835592 | tf_op jit(solution)/shard_map/ppermute | solution.py:139
  33.8 7.0 %collective-permute-done.2 = f32[136,512]{1,0:T(8,128)S(1)} collective-permute-done((f32[136,512]{1,0:T(8,128)S(1)}, f32[136,512]{1,0:T(8,128)S(1)}, u32[]{:S(2)}, u32[]{:S(2)}) %collective-permute-start.2) | collective-permute-done | bytes 278560 | tf_op jit(solution)/shard_map/ppermute | solution.py:139
  40.8 4.0 %collective-permute-start.3 = (f32[136,512]{1,0:T(8,128)S(1)}, f32[136,512]{1,0:T(8,128)S(1)}, u32[]{:S(2)}, u32[]{:S(2)}) collective-permute-start(f32[136,512]{1,0:T(8,128)S(1)} %fusion.27), channel_id=1, source_target_pairs={{0,4},{1,5},{2,6},{3,7},{4,0},{5,1},{6,2},{7,3},{8,12},{9,13},{10,... | collective-permute-start | bytes 835592 | tf_op jit(solution)/shard_map/ppermute | solution.py:139
  45.5 1.9 %collective-permute-start.11 = (bf16[512,256]{1,0:T(8,128)(2,1)}, bf16[512,256]{1,0:T(8,128)(2,1)}, u32[]{:S(2)}, u32[]{:S(2)}) collective-permute-start(bf16[512,256]{1,0:T(8,128)(2,1)} %pad_maximum_fusion.2), channel_id=1, source_target_pairs={{0,16},{8,24},{16,32},{24,40},{32,48},{40,56},{48,64},{56,72},{64,... | collective-permute-start | bytes 786440 | tf_op jit(solution)/shard_map/ppermute | solution.py:22
  47.4 3.5 %collective-permute-start.10 = (bf16[256,256]{1,0:T(8,128)(2,1)S(1)}, bf16[256,256]{1,0:T(8,128)(2,1)}, u32[]{:S(2)}, u32[]{:S(2)}) collective-permute-start(bf16[256,256]{1,0:T(8,128)(2,1)S(1)} %constant_dynamic-update-slice_fusion), channel_id=1, source_target_pairs={{0,64},{8,72},{16,80},{24,88},{32,96},{40,104},{48,112},{56,120},{... | collective-permute-start | bytes 393224 | tf_op jit(solution)/shard_map/ppermute | solution.py:22
  50.9 6.2 %collective-permute-done.3 = f32[136,512]{1,0:T(8,128)S(1)} collective-permute-done((f32[136,512]{1,0:T(8,128)S(1)}, f32[136,512]{1,0:T(8,128)S(1)}, u32[]{:S(2)}, u32[]{:S(2)}) %collective-permute-start.3) | collective-permute-done | bytes 278560 | tf_op jit(solution)/shard_map/ppermute | solution.py:139
  57.9 1.3 add.139
  59.2 1.6 copy.21
  60.8 2.8 %copy.22 = f32[32,8,8,256]{3,2,1,0:T(8,128)} copy(bf16[32,8,8,256]{3,1,2,0:T(8,128)(2,1)} %bitcast.70) | data formatting | bytes 3145728
  63.6 1.3 mul.234
  64.9 1.6 constant_dynamic-update-slice_fusion.6
  66.5 1.5 copy.20
  68.0 1.1 pad_maximum_fusion.1
  69.2 2.8 %collective-permute-start.12 = (bf16[1024,256]{1,0:T(8,128)(2,1)S(1)}, bf16[1024,256]{1,0:T(8,128)(2,1)}, u32[]{:S(2)}, u32[]{:S(2)}) collective-permute-start(bf16[1024,256]{1,0:T(8,128)(2,1)S(1)} %pad_maximum_fusion.1), channel_id=1, source_target_pairs={{0,32},{8,40},{16,48},{24,56},{32,64},{40,72},{48,80},{56,88},{64,... | collective-permute-start | bytes 1572872 | tf_op jit(solution)/shard_map/ppermute | solution.py:22
  72.0 1.5 maximum_select_fusion
  73.6 2.1 %fusion.4 = f32[256,8,256]{2,0,1:T(8,128)} fusion(bf16[64,8,8,256]{3,2,1,0:T(8,128)(2,1)S(1)} %bitcast.69, f32[272,512]{1,0:T(8,128)S(1)} %maximum_select_fusion, f32[512]{0:T(512)S(1)} %copy-done.9, f32[256]{0:T(256)S(1)} %add_rsqrt_fusion), kind=kOutput, calls=%fused_computation.7 | convolution fusion | flops 537264128 | bytes 4721664 | tf_op jit(solution)/shard_map/tr,rsl->tsl/dot_general | solution.py:232
  76.4 4.8 %fusion.20 = (f32[8,256]{1,0:T(8,128)S(1)}, f32[256,8,256]{2,1,0:T(8,128)}) fusion(f32[8,256]{1,0:T(8,128)S(1)} %copy-done.6, f32[256,8,256]{2,0,1:T(8,128)} %fusion.4), kind=kLoop, calls=%fused_computation.66 | loop fusion | flops 4192256 | bytes 4210688 | tf_op jit(solution)/shard_map/reduce_sum | solution.py:238
  81.9 12.7 %shard_map.149 = f32[16,8,256]{2,1,0:T(8,128)} custom-call(f32[32,256]{1,0:T(8,128)} %reshape.54.bc_ref, f32[256,8,256]{2,1,0:T(8,128)} %get-tuple-element.3.dt_ref, f32[256,8,256]{2,1,0:T(8,128)} %bitcast.64, f32[16,8,256]{2,1,0:T(8,128)} %bitcast.66, f32[16,8,256]{2,1,0:T(8,128)} %broadcast_in_dim.5.h0_ref), custom_call_target="tpu_custom_call" | custom-call | flops 33554432 | bytes 6553600 | tf_op jit(solution)/shard_map/pallas_call | solution.py:71
  94.5 1.0 pad_maximum_fusion.4
  95.5 7.2 %collective-permute-start.5 = (f32[17,8,256]{2,1,0:T(8,128)S(1)}, f32[17,8,256]{2,1,0:T(8,128)S(1)}, u32[]{:S(2)}, u32[]{:S(2)}) collective-permute-start(f32[17,8,256]{2,1,0:T(8,128)S(1)} %pad_maximum_fusion.4), channel_id=1, source_target_pairs={{0,8},{8,16},{16,24},{24,32},{32,40},{40,48},{48,56},{56,64},{64,7... | collective-permute-start | bytes 417800 | tf_op jit(solution)/shard_map/ppermute | solution.py:22
  102.7 1.9 %constant_dynamic-update-slice_fusion.5 = bf16[2304,256]{1,0:T(8,128)(2,1)} fusion(bf16[2304,256]{1,0:T(8,128)(2,1)} %constant_dynamic-update-slice_fusion.6, bf16[1024,256]{1,0:T(8,128)(2,1)} %collective-permute-done.12), kind=kLoop, calls=%fused_computation.51 | loop fusion | bytes 1048576
  104.6 1.7 constant_dynamic-update-slice_fusion.4
  106.3 6.8 %collective-permute-done.5 = f32[17,8,256]{2,1,0:T(8,128)S(1)} collective-permute-done((f32[17,8,256]{2,1,0:T(8,128)S(1)}, f32[17,8,256]{2,1,0:T(8,128)S(1)}, u32[]{:S(2)}, u32[]{:S(2)}) %collective-permute-start.5) | collective-permute-done | bytes 139296 | tf_op jit(solution)/shard_map/ppermute | solution.py:22
  113.1 0.9 multiply_add_fusion.3
  114.0 1.9 %collective-permute-start.6 = (f32[17,8,256]{2,1,0:T(8,128)S(1)}, f32[17,8,256]{2,1,0:T(8,128)S(1)}, u32[]{:S(2)}, u32[]{:S(2)}) collective-permute-start(f32[17,8,256]{2,1,0:T(8,128)S(1)} %pad_maximum_fusion.5), channel_id=1, source_target_pairs={{0,16},{8,24},{16,32},{24,40},{32,48},{40,56},{48,64},{56,72},{64,... | collective-permute-start | bytes 417800 | tf_op jit(solution)/shard_map/ppermute | solution.py:22
  116.6 6.8 %collective-permute-done.6 = f32[17,8,256]{2,1,0:T(8,128)S(1)} collective-permute-done((f32[17,8,256]{2,1,0:T(8,128)S(1)}, f32[17,8,256]{2,1,0:T(8,128)S(1)}, u32[]{:S(2)}, u32[]{:S(2)}) %collective-permute-start.6) | collective-permute-done | bytes 139296 | tf_op jit(solution)/shard_map/ppermute | solution.py:22
  123.5 1.9 %collective-permute-start.7 = (f32[17,8,256]{2,1,0:T(8,128)S(1)}, f32[17,8,256]{2,1,0:T(8,128)S(1)}, u32[]{:S(2)}, u32[]{:S(2)}) collective-permute-start(f32[17,8,256]{2,1,0:T(8,128)S(1)} %pad_maximum_fusion.6), channel_id=1, source_target_pairs={{0,32},{8,40},{16,48},{24,56},{32,64},{40,72},{48,80},{56,88},{64,... | collective-permute-start | bytes 417800 | tf_op jit(solution)/shard_map/ppermute | solution.py:22
  126.7 6.1 %collective-permute-done.7 = f32[17,8,256]{2,1,0:T(8,128)S(1)} collective-permute-done((f32[17,8,256]{2,1,0:T(8,128)S(1)}, f32[17,8,256]{2,1,0:T(8,128)S(1)}, u32[]{:S(2)}, u32[]{:S(2)}) %collective-permute-start.7) | collective-permute-done | bytes 139296 | tf_op jit(solution)/shard_map/ppermute | solution.py:22
  133.6 3.5 %collective-permute-start.8 = (f32[17,8,256]{2,1,0:T(8,128)}, f32[17,8,256]{2,1,0:T(8,128)S(1)}, u32[]{:S(2)}, u32[]{:S(2)}) collective-permute-start(f32[17,8,256]{2,1,0:T(8,128)} %pad_maximum_fusion.7), channel_id=1, source_target_pairs={{0,64},{8,72},{16,80},{24,88},{32,96},{40,104},{48,112},{56,120},{... | collective-permute-start | bytes 417800 | tf_op jit(solution)/shard_map/ppermute | solution.py:22
  137.1 1.1 slice_bitcast_fusion
  138.2 1.1 copy.18.k_ref
  139.3 1.5 collective-permute-done.8
  140.8 4.4 %collective-permute-start.9 = (f32[17,8,256]{2,1,0:T(8,128)S(1)}, f32[17,8,256]{2,1,0:T(8,128)S(1)}, u32[]{:S(2)}, u32[]{:S(2)}) collective-permute-start(f32[17,8,256]{2,1,0:T(8,128)S(1)} %pad_maximum_fusion.8), channel_id=1, source_target_pairs={{0,128},{8,136},{16,144},{24,152},{32,160},{40,168},{48,176},{56,1... | collective-permute-start | bytes 417800 | tf_op jit(solution)/shard_map/ppermute | solution.py:22
  145.2 13.3 %shard_map.151 = bf16[256,1024]{1,0:T(8,128)(2,1)} custom-call(s32[1]{0:T(128)} %bitcast.14.base_ref, bf16[256,1024]{1,0:T(8,128)(2,1)} %q_ref.1, bf16[128,2304]{1,0:T(8,128)(2,1)} %copy.18.k_ref, bf16[2304,256]{1,0:T(8,128)(2,1)} %constant_dynamic-update-slice_fusion.7.v_ref), custom_call_target="tpu_custom_call" | custom-call | flops 2415919104 | bytes 3407872 | tf_op jit(solution)/shard_map/pallas_call | solution.py:115
  159.2 15.9 %shard_map.150 = f32[256,8,256]{2,1,0:T(8,128)} custom-call(f32[32,256]{1,0:T(8,128)} %reshape.54.bc_ref, f32[256,8,256]{2,1,0:T(8,128)} %get-tuple-element.3.dt_ref, f32[256,8,256]{2,1,0:T(8,128)} %bitcast.65, f32[16,8,256]{2,1,0:T(8,128)} %bitcast.67, f32[16,8,256]{2,1,0:T(8,128)} %fusion.16.h0_ref), custom_call_target="tpu_custom_call" | custom-call | flops 50331648 | bytes 6553600 | tf_op jit(solution)/shard_map/pallas_call | solution.py:71
  175.1 3.4 %fusion.11 = bf16[256,8,256]{2,1,0:T(8,128)(2,1)S(1)} fusion(f32[32,8,8,256]{3,2,1,0:T(8,128)} %copy.22, f32[256,8,256]{2,1,0:T(8,128)} %shard_map.150, f32[8,256]{1,0:T(8,128)S(1)} %copy-done.7, f32[32,8,8,256]{3,2,1,0:T(8,128)} %copy.20), kind=kLoop, calls=%fused_computation.20 | loop fusion | flops 4194304 | bytes 7348224 | tf_op jit(solution)/shard_map/convert_element_type | solution.py:243
  178.6 1.3 copy.23
  (59 shorter events, 9.1 us)
Async XLA Ops:
  0.6 20.7 %copy-start = (bf16[2048,512]{1,0:T(8,128)(2,1)S(1)}, bf16[2048,512]{1,0:T(8,128)(2,1)}, u32[]{:S(2)}) copy-start(bf16[2048,512]{1,0:T(8,128)(2,1)} %param.21) | copy-start | bytes 6291460
  0.6 19.3 %copy-start.8 = (f32[2048]{0:T(1024)S(1)}, f32[2048]{0:T(1024)}, u32[]{:S(2)}) copy-start(f32[2048]{0:T(1024)} %param.20) | copy-start | bytes 24580
  3.3 15.0 %collective-permute-start = (bf16[280,256]{1,0:T(8,128)(2,1)S(1)}, bf16[280,256]{1,0:T(8,128)(2,1)S(1)}, u32[]{:S(2)}, u32[]{:S(2)}) collective-permute-start(bf16[280,256]{1,0:T(8,128)(2,1)S(1)} %pad_maximum_fusion.3), channel_id=1, source_target_pairs={{0,8},{8,16},{16,24},{24,32},{32,40},{40,48},{48,56},{56,64},{64,7... | collective-permute-start | bytes 430088 | tf_op jit(solution)/shard_map/ppermute | solution.py:22
  21.3 1.5 copy-start.5
  26.5 2.3 %collective-permute-start.1 = (f32[272,512]{1,0:T(8,128)}, f32[272,512]{1,0:T(8,128)}, u32[]{:S(2)}, u32[]{:S(2)}) collective-permute-start(f32[272,512]{1,0:T(8,128)} %pad_maximum_fusion), channel_id=1, source_target_pairs={{0,1},{1,0},{2,3},{3,2},{4,5},{5,4},{6,7},{7,6},{8,9},{9,8},{10,11... | collective-permute-start | bytes 1671176 | tf_op jit(solution)/shard_map/ppermute | solution.py:139
  30.1 10.6 %collective-permute-start.2 = (f32[136,512]{1,0:T(8,128)S(1)}, f32[136,512]{1,0:T(8,128)S(1)}, u32[]{:S(2)}, u32[]{:S(2)}) collective-permute-start(f32[136,512]{1,0:T(8,128)S(1)} %slice_select_fusion), channel_id=1, source_target_pairs={{0,2},{1,3},{2,0},{3,1},{4,6},{5,7},{6,4},{7,5},{8,10},{9,11},{10,... | collective-permute-start | bytes 835592 | tf_op jit(solution)/shard_map/ppermute | solution.py:139
  40.8 16.4 %collective-permute-start.3 = (f32[136,512]{1,0:T(8,128)S(1)}, f32[136,512]{1,0:T(8,128)S(1)}, u32[]{:S(2)}, u32[]{:S(2)}) collective-permute-start(f32[136,512]{1,0:T(8,128)S(1)} %fusion.27), channel_id=1, source_target_pairs={{0,4},{1,5},{2,6},{3,7},{4,0},{5,1},{6,2},{7,3},{8,12},{9,13},{10,... | collective-permute-start | bytes 835592 | tf_op jit(solution)/shard_map/ppermute | solution.py:139
  45.5 22.5 %collective-permute-start.11 = (bf16[512,256]{1,0:T(8,128)(2,1)}, bf16[512,256]{1,0:T(8,128)(2,1)}, u32[]{:S(2)}, u32[]{:S(2)}) collective-permute-start(bf16[512,256]{1,0:T(8,128)(2,1)} %pad_maximum_fusion.2), channel_id=1, source_target_pairs={{0,16},{8,24},{16,32},{24,40},{32,48},{40,56},{48,64},{56,72},{64,... | collective-permute-start | bytes 786440 | tf_op jit(solution)/shard_map/ppermute | solution.py:22
  47.4 17.5 %collective-permute-start.10 = (bf16[256,256]{1,0:T(8,128)(2,1)S(1)}, bf16[256,256]{1,0:T(8,128)(2,1)}, u32[]{:S(2)}, u32[]{:S(2)}) collective-permute-start(bf16[256,256]{1,0:T(8,128)(2,1)S(1)} %constant_dynamic-update-slice_fusion), channel_id=1, source_target_pairs={{0,64},{8,72},{16,80},{24,88},{32,96},{40,104},{48,112},{56,120},{... | collective-permute-start | bytes 393224 | tf_op jit(solution)/shard_map/ppermute | solution.py:22
  57.9 14.1 %collective-permute-start.4 = (f32[136,512]{1,0:T(8,128)}, f32[136,512]{1,0:T(8,128)}, u32[]{:S(2)}, u32[]{:S(2)}) collective-permute-start(f32[136,512]{1,0:T(8,128)} %add.136), channel_id=1, source_target_pairs={{0,1},{1,0},{2,3},{3,2},{4,5},{5,4},{6,7},{7,6},{8,9},{9,8},{10,11... | collective-permute-start | bytes 835592 | tf_op jit(solution)/shard_map/ppermute | solution.py:151
  68.0 5.6 %copy-start.2 = (bf16[512,2048]{1,0:T(8,128)(2,1)S(1)}, bf16[512,2048]{1,0:T(8,128)(2,1)}, u32[]{:S(2)}) copy-start(bf16[512,2048]{1,0:T(8,128)(2,1)} %param.24) | copy-start | bytes 6291460
  68.0 5.6 %copy-start.9 = (f32[512]{0:T(512)S(1)}, f32[512]{0:T(512)}, u32[]{:S(2)}) copy-start(f32[512]{0:T(512)} %param.23) | copy-start | bytes 6148
  69.2 33.5 %collective-permute-start.12 = (bf16[1024,256]{1,0:T(8,128)(2,1)S(1)}, bf16[1024,256]{1,0:T(8,128)(2,1)}, u32[]{:S(2)}, u32[]{:S(2)}) collective-permute-start(bf16[1024,256]{1,0:T(8,128)(2,1)S(1)} %pad_maximum_fusion.1), channel_id=1, source_target_pairs={{0,32},{8,40},{16,48},{24,56},{32,64},{40,72},{48,80},{56,88},{64,... | collective-permute-start | bytes 1572872 | tf_op jit(solution)/shard_map/ppermute | solution.py:22
  73.6 2.8 %copy-start.6 = (f32[8,256]{1,0:T(8,128)S(1)}, f32[8,256]{1,0:T(8,128)}, u32[]{:S(2)}) copy-start(f32[8,256]{1,0:T(8,128)} %add.139) | copy-start | bytes 24580
  81.9 31.2 %copy-start.1 = (f32[2,8,8,256]{3,2,1,0:T(8,128)S(1)}, f32[2,8,8,256]{3,2,1,0:T(8,128)}, u32[]{:S(2)}) copy-start(f32[2,8,8,256]{3,2,1,0:T(8,128)} %copy.21) | copy-start | bytes 393220
  94.5 30.9 %copy-start.3 = (bf16[256,128]{1,0:T(8,128)(2,1)S(1)}, bf16[256,128]{1,0:T(8,128)(2,1)}, u32[]{:S(2)}) copy-start(bf16[256,128]{1,0:T(8,128)(2,1)} %param.17) | copy-start | bytes 196612
  94.5 31.6 %copy-start.4 = (bf16[256,128]{1,0:T(8,128)(2,1)S(1)}, bf16[256,128]{1,0:T(8,128)(2,1)}, u32[]{:S(2)}) copy-start(bf16[256,128]{1,0:T(8,128)(2,1)} %param.18) | copy-start | bytes 196612
  95.5 17.6 %collective-permute-start.5 = (f32[17,8,256]{2,1,0:T(8,128)S(1)}, f32[17,8,256]{2,1,0:T(8,128)S(1)}, u32[]{:S(2)}, u32[]{:S(2)}) collective-permute-start(f32[17,8,256]{2,1,0:T(8,128)S(1)} %pad_maximum_fusion.4), channel_id=1, source_target_pairs={{0,8},{8,16},{16,24},{24,32},{32,40},{40,48},{48,56},{56,64},{64,7... | collective-permute-start | bytes 417800 | tf_op jit(solution)/shard_map/ppermute | solution.py:22
  114.0 9.4 %collective-permute-start.6 = (f32[17,8,256]{2,1,0:T(8,128)S(1)}, f32[17,8,256]{2,1,0:T(8,128)S(1)}, u32[]{:S(2)}, u32[]{:S(2)}) collective-permute-start(f32[17,8,256]{2,1,0:T(8,128)S(1)} %pad_maximum_fusion.5), channel_id=1, source_target_pairs={{0,16},{8,24},{16,32},{24,40},{32,48},{40,56},{48,64},{56,72},{64,... | collective-permute-start | bytes 417800 | tf_op jit(solution)/shard_map/ppermute | solution.py:22
  123.5 9.4 %collective-permute-start.7 = (f32[17,8,256]{2,1,0:T(8,128)S(1)}, f32[17,8,256]{2,1,0:T(8,128)S(1)}, u32[]{:S(2)}, u32[]{:S(2)}) collective-permute-start(f32[17,8,256]{2,1,0:T(8,128)S(1)} %pad_maximum_fusion.6), channel_id=1, source_target_pairs={{0,32},{8,40},{16,48},{24,56},{32,64},{40,72},{48,80},{56,88},{64,... | collective-permute-start | bytes 417800 | tf_op jit(solution)/shard_map/ppermute | solution.py:22
  133.6 7.1 %collective-permute-start.8 = (f32[17,8,256]{2,1,0:T(8,128)}, f32[17,8,256]{2,1,0:T(8,128)S(1)}, u32[]{:S(2)}, u32[]{:S(2)}) collective-permute-start(f32[17,8,256]{2,1,0:T(8,128)} %pad_maximum_fusion.7), channel_id=1, source_target_pairs={{0,64},{8,72},{16,80},{24,88},{32,96},{40,104},{48,112},{56,120},{... | collective-permute-start | bytes 417800 | tf_op jit(solution)/shard_map/ppermute | solution.py:22
  140.8 17.7 %collective-permute-start.9 = (f32[17,8,256]{2,1,0:T(8,128)S(1)}, f32[17,8,256]{2,1,0:T(8,128)S(1)}, u32[]{:S(2)}, u32[]{:S(2)}) collective-permute-start(f32[17,8,256]{2,1,0:T(8,128)S(1)} %pad_maximum_fusion.8), channel_id=1, source_target_pairs={{0,128},{8,136},{16,144},{24,152},{32,160},{40,168},{48,176},{56,1... | collective-permute-start | bytes 417800 | tf_op jit(solution)/shard_map/ppermute | solution.py:22
  159.2 15.9 %copy-start.7 = (f32[8,256]{1,0:T(8,128)S(1)}, f32[8,256]{1,0:T(8,128)}, u32[]{:S(2)}) copy-start(f32[8,256]{1,0:T(8,128)} %mul.234) | copy-start | bytes 24580

commit v12 on v9

--- a/solution.py
+++ b/solution.py
@@ -141,15 +141,19 @@
     return value
 
 
-def chip_first_sum(value, axis):
+def chip_first_sum(value, axis, attend):
     count = lax.axis_size(axis)
     value = butterfly_sum(value, axis, 1, 2)
     half = value.shape[0] // 2
     core = lax.axis_index(axis) % 2
     mine = jnp.where(core == 0, value[:half], value[half:])
-    mine = butterfly_sum(mine, axis, 2, count)
+    mine = butterfly_sum(mine, axis, 2, 4)
+    mine, attended = attend(mine)
+    mine = butterfly_sum(mine, axis, 4, count)
+    mine, attended = lax.optimization_barrier((mine, attended))
     other = lax.ppermute(mine, axis, [(source, source ^ 1) for source in range(count)])
-    return jnp.where(core == 0, jnp.concatenate([mine, other]), jnp.concatenate([other, mine]))
+    both = jnp.where(core == 0, jnp.concatenate([mine, other]), jnp.concatenate([other, mine]))
+    return both, attended
 
 
 def compose(earlier, later, rate3):
@@ -217,7 +221,13 @@
     rank_part = jnp.dot(activated, proj_dt_weight, preferred_element_type=jnp.float32)
     rank_width = rank_part.shape[1]
     packed = jnp.concatenate([rank_part, state_parts.reshape(-1, rank_width)], axis=0)
-    total = chip_first_sum(packed, "tp")
+    base = (lax.axis_index("seq") * tokens_here).astype(jnp.int32).reshape(1)
+
+    def attend(partial):
+        partial, ready = lax.optimization_barrier((partial, window))
+        return partial, run_attention(q_proj, ready, base)
+
+    total, attn_out = chip_first_sum(packed, "tp", attend)
     rank_low = total[:tokens_here]
     state_in = total[tokens_here:].reshape(state_parts.shape)
     rank_normed = rank_norm(rank_low, dt_gain)
@@ -244,8 +254,6 @@
         .astype(jnp.bfloat16)
         .reshape(tokens_here, channels)
     )
-    base = (lax.axis_index("seq") * tokens_here).astype(jnp.int32).reshape(1)
-    attn_out = run_attention(q_proj, window, base)
     return (mamba_out, attn_out)
 
 

time: 179 us -> 183 us (1.022)
  other arithmetic: 18.2 us -> 20.9 us
  starting transfers between devices: 44 us -> 41.5 us
  matrix products: 2.67 us -> 4.9 us
    ppermute x9, waiting for transfers between devices: 31.6 us -> 54.5 us  [shifted(): lax.ppermute(value, axis, [(source, source + steps) for source in range(f...]
    ppermute x3, waiting for transfers between devices: 21.6 us -> 0.01 us  [butterfly_sum(): value = value + lax.ppermute(value, axis, pairs)]
    ppermute x9, starting transfers between devices: 36.3 us -> 32.4 us  [shifted(): lax.ppermute(value, axis, [(source, source + steps) for source in range(f...]
    unnamed x42 -> x40, local copies, waits for them, and re-layouts: 9.43 us -> 9.28 us
  transfers between devices with their start and end apart: 13 -> 13, of which waited for: 9 -> 8; matrix products, arithmetic and copies ran while one was open for 11% -> 6% of each run, Pallas kernels for 15% -> 7%
where the time goes in v12:
time: 183 us; the launch traced here: 180 us
  waiting for transfers between devices  54.5 us (30%)
  Pallas kernels  41.8 us (23%)
  starting transfers between devices  41.5 us (23%)
  other arithmetic  20.9 us (11%)
  local copies, waits for them, and re-layouts  15.3 us (8%)
  matrix products  4.9 us (3%)
    ppermute x9, waiting for transfers between devices, shifted(): lax.ppermute(value, axis, [(source, source + steps) for source in range(f...  54.5 us
    ppermute x9, starting transfers between devices, shifted(): lax.ppermute(value, axis, [(source, source + steps) for source in range(f...  32.4 us
    pallas_call x2, Pallas kernels, run_scan(): pl.pallas_call(functools.partial(scan_kernel, with_out), grid=(blocks,),...  28.4 us
    pallas_call x1, Pallas kernels, run_attention(): pl.pallas_call(attention_kernel, grid=(heads,), in_specs=[pl.BlockSpec(me...  13.4 us
    unnamed x40, local copies, waits for them, and re-layouts  9.28 us
    ppermute x3, starting transfers between devices, butterfly_sum(): value = value + lax.ppermute(value, axis, pairs)  9.06 us
  transfers between devices with their start and end apart: 13, of which 8 were waited for; matrix products, arithmetic and copies ran while one was open for 6% of the time, Pallas kernels for 7%

profile of v12, /device:TPU:8, one launch (start us, length us, event | category | flops | bytes accessed | tf_op | source)
XLA Modules:
  0.0 179.9 jit_solution(2239125608856350494)
XLA Ops:
  0.7 1.0 constant_dynamic-update-slice_fusion.1
  1.7 0.8 slice.82
  2.5 0.9 constant_dynamic-update-slice_fusion
  3.3 9.1 %collective-permute-start = (bf16[280,256]{1,0:T(8,128)(2,1)S(1)}, bf16[280,256]{1,0:T(8,128)(2,1)S(1)}, u32[]{:S(2)}, u32[]{:S(2)}) collective-permute-start(bf16[280,256]{1,0:T(8,128)(2,1)S(1)} %pad_maximum_fusion.3), channel_id=1, source_target_pairs={{0,8},{8,16},{16,24},{24,32},{32,40},{40,48},{48,56},{56,64},{64,7... | collective-permute-start | bytes 430088 | tf_op jit(solution)/shard_map/ppermute | solution.py:22
  12.5 0.9 fusion.22
  13.4 5.0 %collective-permute-done = bf16[280,256]{1,0:T(8,128)(2,1)S(1)} collective-permute-done((bf16[280,256]{1,0:T(8,128)(2,1)S(1)}, bf16[280,256]{1,0:T(8,128)(2,1)S(1)}, u32[]{:S(2)}, u32[]{:S(2)}) %collective-permute-start) | collective-permute-done | bytes 143392 | tf_op jit(solution)/shard_map/ppermute | solution.py:22
  18.4 1.5 maximum_convert_fusion
  19.9 1.3 multiply_convert_fusion
  21.3 1.5 fusion.23
  22.8 1.0 convolution_bitcast_fusion
  24.6 1.9 %pad_maximum_fusion = f32[272,512]{1,0:T(8,128)} fusion(f32[16,512]{1,0:T(8,128)S(1)} %reshape.53, f32[256,512]{1,0:T(8,128)} %fusion.23), kind=kLoop, calls=%fused_computation.26 | loop fusion | flops 139264 | bytes 1114112 | tf_op jit(solution)/shard_map/concatenate | solution.py:223
  27.3 1.9 %collective-permute-start.4 = (bf16[512,256]{1,0:T(8,128)(2,1)}, bf16[512,256]{1,0:T(8,128)(2,1)}, u32[]{:S(2)}, u32[]{:S(2)}) collective-permute-start(bf16[512,256]{1,0:T(8,128)(2,1)} %pad_maximum_fusion.2), channel_id=1, source_target_pairs={{0,16},{8,24},{16,32},{24,40},{32,48},{40,56},{48,64},{56,72},{64,... | collective-permute-start | bytes 786440 | tf_op jit(solution)/shard_map/ppermute | solution.py:22
  29.2 3.5 %collective-permute-start.3 = (bf16[256,256]{1,0:T(8,128)(2,1)S(1)}, bf16[256,256]{1,0:T(8,128)(2,1)}, u32[]{:S(2)}, u32[]{:S(2)}) collective-permute-start(bf16[256,256]{1,0:T(8,128)(2,1)S(1)} %constant_dynamic-update-slice_fusion), channel_id=1, source_target_pairs={{0,64},{8,72},{16,80},{24,88},{32,96},{40,104},{48,112},{56,120},{... | collective-permute-start | bytes 393224 | tf_op jit(solution)/shard_map/ppermute | solution.py:22
  32.7 7.7 %collective-permute-done.4 = bf16[512,256]{1,0:T(8,128)(2,1)} collective-permute-done((bf16[512,256]{1,0:T(8,128)(2,1)}, bf16[512,256]{1,0:T(8,128)(2,1)}, u32[]{:S(2)}, u32[]{:S(2)}) %collective-permute-start.4) | collective-permute-done | bytes 262176 | tf_op jit(solution)/shard_map/ppermute | solution.py:22
  40.4 1.0 pad_maximum_fusion.1
  41.4 1.9 %collective-permute-start.5 = (bf16[1024,256]{1,0:T(8,128)(2,1)S(1)}, bf16[1024,256]{1,0:T(8,128)(2,1)S(1)}, u32[]{:S(2)}, u32[]{:S(2)}) collective-permute-start(bf16[1024,256]{1,0:T(8,128)(2,1)S(1)} %pad_maximum_fusion.1), channel_id=1, source_target_pairs={{0,32},{8,40},{16,48},{24,56},{32,64},{40,72},{48,80},{56,88},{64,... | collective-permute-start | bytes 1572872 | tf_op jit(solution)/shard_map/ppermute | solution.py:22
  43.3 0.9 constant_dynamic-update-slice_fusion.6
  44.3 1.3 fusion.20
  45.7 3.6 %collective-permute-start.2 = (f32[136,512]{1,0:T(8,128)S(1)}, f32[136,512]{1,0:T(8,128)S(1)}, u32[]{:S(2)}, u32[]{:S(2)}) collective-permute-start(f32[136,512]{1,0:T(8,128)S(1)} %slice_select_fusion), channel_id=1, source_target_pairs={{0,2},{1,3},{2,0},{3,1},{4,6},{5,7},{6,4},{7,5},{8,10},{9,11},{10,... | collective-permute-start | bytes 835592 | tf_op jit(solution)/shard_map/ppermute | solution.py:139
  49.3 9.9 %collective-permute-done.5 = bf16[1024,256]{1,0:T(8,128)(2,1)S(1)} collective-permute-done((bf16[1024,256]{1,0:T(8,128)(2,1)S(1)}, bf16[1024,256]{1,0:T(8,128)(2,1)S(1)}, u32[]{:S(2)}, u32[]{:S(2)}) %collective-permute-start.5) | collective-permute-done | bytes 524320 | tf_op jit(solution)/shard_map/ppermute | solution.py:22
  59.2 1.0 constant_dynamic-update-slice_fusion.4
  60.4 0.9 copy-done.11
  61.3 5.4 %collective-permute-start.6 = (f32[136,512]{1,0:T(8,128)S(1)}, f32[136,512]{1,0:T(8,128)}, u32[]{:S(2)}, u32[]{:S(2)}) collective-permute-start(f32[136,512]{1,0:T(8,128)S(1)} %fusion.28), channel_id=1, source_target_pairs={{0,4},{1,5},{2,6},{3,7},{4,0},{5,1},{6,2},{7,3},{8,12},{9,13},{10,... | collective-permute-start | bytes 835592 | tf_op jit(solution)/shard_map/ppermute | solution.py:139
  66.8 13.4 %shard_map.149 = bf16[256,1024]{1,0:T(8,128)(2,1)} custom-call(s32[1]{0:T(128)} %bitcast.5.base_ref, bf16[256,1024]{1,0:T(8,128)(2,1)} %q_ref.1, bf16[2304,256]{1,0:T(8,128)(2,1)} %copy-done.11, bf16[2304,256]{1,0:T(8,128)(2,1)} %copy-done.11), custom_call_target="tpu_custom_call" | custom-call | flops 2415919104 | bytes 3407872 | tf_op jit(solution)/shard_map/pallas_call | solution.py:115
  80.2 1.7 add.136
  81.9 1.3 add.139
  83.9 1.6 copy.19
  85.4 1.1 maximum_select_fusion
  87.3 2.4 %fusion.5 = f32[256,8,256]{2,0,1:T(8,128)S(1)} fusion(bf16[64,8,8,256]{3,2,1,0:T(8,128)(2,1)} %bitcast.72, f32[272,512]{1,0:T(8,128)S(1)} %maximum_select_fusion, f32[512]{0:T(512)S(1)} %copy-done.14, f32[256]{0:T(256)S(1)} %add_rsqrt_fusion), kind=kOutput, calls=%fused_computation.10 | convolution fusion | flops 537264128 | bytes 4721664 | tf_op jit(solution)/shard_map/tr,rsl->tsl/dot_general | solution.py:242
  89.7 1.9 %fusion.21 = (f32[8,256]{1,0:T(8,128)S(1)}, f32[256,8,256]{2,1,0:T(8,128)S(1)}) fusion(f32[8,256]{1,0:T(8,128)S(1)} %copy-done.10, f32[256,8,256]{2,0,1:T(8,128)S(1)} %fusion.5), kind=kLoop, calls=%fused_computation.68 | loop fusion | flops 4192256 | bytes 4210688 | tf_op jit(solution)/shard_map/reduce_sum | solution.py:249
  91.6 1.8 %bitcast_multiply_fusion.2.dr_ref = f32[256,8,256]{2,1,0:T(8,128)} fusion(f32[256,8,256]{2,1,0:T(8,128)S(1)} %get-tuple-element.11.dt_ref, f32[32,8,8,256]{3,2,1,0:T(8,128)S(1)} %copy-done.1), kind=kLoop, calls=%fused_computation.8 | loop fusion | flops 524288 | bytes 6291456 | tf_op jit(solution)/shard_map/mul | solution.py:245
  94.3 12.5 %shard_map.150 = f32[16,8,256]{2,1,0:T(8,128)} custom-call(f32[32,256]{1,0:T(8,128)} %reshape.55.bc_ref, f32[256,8,256]{2,1,0:T(8,128)} %copy-done.2, f32[256,8,256]{2,1,0:T(8,128)} %bitcast_multiply_fusion.2.dr_ref, f32[16,8,256]{2,1,0:T(8,128)} %bitcast.69, f32[16,8,256]{2,1,0:T(8,128)} %broadcast_in_dim.5.h0_ref), custom_call_target="tpu_custom_call" | custom-call | flops 33554432 | bytes 6553600 | tf_op jit(solution)/shard_map/pallas_call | solution.py:71
  106.8 1.0 pad_maximum_fusion.4
  107.8 4.3 %collective-permute-start.8 = (f32[17,8,256]{2,1,0:T(8,128)S(1)}, f32[17,8,256]{2,1,0:T(8,128)S(1)}, u32[]{:S(2)}, u32[]{:S(2)}) collective-permute-start(f32[17,8,256]{2,1,0:T(8,128)S(1)} %pad_maximum_fusion.4), channel_id=1, source_target_pairs={{0,8},{8,16},{16,24},{24,32},{32,40},{40,48},{48,56},{56,64},{64,7... | collective-permute-start | bytes 417800 | tf_op jit(solution)/shard_map/ppermute | solution.py:22
  112.1 12.8 %collective-permute-done.8 = f32[17,8,256]{2,1,0:T(8,128)S(1)} collective-permute-done((f32[17,8,256]{2,1,0:T(8,128)S(1)}, f32[17,8,256]{2,1,0:T(8,128)S(1)}, u32[]{:S(2)}, u32[]{:S(2)}) %collective-permute-start.8) | collective-permute-done | bytes 139296 | tf_op jit(solution)/shard_map/ppermute | solution.py:22
  124.9 0.9 multiply_add_fusion.3
  125.9 1.9 %collective-permute-start.9 = (f32[17,8,256]{2,1,0:T(8,128)S(1)}, f32[17,8,256]{2,1,0:T(8,128)S(1)}, u32[]{:S(2)}, u32[]{:S(2)}) collective-permute-start(f32[17,8,256]{2,1,0:T(8,128)S(1)} %pad_maximum_fusion.5), channel_id=1, source_target_pairs={{0,16},{8,24},{16,32},{24,40},{32,48},{40,56},{48,64},{56,72},{64,... | collective-permute-start | bytes 417800 | tf_op jit(solution)/shard_map/ppermute | solution.py:22
  127.8 7.3 %collective-permute-done.9 = f32[17,8,256]{2,1,0:T(8,128)S(1)} collective-permute-done((f32[17,8,256]{2,1,0:T(8,128)S(1)}, f32[17,8,256]{2,1,0:T(8,128)S(1)}, u32[]{:S(2)}, u32[]{:S(2)}) %collective-permute-start.9) | collective-permute-done | bytes 139296 | tf_op jit(solution)/shard_map/ppermute | solution.py:22
  135.2 1.9 %collective-permute-start.10 = (f32[17,8,256]{2,1,0:T(8,128)S(1)}, f32[17,8,256]{2,1,0:T(8,128)S(1)}, u32[]{:S(2)}, u32[]{:S(2)}) collective-permute-start(f32[17,8,256]{2,1,0:T(8,128)S(1)} %pad_maximum_fusion.6), channel_id=1, source_target_pairs={{0,32},{8,40},{16,48},{24,56},{32,64},{40,72},{48,80},{56,88},{64,... | collective-permute-start | bytes 417800 | tf_op jit(solution)/shard_map/ppermute | solution.py:22
  137.1 7.4 %collective-permute-done.10 = f32[17,8,256]{2,1,0:T(8,128)S(1)} collective-permute-done((f32[17,8,256]{2,1,0:T(8,128)S(1)}, f32[17,8,256]{2,1,0:T(8,128)S(1)}, u32[]{:S(2)}, u32[]{:S(2)}) %collective-permute-start.10) | collective-permute-done | bytes 139296 | tf_op jit(solution)/shard_map/ppermute | solution.py:22
  144.6 3.5 %collective-permute-start.11 = (f32[17,8,256]{2,1,0:T(8,128)S(1)}, f32[17,8,256]{2,1,0:T(8,128)S(1)}, u32[]{:S(2)}, u32[]{:S(2)}) collective-permute-start(f32[17,8,256]{2,1,0:T(8,128)S(1)} %pad_maximum_fusion.7), channel_id=1, source_target_pairs={{0,64},{8,72},{16,80},{24,88},{32,96},{40,104},{48,112},{56,120},{... | collective-permute-start | bytes 417800 | tf_op jit(solution)/shard_map/ppermute | solution.py:22
  148.1 3.5 %collective-permute-done.11 = f32[17,8,256]{2,1,0:T(8,128)S(1)} collective-permute-done((f32[17,8,256]{2,1,0:T(8,128)S(1)}, f32[17,8,256]{2,1,0:T(8,128)S(1)}, u32[]{:S(2)}, u32[]{:S(2)}) %collective-permute-start.11) | collective-permute-done | bytes 139296 | tf_op jit(solution)/shard_map/ppermute | solution.py:22
  151.6 4.4 %collective-permute-start.12 = (f32[17,8,256]{2,1,0:T(8,128)S(1)}, f32[17,8,256]{2,1,0:T(8,128)S(1)}, u32[]{:S(2)}, u32[]{:S(2)}) collective-permute-start(f32[17,8,256]{2,1,0:T(8,128)S(1)} %pad_maximum_fusion.8), channel_id=1, source_target_pairs={{0,128},{8,136},{16,144},{24,152},{32,160},{40,168},{48,176},{56,1... | collective-permute-start | bytes 417800 | tf_op jit(solution)/shard_map/ppermute | solution.py:22
  156.0 1.6 copy.21
  157.7 0.9 collective-permute-done.12
  159.4 15.8 %shard_map.151 = f32[256,8,256]{2,1,0:T(8,128)} custom-call(f32[32,256]{1,0:T(8,128)} %reshape.55.bc_ref, f32[256,8,256]{2,1,0:T(8,128)} %copy-done.2, f32[256,8,256]{2,1,0:T(8,128)} %bitcast_multiply_fusion.2.dr_ref, f32[16,8,256]{2,1,0:T(8,128)} %bitcast.70, f32[16,8,256]{2,1,0:T(8,128)} %fusion.17.h0_ref), custom_call_target="tpu_custom_call" | custom-call | flops 50331648 | bytes 6553600 | tf_op jit(solution)/shard_map/pallas_call | solution.py:71
  175.2 3.4 %fusion.12 = bf16[256,8,256]{2,1,0:T(8,128)(2,1)S(1)} fusion(f32[32,8,8,256]{3,2,1,0:T(8,128)} %copy.21, f32[256,8,256]{2,1,0:T(8,128)} %shard_map.151, f32[32,8,8,256]{3,2,1,0:T(8,128)} %copy.19, f32[8,256]{1,0:T(8,128)S(1)} %mul.239), kind=kLoop, calls=%fused_computation.23 | loop fusion | flops 4194304 | bytes 7348224 | tf_op jit(solution)/shard_map/convert_element_type | solution.py:254
  178.6 1.3 copy.22
  (68 shorter events, 5.0 us)
Async XLA Ops:
  0.6 20.7 %copy-start = (bf16[2048,512]{1,0:T(8,128)(2,1)S(1)}, bf16[2048,512]{1,0:T(8,128)(2,1)}, u32[]{:S(2)}) copy-start(bf16[2048,512]{1,0:T(8,128)(2,1)} %param.21) | copy-start | bytes 6291460
  0.6 19.3 %copy-start.13 = (f32[2048]{0:T(1024)S(1)}, f32[2048]{0:T(1024)}, u32[]{:S(2)}) copy-start(f32[2048]{0:T(1024)} %param.20) | copy-start | bytes 24580
  3.3 15.0 %collective-permute-start = (bf16[280,256]{1,0:T(8,128)(2,1)S(1)}, bf16[280,256]{1,0:T(8,128)(2,1)S(1)}, u32[]{:S(2)}, u32[]{:S(2)}) collective-permute-start(bf16[280,256]{1,0:T(8,128)(2,1)S(1)} %pad_maximum_fusion.3), channel_id=1, source_target_pairs={{0,8},{8,16},{16,24},{24,32},{32,40},{40,48},{48,56},{56,64},{64,7... | collective-permute-start | bytes 430088 | tf_op jit(solution)/shard_map/ppermute | solution.py:22
  21.3 1.5 copy-start.8
  24.6 1.9 %copy-start.5 = (f32[16,512]{1,0:T(8,128)}, f32[16,512]{1,0:T(8,128)S(1)}, u32[]{:S(2)}) copy-start(f32[16,512]{1,0:T(8,128)S(1)} %reshape.53) | copy-start | bytes 98308
  26.5 17.7 %collective-permute-start.1 = (f32[272,512]{1,0:T(8,128)}, f32[272,512]{1,0:T(8,128)}, u32[]{:S(2)}, u32[]{:S(2)}) collective-permute-start(f32[272,512]{1,0:T(8,128)} %pad_maximum_fusion), channel_id=1, source_target_pairs={{0,1},{1,0},{2,3},{3,2},{4,5},{5,4},{6,7},{7,6},{8,9},{9,8},{10,11... | collective-permute-start | bytes 1671176 | tf_op jit(solution)/shard_map/ppermute | solution.py:139
  27.3 13.1 %collective-permute-start.4 = (bf16[512,256]{1,0:T(8,128)(2,1)}, bf16[512,256]{1,0:T(8,128)(2,1)}, u32[]{:S(2)}, u32[]{:S(2)}) collective-permute-start(bf16[512,256]{1,0:T(8,128)(2,1)} %pad_maximum_fusion.2), channel_id=1, source_target_pairs={{0,16},{8,24},{16,32},{24,40},{32,48},{40,56},{48,64},{56,72},{64,... | collective-permute-start | bytes 786440 | tf_op jit(solution)/shard_map/ppermute | solution.py:22
  29.2 14.1 %collective-permute-start.3 = (bf16[256,256]{1,0:T(8,128)(2,1)S(1)}, bf16[256,256]{1,0:T(8,128)(2,1)}, u32[]{:S(2)}, u32[]{:S(2)}) collective-permute-start(bf16[256,256]{1,0:T(8,128)(2,1)S(1)} %constant_dynamic-update-slice_fusion), channel_id=1, source_target_pairs={{0,64},{8,72},{16,80},{24,88},{32,96},{40,104},{48,112},{56,120},{... | collective-permute-start | bytes 393224 | tf_op jit(solution)/shard_map/ppermute | solution.py:22
  41.4 17.8 %collective-permute-start.5 = (bf16[1024,256]{1,0:T(8,128)(2,1)S(1)}, bf16[1024,256]{1,0:T(8,128)(2,1)S(1)}, u32[]{:S(2)}, u32[]{:S(2)}) collective-permute-start(bf16[1024,256]{1,0:T(8,128)(2,1)S(1)} %pad_maximum_fusion.1), channel_id=1, source_target_pairs={{0,32},{8,40},{16,48},{24,56},{32,64},{40,72},{48,80},{56,88},{64,... | collective-permute-start | bytes 1572872 | tf_op jit(solution)/shard_map/ppermute | solution.py:22
  44.2 16.0 %copy-start.6 = (bf16[256,128]{1,0:T(8,128)(2,1)S(1)}, bf16[256,128]{1,0:T(8,128)(2,1)}, u32[]{:S(2)}) copy-start(bf16[256,128]{1,0:T(8,128)(2,1)} %param.17) | copy-start | bytes 196612
  44.3 16.0 %copy-start.7 = (bf16[256,128]{1,0:T(8,128)(2,1)S(1)}, bf16[256,128]{1,0:T(8,128)(2,1)}, u32[]{:S(2)}) copy-start(bf16[256,128]{1,0:T(8,128)(2,1)} %param.18) | copy-start | bytes 196612
  45.7 14.6 %collective-permute-start.2 = (f32[136,512]{1,0:T(8,128)S(1)}, f32[136,512]{1,0:T(8,128)S(1)}, u32[]{:S(2)}, u32[]{:S(2)}) collective-permute-start(f32[136,512]{1,0:T(8,128)S(1)} %slice_select_fusion), channel_id=1, source_target_pairs={{0,2},{1,3},{2,0},{3,1},{4,6},{5,7},{6,4},{7,5},{8,10},{9,11},{10,... | collective-permute-start | bytes 835592 | tf_op jit(solution)/shard_map/ppermute | solution.py:139
  60.3 1.0 copy-start.11
  61.3 18.9 %collective-permute-start.6 = (f32[136,512]{1,0:T(8,128)S(1)}, f32[136,512]{1,0:T(8,128)}, u32[]{:S(2)}, u32[]{:S(2)}) collective-permute-start(f32[136,512]{1,0:T(8,128)S(1)} %fusion.28), channel_id=1, source_target_pairs={{0,4},{1,5},{2,6},{3,7},{4,0},{5,1},{6,2},{7,3},{8,12},{9,13},{10,... | collective-permute-start | bytes 835592 | tf_op jit(solution)/shard_map/ppermute | solution.py:139
  66.8 16.4 %copy-start.9 = (f32[16,2048]{1,0:T(8,128)S(1)}, f32[16,2048]{1,0:T(8,128)}, u32[]{:S(2)}) copy-start(f32[16,2048]{1,0:T(8,128)} %param.26) | copy-start | bytes 393220
  81.9 3.5 %collective-permute-start.7 = (f32[136,512]{1,0:T(8,128)}, f32[136,512]{1,0:T(8,128)S(1)}, u32[]{:S(2)}, u32[]{:S(2)}) collective-permute-start(f32[136,512]{1,0:T(8,128)} %add.136), channel_id=1, source_target_pairs={{0,1},{1,0},{2,3},{3,2},{4,5},{5,4},{6,7},{7,6},{8,9},{9,8},{10,11... | collective-permute-start | bytes 835592 | tf_op jit(solution)/shard_map/ppermute | solution.py:154
  83.9 3.4 %copy-start.14 = (f32[512]{0:T(512)S(1)}, f32[512]{0:T(512)}, u32[]{:S(2)}) copy-start(f32[512]{0:T(512)} %param.23) | copy-start | bytes 6148
  87.3 2.4 %copy-start.10 = (f32[8,256]{1,0:T(8,128)S(1)}, f32[8,256]{1,0:T(8,128)}, u32[]{:S(2)}) copy-start(f32[8,256]{1,0:T(8,128)} %add.139) | copy-start | bytes 24580
  89.7 1.9 %copy-start.1 = (f32[32,8,8,256]{3,2,1,0:T(8,128)S(1)}, f32[32,8,8,256]{3,2,1,0:T(8,128)}, u32[]{:S(2)}) copy-start(f32[32,8,8,256]{3,2,1,0:T(8,128)} %copy.19) | copy-start | bytes 6291460
  91.6 2.0 %copy-start.2 = (f32[256,8,256]{2,1,0:T(8,128)}, f32[256,8,256]{2,1,0:T(8,128)S(1)}, u32[]{:S(2)}) copy-start(f32[256,8,256]{2,1,0:T(8,128)S(1)} %get-tuple-element.11.dt_ref) | copy-start | bytes 6291460
  94.3 30.6 %copy-start.3 = (f32[2,8,8,256]{3,2,1,0:T(8,128)S(1)}, f32[2,8,8,256]{3,2,1,0:T(8,128)}, u32[]{:S(2)}) copy-start(f32[2,8,8,256]{3,2,1,0:T(8,128)} %copy.20) | copy-start | bytes 393220
  106.8 49.2 %copy-start.4 = (bf16[256,2048]{1,0:T(8,128)(2,1)S(1)}, bf16[256,2048]{1,0:T(8,128)(2,1)}, u32[]{:S(2)}) copy-start(bf16[256,2048]{1,0:T(8,128)(2,1)} %param.15) | copy-start | bytes 3145732
  107.8 17.1 %collective-permute-start.8 = (f32[17,8,256]{2,1,0:T(8,128)S(1)}, f32[17,8,256]{2,1,0:T(8,128)S(1)}, u32[]{:S(2)}, u32[]{:S(2)}) collective-permute-start(f32[17,8,256]{2,1,0:T(8,128)S(1)} %pad_maximum_fusion.4), channel_id=1, source_target_pairs={{0,8},{8,16},{16,24},{24,32},{32,40},{40,48},{48,56},{56,64},{64,7... | collective-permute-start | bytes 417800 | tf_op jit(solution)/shard_map/ppermute | solution.py:22
  125.9 9.3 %collective-permute-start.9 = (f32[17,8,256]{2,1,0:T(8,128)S(1)}, f32[17,8,256]{2,1,0:T(8,128)S(1)}, u32[]{:S(2)}, u32[]{:S(2)}) collective-permute-start(f32[17,8,256]{2,1,0:T(8,128)S(1)} %pad_maximum_fusion.5), channel_id=1, source_target_pairs={{0,16},{8,24},{16,32},{24,40},{32,48},{40,56},{48,64},{56,72},{64,... | collective-permute-start | bytes 417800 | tf_op jit(solution)/shard_map/ppermute | solution.py:22
  135.2 9.4 %collective-permute-start.10 = (f32[17,8,256]{2,1,0:T(8,128)S(1)}, f32[17,8,256]{2,1,0:T(8,128)S(1)}, u32[]{:S(2)}, u32[]{:S(2)}) collective-permute-start(f32[17,8,256]{2,1,0:T(8,128)S(1)} %pad_maximum_fusion.6), channel_id=1, source_target_pairs={{0,32},{8,40},{16,48},{24,56},{32,64},{40,72},{48,80},{56,88},{64,... | collective-permute-start | bytes 417800 | tf_op jit(solution)/shard_map/ppermute | solution.py:22
  144.6 13.1 %copy-start.12 = (f32[2048]{0:T(1024)S(1)}, f32[2048]{0:T(1024)}, u32[]{:S(2)}) copy-start(f32[2048]{0:T(1024)} %param.27) | copy-start | bytes 24580
  144.6 6.9 %collective-permute-start.11 = (f32[17,8,256]{2,1,0:T(8,128)S(1)}, f32[17,8,256]{2,1,0:T(8,128)S(1)}, u32[]{:S(2)}, u32[]{:S(2)}) collective-permute-start(f32[17,8,256]{2,1,0:T(8,128)S(1)} %pad_maximum_fusion.7), channel_id=1, source_target_pairs={{0,64},{8,72},{16,80},{24,88},{32,96},{40,104},{48,112},{56,120},{... | collective-permute-start | bytes 417800 | tf_op jit(solution)/shard_map/ppermute | solution.py:22
  151.6 7.0 %collective-permute-start.12 = (f32[17,8,256]{2,1,0:T(8,128)S(1)}, f32[17,8,256]{2,1,0:T(8,128)S(1)}, u32[]{:S(2)}, u32[]{:S(2)}) collective-permute-start(f32[17,8,256]{2,1,0:T(8,128)S(1)} %pad_maximum_fusion.8), channel_id=1, source_target_pairs={{0,128},{8,136},{16,144},{24,152},{32,160},{40,168},{48,176},{56,1... | collective-permute-start | bytes 417800 | tf_op jit(solution)/shard_map/ppermute | solution.py:22

commit v13 on v9

--- a/solution.py
+++ b/solution.py
@@ -12,7 +12,7 @@
 HD = 128
 WINDOW = 2048
 SUBLANES = 8
-LANE_BLOCK = 128
+LANE_BLOCK = 256
 epsilon = 1e-06
 
 
@@ -37,7 +37,6 @@
 def scan_kernel(with_out, bc_ref, dt_ref, dr_ref, rate_ref, h0_ref, out_ref):
     states = rate_ref.shape[0]
     tokens = dt_ref.shape[0]
-    neg_rate = [-rate_ref[n] for n in range(states)]
 
     def body(t, hs):
         dt = dt_ref[t]
@@ -45,7 +44,7 @@
         new = []
         acc = None
         for n in range(states):
-            h = jnp.exp(neg_rate[n] * dt) * hs[n] + bc_ref[n, t] * dr
+            h = jnp.exp(rate_ref[n] * dt) * hs[n] + bc_ref[n, t] * dr
             new.append(h)
             if with_out:
                 term = bc_ref[states + n, t] * h
@@ -234,11 +233,12 @@
     )
     dr3 = dt3 * act3
     rate3 = cube(decay_rate)
+    neg_rate3 = -rate3
     zero_state = jnp.zeros((state_count, SUBLANES, lanes), jnp.float32)
-    local_final = run_scan(state_in, dt3, dr3, rate3, zero_state, False)
+    local_final = run_scan(state_in, dt3, dr3, neg_rate3, zero_state, False)
     step_sum = jnp.sum(dt3, axis=0)
     entering = entering_state(step_sum, local_final, rate3)
-    mamba_sum = run_scan(state_in, dt3, dr3, rate3, entering, True)
+    mamba_sum = run_scan(state_in, dt3, dr3, neg_rate3, entering, True)
     mamba_out = (
         ((mamba_sum + cube(skip_weight)[None] * act3) * jax.nn.silu(cube(gate_in).astype(jnp.float32)))
         .astype(jnp.bfloat16)

time: 179 us -> 178 us (level)
  transfers between devices with their start and end apart: 13 -> 13, of which waited for: 9 -> 9; matrix products, arithmetic and copies ran while one was open for 11% -> 11% of each run, Pallas kernels for 15% -> 14%
where the time goes in v13:
time: 178 us; the launch traced here: 176 us
  waiting for transfers between devices  53.3 us (30%)
  starting transfers between devices  44 us (25%)
  Pallas kernels  41.1 us (23%)
  other arithmetic  19.2 us (11%)
  local copies, waits for them, and re-layouts  15.1 us (8%)
  matrix products  2.67 us (2%)
    ppermute x9, starting transfers between devices, shifted(): lax.ppermute(value, axis, [(source, source + steps) for source in range(f...  36.3 us
    ppermute x9, waiting for transfers between devices, shifted(): lax.ppermute(value, axis, [(source, source + steps) for source in range(f...  31.6 us
    pallas_call x2, Pallas kernels, run_scan(): pl.pallas_call(functools.partial(scan_kernel, with_out), grid=(blocks,),...  27.7 us
    ppermute x3, waiting for transfers between devices, butterfly_sum(): value = value + lax.ppermute(value, axis, pairs)  21.6 us
    pallas_call x1, Pallas kernels, run_attention(): pl.pallas_call(attention_kernel, grid=(heads,), in_specs=[pl.BlockSpec(me...  13.4 us
    unnamed x42, local copies, waits for them, and re-layouts  8.53 us
    ppermute x3, starting transfers between devices, butterfly_sum(): value = value + lax.ppermute(value, axis, pairs)  7.61 us
  transfers between devices with their start and end apart: 13, of which 9 were waited for; matrix products, arithmetic and copies ran while one was open for 11% of the time, Pallas kernels for 14%

profile of v13, /device:TPU:8, one launch (start us, length us, event | category | flops | bytes accessed | tf_op | source)
XLA Modules:
  0.0 176.3 jit_solution(7154814644389093324)
XLA Ops:
  0.7 1.0 constant_dynamic-update-slice_fusion.1
  1.7 0.8 slice.82
  2.5 0.9 constant_dynamic-update-slice_fusion
  3.3 9.1 %collective-permute-start = (bf16[280,256]{1,0:T(8,128)(2,1)S(1)}, bf16[280,256]{1,0:T(8,128)(2,1)S(1)}, u32[]{:S(2)}, u32[]{:S(2)}) collective-permute-start(bf16[280,256]{1,0:T(8,128)(2,1)S(1)} %pad_maximum_fusion.3), channel_id=1, source_target_pairs={{0,8},{8,16},{16,24},{24,32},{32,40},{40,48},{48,56},{56,64},{64,7... | collective-permute-start | bytes 430088 | tf_op jit(solution)/shard_map/ppermute | solution.py:22
  12.5 0.9 fusion.22
  13.4 5.0 %collective-permute-done = bf16[280,256]{1,0:T(8,128)(2,1)S(1)} collective-permute-done((bf16[280,256]{1,0:T(8,128)(2,1)S(1)}, bf16[280,256]{1,0:T(8,128)(2,1)S(1)}, u32[]{:S(2)}, u32[]{:S(2)}) %collective-permute-start) | collective-permute-done | bytes 143392 | tf_op jit(solution)/shard_map/ppermute | solution.py:22
  19.1 1.5 maximum_convert_fusion
  20.6 1.3 multiply_convert_fusion
  22.0 1.5 fusion.23
  23.9 1.9 %pad_maximum_fusion = f32[272,512]{1,0:T(8,128)} fusion(f32[16,512]{1,0:T(8,128)S(1)} %reshape.52, f32[256,512]{1,0:T(8,128)} %fusion.23), kind=kLoop, calls=%fused_computation.26 | loop fusion | flops 139264 | bytes 1114112 | tf_op jit(solution)/shard_map/concatenate | solution.py:218
  25.8 2.3 %collective-permute-done.1 = f32[272,512]{1,0:T(8,128)} collective-permute-done((f32[272,512]{1,0:T(8,128)}, f32[272,512]{1,0:T(8,128)}, u32[]{:S(2)}, u32[]{:S(2)}) %collective-permute-start.1) | collective-permute-done | bytes 557088 | tf_op jit(solution)/shard_map/ppermute | solution.py:138
  28.1 1.3 fusion.20
  29.4 3.6 %collective-permute-start.2 = (f32[136,512]{1,0:T(8,128)S(1)}, f32[136,512]{1,0:T(8,128)S(1)}, u32[]{:S(2)}, u32[]{:S(2)}) collective-permute-start(f32[136,512]{1,0:T(8,128)S(1)} %slice_select_fusion), channel_id=1, source_target_pairs={{0,2},{1,3},{2,0},{3,1},{4,6},{5,7},{6,4},{7,5},{8,10},{9,11},{10,... | collective-permute-start | bytes 835592 | tf_op jit(solution)/shard_map/ppermute | solution.py:138
  33.1 7.0 %collective-permute-done.2 = f32[136,512]{1,0:T(8,128)S(1)} collective-permute-done((f32[136,512]{1,0:T(8,128)S(1)}, f32[136,512]{1,0:T(8,128)S(1)}, u32[]{:S(2)}, u32[]{:S(2)}) %collective-permute-start.2) | collective-permute-done | bytes 278560 | tf_op jit(solution)/shard_map/ppermute | solution.py:138
  40.1 4.0 %collective-permute-start.3 = (f32[136,512]{1,0:T(8,128)S(1)}, f32[136,512]{1,0:T(8,128)S(1)}, u32[]{:S(2)}, u32[]{:S(2)}) collective-permute-start(f32[136,512]{1,0:T(8,128)S(1)} %fusion.28), channel_id=1, source_target_pairs={{0,4},{1,5},{2,6},{3,7},{4,0},{5,1},{6,2},{7,3},{8,12},{9,13},{10,... | collective-permute-start | bytes 835592 | tf_op jit(solution)/shard_map/ppermute | solution.py:138
  44.1 12.4 %collective-permute-done.3 = f32[136,512]{1,0:T(8,128)S(1)} collective-permute-done((f32[136,512]{1,0:T(8,128)S(1)}, f32[136,512]{1,0:T(8,128)S(1)}, u32[]{:S(2)}, u32[]{:S(2)}) %collective-permute-start.3) | collective-permute-done | bytes 278560 | tf_op jit(solution)/shard_map/ppermute | solution.py:138
  56.6 3.5 %collective-permute-start.10 = (bf16[256,256]{1,0:T(8,128)(2,1)S(1)}, bf16[256,256]{1,0:T(8,128)(2,1)}, u32[]{:S(2)}, u32[]{:S(2)}) collective-permute-start(bf16[256,256]{1,0:T(8,128)(2,1)S(1)} %constant_dynamic-update-slice_fusion), channel_id=1, source_target_pairs={{0,64},{8,72},{16,80},{24,88},{32,96},{40,104},{48,112},{56,120},{... | collective-permute-start | bytes 393224 | tf_op jit(solution)/shard_map/ppermute | solution.py:22
  60.1 1.3 add.139
  61.4 0.9 neg.27
  62.3 0.7 copy.20
  63.0 2.8 %copy.21 = f32[32,8,8,256]{3,2,1,0:T(8,128)} copy(bf16[32,8,8,256]{3,1,2,0:T(8,128)(2,1)} %bitcast.73) | data formatting | bytes 3145728
  65.8 1.3 mul.238
  68.0 0.8 pad_maximum_fusion.2
  68.8 1.9 %collective-permute-start.11 = (bf16[512,256]{1,0:T(8,128)(2,1)}, bf16[512,256]{1,0:T(8,128)(2,1)S(1)}, u32[]{:S(2)}, u32[]{:S(2)}) collective-permute-start(bf16[512,256]{1,0:T(8,128)(2,1)} %pad_maximum_fusion.2), channel_id=1, source_target_pairs={{0,16},{8,24},{16,32},{24,40},{32,48},{40,56},{48,64},{56,72},{64,... | collective-permute-start | bytes 786440 | tf_op jit(solution)/shard_map/ppermute | solution.py:22
  70.7 1.1 maximum_select_fusion
  72.0 0.8 fusion.5
  72.8 1.9 %fusion.21 = (f32[8,256]{1,0:T(8,128)S(1)}, f32[256,8,256]{2,1,0:T(8,128)S(1)}) fusion(f32[8,256]{1,0:T(8,128)S(1)} %copy-done.11, f32[256,8,256]{2,0,1:T(8,128)S(1)} %fusion.5), kind=kLoop, calls=%fused_computation.68 | loop fusion | flops 4192256 | bytes 4210688 | tf_op jit(solution)/shard_map/reduce_sum | solution.py:239
  74.7 1.8 %bitcast_multiply_fusion.2.dr_ref = f32[256,8,256]{2,1,0:T(8,128)} fusion(f32[256,8,256]{2,1,0:T(8,128)S(1)} %get-tuple-element.3.dt_ref, f32[32,8,8,256]{3,2,1,0:T(8,128)S(1)} %copy.19), kind=kLoop, calls=%fused_computation.8 | loop fusion | flops 524288 | bytes 6291456 | tf_op jit(solution)/shard_map/mul | solution.py:234
  78.0 11.2 %shard_map.149 = f32[16,8,256]{2,1,0:T(8,128)} custom-call(f32[32,256]{1,0:T(8,128)} %reshape.53.bc_ref, f32[256,8,256]{2,1,0:T(8,128)} %copy-done.2, f32[256,8,256]{2,1,0:T(8,128)} %bitcast_multiply_fusion.2.dr_ref, f32[16,8,256]{2,1,0:T(8,128)} %bitcast.69, f32[16,8,256]{2,1,0:T(8,128)} %broadcast_in_dim.5.h0_ref), custom_call_target="tpu_custom_call" | custom-call | flops 33554432 | bytes 6553600 | tf_op jit(solution)/shard_map/pallas_call | solution.py:70
  89.2 0.9 pad_maximum_fusion.4
  90.1 6.4 %collective-permute-start.5 = (f32[17,8,256]{2,1,0:T(8,128)S(1)}, f32[17,8,256]{2,1,0:T(8,128)S(1)}, u32[]{:S(2)}, u32[]{:S(2)}) collective-permute-start(f32[17,8,256]{2,1,0:T(8,128)S(1)} %pad_maximum_fusion.4), channel_id=1, source_target_pairs={{0,8},{8,16},{16,24},{24,32},{32,40},{40,48},{48,56},{56,64},{64,7... | collective-permute-start | bytes 417800 | tf_op jit(solution)/shard_map/ppermute | solution.py:22
  96.5 0.9 constant_dynamic-update-slice_fusion.6
  97.4 4.8 %collective-permute-start.12 = (bf16[1024,256]{1,0:T(8,128)(2,1)S(1)}, bf16[1024,256]{1,0:T(8,128)(2,1)S(1)}, u32[]{:S(2)}, u32[]{:S(2)}) collective-permute-start(bf16[1024,256]{1,0:T(8,128)(2,1)S(1)} %pad_maximum_fusion.1), channel_id=1, source_target_pairs={{0,32},{8,40},{16,48},{24,56},{32,64},{40,72},{48,80},{56,88},{64,... | collective-permute-start | bytes 1572872 | tf_op jit(solution)/shard_map/ppermute | solution.py:22
  102.3 6.0 %collective-permute-done.5 = f32[17,8,256]{2,1,0:T(8,128)S(1)} collective-permute-done((f32[17,8,256]{2,1,0:T(8,128)S(1)}, f32[17,8,256]{2,1,0:T(8,128)S(1)}, u32[]{:S(2)}, u32[]{:S(2)}) %collective-permute-start.5) | collective-permute-done | bytes 139296 | tf_op jit(solution)/shard_map/ppermute | solution.py:22
  108.3 1.0 multiply_add_fusion.3
  109.3 1.9 %collective-permute-start.6 = (f32[17,8,256]{2,1,0:T(8,128)S(1)}, f32[17,8,256]{2,1,0:T(8,128)S(1)}, u32[]{:S(2)}, u32[]{:S(2)}) collective-permute-start(f32[17,8,256]{2,1,0:T(8,128)S(1)} %pad_maximum_fusion.5), channel_id=1, source_target_pairs={{0,16},{8,24},{16,32},{24,40},{32,48},{40,56},{48,64},{56,72},{64,... | collective-permute-start | bytes 417800 | tf_op jit(solution)/shard_map/ppermute | solution.py:22
  111.2 8.3 %collective-permute-done.12 = bf16[1024,256]{1,0:T(8,128)(2,1)S(1)} collective-permute-done((bf16[1024,256]{1,0:T(8,128)(2,1)S(1)}, bf16[1024,256]{1,0:T(8,128)(2,1)S(1)}, u32[]{:S(2)}, u32[]{:S(2)}) %collective-permute-start.12) | collective-permute-done | bytes 524320 | tf_op jit(solution)/shard_map/ppermute | solution.py:22
  119.5 1.6 collective-permute-done.6
  121.1 2.7 %collective-permute-start.7 = (f32[17,8,256]{2,1,0:T(8,128)S(1)}, f32[17,8,256]{2,1,0:T(8,128)S(1)}, u32[]{:S(2)}, u32[]{:S(2)}) collective-permute-start(f32[17,8,256]{2,1,0:T(8,128)S(1)} %pad_maximum_fusion.6), channel_id=1, source_target_pairs={{0,32},{8,40},{16,48},{24,56},{32,64},{40,72},{48,80},{56,88},{64,... | collective-permute-start | bytes 417800 | tf_op jit(solution)/shard_map/ppermute | solution.py:22
  123.9 7.2 %collective-permute-done.7 = f32[17,8,256]{2,1,0:T(8,128)S(1)} collective-permute-done((f32[17,8,256]{2,1,0:T(8,128)S(1)}, f32[17,8,256]{2,1,0:T(8,128)S(1)}, u32[]{:S(2)}, u32[]{:S(2)}) %collective-permute-start.7) | collective-permute-done | bytes 139296 | tf_op jit(solution)/shard_map/ppermute | solution.py:22
  131.1 3.2 %collective-permute-start.8 = (f32[17,8,256]{2,1,0:T(8,128)S(1)}, f32[17,8,256]{2,1,0:T(8,128)S(1)}, u32[]{:S(2)}, u32[]{:S(2)}) collective-permute-start(f32[17,8,256]{2,1,0:T(8,128)S(1)} %pad_maximum_fusion.7), channel_id=1, source_target_pairs={{0,64},{8,72},{16,80},{24,88},{32,96},{40,104},{48,112},{56,120},{... | collective-permute-start | bytes 417800 | tf_op jit(solution)/shard_map/ppermute | solution.py:22
  134.4 3.7 %collective-permute-done.8 = f32[17,8,256]{2,1,0:T(8,128)S(1)} collective-permute-done((f32[17,8,256]{2,1,0:T(8,128)S(1)}, f32[17,8,256]{2,1,0:T(8,128)S(1)}, u32[]{:S(2)}, u32[]{:S(2)}) %collective-permute-start.8) | collective-permute-done | bytes 139296 | tf_op jit(solution)/shard_map/ppermute | solution.py:22
  138.1 2.8 %collective-permute-start.9 = (f32[17,8,256]{2,1,0:T(8,128)S(1)}, f32[17,8,256]{2,1,0:T(8,128)S(1)}, u32[]{:S(2)}, u32[]{:S(2)}) collective-permute-start(f32[17,8,256]{2,1,0:T(8,128)S(1)} %pad_maximum_fusion.8), channel_id=1, source_target_pairs={{0,128},{8,136},{16,144},{24,152},{32,160},{40,168},{48,176},{56,1... | collective-permute-start | bytes 417800 | tf_op jit(solution)/shard_map/ppermute | solution.py:22
  141.0 13.4 %shard_map.151 = bf16[256,1024]{1,0:T(8,128)(2,1)} custom-call(s32[1]{0:T(128)} %bitcast.14.base_ref, bf16[256,1024]{1,0:T(8,128)(2,1)} %q_ref.1, bf16[2304,256]{1,0:T(8,128)(2,1)} %copy-done.13, bf16[2304,256]{1,0:T(8,128)(2,1)} %copy-done.13), custom_call_target="tpu_custom_call" | custom-call | flops 2415919104 | bytes 3407872 | tf_op jit(solution)/shard_map/pallas_call | solution.py:114
  154.4 0.8 fusion.17.h0_ref
  155.2 16.5 %shard_map.150 = f32[256,8,256]{2,1,0:T(8,128)} custom-call(f32[32,256]{1,0:T(8,128)} %reshape.53.bc_ref, f32[256,8,256]{2,1,0:T(8,128)} %copy-done.2, f32[256,8,256]{2,1,0:T(8,128)} %bitcast_multiply_fusion.2.dr_ref, f32[16,8,256]{2,1,0:T(8,128)} %bitcast.70, f32[16,8,256]{2,1,0:T(8,128)} %fusion.17.h0_ref), custom_call_target="tpu_custom_call" | custom-call | flops 50331648 | bytes 6553600 | tf_op jit(solution)/shard_map/pallas_call | solution.py:70
  171.6 3.4 %fusion.12 = bf16[256,8,256]{2,1,0:T(8,128)(2,1)S(1)} fusion(f32[32,8,8,256]{3,2,1,0:T(8,128)} %copy.21, f32[256,8,256]{2,1,0:T(8,128)} %shard_map.150, f32[32,8,8,256]{3,2,1,0:T(8,128)} %copy-done.1, f32[8,256]{1,0:T(8,128)S(1)} %copy-done.12), kind=kLoop, calls=%fused_computation.23 | loop fusion | flops 4194304 | bytes 7348224 | tf_op jit(solution)/shard_map/convert_element_type | solution.py:244
  175.1 1.3 copy.22
  (71 shorter events, 4.2 us)
Async XLA Ops:
  0.6 21.3 %copy-start = (bf16[2048,512]{1,0:T(8,128)(2,1)S(1)}, bf16[2048,512]{1,0:T(8,128)(2,1)}, u32[]{:S(2)}) copy-start(bf16[2048,512]{1,0:T(8,128)(2,1)} %param.21) | copy-start | bytes 6291460
  0.6 19.9 %copy-start.14 = (f32[2048]{0:T(1024)S(1)}, f32[2048]{0:T(1024)}, u32[]{:S(2)}) copy-start(f32[2048]{0:T(1024)} %param.20) | copy-start | bytes 24580
  3.3 15.0 %collective-permute-start = (bf16[280,256]{1,0:T(8,128)(2,1)S(1)}, bf16[280,256]{1,0:T(8,128)(2,1)S(1)}, u32[]{:S(2)}, u32[]{:S(2)}) collective-permute-start(bf16[280,256]{1,0:T(8,128)(2,1)S(1)} %pad_maximum_fusion.3), channel_id=1, source_target_pairs={{0,8},{8,16},{16,24},{24,32},{32,40},{40,48},{48,56},{56,64},{64,7... | collective-permute-start | bytes 430088 | tf_op jit(solution)/shard_map/ppermute | solution.py:22
  18.4 0.7 copy-start.5
  21.9 1.5 copy-start.10
  25.8 2.3 %collective-permute-start.1 = (f32[272,512]{1,0:T(8,128)}, f32[272,512]{1,0:T(8,128)}, u32[]{:S(2)}, u32[]{:S(2)}) collective-permute-start(f32[272,512]{1,0:T(8,128)} %pad_maximum_fusion), channel_id=1, source_target_pairs={{0,1},{1,0},{2,3},{3,2},{4,5},{5,4},{6,7},{7,6},{8,9},{9,8},{10,11... | collective-permute-start | bytes 1671176 | tf_op jit(solution)/shard_map/ppermute | solution.py:138
  29.4 10.6 %collective-permute-start.2 = (f32[136,512]{1,0:T(8,128)S(1)}, f32[136,512]{1,0:T(8,128)S(1)}, u32[]{:S(2)}, u32[]{:S(2)}) collective-permute-start(f32[136,512]{1,0:T(8,128)S(1)} %slice_select_fusion), channel_id=1, source_target_pairs={{0,2},{1,3},{2,0},{3,1},{4,6},{5,7},{6,4},{7,5},{8,10},{9,11},{10,... | collective-permute-start | bytes 835592 | tf_op jit(solution)/shard_map/ppermute | solution.py:138
  40.1 16.4 %collective-permute-start.3 = (f32[136,512]{1,0:T(8,128)S(1)}, f32[136,512]{1,0:T(8,128)S(1)}, u32[]{:S(2)}, u32[]{:S(2)}) collective-permute-start(f32[136,512]{1,0:T(8,128)S(1)} %fusion.28), channel_id=1, source_target_pairs={{0,4},{1,5},{2,6},{3,7},{4,0},{5,1},{6,2},{7,3},{8,12},{9,13},{10,... | collective-permute-start | bytes 835592 | tf_op jit(solution)/shard_map/ppermute | solution.py:138
  56.5 14.2 %collective-permute-start.4 = (f32[136,512]{1,0:T(8,128)S(1)}, f32[136,512]{1,0:T(8,128)}, u32[]{:S(2)}, u32[]{:S(2)}) collective-permute-start(f32[136,512]{1,0:T(8,128)S(1)} %add.136), channel_id=1, source_target_pairs={{0,1},{1,0},{2,3},{3,2},{4,5},{5,4},{6,7},{7,6},{8,9},{9,8},{10,11... | collective-permute-start | bytes 835592 | tf_op jit(solution)/shard_map/ppermute | solution.py:150
  56.6 39.9 %collective-permute-start.10 = (bf16[256,256]{1,0:T(8,128)(2,1)S(1)}, bf16[256,256]{1,0:T(8,128)(2,1)}, u32[]{:S(2)}, u32[]{:S(2)}) collective-permute-start(bf16[256,256]{1,0:T(8,128)(2,1)S(1)} %constant_dynamic-update-slice_fusion), channel_id=1, source_target_pairs={{0,64},{8,72},{16,80},{24,88},{32,96},{40,104},{48,112},{56,120},{... | collective-permute-start | bytes 393224 | tf_op jit(solution)/shard_map/ppermute | solution.py:22
  67.1 0.9 copy-start.6
  67.1 4.9 %copy-start.4 = (bf16[512,2048]{1,0:T(8,128)(2,1)S(1)}, bf16[512,2048]{1,0:T(8,128)(2,1)}, u32[]{:S(2)}) copy-start(bf16[512,2048]{1,0:T(8,128)(2,1)} %param.24) | copy-start | bytes 6291460
  67.1 4.9 %copy-start.15 = (f32[512]{0:T(512)S(1)}, f32[512]{0:T(512)}, u32[]{:S(2)}) copy-start(f32[512]{0:T(512)} %param.23) | copy-start | bytes 6148
  68.0 6.7 %copy-start.1 = (f32[32,8,8,256]{3,2,1,0:T(8,128)}, f32[32,8,8,256]{3,2,1,0:T(8,128)S(1)}, u32[]{:S(2)}) copy-start(f32[32,8,8,256]{3,2,1,0:T(8,128)S(1)} %copy.19) | copy-start | bytes 6291460
  68.8 28.6 %collective-permute-start.11 = (bf16[512,256]{1,0:T(8,128)(2,1)}, bf16[512,256]{1,0:T(8,128)(2,1)S(1)}, u32[]{:S(2)}, u32[]{:S(2)}) collective-permute-start(bf16[512,256]{1,0:T(8,128)(2,1)} %pad_maximum_fusion.2), channel_id=1, source_target_pairs={{0,16},{8,24},{16,32},{24,40},{32,48},{40,56},{48,64},{56,72},{64,... | collective-permute-start | bytes 786440 | tf_op jit(solution)/shard_map/ppermute | solution.py:22
  72.0 0.8 copy-start.11
  74.7 2.0 %copy-start.2 = (f32[256,8,256]{2,1,0:T(8,128)}, f32[256,8,256]{2,1,0:T(8,128)S(1)}, u32[]{:S(2)}) copy-start(f32[256,8,256]{2,1,0:T(8,128)S(1)} %get-tuple-element.3.dt_ref) | copy-start | bytes 6291460
  78.0 30.3 %copy-start.3 = (f32[2,8,8,256]{3,2,1,0:T(8,128)S(1)}, f32[2,8,8,256]{3,2,1,0:T(8,128)}, u32[]{:S(2)}) copy-start(f32[2,8,8,256]{3,2,1,0:T(8,128)} %copy.20) | copy-start | bytes 393220
  90.1 18.1 %collective-permute-start.5 = (f32[17,8,256]{2,1,0:T(8,128)S(1)}, f32[17,8,256]{2,1,0:T(8,128)S(1)}, u32[]{:S(2)}, u32[]{:S(2)}) collective-permute-start(f32[17,8,256]{2,1,0:T(8,128)S(1)} %pad_maximum_fusion.4), channel_id=1, source_target_pairs={{0,8},{8,16},{16,24},{24,32},{32,40},{40,48},{48,56},{56,64},{64,7... | collective-permute-start | bytes 417800 | tf_op jit(solution)/shard_map/ppermute | solution.py:22
  97.4 26.5 %copy-start.7 = (bf16[280,256]{1,0:T(8,128)(2,1)S(1)}, bf16[280,256]{1,0:T(8,128)(2,1)}, u32[]{:S(2)}) copy-start(bf16[280,256]{1,0:T(8,128)(2,1)} %copy-done.5) | copy-start | bytes 430084
  97.4 22.0 %collective-permute-start.12 = (bf16[1024,256]{1,0:T(8,128)(2,1)S(1)}, bf16[1024,256]{1,0:T(8,128)(2,1)S(1)}, u32[]{:S(2)}, u32[]{:S(2)}) collective-permute-start(bf16[1024,256]{1,0:T(8,128)(2,1)S(1)} %pad_maximum_fusion.1), channel_id=1, source_target_pairs={{0,32},{8,40},{16,48},{24,56},{32,64},{40,72},{48,80},{56,88},{64,... | collective-permute-start | bytes 1572872 | tf_op jit(solution)/shard_map/ppermute | solution.py:22
  108.2 26.1 %copy-start.8 = (bf16[256,128]{1,0:T(8,128)(2,1)S(1)}, bf16[256,128]{1,0:T(8,128)(2,1)}, u32[]{:S(2)}) copy-start(bf16[256,128]{1,0:T(8,128)(2,1)} %param.17) | copy-start | bytes 196612
  108.2 26.1 %copy-start.9 = (bf16[256,128]{1,0:T(8,128)(2,1)S(1)}, bf16[256,128]{1,0:T(8,128)(2,1)}, u32[]{:S(2)}) copy-start(bf16[256,128]{1,0:T(8,128)(2,1)} %param.18) | copy-start | bytes 196612
  109.3 11.8 %collective-permute-start.6 = (f32[17,8,256]{2,1,0:T(8,128)S(1)}, f32[17,8,256]{2,1,0:T(8,128)S(1)}, u32[]{:S(2)}, u32[]{:S(2)}) collective-permute-start(f32[17,8,256]{2,1,0:T(8,128)S(1)} %pad_maximum_fusion.5), channel_id=1, source_target_pairs={{0,16},{8,24},{16,32},{24,40},{32,48},{40,56},{48,64},{56,72},{64,... | collective-permute-start | bytes 417800 | tf_op jit(solution)/shard_map/ppermute | solution.py:22
  121.1 9.9 %collective-permute-start.7 = (f32[17,8,256]{2,1,0:T(8,128)S(1)}, f32[17,8,256]{2,1,0:T(8,128)S(1)}, u32[]{:S(2)}, u32[]{:S(2)}) collective-permute-start(f32[17,8,256]{2,1,0:T(8,128)S(1)} %pad_maximum_fusion.6), channel_id=1, source_target_pairs={{0,32},{8,40},{16,48},{24,56},{32,64},{40,72},{48,80},{56,88},{64,... | collective-permute-start | bytes 417800 | tf_op jit(solution)/shard_map/ppermute | solution.py:22
  131.1 6.9 %collective-permute-start.8 = (f32[17,8,256]{2,1,0:T(8,128)S(1)}, f32[17,8,256]{2,1,0:T(8,128)S(1)}, u32[]{:S(2)}, u32[]{:S(2)}) collective-permute-start(f32[17,8,256]{2,1,0:T(8,128)S(1)} %pad_maximum_fusion.7), channel_id=1, source_target_pairs={{0,64},{8,72},{16,80},{24,88},{32,96},{40,104},{48,112},{56,120},{... | collective-permute-start | bytes 417800 | tf_op jit(solution)/shard_map/ppermute | solution.py:22
  134.4 6.6 %copy-start.13 = (bf16[2304,256]{1,0:T(8,128)(2,1)}, bf16[2304,256]{1,0:T(8,128)(2,1)S(1)}, u32[]{:S(2)}) copy-start(bf16[2304,256]{1,0:T(8,128)(2,1)S(1)} %constant_dynamic-update-slice_fusion.7.k_ref.v_ref) | copy-start | bytes 3538948
  138.1 16.3 %collective-permute-start.9 = (f32[17,8,256]{2,1,0:T(8,128)S(1)}, f32[17,8,256]{2,1,0:T(8,128)S(1)}, u32[]{:S(2)}, u32[]{:S(2)}) collective-permute-start(f32[17,8,256]{2,1,0:T(8,128)S(1)} %pad_maximum_fusion.8), channel_id=1, source_target_pairs={{0,128},{8,136},{16,144},{24,152},{32,160},{40,168},{48,176},{56,1... | collective-permute-start | bytes 417800 | tf_op jit(solution)/shard_map/ppermute | solution.py:22
  155.1 16.5 %copy-start.12 = (f32[8,256]{1,0:T(8,128)S(1)}, f32[8,256]{1,0:T(8,128)}, u32[]{:S(2)}) copy-start(f32[8,256]{1,0:T(8,128)} %mul.238) | copy-start | bytes 24580

commit v14 on v13

--- a/solution.py
+++ b/solution.py
@@ -12,7 +12,7 @@
 HD = 128
 WINDOW = 2048
 SUBLANES = 8
-LANE_BLOCK = 256
+LANE_BLOCK = 128
 epsilon = 1e-06
 
 
@@ -37,6 +37,7 @@
 def scan_kernel(with_out, bc_ref, dt_ref, dr_ref, rate_ref, h0_ref, out_ref):
     states = rate_ref.shape[0]
     tokens = dt_ref.shape[0]
+    held = [rate_ref[n] for n in range(states)] if with_out else None
 
     def body(t, hs):
         dt = dt_ref[t]
@@ -44,7 +45,8 @@
         new = []
         acc = None
         for n in range(states):
-            h = jnp.exp(rate_ref[n] * dt) * hs[n] + bc_ref[n, t] * dr
+            rate = held[n] if with_out else rate_ref[n]
+            h = jnp.exp(rate * dt) * hs[n] + bc_ref[n, t] * dr
             new.append(h)
             if with_out:
                 term = bc_ref[states + n, t] * h
@@ -62,9 +64,10 @@
 def run_scan(bc, dt3, dr3, rate3, h0, with_out):
     tokens, sub, lanes = dt3.shape
     states = rate3.shape[0]
-    blocks = lanes // LANE_BLOCK
-    row_spec = pl.BlockSpec((tokens, sub, LANE_BLOCK), lambda j: (0, 0, j))
-    state_spec = pl.BlockSpec((states, sub, LANE_BLOCK), lambda j: (0, 0, j))
+    width = LANE_BLOCK if with_out else 2 * LANE_BLOCK
+    blocks = lanes // width
+    row_spec = pl.BlockSpec((tokens, sub, width), lambda j: (0, 0, j))
+    state_spec = pl.BlockSpec((states, sub, width), lambda j: (0, 0, j))
     out_shape = (tokens, sub, lanes) if with_out else (states, sub, lanes)
     elems = tokens * states * sub * lanes
     return pl.pallas_call(

time: 178 us -> 177 us (level)
  no operation moved by 1% of the time
where the time goes in v14:
time: 177 us; the launch traced here: 176 us
  waiting for transfers between devices  53.3 us (30%)
  starting transfers between devices  44 us (25%)
  Pallas kernels  40.3 us (23%)
  other arithmetic  19.2 us (11%)
  local copies, waits for them, and re-layouts  15.1 us (9%)
  matrix products  2.67 us (2%)
    ppermute x9, starting transfers between devices, shifted(): lax.ppermute(value, axis, [(source, source + steps) for source in range(f...  36.3 us
    ppermute x9, waiting for transfers between devices, shifted(): lax.ppermute(value, axis, [(source, source + steps) for source in range(f...  31.6 us
    pallas_call x2, Pallas kernels, run_scan(): pl.pallas_call(functools.partial(scan_kernel, with_out), grid=(blocks,),...  26.9 us
    ppermute x3, waiting for transfers between devices, butterfly_sum(): value = value + lax.ppermute(value, axis, pairs)  21.6 us
    pallas_call x1, Pallas kernels, run_attention(): pl.pallas_call(attention_kernel, grid=(heads,), in_specs=[pl.BlockSpec(me...  13.4 us
    unnamed x42, local copies, waits for them, and re-layouts  8.53 us
    ppermute x3, starting transfers between devices, butterfly_sum(): value = value + lax.ppermute(value, axis, pairs)  7.61 us
  transfers between devices with their start and end apart: 13, of which 9 were waited for; matrix products, arithmetic and copies ran while one was open for 11% of the time, Pallas kernels for 14%

profile of v14, /device:TPU:8, one launch (start us, length us, event | category | flops | bytes accessed | tf_op | source)
XLA Modules:
  0.0 175.6 jit_solution(2147149785709565834)
XLA Ops:
  0.7 1.0 constant_dynamic-update-slice_fusion.1
  1.7 0.8 slice.82
  2.5 0.9 constant_dynamic-update-slice_fusion
  3.3 9.1 %collective-permute-start = (bf16[280,256]{1,0:T(8,128)(2,1)S(1)}, bf16[280,256]{1,0:T(8,128)(2,1)S(1)}, u32[]{:S(2)}, u32[]{:S(2)}) collective-permute-start(bf16[280,256]{1,0:T(8,128)(2,1)S(1)} %pad_maximum_fusion.3), channel_id=1, source_target_pairs={{0,8},{8,16},{16,24},{24,32},{32,40},{40,48},{48,56},{56,64},{64,7... | collective-permute-start | bytes 430088 | tf_op jit(solution)/shard_map/ppermute | solution.py:22
  12.5 0.9 fusion.22
  13.4 5.0 %collective-permute-done = bf16[280,256]{1,0:T(8,128)(2,1)S(1)} collective-permute-done((bf16[280,256]{1,0:T(8,128)(2,1)S(1)}, bf16[280,256]{1,0:T(8,128)(2,1)S(1)}, u32[]{:S(2)}, u32[]{:S(2)}) %collective-permute-start) | collective-permute-done | bytes 143392 | tf_op jit(solution)/shard_map/ppermute | solution.py:22
  19.1 1.5 maximum_convert_fusion
  20.6 1.3 multiply_convert_fusion
  22.0 1.5 fusion.23
  23.9 1.9 %pad_maximum_fusion = f32[272,512]{1,0:T(8,128)} fusion(f32[16,512]{1,0:T(8,128)S(1)} %reshape.52, f32[256,512]{1,0:T(8,128)} %fusion.23), kind=kLoop, calls=%fused_computation.26 | loop fusion | flops 139264 | bytes 1114112 | tf_op jit(solution)/shard_map/concatenate | solution.py:221
  25.8 2.3 %collective-permute-done.1 = f32[272,512]{1,0:T(8,128)} collective-permute-done((f32[272,512]{1,0:T(8,128)}, f32[272,512]{1,0:T(8,128)}, u32[]{:S(2)}, u32[]{:S(2)}) %collective-permute-start.1) | collective-permute-done | bytes 557088 | tf_op jit(solution)/shard_map/ppermute | solution.py:141
  28.1 1.3 fusion.20
  29.4 3.6 %collective-permute-start.2 = (f32[136,512]{1,0:T(8,128)S(1)}, f32[136,512]{1,0:T(8,128)S(1)}, u32[]{:S(2)}, u32[]{:S(2)}) collective-permute-start(f32[136,512]{1,0:T(8,128)S(1)} %slice_select_fusion), channel_id=1, source_target_pairs={{0,2},{1,3},{2,0},{3,1},{4,6},{5,7},{6,4},{7,5},{8,10},{9,11},{10,... | collective-permute-start | bytes 835592 | tf_op jit(solution)/shard_map/ppermute | solution.py:141
  33.1 7.0 %collective-permute-done.2 = f32[136,512]{1,0:T(8,128)S(1)} collective-permute-done((f32[136,512]{1,0:T(8,128)S(1)}, f32[136,512]{1,0:T(8,128)S(1)}, u32[]{:S(2)}, u32[]{:S(2)}) %collective-permute-start.2) | collective-permute-done | bytes 278560 | tf_op jit(solution)/shard_map/ppermute | solution.py:141
  40.1 4.0 %collective-permute-start.3 = (f32[136,512]{1,0:T(8,128)S(1)}, f32[136,512]{1,0:T(8,128)S(1)}, u32[]{:S(2)}, u32[]{:S(2)}) collective-permute-start(f32[136,512]{1,0:T(8,128)S(1)} %fusion.28), channel_id=1, source_target_pairs={{0,4},{1,5},{2,6},{3,7},{4,0},{5,1},{6,2},{7,3},{8,12},{9,13},{10,... | collective-permute-start | bytes 835592 | tf_op jit(solution)/shard_map/ppermute | solution.py:141
  44.1 12.4 %collective-permute-done.3 = f32[136,512]{1,0:T(8,128)S(1)} collective-permute-done((f32[136,512]{1,0:T(8,128)S(1)}, f32[136,512]{1,0:T(8,128)S(1)}, u32[]{:S(2)}, u32[]{:S(2)}) %collective-permute-start.3) | collective-permute-done | bytes 278560 | tf_op jit(solution)/shard_map/ppermute | solution.py:141
  56.6 3.5 %collective-permute-start.10 = (bf16[256,256]{1,0:T(8,128)(2,1)S(1)}, bf16[256,256]{1,0:T(8,128)(2,1)}, u32[]{:S(2)}, u32[]{:S(2)}) collective-permute-start(bf16[256,256]{1,0:T(8,128)(2,1)S(1)} %constant_dynamic-update-slice_fusion), channel_id=1, source_target_pairs={{0,64},{8,72},{16,80},{24,88},{32,96},{40,104},{48,112},{56,120},{... | collective-permute-start | bytes 393224 | tf_op jit(solution)/shard_map/ppermute | solution.py:22
  60.1 1.3 add.139
  61.4 0.9 neg.27
  62.3 0.7 copy.20
  63.0 2.8 %copy.21 = f32[32,8,8,256]{3,2,1,0:T(8,128)} copy(bf16[32,8,8,256]{3,1,2,0:T(8,128)(2,1)} %bitcast.73) | data formatting | bytes 3145728
  65.8 1.3 mul.238
  68.0 0.8 pad_maximum_fusion.2
  68.8 1.9 %collective-permute-start.11 = (bf16[512,256]{1,0:T(8,128)(2,1)}, bf16[512,256]{1,0:T(8,128)(2,1)S(1)}, u32[]{:S(2)}, u32[]{:S(2)}) collective-permute-start(bf16[512,256]{1,0:T(8,128)(2,1)} %pad_maximum_fusion.2), channel_id=1, source_target_pairs={{0,16},{8,24},{16,32},{24,40},{32,48},{40,56},{48,64},{56,72},{64,... | collective-permute-start | bytes 786440 | tf_op jit(solution)/shard_map/ppermute | solution.py:22
  70.7 1.1 maximum_select_fusion
  72.0 0.8 fusion.5
  72.8 1.9 %fusion.21 = (f32[8,256]{1,0:T(8,128)S(1)}, f32[256,8,256]{2,1,0:T(8,128)S(1)}) fusion(f32[8,256]{1,0:T(8,128)S(1)} %copy-done.11, f32[256,8,256]{2,0,1:T(8,128)S(1)} %fusion.5), kind=kLoop, calls=%fused_computation.68 | loop fusion | flops 4192256 | bytes 4210688 | tf_op jit(solution)/shard_map/reduce_sum | solution.py:242
  74.7 1.8 %bitcast_multiply_fusion.2.dr_ref = f32[256,8,256]{2,1,0:T(8,128)} fusion(f32[256,8,256]{2,1,0:T(8,128)S(1)} %get-tuple-element.3.dt_ref, f32[32,8,8,256]{3,2,1,0:T(8,128)S(1)} %copy.19), kind=kLoop, calls=%fused_computation.8 | loop fusion | flops 524288 | bytes 6291456 | tf_op jit(solution)/shard_map/mul | solution.py:237
  78.0 11.2 %shard_map.149 = f32[16,8,256]{2,1,0:T(8,128)} custom-call(f32[32,256]{1,0:T(8,128)} %reshape.53.bc_ref, f32[256,8,256]{2,1,0:T(8,128)} %copy-done.2, f32[256,8,256]{2,1,0:T(8,128)} %bitcast_multiply_fusion.2.dr_ref, f32[16,8,256]{2,1,0:T(8,128)} %bitcast.69, f32[16,8,256]{2,1,0:T(8,128)} %broadcast_in_dim.5.h0_ref), custom_call_target="tpu_custom_call" | custom-call | flops 33554432 | bytes 6553600 | tf_op jit(solution)/shard_map/pallas_call | solution.py:73
  89.2 0.9 pad_maximum_fusion.4
  90.1 6.4 %collective-permute-start.5 = (f32[17,8,256]{2,1,0:T(8,128)S(1)}, f32[17,8,256]{2,1,0:T(8,128)S(1)}, u32[]{:S(2)}, u32[]{:S(2)}) collective-permute-start(f32[17,8,256]{2,1,0:T(8,128)S(1)} %pad_maximum_fusion.4), channel_id=1, source_target_pairs={{0,8},{8,16},{16,24},{24,32},{32,40},{40,48},{48,56},{56,64},{64,7... | collective-permute-start | bytes 417800 | tf_op jit(solution)/shard_map/ppermute | solution.py:22
  96.5 0.9 constant_dynamic-update-slice_fusion.6
  97.4 4.8 %collective-permute-start.12 = (bf16[1024,256]{1,0:T(8,128)(2,1)S(1)}, bf16[1024,256]{1,0:T(8,128)(2,1)S(1)}, u32[]{:S(2)}, u32[]{:S(2)}) collective-permute-start(bf16[1024,256]{1,0:T(8,128)(2,1)S(1)} %pad_maximum_fusion.1), channel_id=1, source_target_pairs={{0,32},{8,40},{16,48},{24,56},{32,64},{40,72},{48,80},{56,88},{64,... | collective-permute-start | bytes 1572872 | tf_op jit(solution)/shard_map/ppermute | solution.py:22
  102.3 6.0 %collective-permute-done.5 = f32[17,8,256]{2,1,0:T(8,128)S(1)} collective-permute-done((f32[17,8,256]{2,1,0:T(8,128)S(1)}, f32[17,8,256]{2,1,0:T(8,128)S(1)}, u32[]{:S(2)}, u32[]{:S(2)}) %collective-permute-start.5) | collective-permute-done | bytes 139296 | tf_op jit(solution)/shard_map/ppermute | solution.py:22
  108.3 1.0 multiply_add_fusion.3
  109.3 1.9 %collective-permute-start.6 = (f32[17,8,256]{2,1,0:T(8,128)S(1)}, f32[17,8,256]{2,1,0:T(8,128)S(1)}, u32[]{:S(2)}, u32[]{:S(2)}) collective-permute-start(f32[17,8,256]{2,1,0:T(8,128)S(1)} %pad_maximum_fusion.5), channel_id=1, source_target_pairs={{0,16},{8,24},{16,32},{24,40},{32,48},{40,56},{48,64},{56,72},{64,... | collective-permute-start | bytes 417800 | tf_op jit(solution)/shard_map/ppermute | solution.py:22
  111.2 8.3 %collective-permute-done.12 = bf16[1024,256]{1,0:T(8,128)(2,1)S(1)} collective-permute-done((bf16[1024,256]{1,0:T(8,128)(2,1)S(1)}, bf16[1024,256]{1,0:T(8,128)(2,1)S(1)}, u32[]{:S(2)}, u32[]{:S(2)}) %collective-permute-start.12) | collective-permute-done | bytes 524320 | tf_op jit(solution)/shard_map/ppermute | solution.py:22
  119.5 1.6 collective-permute-done.6
  121.1 2.7 %collective-permute-start.7 = (f32[17,8,256]{2,1,0:T(8,128)S(1)}, f32[17,8,256]{2,1,0:T(8,128)S(1)}, u32[]{:S(2)}, u32[]{:S(2)}) collective-permute-start(f32[17,8,256]{2,1,0:T(8,128)S(1)} %pad_maximum_fusion.6), channel_id=1, source_target_pairs={{0,32},{8,40},{16,48},{24,56},{32,64},{40,72},{48,80},{56,88},{64,... | collective-permute-start | bytes 417800 | tf_op jit(solution)/shard_map/ppermute | solution.py:22
  123.9 7.2 %collective-permute-done.7 = f32[17,8,256]{2,1,0:T(8,128)S(1)} collective-permute-done((f32[17,8,256]{2,1,0:T(8,128)S(1)}, f32[17,8,256]{2,1,0:T(8,128)S(1)}, u32[]{:S(2)}, u32[]{:S(2)}) %collective-permute-start.7) | collective-permute-done | bytes 139296 | tf_op jit(solution)/shard_map/ppermute | solution.py:22
  131.1 3.2 %collective-permute-start.8 = (f32[17,8,256]{2,1,0:T(8,128)S(1)}, f32[17,8,256]{2,1,0:T(8,128)S(1)}, u32[]{:S(2)}, u32[]{:S(2)}) collective-permute-start(f32[17,8,256]{2,1,0:T(8,128)S(1)} %pad_maximum_fusion.7), channel_id=1, source_target_pairs={{0,64},{8,72},{16,80},{24,88},{32,96},{40,104},{48,112},{56,120},{... | collective-permute-start | bytes 417800 | tf_op jit(solution)/shard_map/ppermute | solution.py:22
  134.4 3.7 %collective-permute-done.8 = f32[17,8,256]{2,1,0:T(8,128)S(1)} collective-permute-done((f32[17,8,256]{2,1,0:T(8,128)S(1)}, f32[17,8,256]{2,1,0:T(8,128)S(1)}, u32[]{:S(2)}, u32[]{:S(2)}) %collective-permute-start.8) | collective-permute-done | bytes 139296 | tf_op jit(solution)/shard_map/ppermute | solution.py:22
  138.1 2.8 %collective-permute-start.9 = (f32[17,8,256]{2,1,0:T(8,128)S(1)}, f32[17,8,256]{2,1,0:T(8,128)S(1)}, u32[]{:S(2)}, u32[]{:S(2)}) collective-permute-start(f32[17,8,256]{2,1,0:T(8,128)S(1)} %pad_maximum_fusion.8), channel_id=1, source_target_pairs={{0,128},{8,136},{16,144},{24,152},{32,160},{40,168},{48,176},{56,1... | collective-permute-start | bytes 417800 | tf_op jit(solution)/shard_map/ppermute | solution.py:22
  141.0 13.4 %shard_map.151 = bf16[256,1024]{1,0:T(8,128)(2,1)} custom-call(s32[1]{0:T(128)} %bitcast.14.base_ref, bf16[256,1024]{1,0:T(8,128)(2,1)} %q_ref.1, bf16[2304,256]{1,0:T(8,128)(2,1)} %copy-done.13, bf16[2304,256]{1,0:T(8,128)(2,1)} %copy-done.13), custom_call_target="tpu_custom_call" | custom-call | flops 2415919104 | bytes 3407872 | tf_op jit(solution)/shard_map/pallas_call | solution.py:117
  154.4 0.8 fusion.17.h0_ref
  155.2 15.7 %shard_map.150 = f32[256,8,256]{2,1,0:T(8,128)} custom-call(f32[32,256]{1,0:T(8,128)} %reshape.53.bc_ref, f32[256,8,256]{2,1,0:T(8,128)} %copy-done.2, f32[256,8,256]{2,1,0:T(8,128)} %bitcast_multiply_fusion.2.dr_ref, f32[16,8,256]{2,1,0:T(8,128)} %bitcast.70, f32[16,8,256]{2,1,0:T(8,128)} %fusion.17.h0_ref), custom_call_target="tpu_custom_call" | custom-call | flops 50331648 | bytes 6553600 | tf_op jit(solution)/shard_map/pallas_call | solution.py:73
  170.9 3.4 %fusion.12 = bf16[256,8,256]{2,1,0:T(8,128)(2,1)S(1)} fusion(f32[32,8,8,256]{3,2,1,0:T(8,128)} %copy.21, f32[256,8,256]{2,1,0:T(8,128)} %shard_map.150, f32[32,8,8,256]{3,2,1,0:T(8,128)} %copy-done.1, f32[8,256]{1,0:T(8,128)S(1)} %copy-done.12), kind=kLoop, calls=%fused_computation.23 | loop fusion | flops 4194304 | bytes 7348224 | tf_op jit(solution)/shard_map/convert_element_type | solution.py:247
  174.3 1.3 copy.22
  (71 shorter events, 4.2 us)
Async XLA Ops:
  0.6 21.3 %copy-start = (bf16[2048,512]{1,0:T(8,128)(2,1)S(1)}, bf16[2048,512]{1,0:T(8,128)(2,1)}, u32[]{:S(2)}) copy-start(bf16[2048,512]{1,0:T(8,128)(2,1)} %param.21) | copy-start | bytes 6291460
  0.6 19.9 %copy-start.14 = (f32[2048]{0:T(1024)S(1)}, f32[2048]{0:T(1024)}, u32[]{:S(2)}) copy-start(f32[2048]{0:T(1024)} %param.20) | copy-start | bytes 24580
  3.3 15.0 %collective-permute-start = (bf16[280,256]{1,0:T(8,128)(2,1)S(1)}, bf16[280,256]{1,0:T(8,128)(2,1)S(1)}, u32[]{:S(2)}, u32[]{:S(2)}) collective-permute-start(bf16[280,256]{1,0:T(8,128)(2,1)S(1)} %pad_maximum_fusion.3), channel_id=1, source_target_pairs={{0,8},{8,16},{16,24},{24,32},{32,40},{40,48},{48,56},{56,64},{64,7... | collective-permute-start | bytes 430088 | tf_op jit(solution)/shard_map/ppermute | solution.py:22
  18.4 0.7 copy-start.5
  21.9 1.5 copy-start.10
  25.8 2.3 %collective-permute-start.1 = (f32[272,512]{1,0:T(8,128)}, f32[272,512]{1,0:T(8,128)}, u32[]{:S(2)}, u32[]{:S(2)}) collective-permute-start(f32[272,512]{1,0:T(8,128)} %pad_maximum_fusion), channel_id=1, source_target_pairs={{0,1},{1,0},{2,3},{3,2},{4,5},{5,4},{6,7},{7,6},{8,9},{9,8},{10,11... | collective-permute-start | bytes 1671176 | tf_op jit(solution)/shard_map/ppermute | solution.py:141
  29.4 10.6 %collective-permute-start.2 = (f32[136,512]{1,0:T(8,128)S(1)}, f32[136,512]{1,0:T(8,128)S(1)}, u32[]{:S(2)}, u32[]{:S(2)}) collective-permute-start(f32[136,512]{1,0:T(8,128)S(1)} %slice_select_fusion), channel_id=1, source_target_pairs={{0,2},{1,3},{2,0},{3,1},{4,6},{5,7},{6,4},{7,5},{8,10},{9,11},{10,... | collective-permute-start | bytes 835592 | tf_op jit(solution)/shard_map/ppermute | solution.py:141
  40.1 16.4 %collective-permute-start.3 = (f32[136,512]{1,0:T(8,128)S(1)}, f32[136,512]{1,0:T(8,128)S(1)}, u32[]{:S(2)}, u32[]{:S(2)}) collective-permute-start(f32[136,512]{1,0:T(8,128)S(1)} %fusion.28), channel_id=1, source_target_pairs={{0,4},{1,5},{2,6},{3,7},{4,0},{5,1},{6,2},{7,3},{8,12},{9,13},{10,... | collective-permute-start | bytes 835592 | tf_op jit(solution)/shard_map/ppermute | solution.py:141
  56.5 14.2 %collective-permute-start.4 = (f32[136,512]{1,0:T(8,128)S(1)}, f32[136,512]{1,0:T(8,128)}, u32[]{:S(2)}, u32[]{:S(2)}) collective-permute-start(f32[136,512]{1,0:T(8,128)S(1)} %add.136), channel_id=1, source_target_pairs={{0,1},{1,0},{2,3},{3,2},{4,5},{5,4},{6,7},{7,6},{8,9},{9,8},{10,11... | collective-permute-start | bytes 835592 | tf_op jit(solution)/shard_map/ppermute | solution.py:153
  56.6 39.9 %collective-permute-start.10 = (bf16[256,256]{1,0:T(8,128)(2,1)S(1)}, bf16[256,256]{1,0:T(8,128)(2,1)}, u32[]{:S(2)}, u32[]{:S(2)}) collective-permute-start(bf16[256,256]{1,0:T(8,128)(2,1)S(1)} %constant_dynamic-update-slice_fusion), channel_id=1, source_target_pairs={{0,64},{8,72},{16,80},{24,88},{32,96},{40,104},{48,112},{56,120},{... | collective-permute-start | bytes 393224 | tf_op jit(solution)/shard_map/ppermute | solution.py:22
  67.1 0.9 copy-start.6
  67.1 4.9 %copy-start.4 = (bf16[512,2048]{1,0:T(8,128)(2,1)S(1)}, bf16[512,2048]{1,0:T(8,128)(2,1)}, u32[]{:S(2)}) copy-start(bf16[512,2048]{1,0:T(8,128)(2,1)} %param.24) | copy-start | bytes 6291460
  67.1 4.9 %copy-start.15 = (f32[512]{0:T(512)S(1)}, f32[512]{0:T(512)}, u32[]{:S(2)}) copy-start(f32[512]{0:T(512)} %param.23) | copy-start | bytes 6148
  68.0 6.7 %copy-start.1 = (f32[32,8,8,256]{3,2,1,0:T(8,128)}, f32[32,8,8,256]{3,2,1,0:T(8,128)S(1)}, u32[]{:S(2)}) copy-start(f32[32,8,8,256]{3,2,1,0:T(8,128)S(1)} %copy.19) | copy-start | bytes 6291460
  68.8 28.6 %collective-permute-start.11 = (bf16[512,256]{1,0:T(8,128)(2,1)}, bf16[512,256]{1,0:T(8,128)(2,1)S(1)}, u32[]{:S(2)}, u32[]{:S(2)}) collective-permute-start(bf16[512,256]{1,0:T(8,128)(2,1)} %pad_maximum_fusion.2), channel_id=1, source_target_pairs={{0,16},{8,24},{16,32},{24,40},{32,48},{40,56},{48,64},{56,72},{64,... | collective-permute-start | bytes 786440 | tf_op jit(solution)/shard_map/ppermute | solution.py:22
  72.0 0.8 copy-start.11
  74.7 2.0 %copy-start.2 = (f32[256,8,256]{2,1,0:T(8,128)}, f32[256,8,256]{2,1,0:T(8,128)S(1)}, u32[]{:S(2)}) copy-start(f32[256,8,256]{2,1,0:T(8,128)S(1)} %get-tuple-element.3.dt_ref) | copy-start | bytes 6291460
  78.0 30.3 %copy-start.3 = (f32[2,8,8,256]{3,2,1,0:T(8,128)S(1)}, f32[2,8,8,256]{3,2,1,0:T(8,128)}, u32[]{:S(2)}) copy-start(f32[2,8,8,256]{3,2,1,0:T(8,128)} %copy.20) | copy-start | bytes 393220
  90.1 18.1 %collective-permute-start.5 = (f32[17,8,256]{2,1,0:T(8,128)S(1)}, f32[17,8,256]{2,1,0:T(8,128)S(1)}, u32[]{:S(2)}, u32[]{:S(2)}) collective-permute-start(f32[17,8,256]{2,1,0:T(8,128)S(1)} %pad_maximum_fusion.4), channel_id=1, source_target_pairs={{0,8},{8,16},{16,24},{24,32},{32,40},{40,48},{48,56},{56,64},{64,7... | collective-permute-start | bytes 417800 | tf_op jit(solution)/shard_map/ppermute | solution.py:22
  97.4 26.5 %copy-start.7 = (bf16[280,256]{1,0:T(8,128)(2,1)S(1)}, bf16[280,256]{1,0:T(8,128)(2,1)}, u32[]{:S(2)}) copy-start(bf16[280,256]{1,0:T(8,128)(2,1)} %copy-done.5) | copy-start | bytes 430084
  97.4 22.0 %collective-permute-start.12 = (bf16[1024,256]{1,0:T(8,128)(2,1)S(1)}, bf16[1024,256]{1,0:T(8,128)(2,1)S(1)}, u32[]{:S(2)}, u32[]{:S(2)}) collective-permute-start(bf16[1024,256]{1,0:T(8,128)(2,1)S(1)} %pad_maximum_fusion.1), channel_id=1, source_target_pairs={{0,32},{8,40},{16,48},{24,56},{32,64},{40,72},{48,80},{56,88},{64,... | collective-permute-start | bytes 1572872 | tf_op jit(solution)/shard_map/ppermute | solution.py:22
  108.2 26.1 %copy-start.8 = (bf16[256,128]{1,0:T(8,128)(2,1)S(1)}, bf16[256,128]{1,0:T(8,128)(2,1)}, u32[]{:S(2)}) copy-start(bf16[256,128]{1,0:T(8,128)(2,1)} %param.17) | copy-start | bytes 196612
  108.2 26.1 %copy-start.9 = (bf16[256,128]{1,0:T(8,128)(2,1)S(1)}, bf16[256,128]{1,0:T(8,128)(2,1)}, u32[]{:S(2)}) copy-start(bf16[256,128]{1,0:T(8,128)(2,1)} %param.18) | copy-start | bytes 196612
  109.3 11.8 %collective-permute-start.6 = (f32[17,8,256]{2,1,0:T(8,128)S(1)}, f32[17,8,256]{2,1,0:T(8,128)S(1)}, u32[]{:S(2)}, u32[]{:S(2)}) collective-permute-start(f32[17,8,256]{2,1,0:T(8,128)S(1)} %pad_maximum_fusion.5), channel_id=1, source_target_pairs={{0,16},{8,24},{16,32},{24,40},{32,48},{40,56},{48,64},{56,72},{64,... | collective-permute-start | bytes 417800 | tf_op jit(solution)/shard_map/ppermute | solution.py:22
  121.1 9.9 %collective-permute-start.7 = (f32[17,8,256]{2,1,0:T(8,128)S(1)}, f32[17,8,256]{2,1,0:T(8,128)S(1)}, u32[]{:S(2)}, u32[]{:S(2)}) collective-permute-start(f32[17,8,256]{2,1,0:T(8,128)S(1)} %pad_maximum_fusion.6), channel_id=1, source_target_pairs={{0,32},{8,40},{16,48},{24,56},{32,64},{40,72},{48,80},{56,88},{64,... | collective-permute-start | bytes 417800 | tf_op jit(solution)/shard_map/ppermute | solution.py:22
  131.1 6.9 %collective-permute-start.8 = (f32[17,8,256]{2,1,0:T(8,128)S(1)}, f32[17,8,256]{2,1,0:T(8,128)S(1)}, u32[]{:S(2)}, u32[]{:S(2)}) collective-permute-start(f32[17,8,256]{2,1,0:T(8,128)S(1)} %pad_maximum_fusion.7), channel_id=1, source_target_pairs={{0,64},{8,72},{16,80},{24,88},{32,96},{40,104},{48,112},{56,120},{... | collective-permute-start | bytes 417800 | tf_op jit(solution)/shard_map/ppermute | solution.py:22
  134.4 6.6 %copy-start.13 = (bf16[2304,256]{1,0:T(8,128)(2,1)}, bf16[2304,256]{1,0:T(8,128)(2,1)S(1)}, u32[]{:S(2)}) copy-start(bf16[2304,256]{1,0:T(8,128)(2,1)S(1)} %constant_dynamic-update-slice_fusion.7.k_ref.v_ref) | copy-start | bytes 3538948
  138.1 16.3 %collective-permute-start.9 = (f32[17,8,256]{2,1,0:T(8,128)S(1)}, f32[17,8,256]{2,1,0:T(8,128)S(1)}, u32[]{:S(2)}, u32[]{:S(2)}) collective-permute-start(f32[17,8,256]{2,1,0:T(8,128)S(1)} %pad_maximum_fusion.8), channel_id=1, source_target_pairs={{0,128},{8,136},{16,144},{24,152},{32,160},{40,168},{48,176},{56,1... | collective-permute-start | bytes 417800 | tf_op jit(solution)/shard_map/ppermute | solution.py:22
  155.1 15.7 %copy-start.12 = (f32[8,256]{1,0:T(8,128)S(1)}, f32[8,256]{1,0:T(8,128)}, u32[]{:S(2)}) copy-start(f32[8,256]{1,0:T(8,128)} %mul.238) | copy-start | bytes 24580

commit v15 on v14

--- a/solution.py
+++ b/solution.py
@@ -34,7 +34,11 @@
     return (rank_low * lax.rsqrt(mean_square + epsilon) * dt_gain[None, :]).astype(jnp.bfloat16)
 
 
-def scan_kernel(with_out, bc_ref, dt_ref, dr_ref, rate_ref, h0_ref, out_ref):
+def scan_kernel(with_out, bc_ref, dt_ref, dr_ref, rate_ref, h0_ref, *rest):
+    if with_out:
+        skip_ref, act_ref, gate_ref, out_ref = rest
+    else:
+        (out_ref,) = rest
     states = rate_ref.shape[0]
     tokens = dt_ref.shape[0]
     held = [rate_ref[n] for n in range(states)] if with_out else None
@@ -52,7 +56,7 @@
                 term = bc_ref[states + n, t] * h
                 acc = term if acc is None else acc + term
         if with_out:
-            out_ref[t] = acc
+            out_ref[t] = (acc + skip_ref[...] * act_ref[t]) * gate_ref[t]
         return tuple(new)
 
     hs = lax.fori_loop(0, tokens, body, tuple(h0_ref[n] for n in range(states)), unroll=2)
@@ -61,7 +65,7 @@
             out_ref[n] = hs[n]
 
 
-def run_scan(bc, dt3, dr3, rate3, h0, with_out):
+def run_scan(bc, dt3, dr3, rate3, h0, with_out, extra=()):
     tokens, sub, lanes = dt3.shape
     states = rate3.shape[0]
     width = LANE_BLOCK if with_out else 2 * LANE_BLOCK
@@ -79,7 +83,7 @@
             row_spec,
             state_spec,
             state_spec,
-        ],
+        ] + ([pl.BlockSpec((sub, width), lambda j: (0, j)), row_spec, row_spec] if with_out else []),
         out_specs=row_spec if with_out else state_spec,
         out_shape=jax.ShapeDtypeStruct(out_shape, jnp.float32),
         cost_estimate=pl.CostEstimate(
@@ -87,7 +91,7 @@
             transcendentals=elems,
             bytes_accessed=4 * (3 * tokens * sub * lanes + 2 * states * sub * lanes),
         ),
-    )(bc, dt3, dr3, rate3, h0)
+    )(bc, dt3, dr3, rate3, h0, *extra)
 
 
 def attention_kernel(base_ref, q_ref, k_ref, v_ref, o_ref, bias_ref):
@@ -241,12 +245,11 @@
     local_final = run_scan(state_in, dt3, dr3, neg_rate3, zero_state, False)
     step_sum = jnp.sum(dt3, axis=0)
     entering = entering_state(step_sum, local_final, rate3)
-    mamba_sum = run_scan(state_in, dt3, dr3, neg_rate3, entering, True)
-    mamba_out = (
-        ((mamba_sum + cube(skip_weight)[None] * act3) * jax.nn.silu(cube(gate_in).astype(jnp.float32)))
-        .astype(jnp.bfloat16)
-        .reshape(tokens_here, channels)
-    )
+    gate3 = jax.nn.silu(cube(gate_in).astype(jnp.float32))
+    mixed = run_scan(
+        state_in, dt3, dr3, neg_rate3, entering, True, (cube(skip_weight), act3, gate3)
+    )
+    mamba_out = mixed.astype(jnp.bfloat16).reshape(tokens_here, channels)
     base = (lax.axis_index("seq") * tokens_here).astype(jnp.int32).reshape(1)
     attn_out = run_attention(q_proj, window, base)
     return (mamba_out, attn_out)

time: 177 us -> 173 us (0.977)
  waiting for transfers between devices: 53.3 us -> 49.7 us
  local copies, waits for them, and re-layouts: 15.1 us -> 12.5 us
    ppermute x3, waiting for transfers between devices: 21.6 us -> 17.9 us  [butterfly_sum(): value = value + lax.ppermute(value, axis, pairs)]
    unnamed x42, local copies, waits for them, and re-layouts: 8.53 us -> 5.98 us
    mul x0 -> x1, other arithmetic: none -> 1.88 us  [per_device(): gate3 = jax.nn.silu(cube(gate_in).astype(jnp.float32))]
where the time goes in v15:
time: 173 us
  waiting for transfers between devices  49.7 us (29%)
  starting transfers between devices  45.4 us (26%)
  Pallas kernels  41.8 us (24%)
  other arithmetic  19.3 us (11%)
  local copies, waits for them, and re-layouts  12.5 us (7%)
  matrix products  2.67 us (2%)
    ppermute x9, starting transfers between devices, shifted(): lax.ppermute(value, axis, [(source, source + steps) for source in range(f...  37.7 us
    ppermute x9, waiting for transfers between devices, shifted(): lax.ppermute(value, axis, [(source, source + steps) for source in range(f...  31.8 us
    pallas_call x2, Pallas kernels, run_scan(): pl.pallas_call(functools.partial(scan_kernel, with_out), grid=(blocks,),...  28.4 us
    ppermute x3, waiting for transfers between devices, butterfly_sum(): value = value + lax.ppermute(value, axis, pairs)  17.9 us
    pallas_call x1, Pallas kernels, run_attention(): pl.pallas_call(attention_kernel, grid=(heads,), in_specs=[pl.BlockSpec(me...  13.4 us
    ppermute x3, starting transfers between devices, butterfly_sum(): value = value + lax.ppermute(value, axis, pairs)  7.61 us
    unnamed x42, local copies, waits for them, and re-layouts  5.98 us
  transfers between devices with their start and end apart: 13, of which 9 were waited for; matrix products, arithmetic and copies ran while one was open for 11% of the time, Pallas kernels for 14%

profile of v15, /device:TPU:8, one launch (start us, length us, event | category | flops | bytes accessed | tf_op | source)
XLA Modules:
  0.0 172.6 jit_solution(15215450893160632822)
XLA Ops:
  0.7 1.0 constant_dynamic-update-slice_fusion.1
  1.7 0.8 slice.82
  2.5 0.9 constant_dynamic-update-slice_fusion
  3.3 9.1 %collective-permute-start = (bf16[280,256]{1,0:T(8,128)(2,1)S(1)}, bf16[280,256]{1,0:T(8,128)(2,1)S(1)}, u32[]{:S(2)}, u32[]{:S(2)}) collective-permute-start(bf16[280,256]{1,0:T(8,128)(2,1)S(1)} %pad_maximum_fusion.3), channel_id=1, source_target_pairs={{0,8},{8,16},{16,24},{24,32},{32,40},{40,48},{48,56},{56,64},{64,7... | collective-permute-start | bytes 430088 | tf_op jit(solution)/shard_map/ppermute | solution.py:22
  12.5 0.9 fusion.19
  13.4 5.0 %collective-permute-done = bf16[280,256]{1,0:T(8,128)(2,1)S(1)} collective-permute-done((bf16[280,256]{1,0:T(8,128)(2,1)S(1)}, bf16[280,256]{1,0:T(8,128)(2,1)S(1)}, u32[]{:S(2)}, u32[]{:S(2)}) %collective-permute-start) | collective-permute-done | bytes 143392 | tf_op jit(solution)/shard_map/ppermute | solution.py:22
  19.1 1.5 maximum_convert_fusion
  20.6 1.3 multiply_convert_fusion
  22.0 1.5 fusion.20
  23.9 1.9 %pad_maximum_fusion = f32[272,512]{1,0:T(8,128)} fusion(f32[16,512]{1,0:T(8,128)S(1)} %reshape.54, f32[256,512]{1,0:T(8,128)} %fusion.20), kind=kLoop, calls=%fused_computation.21 | loop fusion | flops 139264 | bytes 1114112 | tf_op jit(solution)/shard_map/concatenate | solution.py:225
  25.8 2.3 %collective-permute-done.1 = f32[272,512]{1,0:T(8,128)} collective-permute-done((f32[272,512]{1,0:T(8,128)}, f32[272,512]{1,0:T(8,128)}, u32[]{:S(2)}, u32[]{:S(2)}) %collective-permute-start.1) | collective-permute-done | bytes 557088 | tf_op jit(solution)/shard_map/ppermute | solution.py:145
  28.1 1.3 fusion.17
  29.4 3.6 %collective-permute-start.2 = (f32[136,512]{1,0:T(8,128)S(1)}, f32[136,512]{1,0:T(8,128)S(1)}, u32[]{:S(2)}, u32[]{:S(2)}) collective-permute-start(f32[136,512]{1,0:T(8,128)S(1)} %slice_select_fusion), channel_id=1, source_target_pairs={{0,2},{1,3},{2,0},{3,1},{4,6},{5,7},{6,4},{7,5},{8,10},{9,11},{10,... | collective-permute-start | bytes 835592 | tf_op jit(solution)/shard_map/ppermute | solution.py:145
  33.1 7.0 %collective-permute-done.2 = f32[136,512]{1,0:T(8,128)S(1)} collective-permute-done((f32[136,512]{1,0:T(8,128)S(1)}, f32[136,512]{1,0:T(8,128)S(1)}, u32[]{:S(2)}, u32[]{:S(2)}) %collective-permute-start.2) | collective-permute-done | bytes 278560 | tf_op jit(solution)/shard_map/ppermute | solution.py:145
  40.1 4.0 %collective-permute-start.3 = (f32[136,512]{1,0:T(8,128)S(1)}, f32[136,512]{1,0:T(8,128)S(1)}, u32[]{:S(2)}, u32[]{:S(2)}) collective-permute-start(f32[136,512]{1,0:T(8,128)S(1)} %fusion.25), channel_id=1, source_target_pairs={{0,4},{1,5},{2,6},{3,7},{4,0},{5,1},{6,2},{7,3},{8,12},{9,13},{10,... | collective-permute-start | bytes 835592 | tf_op jit(solution)/shard_map/ppermute | solution.py:145
  44.1 3.5 %collective-permute-start.10 = (bf16[256,256]{1,0:T(8,128)(2,1)S(1)}, bf16[256,256]{1,0:T(8,128)(2,1)}, u32[]{:S(2)}, u32[]{:S(2)}) collective-permute-start(bf16[256,256]{1,0:T(8,128)(2,1)S(1)} %constant_dynamic-update-slice_fusion), channel_id=1, source_target_pairs={{0,64},{8,72},{16,80},{24,88},{32,96},{40,104},{48,112},{56,120},{... | collective-permute-start | bytes 393224 | tf_op jit(solution)/shard_map/ppermute | solution.py:22
  47.8 8.7 %collective-permute-done.3 = f32[136,512]{1,0:T(8,128)S(1)} collective-permute-done((f32[136,512]{1,0:T(8,128)S(1)}, f32[136,512]{1,0:T(8,128)S(1)}, u32[]{:S(2)}, u32[]{:S(2)}) %collective-permute-start.3) | collective-permute-done | bytes 278560 | tf_op jit(solution)/shard_map/ppermute | solution.py:145
  56.6 1.9 %bitcast_multiply_fusion.rest_2_ = f32[256,8,256]{2,1,0:T(8,128)} fusion(f32[32,8,8,256]{3,2,1,0:T(8,128)S(1)} %copy.21), kind=kLoop, calls=%fused_computation.1 | loop fusion | flops 2097152 | bytes 4194304 | tf_op jit(solution)/shard_map/jit(silu)/mul | solution.py:248
  58.5 1.3 add.136
  59.8 0.9 neg.27
  60.7 0.7 copy.20
  61.4 1.3 reshape.57.rest_0_
  63.6 0.8 pad_maximum_fusion.2
  64.4 1.9 %collective-permute-start.11 = (bf16[512,256]{1,0:T(8,128)(2,1)}, bf16[512,256]{1,0:T(8,128)(2,1)S(1)}, u32[]{:S(2)}, u32[]{:S(2)}) collective-permute-start(bf16[512,256]{1,0:T(8,128)(2,1)} %pad_maximum_fusion.2), channel_id=1, source_target_pairs={{0,16},{8,24},{16,32},{24,40},{32,48},{40,56},{48,64},{56,72},{64,... | collective-permute-start | bytes 786440 | tf_op jit(solution)/shard_map/ppermute | solution.py:22
  66.3 1.1 maximum_select_fusion
  67.6 0.8 fusion.3
  68.3 1.9 %fusion.18 = (f32[8,256]{1,0:T(8,128)S(1)}, f32[256,8,256]{2,1,0:T(8,128)S(1)}) fusion(f32[8,256]{1,0:T(8,128)S(1)} %copy-done.12, f32[256,8,256]{2,0,1:T(8,128)S(1)} %fusion.3), kind=kLoop, calls=%fused_computation.64 | loop fusion | flops 4192256 | bytes 4210688 | tf_op jit(solution)/shard_map/reduce_sum | solution.py:246
  70.2 1.8 %bitcast_multiply_fusion.1.dr_ref = f32[256,8,256]{2,1,0:T(8,128)} fusion(f32[256,8,256]{2,1,0:T(8,128)S(1)} %get-tuple-element.3.dt_ref, f32[32,8,8,256]{3,2,1,0:T(8,128)S(1)} %copy.19), kind=kLoop, calls=%fused_computation.61 | loop fusion | flops 524288 | bytes 6291456 | tf_op jit(solution)/shard_map/mul | solution.py:241
  73.5 11.2 %shard_map.149 = f32[16,8,256]{2,1,0:T(8,128)} custom-call(f32[32,256]{1,0:T(8,128)} %reshape.55.bc_ref, f32[256,8,256]{2,1,0:T(8,128)} %copy-done.2, f32[256,8,256]{2,1,0:T(8,128)} %bitcast_multiply_fusion.1.dr_ref, f32[16,8,256]{2,1,0:T(8,128)} %bitcast.59, f32[16,8,256]{2,1,0:T(8,128)} %broadcast_in_dim.5.h0_ref), custom_call_target="tpu_custom_call" | custom-call | flops 33554432 | bytes 6553600 | tf_op jit(solution)/shard_map/pallas_call | solution.py:77
  84.8 0.9 pad_maximum_fusion.4
  85.7 6.4 %collective-permute-start.5 = (f32[17,8,256]{2,1,0:T(8,128)S(1)}, f32[17,8,256]{2,1,0:T(8,128)S(1)}, u32[]{:S(2)}, u32[]{:S(2)}) collective-permute-start(f32[17,8,256]{2,1,0:T(8,128)S(1)} %pad_maximum_fusion.4), channel_id=1, source_target_pairs={{0,8},{8,16},{16,24},{24,32},{32,40},{40,48},{48,56},{56,64},{64,7... | collective-permute-start | bytes 417800 | tf_op jit(solution)/shard_map/ppermute | solution.py:22
  92.0 0.9 constant_dynamic-update-slice_fusion.6
  93.0 4.6 %collective-permute-start.12 = (bf16[1024,256]{1,0:T(8,128)(2,1)S(1)}, bf16[1024,256]{1,0:T(8,128)(2,1)S(1)}, u32[]{:S(2)}, u32[]{:S(2)}) collective-permute-start(bf16[1024,256]{1,0:T(8,128)(2,1)S(1)} %pad_maximum_fusion.1), channel_id=1, source_target_pairs={{0,32},{8,40},{16,48},{24,56},{32,64},{40,72},{48,80},{56,88},{64,... | collective-permute-start | bytes 1572872 | tf_op jit(solution)/shard_map/ppermute | solution.py:22
  97.7 5.7 %collective-permute-done.5 = f32[17,8,256]{2,1,0:T(8,128)S(1)} collective-permute-done((f32[17,8,256]{2,1,0:T(8,128)S(1)}, f32[17,8,256]{2,1,0:T(8,128)S(1)}, u32[]{:S(2)}, u32[]{:S(2)}) %collective-permute-start.5) | collective-permute-done | bytes 139296 | tf_op jit(solution)/shard_map/ppermute | solution.py:22
  103.4 1.0 multiply_add_fusion.3
  104.4 1.9 %collective-permute-start.6 = (f32[17,8,256]{2,1,0:T(8,128)S(1)}, f32[17,8,256]{2,1,0:T(8,128)S(1)}, u32[]{:S(2)}, u32[]{:S(2)}) collective-permute-start(f32[17,8,256]{2,1,0:T(8,128)S(1)} %pad_maximum_fusion.5), channel_id=1, source_target_pairs={{0,16},{8,24},{16,32},{24,40},{32,48},{40,56},{48,64},{56,72},{64,... | collective-permute-start | bytes 417800 | tf_op jit(solution)/shard_map/ppermute | solution.py:22
  106.4 8.3 %collective-permute-done.12 = bf16[1024,256]{1,0:T(8,128)(2,1)S(1)} collective-permute-done((bf16[1024,256]{1,0:T(8,128)(2,1)S(1)}, bf16[1024,256]{1,0:T(8,128)(2,1)S(1)}, u32[]{:S(2)}, u32[]{:S(2)}) %collective-permute-start.12) | collective-permute-done | bytes 524320 | tf_op jit(solution)/shard_map/ppermute | solution.py:22
  114.8 2.2 %collective-permute-done.6 = f32[17,8,256]{2,1,0:T(8,128)S(1)} collective-permute-done((f32[17,8,256]{2,1,0:T(8,128)S(1)}, f32[17,8,256]{2,1,0:T(8,128)S(1)}, u32[]{:S(2)}, u32[]{:S(2)}) %collective-permute-start.6) | collective-permute-done | bytes 139296 | tf_op jit(solution)/shard_map/ppermute | solution.py:22
  117.0 2.7 %collective-permute-start.7 = (f32[17,8,256]{2,1,0:T(8,128)S(1)}, f32[17,8,256]{2,1,0:T(8,128)S(1)}, u32[]{:S(2)}, u32[]{:S(2)}) collective-permute-start(f32[17,8,256]{2,1,0:T(8,128)S(1)} %pad_maximum_fusion.6), channel_id=1, source_target_pairs={{0,32},{8,40},{16,48},{24,56},{32,64},{40,72},{48,80},{56,88},{64,... | collective-permute-start | bytes 417800 | tf_op jit(solution)/shard_map/ppermute | solution.py:22
  119.7 7.2 %collective-permute-done.7 = f32[17,8,256]{2,1,0:T(8,128)S(1)} collective-permute-done((f32[17,8,256]{2,1,0:T(8,128)S(1)}, f32[17,8,256]{2,1,0:T(8,128)S(1)}, u32[]{:S(2)}, u32[]{:S(2)}) %collective-permute-start.7) | collective-permute-done | bytes 139296 | tf_op jit(solution)/shard_map/ppermute | solution.py:22
  127.0 3.5 %collective-permute-start.8 = (f32[17,8,256]{2,1,0:T(8,128)S(1)}, f32[17,8,256]{2,1,0:T(8,128)S(1)}, u32[]{:S(2)}, u32[]{:S(2)}) collective-permute-start(f32[17,8,256]{2,1,0:T(8,128)S(1)} %pad_maximum_fusion.7), channel_id=1, source_target_pairs={{0,64},{8,72},{16,80},{24,88},{32,96},{40,104},{48,112},{56,120},{... | collective-permute-start | bytes 417800 | tf_op jit(solution)/shard_map/ppermute | solution.py:22
  130.6 3.4 %collective-permute-done.8 = f32[17,8,256]{2,1,0:T(8,128)S(1)} collective-permute-done((f32[17,8,256]{2,1,0:T(8,128)S(1)}, f32[17,8,256]{2,1,0:T(8,128)S(1)}, u32[]{:S(2)}, u32[]{:S(2)}) %collective-permute-start.8) | collective-permute-done | bytes 139296 | tf_op jit(solution)/shard_map/ppermute | solution.py:22
  134.0 4.2 %collective-permute-start.9 = (f32[17,8,256]{2,1,0:T(8,128)S(1)}, f32[17,8,256]{2,1,0:T(8,128)S(1)}, u32[]{:S(2)}, u32[]{:S(2)}) collective-permute-start(f32[17,8,256]{2,1,0:T(8,128)S(1)} %pad_maximum_fusion.8), channel_id=1, source_target_pairs={{0,128},{8,136},{16,144},{24,152},{32,160},{40,168},{48,176},{56,1... | collective-permute-start | bytes 417800 | tf_op jit(solution)/shard_map/ppermute | solution.py:22
  138.2 13.4 %shard_map.151 = bf16[256,1024]{1,0:T(8,128)(2,1)} custom-call(s32[1]{0:T(128)} %bitcast.14.base_ref, bf16[256,1024]{1,0:T(8,128)(2,1)} %q_ref.1, bf16[2304,256]{1,0:T(8,128)(2,1)} %copy-done.13, bf16[2304,256]{1,0:T(8,128)(2,1)} %copy-done.13), custom_call_target="tpu_custom_call" | custom-call | flops 2415919104 | bytes 3407872 | tf_op jit(solution)/shard_map/pallas_call | solution.py:121
  151.6 0.8 fusion.14.h0_ref
  152.4 17.2 %shard_map.150 = f32[256,8,256]{2,1,0:T(8,128)} custom-call(f32[32,256]{1,0:T(8,128)} %reshape.55.bc_ref, f32[256,8,256]{2,1,0:T(8,128)} %copy-done.2, f32[256,8,256]{2,1,0:T(8,128)} %bitcast_multiply_fusion.1.dr_ref, f32[16,8,256]{2,1,0:T(8,128)} %bitcast.60, f32[16,8,256]{2,1,0:T(8,128)} %fusion.14.h0_ref, f32[8,256]{1,0:T(8,128)} %reshape.57.rest_0_, ...), custom_call_target="tpu_custom_call" | custom-call | flops 50331648 | bytes 6553600 | tf_op jit(solution)/shard_map/pallas_call | solution.py:77
  169.6 1.7 convert_element_type.30
  171.3 1.3 copy.22
  (72 shorter events, 4.5 us)
Async XLA Ops:
  0.6 21.3 %copy-start = (bf16[2048,512]{1,0:T(8,128)(2,1)S(1)}, bf16[2048,512]{1,0:T(8,128)(2,1)}, u32[]{:S(2)}) copy-start(bf16[2048,512]{1,0:T(8,128)(2,1)} %param.21) | copy-start | bytes 6291460
  0.6 19.9 %copy-start.14 = (f32[2048]{0:T(1024)S(1)}, f32[2048]{0:T(1024)}, u32[]{:S(2)}) copy-start(f32[2048]{0:T(1024)} %param.20) | copy-start | bytes 24580
  3.3 15.0 %collective-permute-start = (bf16[280,256]{1,0:T(8,128)(2,1)S(1)}, bf16[280,256]{1,0:T(8,128)(2,1)S(1)}, u32[]{:S(2)}, u32[]{:S(2)}) collective-permute-start(bf16[280,256]{1,0:T(8,128)(2,1)S(1)} %pad_maximum_fusion.3), channel_id=1, source_target_pairs={{0,8},{8,16},{16,24},{24,32},{32,40},{40,48},{48,56},{56,64},{64,7... | collective-permute-start | bytes 430088 | tf_op jit(solution)/shard_map/ppermute | solution.py:22
  18.4 0.7 copy-start.6
  21.9 1.5 copy-start.11
  25.8 2.3 %collective-permute-start.1 = (f32[272,512]{1,0:T(8,128)}, f32[272,512]{1,0:T(8,128)}, u32[]{:S(2)}, u32[]{:S(2)}) collective-permute-start(f32[272,512]{1,0:T(8,128)} %pad_maximum_fusion), channel_id=1, source_target_pairs={{0,1},{1,0},{2,3},{3,2},{4,5},{5,4},{6,7},{7,6},{8,9},{9,8},{10,11... | collective-permute-start | bytes 1671176 | tf_op jit(solution)/shard_map/ppermute | solution.py:145
  25.8 21.8 %copy-start.5 = (bf16[256,2048]{1,0:T(8,128)(2,1)S(1)}, bf16[256,2048]{1,0:T(8,128)(2,1)}, u32[]{:S(2)}) copy-start(bf16[256,2048]{1,0:T(8,128)(2,1)} %param.15) | copy-start | bytes 3145732
  29.4 10.6 %collective-permute-start.2 = (f32[136,512]{1,0:T(8,128)S(1)}, f32[136,512]{1,0:T(8,128)S(1)}, u32[]{:S(2)}, u32[]{:S(2)}) collective-permute-start(f32[136,512]{1,0:T(8,128)S(1)} %slice_select_fusion), channel_id=1, source_target_pairs={{0,2},{1,3},{2,0},{3,1},{4,6},{5,7},{6,4},{7,5},{8,10},{9,11},{10,... | collective-permute-start | bytes 835592 | tf_op jit(solution)/shard_map/ppermute | solution.py:145
  40.1 16.4 %collective-permute-start.3 = (f32[136,512]{1,0:T(8,128)S(1)}, f32[136,512]{1,0:T(8,128)S(1)}, u32[]{:S(2)}, u32[]{:S(2)}) collective-permute-start(f32[136,512]{1,0:T(8,128)S(1)} %fusion.25), channel_id=1, source_target_pairs={{0,4},{1,5},{2,6},{3,7},{4,0},{5,1},{6,2},{7,3},{8,12},{9,13},{10,... | collective-permute-start | bytes 835592 | tf_op jit(solution)/shard_map/ppermute | solution.py:145
  44.1 48.0 %collective-permute-start.10 = (bf16[256,256]{1,0:T(8,128)(2,1)S(1)}, bf16[256,256]{1,0:T(8,128)(2,1)}, u32[]{:S(2)}, u32[]{:S(2)}) collective-permute-start(bf16[256,256]{1,0:T(8,128)(2,1)S(1)} %constant_dynamic-update-slice_fusion), channel_id=1, source_target_pairs={{0,64},{8,72},{16,80},{24,88},{32,96},{40,104},{48,112},{56,120},{... | collective-permute-start | bytes 393224 | tf_op jit(solution)/shard_map/ppermute | solution.py:22
  56.5 9.8 %collective-permute-start.4 = (f32[136,512]{1,0:T(8,128)S(1)}, f32[136,512]{1,0:T(8,128)}, u32[]{:S(2)}, u32[]{:S(2)}) collective-permute-start(f32[136,512]{1,0:T(8,128)S(1)} %add.133), channel_id=1, source_target_pairs={{0,1},{1,0},{2,3},{3,2},{4,5},{5,4},{6,7},{7,6},{8,9},{9,8},{10,11... | collective-permute-start | bytes 835592 | tf_op jit(solution)/shard_map/ppermute | solution.py:157
  62.7 0.9 copy-start.7
  62.7 4.9 %copy-start.4 = (bf16[512,2048]{1,0:T(8,128)(2,1)S(1)}, bf16[512,2048]{1,0:T(8,128)(2,1)}, u32[]{:S(2)}) copy-start(bf16[512,2048]{1,0:T(8,128)(2,1)} %param.24) | copy-start | bytes 6291460
  62.7 4.9 %copy-start.15 = (f32[512]{0:T(512)S(1)}, f32[512]{0:T(512)}, u32[]{:S(2)}) copy-start(f32[512]{0:T(512)} %param.23) | copy-start | bytes 6148
  63.6 6.7 %copy-start.1 = (f32[32,8,8,256]{3,2,1,0:T(8,128)}, f32[32,8,8,256]{3,2,1,0:T(8,128)S(1)}, u32[]{:S(2)}) copy-start(f32[32,8,8,256]{3,2,1,0:T(8,128)S(1)} %copy.19) | copy-start | bytes 6291460
  64.4 28.6 %collective-permute-start.11 = (bf16[512,256]{1,0:T(8,128)(2,1)}, bf16[512,256]{1,0:T(8,128)(2,1)S(1)}, u32[]{:S(2)}, u32[]{:S(2)}) collective-permute-start(bf16[512,256]{1,0:T(8,128)(2,1)} %pad_maximum_fusion.2), channel_id=1, source_target_pairs={{0,16},{8,24},{16,32},{24,40},{32,48},{40,56},{48,64},{56,72},{64,... | collective-permute-start | bytes 786440 | tf_op jit(solution)/shard_map/ppermute | solution.py:22
  67.5 0.8 copy-start.12
  70.2 2.0 %copy-start.2 = (f32[256,8,256]{2,1,0:T(8,128)}, f32[256,8,256]{2,1,0:T(8,128)S(1)}, u32[]{:S(2)}) copy-start(f32[256,8,256]{2,1,0:T(8,128)S(1)} %get-tuple-element.3.dt_ref) | copy-start | bytes 6291460
  73.5 29.9 %copy-start.3 = (f32[2,8,8,256]{3,2,1,0:T(8,128)S(1)}, f32[2,8,8,256]{3,2,1,0:T(8,128)}, u32[]{:S(2)}) copy-start(f32[2,8,8,256]{3,2,1,0:T(8,128)} %copy.20) | copy-start | bytes 393220
  85.7 17.7 %collective-permute-start.5 = (f32[17,8,256]{2,1,0:T(8,128)S(1)}, f32[17,8,256]{2,1,0:T(8,128)S(1)}, u32[]{:S(2)}, u32[]{:S(2)}) collective-permute-start(f32[17,8,256]{2,1,0:T(8,128)S(1)} %pad_maximum_fusion.4), channel_id=1, source_target_pairs={{0,8},{8,16},{16,24},{24,32},{32,40},{40,48},{48,56},{56,64},{64,7... | collective-permute-start | bytes 417800 | tf_op jit(solution)/shard_map/ppermute | solution.py:22
  93.0 26.7 %copy-start.8 = (bf16[280,256]{1,0:T(8,128)(2,1)S(1)}, bf16[280,256]{1,0:T(8,128)(2,1)}, u32[]{:S(2)}) copy-start(bf16[280,256]{1,0:T(8,128)(2,1)} %copy-done.6) | copy-start | bytes 430084
  93.0 21.7 %collective-permute-start.12 = (bf16[1024,256]{1,0:T(8,128)(2,1)S(1)}, bf16[1024,256]{1,0:T(8,128)(2,1)S(1)}, u32[]{:S(2)}, u32[]{:S(2)}) collective-permute-start(bf16[1024,256]{1,0:T(8,128)(2,1)S(1)} %pad_maximum_fusion.1), channel_id=1, source_target_pairs={{0,32},{8,40},{16,48},{24,56},{32,64},{40,72},{48,80},{56,88},{64,... | collective-permute-start | bytes 1572872 | tf_op jit(solution)/shard_map/ppermute | solution.py:22
  103.4 27.1 %copy-start.9 = (bf16[256,128]{1,0:T(8,128)(2,1)S(1)}, bf16[256,128]{1,0:T(8,128)(2,1)}, u32[]{:S(2)}) copy-start(bf16[256,128]{1,0:T(8,128)(2,1)} %param.17) | copy-start | bytes 196612
  103.4 27.1 %copy-start.10 = (bf16[256,128]{1,0:T(8,128)(2,1)S(1)}, bf16[256,128]{1,0:T(8,128)(2,1)}, u32[]{:S(2)}) copy-start(bf16[256,128]{1,0:T(8,128)(2,1)} %param.18) | copy-start | bytes 196612
  104.4 12.5 %collective-permute-start.6 = (f32[17,8,256]{2,1,0:T(8,128)S(1)}, f32[17,8,256]{2,1,0:T(8,128)S(1)}, u32[]{:S(2)}, u32[]{:S(2)}) collective-permute-start(f32[17,8,256]{2,1,0:T(8,128)S(1)} %pad_maximum_fusion.5), channel_id=1, source_target_pairs={{0,16},{8,24},{16,32},{24,40},{32,48},{40,56},{48,64},{56,72},{64,... | collective-permute-start | bytes 417800 | tf_op jit(solution)/shard_map/ppermute | solution.py:22
  117.0 9.9 %collective-permute-start.7 = (f32[17,8,256]{2,1,0:T(8,128)S(1)}, f32[17,8,256]{2,1,0:T(8,128)S(1)}, u32[]{:S(2)}, u32[]{:S(2)}) collective-permute-start(f32[17,8,256]{2,1,0:T(8,128)S(1)} %pad_maximum_fusion.6), channel_id=1, source_target_pairs={{0,32},{8,40},{16,48},{24,56},{32,64},{40,72},{48,80},{56,88},{64,... | collective-permute-start | bytes 417800 | tf_op jit(solution)/shard_map/ppermute | solution.py:22
  127.0 6.9 %collective-permute-start.8 = (f32[17,8,256]{2,1,0:T(8,128)S(1)}, f32[17,8,256]{2,1,0:T(8,128)S(1)}, u32[]{:S(2)}, u32[]{:S(2)}) collective-permute-start(f32[17,8,256]{2,1,0:T(8,128)S(1)} %pad_maximum_fusion.7), channel_id=1, source_target_pairs={{0,64},{8,72},{16,80},{24,88},{32,96},{40,104},{48,112},{56,120},{... | collective-permute-start | bytes 417800 | tf_op jit(solution)/shard_map/ppermute | solution.py:22
  130.6 7.6 %copy-start.13 = (bf16[2304,256]{1,0:T(8,128)(2,1)}, bf16[2304,256]{1,0:T(8,128)(2,1)S(1)}, u32[]{:S(2)}) copy-start(bf16[2304,256]{1,0:T(8,128)(2,1)S(1)} %constant_dynamic-update-slice_fusion.7.k_ref.v_ref) | copy-start | bytes 3538948
  134.0 17.6 %collective-permute-start.9 = (f32[17,8,256]{2,1,0:T(8,128)S(1)}, f32[17,8,256]{2,1,0:T(8,128)S(1)}, u32[]{:S(2)}, u32[]{:S(2)}) collective-permute-start(f32[17,8,256]{2,1,0:T(8,128)S(1)} %pad_maximum_fusion.8), channel_id=1, source_target_pairs={{0,128},{8,136},{16,144},{24,152},{32,160},{40,168},{48,176},{56,1... | collective-permute-start | bytes 417800 | tf_op jit(solution)/shard_map/ppermute | solution.py:22

commit v16 on v15

--- a/solution.py
+++ b/solution.py
@@ -59,7 +59,7 @@
             out_ref[t] = (acc + skip_ref[...] * act_ref[t]) * gate_ref[t]
         return tuple(new)
 
-    hs = lax.fori_loop(0, tokens, body, tuple(h0_ref[n] for n in range(states)), unroll=2)
+    hs = lax.fori_loop(0, tokens, body, tuple(h0_ref[n] for n in range(states)), unroll=4)
     if not with_out:
         for n in range(states):
             out_ref[n] = hs[n]

time: 173 us -> 171 us (0.988)
  Pallas kernels: 41.8 us -> 39.8 us
    pallas_call x2, Pallas kernels: 28.4 us -> 26.4 us  [run_scan(): pl.pallas_call(functools.partial(scan_kernel, with_out), grid=(blocks,),...]
where the time goes in v16:
time: 171 us
  waiting for transfers between devices  49.7 us (29%)
  starting transfers between devices  45.4 us (27%)
  Pallas kernels  39.8 us (23%)
  other arithmetic  19.3 us (11%)
  local copies, waits for them, and re-layouts  12.5 us (7%)
  matrix products  2.67 us (2%)
    ppermute x9, starting transfers between devices, shifted(): lax.ppermute(value, axis, [(source, source + steps) for source in range(f...  37.7 us
    ppermute x9, waiting for transfers between devices, shifted(): lax.ppermute(value, axis, [(source, source + steps) for source in range(f...  31.8 us
    pallas_call x2, Pallas kernels, run_scan(): pl.pallas_call(functools.partial(scan_kernel, with_out), grid=(blocks,),...  26.4 us
    ppermute x3, waiting for transfers between devices, butterfly_sum(): value = value + lax.ppermute(value, axis, pairs)  17.9 us
    pallas_call x1, Pallas kernels, run_attention(): pl.pallas_call(attention_kernel, grid=(heads,), in_specs=[pl.BlockSpec(me...  13.4 us
    ppermute x3, starting transfers between devices, butterfly_sum(): value = value + lax.ppermute(value, axis, pairs)  7.61 us
    unnamed x42, local copies, waits for them, and re-layouts  5.98 us
  transfers between devices with their start and end apart: 13, of which 9 were waited for; matrix products, arithmetic and copies ran while one was open for 11% of the time, Pallas kernels for 14%

profile of v16, /device:TPU:8, one launch (start us, length us, event | category | flops | bytes accessed | tf_op | source)
XLA Modules:
  0.0 170.5 jit_solution(17212432872903184903)
XLA Ops:
  0.7 1.0 constant_dynamic-update-slice_fusion.1
  1.7 0.8 slice.82
  2.5 0.9 constant_dynamic-update-slice_fusion
  3.3 9.1 %collective-permute-start = (bf16[280,256]{1,0:T(8,128)(2,1)S(1)}, bf16[280,256]{1,0:T(8,128)(2,1)S(1)}, u32[]{:S(2)}, u32[]{:S(2)}) collective-permute-start(bf16[280,256]{1,0:T(8,128)(2,1)S(1)} %pad_maximum_fusion.3), channel_id=1, source_target_pairs={{0,8},{8,16},{16,24},{24,32},{32,40},{40,48},{48,56},{56,64},{64,7... | collective-permute-start | bytes 430088 | tf_op jit(solution)/shard_map/ppermute | solution.py:22
  12.5 0.9 fusion.19
  13.4 5.0 %collective-permute-done = bf16[280,256]{1,0:T(8,128)(2,1)S(1)} collective-permute-done((bf16[280,256]{1,0:T(8,128)(2,1)S(1)}, bf16[280,256]{1,0:T(8,128)(2,1)S(1)}, u32[]{:S(2)}, u32[]{:S(2)}) %collective-permute-start) | collective-permute-done | bytes 143392 | tf_op jit(solution)/shard_map/ppermute | solution.py:22
  19.1 1.5 maximum_convert_fusion
  20.6 1.3 multiply_convert_fusion
  22.0 1.5 fusion.20
  23.9 1.9 %pad_maximum_fusion = f32[272,512]{1,0:T(8,128)} fusion(f32[16,512]{1,0:T(8,128)S(1)} %reshape.54, f32[256,512]{1,0:T(8,128)} %fusion.20), kind=kLoop, calls=%fused_computation.21 | loop fusion | flops 139264 | bytes 1114112 | tf_op jit(solution)/shard_map/concatenate | solution.py:225
  25.8 2.3 %collective-permute-done.1 = f32[272,512]{1,0:T(8,128)} collective-permute-done((f32[272,512]{1,0:T(8,128)}, f32[272,512]{1,0:T(8,128)}, u32[]{:S(2)}, u32[]{:S(2)}) %collective-permute-start.1) | collective-permute-done | bytes 557088 | tf_op jit(solution)/shard_map/ppermute | solution.py:145
  28.1 1.3 fusion.17
  29.4 3.6 %collective-permute-start.2 = (f32[136,512]{1,0:T(8,128)S(1)}, f32[136,512]{1,0:T(8,128)S(1)}, u32[]{:S(2)}, u32[]{:S(2)}) collective-permute-start(f32[136,512]{1,0:T(8,128)S(1)} %slice_select_fusion), channel_id=1, source_target_pairs={{0,2},{1,3},{2,0},{3,1},{4,6},{5,7},{6,4},{7,5},{8,10},{9,11},{10,... | collective-permute-start | bytes 835592 | tf_op jit(solution)/shard_map/ppermute | solution.py:145
  33.1 7.0 %collective-permute-done.2 = f32[136,512]{1,0:T(8,128)S(1)} collective-permute-done((f32[136,512]{1,0:T(8,128)S(1)}, f32[136,512]{1,0:T(8,128)S(1)}, u32[]{:S(2)}, u32[]{:S(2)}) %collective-permute-start.2) | collective-permute-done | bytes 278560 | tf_op jit(solution)/shard_map/ppermute | solution.py:145
  40.1 4.0 %collective-permute-start.3 = (f32[136,512]{1,0:T(8,128)S(1)}, f32[136,512]{1,0:T(8,128)S(1)}, u32[]{:S(2)}, u32[]{:S(2)}) collective-permute-start(f32[136,512]{1,0:T(8,128)S(1)} %fusion.25), channel_id=1, source_target_pairs={{0,4},{1,5},{2,6},{3,7},{4,0},{5,1},{6,2},{7,3},{8,12},{9,13},{10,... | collective-permute-start | bytes 835592 | tf_op jit(solution)/shard_map/ppermute | solution.py:145
  44.1 3.5 %collective-permute-start.10 = (bf16[256,256]{1,0:T(8,128)(2,1)S(1)}, bf16[256,256]{1,0:T(8,128)(2,1)}, u32[]{:S(2)}, u32[]{:S(2)}) collective-permute-start(bf16[256,256]{1,0:T(8,128)(2,1)S(1)} %constant_dynamic-update-slice_fusion), channel_id=1, source_target_pairs={{0,64},{8,72},{16,80},{24,88},{32,96},{40,104},{48,112},{56,120},{... | collective-permute-start | bytes 393224 | tf_op jit(solution)/shard_map/ppermute | solution.py:22
  47.8 8.7 %collective-permute-done.3 = f32[136,512]{1,0:T(8,128)S(1)} collective-permute-done((f32[136,512]{1,0:T(8,128)S(1)}, f32[136,512]{1,0:T(8,128)S(1)}, u32[]{:S(2)}, u32[]{:S(2)}) %collective-permute-start.3) | collective-permute-done | bytes 278560 | tf_op jit(solution)/shard_map/ppermute | solution.py:145
  56.6 1.9 %bitcast_multiply_fusion.rest_2_ = f32[256,8,256]{2,1,0:T(8,128)} fusion(f32[32,8,8,256]{3,2,1,0:T(8,128)S(1)} %copy.21), kind=kLoop, calls=%fused_computation.1 | loop fusion | flops 2097152 | bytes 4194304 | tf_op jit(solution)/shard_map/jit(silu)/mul | solution.py:248
  58.5 1.3 add.136
  59.8 0.9 neg.27
  60.7 0.7 copy.20
  61.4 1.3 reshape.57.rest_0_
  63.6 0.8 pad_maximum_fusion.2
  64.4 1.9 %collective-permute-start.11 = (bf16[512,256]{1,0:T(8,128)(2,1)}, bf16[512,256]{1,0:T(8,128)(2,1)S(1)}, u32[]{:S(2)}, u32[]{:S(2)}) collective-permute-start(bf16[512,256]{1,0:T(8,128)(2,1)} %pad_maximum_fusion.2), channel_id=1, source_target_pairs={{0,16},{8,24},{16,32},{24,40},{32,48},{40,56},{48,64},{56,72},{64,... | collective-permute-start | bytes 786440 | tf_op jit(solution)/shard_map/ppermute | solution.py:22
  66.3 1.1 maximum_select_fusion
  67.6 0.8 fusion.3
  68.3 1.9 %fusion.18 = (f32[8,256]{1,0:T(8,128)S(1)}, f32[256,8,256]{2,1,0:T(8,128)S(1)}) fusion(f32[8,256]{1,0:T(8,128)S(1)} %copy-done.12, f32[256,8,256]{2,0,1:T(8,128)S(1)} %fusion.3), kind=kLoop, calls=%fused_computation.64 | loop fusion | flops 4192256 | bytes 4210688 | tf_op jit(solution)/shard_map/reduce_sum | solution.py:246
  70.2 1.8 %bitcast_multiply_fusion.1.dr_ref = f32[256,8,256]{2,1,0:T(8,128)} fusion(f32[256,8,256]{2,1,0:T(8,128)S(1)} %get-tuple-element.3.dt_ref, f32[32,8,8,256]{3,2,1,0:T(8,128)S(1)} %copy.19), kind=kLoop, calls=%fused_computation.61 | loop fusion | flops 524288 | bytes 6291456 | tf_op jit(solution)/shard_map/mul | solution.py:241
  73.5 10.6 %shard_map.149 = f32[16,8,256]{2,1,0:T(8,128)} custom-call(f32[32,256]{1,0:T(8,128)} %reshape.55.bc_ref, f32[256,8,256]{2,1,0:T(8,128)} %copy-done.2, f32[256,8,256]{2,1,0:T(8,128)} %bitcast_multiply_fusion.1.dr_ref, f32[16,8,256]{2,1,0:T(8,128)} %bitcast.59, f32[16,8,256]{2,1,0:T(8,128)} %broadcast_in_dim.5.h0_ref), custom_call_target="tpu_custom_call" | custom-call | flops 33554432 | bytes 6553600 | tf_op jit(solution)/shard_map/pallas_call | solution.py:77
  84.2 0.9 pad_maximum_fusion.4
  85.1 6.4 %collective-permute-start.5 = (f32[17,8,256]{2,1,0:T(8,128)S(1)}, f32[17,8,256]{2,1,0:T(8,128)S(1)}, u32[]{:S(2)}, u32[]{:S(2)}) collective-permute-start(f32[17,8,256]{2,1,0:T(8,128)S(1)} %pad_maximum_fusion.4), channel_id=1, source_target_pairs={{0,8},{8,16},{16,24},{24,32},{32,40},{40,48},{48,56},{56,64},{64,7... | collective-permute-start | bytes 417800 | tf_op jit(solution)/shard_map/ppermute | solution.py:22
  91.5 0.9 constant_dynamic-update-slice_fusion.6
  92.4 4.6 %collective-permute-start.12 = (bf16[1024,256]{1,0:T(8,128)(2,1)S(1)}, bf16[1024,256]{1,0:T(8,128)(2,1)S(1)}, u32[]{:S(2)}, u32[]{:S(2)}) collective-permute-start(bf16[1024,256]{1,0:T(8,128)(2,1)S(1)} %pad_maximum_fusion.1), channel_id=1, source_target_pairs={{0,32},{8,40},{16,48},{24,56},{32,64},{40,72},{48,80},{56,88},{64,... | collective-permute-start | bytes 1572872 | tf_op jit(solution)/shard_map/ppermute | solution.py:22
  97.1 5.7 %collective-permute-done.5 = f32[17,8,256]{2,1,0:T(8,128)S(1)} collective-permute-done((f32[17,8,256]{2,1,0:T(8,128)S(1)}, f32[17,8,256]{2,1,0:T(8,128)S(1)}, u32[]{:S(2)}, u32[]{:S(2)}) %collective-permute-start.5) | collective-permute-done | bytes 139296 | tf_op jit(solution)/shard_map/ppermute | solution.py:22
  102.9 1.0 multiply_add_fusion.3
  103.9 1.9 %collective-permute-start.6 = (f32[17,8,256]{2,1,0:T(8,128)S(1)}, f32[17,8,256]{2,1,0:T(8,128)S(1)}, u32[]{:S(2)}, u32[]{:S(2)}) collective-permute-start(f32[17,8,256]{2,1,0:T(8,128)S(1)} %pad_maximum_fusion.5), channel_id=1, source_target_pairs={{0,16},{8,24},{16,32},{24,40},{32,48},{40,56},{48,64},{56,72},{64,... | collective-permute-start | bytes 417800 | tf_op jit(solution)/shard_map/ppermute | solution.py:22
  105.8 8.3 %collective-permute-done.12 = bf16[1024,256]{1,0:T(8,128)(2,1)S(1)} collective-permute-done((bf16[1024,256]{1,0:T(8,128)(2,1)S(1)}, bf16[1024,256]{1,0:T(8,128)(2,1)S(1)}, u32[]{:S(2)}, u32[]{:S(2)}) %collective-permute-start.12) | collective-permute-done | bytes 524320 | tf_op jit(solution)/shard_map/ppermute | solution.py:22
  114.2 2.2 %collective-permute-done.6 = f32[17,8,256]{2,1,0:T(8,128)S(1)} collective-permute-done((f32[17,8,256]{2,1,0:T(8,128)S(1)}, f32[17,8,256]{2,1,0:T(8,128)S(1)}, u32[]{:S(2)}, u32[]{:S(2)}) %collective-permute-start.6) | collective-permute-done | bytes 139296 | tf_op jit(solution)/shard_map/ppermute | solution.py:22
  116.5 2.7 %collective-permute-start.7 = (f32[17,8,256]{2,1,0:T(8,128)S(1)}, f32[17,8,256]{2,1,0:T(8,128)S(1)}, u32[]{:S(2)}, u32[]{:S(2)}) collective-permute-start(f32[17,8,256]{2,1,0:T(8,128)S(1)} %pad_maximum_fusion.6), channel_id=1, source_target_pairs={{0,32},{8,40},{16,48},{24,56},{32,64},{40,72},{48,80},{56,88},{64,... | collective-permute-start | bytes 417800 | tf_op jit(solution)/shard_map/ppermute | solution.py:22
  119.2 7.2 %collective-permute-done.7 = f32[17,8,256]{2,1,0:T(8,128)S(1)} collective-permute-done((f32[17,8,256]{2,1,0:T(8,128)S(1)}, f32[17,8,256]{2,1,0:T(8,128)S(1)}, u32[]{:S(2)}, u32[]{:S(2)}) %collective-permute-start.7) | collective-permute-done | bytes 139296 | tf_op jit(solution)/shard_map/ppermute | solution.py:22
  126.4 3.5 %collective-permute-start.8 = (f32[17,8,256]{2,1,0:T(8,128)S(1)}, f32[17,8,256]{2,1,0:T(8,128)S(1)}, u32[]{:S(2)}, u32[]{:S(2)}) collective-permute-start(f32[17,8,256]{2,1,0:T(8,128)S(1)} %pad_maximum_fusion.7), channel_id=1, source_target_pairs={{0,64},{8,72},{16,80},{24,88},{32,96},{40,104},{48,112},{56,120},{... | collective-permute-start | bytes 417800 | tf_op jit(solution)/shard_map/ppermute | solution.py:22
  130.0 3.4 %collective-permute-done.8 = f32[17,8,256]{2,1,0:T(8,128)S(1)} collective-permute-done((f32[17,8,256]{2,1,0:T(8,128)S(1)}, f32[17,8,256]{2,1,0:T(8,128)S(1)}, u32[]{:S(2)}, u32[]{:S(2)}) %collective-permute-start.8) | collective-permute-done | bytes 139296 | tf_op jit(solution)/shard_map/ppermute | solution.py:22
  133.4 4.2 %collective-permute-start.9 = (f32[17,8,256]{2,1,0:T(8,128)S(1)}, f32[17,8,256]{2,1,0:T(8,128)S(1)}, u32[]{:S(2)}, u32[]{:S(2)}) collective-permute-start(f32[17,8,256]{2,1,0:T(8,128)S(1)} %pad_maximum_fusion.8), channel_id=1, source_target_pairs={{0,128},{8,136},{16,144},{24,152},{32,160},{40,168},{48,176},{56,1... | collective-permute-start | bytes 417800 | tf_op jit(solution)/shard_map/ppermute | solution.py:22
  137.6 13.4 %shard_map.151 = bf16[256,1024]{1,0:T(8,128)(2,1)} custom-call(s32[1]{0:T(128)} %bitcast.14.base_ref, bf16[256,1024]{1,0:T(8,128)(2,1)} %q_ref.1, bf16[2304,256]{1,0:T(8,128)(2,1)} %copy-done.13, bf16[2304,256]{1,0:T(8,128)(2,1)} %copy-done.13), custom_call_target="tpu_custom_call" | custom-call | flops 2415919104 | bytes 3407872 | tf_op jit(solution)/shard_map/pallas_call | solution.py:121
  151.1 0.8 fusion.14.h0_ref
  151.8 15.7 %shard_map.150 = f32[256,8,256]{2,1,0:T(8,128)} custom-call(f32[32,256]{1,0:T(8,128)} %reshape.55.bc_ref, f32[256,8,256]{2,1,0:T(8,128)} %copy-done.2, f32[256,8,256]{2,1,0:T(8,128)} %bitcast_multiply_fusion.1.dr_ref, f32[16,8,256]{2,1,0:T(8,128)} %bitcast.60, f32[16,8,256]{2,1,0:T(8,128)} %fusion.14.h0_ref, f32[8,256]{1,0:T(8,128)} %reshape.57.rest_0_, ...), custom_call_target="tpu_custom_call" | custom-call | flops 50331648 | bytes 6553600 | tf_op jit(solution)/shard_map/pallas_call | solution.py:77
  167.5 1.7 convert_element_type.30
  169.2 1.3 copy.22
  (72 shorter events, 4.5 us)
Async XLA Ops:
  0.6 21.3 %copy-start = (bf16[2048,512]{1,0:T(8,128)(2,1)S(1)}, bf16[2048,512]{1,0:T(8,128)(2,1)}, u32[]{:S(2)}) copy-start(bf16[2048,512]{1,0:T(8,128)(2,1)} %param.21) | copy-start | bytes 6291460
  0.6 19.9 %copy-start.14 = (f32[2048]{0:T(1024)S(1)}, f32[2048]{0:T(1024)}, u32[]{:S(2)}) copy-start(f32[2048]{0:T(1024)} %param.20) | copy-start | bytes 24580
  3.3 15.0 %collective-permute-start = (bf16[280,256]{1,0:T(8,128)(2,1)S(1)}, bf16[280,256]{1,0:T(8,128)(2,1)S(1)}, u32[]{:S(2)}, u32[]{:S(2)}) collective-permute-start(bf16[280,256]{1,0:T(8,128)(2,1)S(1)} %pad_maximum_fusion.3), channel_id=1, source_target_pairs={{0,8},{8,16},{16,24},{24,32},{32,40},{40,48},{48,56},{56,64},{64,7... | collective-permute-start | bytes 430088 | tf_op jit(solution)/shard_map/ppermute | solution.py:22
  18.4 0.7 copy-start.6
  21.9 1.5 copy-start.11
  25.8 2.3 %collective-permute-start.1 = (f32[272,512]{1,0:T(8,128)}, f32[272,512]{1,0:T(8,128)}, u32[]{:S(2)}, u32[]{:S(2)}) collective-permute-start(f32[272,512]{1,0:T(8,128)} %pad_maximum_fusion), channel_id=1, source_target_pairs={{0,1},{1,0},{2,3},{3,2},{4,5},{5,4},{6,7},{7,6},{8,9},{9,8},{10,11... | collective-permute-start | bytes 1671176 | tf_op jit(solution)/shard_map/ppermute | solution.py:145
  25.8 21.8 %copy-start.5 = (bf16[256,2048]{1,0:T(8,128)(2,1)S(1)}, bf16[256,2048]{1,0:T(8,128)(2,1)}, u32[]{:S(2)}) copy-start(bf16[256,2048]{1,0:T(8,128)(2,1)} %param.15) | copy-start | bytes 3145732
  29.4 10.6 %collective-permute-start.2 = (f32[136,512]{1,0:T(8,128)S(1)}, f32[136,512]{1,0:T(8,128)S(1)}, u32[]{:S(2)}, u32[]{:S(2)}) collective-permute-start(f32[136,512]{1,0:T(8,128)S(1)} %slice_select_fusion), channel_id=1, source_target_pairs={{0,2},{1,3},{2,0},{3,1},{4,6},{5,7},{6,4},{7,5},{8,10},{9,11},{10,... | collective-permute-start | bytes 835592 | tf_op jit(solution)/shard_map/ppermute | solution.py:145
  40.1 16.4 %collective-permute-start.3 = (f32[136,512]{1,0:T(8,128)S(1)}, f32[136,512]{1,0:T(8,128)S(1)}, u32[]{:S(2)}, u32[]{:S(2)}) collective-permute-start(f32[136,512]{1,0:T(8,128)S(1)} %fusion.25), channel_id=1, source_target_pairs={{0,4},{1,5},{2,6},{3,7},{4,0},{5,1},{6,2},{7,3},{8,12},{9,13},{10,... | collective-permute-start | bytes 835592 | tf_op jit(solution)/shard_map/ppermute | solution.py:145
  44.1 47.4 %collective-permute-start.10 = (bf16[256,256]{1,0:T(8,128)(2,1)S(1)}, bf16[256,256]{1,0:T(8,128)(2,1)}, u32[]{:S(2)}, u32[]{:S(2)}) collective-permute-start(bf16[256,256]{1,0:T(8,128)(2,1)S(1)} %constant_dynamic-update-slice_fusion), channel_id=1, source_target_pairs={{0,64},{8,72},{16,80},{24,88},{32,96},{40,104},{48,112},{56,120},{... | collective-permute-start | bytes 393224 | tf_op jit(solution)/shard_map/ppermute | solution.py:22
  56.5 9.8 %collective-permute-start.4 = (f32[136,512]{1,0:T(8,128)S(1)}, f32[136,512]{1,0:T(8,128)}, u32[]{:S(2)}, u32[]{:S(2)}) collective-permute-start(f32[136,512]{1,0:T(8,128)S(1)} %add.133), channel_id=1, source_target_pairs={{0,1},{1,0},{2,3},{3,2},{4,5},{5,4},{6,7},{7,6},{8,9},{9,8},{10,11... | collective-permute-start | bytes 835592 | tf_op jit(solution)/shard_map/ppermute | solution.py:157
  62.7 0.9 copy-start.7
  62.7 4.9 %copy-start.4 = (bf16[512,2048]{1,0:T(8,128)(2,1)S(1)}, bf16[512,2048]{1,0:T(8,128)(2,1)}, u32[]{:S(2)}) copy-start(bf16[512,2048]{1,0:T(8,128)(2,1)} %param.24) | copy-start | bytes 6291460
  62.7 4.9 %copy-start.15 = (f32[512]{0:T(512)S(1)}, f32[512]{0:T(512)}, u32[]{:S(2)}) copy-start(f32[512]{0:T(512)} %param.23) | copy-start | bytes 6148
  63.6 6.7 %copy-start.1 = (f32[32,8,8,256]{3,2,1,0:T(8,128)}, f32[32,8,8,256]{3,2,1,0:T(8,128)S(1)}, u32[]{:S(2)}) copy-start(f32[32,8,8,256]{3,2,1,0:T(8,128)S(1)} %copy.19) | copy-start | bytes 6291460
  64.4 28.0 %collective-permute-start.11 = (bf16[512,256]{1,0:T(8,128)(2,1)}, bf16[512,256]{1,0:T(8,128)(2,1)S(1)}, u32[]{:S(2)}, u32[]{:S(2)}) collective-permute-start(bf16[512,256]{1,0:T(8,128)(2,1)} %pad_maximum_fusion.2), channel_id=1, source_target_pairs={{0,16},{8,24},{16,32},{24,40},{32,48},{40,56},{48,64},{56,72},{64,... | collective-permute-start | bytes 786440 | tf_op jit(solution)/shard_map/ppermute | solution.py:22
  67.5 0.8 copy-start.12
  70.2 2.0 %copy-start.2 = (f32[256,8,256]{2,1,0:T(8,128)}, f32[256,8,256]{2,1,0:T(8,128)S(1)}, u32[]{:S(2)}) copy-start(f32[256,8,256]{2,1,0:T(8,128)S(1)} %get-tuple-element.3.dt_ref) | copy-start | bytes 6291460
  73.5 29.3 %copy-start.3 = (f32[2,8,8,256]{3,2,1,0:T(8,128)S(1)}, f32[2,8,8,256]{3,2,1,0:T(8,128)}, u32[]{:S(2)}) copy-start(f32[2,8,8,256]{3,2,1,0:T(8,128)} %copy.20) | copy-start | bytes 393220
  85.1 17.7 %collective-permute-start.5 = (f32[17,8,256]{2,1,0:T(8,128)S(1)}, f32[17,8,256]{2,1,0:T(8,128)S(1)}, u32[]{:S(2)}, u32[]{:S(2)}) collective-permute-start(f32[17,8,256]{2,1,0:T(8,128)S(1)} %pad_maximum_fusion.4), channel_id=1, source_target_pairs={{0,8},{8,16},{16,24},{24,32},{32,40},{40,48},{48,56},{56,64},{64,7... | collective-permute-start | bytes 417800 | tf_op jit(solution)/shard_map/ppermute | solution.py:22
  92.4 26.7 %copy-start.8 = (bf16[280,256]{1,0:T(8,128)(2,1)S(1)}, bf16[280,256]{1,0:T(8,128)(2,1)}, u32[]{:S(2)}) copy-start(bf16[280,256]{1,0:T(8,128)(2,1)} %copy-done.6) | copy-start | bytes 430084
  92.4 21.7 %collective-permute-start.12 = (bf16[1024,256]{1,0:T(8,128)(2,1)S(1)}, bf16[1024,256]{1,0:T(8,128)(2,1)S(1)}, u32[]{:S(2)}, u32[]{:S(2)}) collective-permute-start(bf16[1024,256]{1,0:T(8,128)(2,1)S(1)} %pad_maximum_fusion.1), channel_id=1, source_target_pairs={{0,32},{8,40},{16,48},{24,56},{32,64},{40,72},{48,80},{56,88},{64,... | collective-permute-start | bytes 1572872 | tf_op jit(solution)/shard_map/ppermute | solution.py:22
  102.8 27.1 %copy-start.9 = (bf16[256,128]{1,0:T(8,128)(2,1)S(1)}, bf16[256,128]{1,0:T(8,128)(2,1)}, u32[]{:S(2)}) copy-start(bf16[256,128]{1,0:T(8,128)(2,1)} %param.17) | copy-start | bytes 196612
  102.9 27.1 %copy-start.10 = (bf16[256,128]{1,0:T(8,128)(2,1)S(1)}, bf16[256,128]{1,0:T(8,128)(2,1)}, u32[]{:S(2)}) copy-start(bf16[256,128]{1,0:T(8,128)(2,1)} %param.18) | copy-start | bytes 196612
  103.9 12.5 %collective-permute-start.6 = (f32[17,8,256]{2,1,0:T(8,128)S(1)}, f32[17,8,256]{2,1,0:T(8,128)S(1)}, u32[]{:S(2)}, u32[]{:S(2)}) collective-permute-start(f32[17,8,256]{2,1,0:T(8,128)S(1)} %pad_maximum_fusion.5), channel_id=1, source_target_pairs={{0,16},{8,24},{16,32},{24,40},{32,48},{40,56},{48,64},{56,72},{64,... | collective-permute-start | bytes 417800 | tf_op jit(solution)/shard_map/ppermute | solution.py:22
  116.5 9.9 %collective-permute-start.7 = (f32[17,8,256]{2,1,0:T(8,128)S(1)}, f32[17,8,256]{2,1,0:T(8,128)S(1)}, u32[]{:S(2)}, u32[]{:S(2)}) collective-permute-start(f32[17,8,256]{2,1,0:T(8,128)S(1)} %pad_maximum_fusion.6), channel_id=1, source_target_pairs={{0,32},{8,40},{16,48},{24,56},{32,64},{40,72},{48,80},{56,88},{64,... | collective-permute-start | bytes 417800 | tf_op jit(solution)/shard_map/ppermute | solution.py:22
  126.4 6.9 %collective-permute-start.8 = (f32[17,8,256]{2,1,0:T(8,128)S(1)}, f32[17,8,256]{2,1,0:T(8,128)S(1)}, u32[]{:S(2)}, u32[]{:S(2)}) collective-permute-start(f32[17,8,256]{2,1,0:T(8,128)S(1)} %pad_maximum_fusion.7), channel_id=1, source_target_pairs={{0,64},{8,72},{16,80},{24,88},{32,96},{40,104},{48,112},{56,120},{... | collective-permute-start | bytes 417800 | tf_op jit(solution)/shard_map/ppermute | solution.py:22
  130.0 7.6 %copy-start.13 = (bf16[2304,256]{1,0:T(8,128)(2,1)}, bf16[2304,256]{1,0:T(8,128)(2,1)S(1)}, u32[]{:S(2)}) copy-start(bf16[2304,256]{1,0:T(8,128)(2,1)S(1)} %constant_dynamic-update-slice_fusion.7.k_ref.v_ref) | copy-start | bytes 3538948
  133.4 17.6 %collective-permute-start.9 = (f32[17,8,256]{2,1,0:T(8,128)S(1)}, f32[17,8,256]{2,1,0:T(8,128)S(1)}, u32[]{:S(2)}, u32[]{:S(2)}) collective-permute-start(f32[17,8,256]{2,1,0:T(8,128)S(1)} %pad_maximum_fusion.8), channel_id=1, source_target_pairs={{0,128},{8,136},{16,144},{24,152},{32,160},{40,168},{48,176},{56,1... | collective-permute-start | bytes 417800 | tf_op jit(solution)/shard_map/ppermute | solution.py:22

commit v17 on v16

--- a/solution.py
+++ b/solution.py
@@ -59,7 +59,7 @@
             out_ref[t] = (acc + skip_ref[...] * act_ref[t]) * gate_ref[t]
         return tuple(new)
 
-    hs = lax.fori_loop(0, tokens, body, tuple(h0_ref[n] for n in range(states)), unroll=4)
+    hs = lax.fori_loop(0, tokens, body, tuple(h0_ref[n] for n in range(states)), unroll=8)
     if not with_out:
         for n in range(states):
             out_ref[n] = hs[n]

time: 171 us -> 170 us (level)
  no operation moved by 1% of the time
where the time goes in v17:
time: 170 us; the launch traced here: 169 us
  waiting for transfers between devices  49.7 us (29%)
  starting transfers between devices  45.4 us (27%)
  Pallas kernels  38.7 us (23%)
  other arithmetic  19.3 us (11%)
  local copies, waits for them, and re-layouts  12.5 us (7%)
  matrix products  2.67 us (2%)
    ppermute x9, starting transfers between devices, shifted(): lax.ppermute(value, axis, [(source, source + steps) for source in range(f...  37.7 us
    ppermute x9, waiting for transfers between devices, shifted(): lax.ppermute(value, axis, [(source, source + steps) for source in range(f...  31.8 us
    pallas_call x2, Pallas kernels, run_scan(): pl.pallas_call(functools.partial(scan_kernel, with_out), grid=(blocks,),...  25.3 us
    ppermute x3, waiting for transfers between devices, butterfly_sum(): value = value + lax.ppermute(value, axis, pairs)  17.9 us
    pallas_call x1, Pallas kernels, run_attention(): pl.pallas_call(attention_kernel, grid=(heads,), in_specs=[pl.BlockSpec(me...  13.4 us
    ppermute x3, starting transfers between devices, butterfly_sum(): value = value + lax.ppermute(value, axis, pairs)  7.61 us
    unnamed x42, local copies, waits for them, and re-layouts  5.98 us
  transfers between devices with their start and end apart: 13, of which 9 were waited for; matrix products, arithmetic and copies ran while one was open for 11% of the time, Pallas kernels for 14%

profile of v17, /device:TPU:8, one launch (start us, length us, event | category | flops | bytes accessed | tf_op | source)
XLA Modules:
  0.0 169.4 jit_solution(5662791841425500203)
XLA Ops:
  0.7 1.0 constant_dynamic-update-slice_fusion.1
  1.7 0.8 slice.82
  2.5 0.9 constant_dynamic-update-slice_fusion
  3.3 9.1 %collective-permute-start = (bf16[280,256]{1,0:T(8,128)(2,1)S(1)}, bf16[280,256]{1,0:T(8,128)(2,1)S(1)}, u32[]{:S(2)}, u32[]{:S(2)}) collective-permute-start(bf16[280,256]{1,0:T(8,128)(2,1)S(1)} %pad_maximum_fusion.3), channel_id=1, source_target_pairs={{0,8},{8,16},{16,24},{24,32},{32,40},{40,48},{48,56},{56,64},{64,7... | collective-permute-start | bytes 430088 | tf_op jit(solution)/shard_map/ppermute | solution.py:22
  12.5 0.9 fusion.19
  13.4 5.0 %collective-permute-done = bf16[280,256]{1,0:T(8,128)(2,1)S(1)} collective-permute-done((bf16[280,256]{1,0:T(8,128)(2,1)S(1)}, bf16[280,256]{1,0:T(8,128)(2,1)S(1)}, u32[]{:S(2)}, u32[]{:S(2)}) %collective-permute-start) | collective-permute-done | bytes 143392 | tf_op jit(solution)/shard_map/ppermute | solution.py:22
  19.1 1.5 maximum_convert_fusion
  20.6 1.3 multiply_convert_fusion
  22.0 1.5 fusion.20
  23.9 1.9 %pad_maximum_fusion = f32[272,512]{1,0:T(8,128)} fusion(f32[16,512]{1,0:T(8,128)S(1)} %reshape.54, f32[256,512]{1,0:T(8,128)} %fusion.20), kind=kLoop, calls=%fused_computation.21 | loop fusion | flops 139264 | bytes 1114112 | tf_op jit(solution)/shard_map/concatenate | solution.py:225
  25.8 2.3 %collective-permute-done.1 = f32[272,512]{1,0:T(8,128)} collective-permute-done((f32[272,512]{1,0:T(8,128)}, f32[272,512]{1,0:T(8,128)}, u32[]{:S(2)}, u32[]{:S(2)}) %collective-permute-start.1) | collective-permute-done | bytes 557088 | tf_op jit(solution)/shard_map/ppermute | solution.py:145
  28.1 1.3 fusion.17
  29.4 3.6 %collective-permute-start.2 = (f32[136,512]{1,0:T(8,128)S(1)}, f32[136,512]{1,0:T(8,128)S(1)}, u32[]{:S(2)}, u32[]{:S(2)}) collective-permute-start(f32[136,512]{1,0:T(8,128)S(1)} %slice_select_fusion), channel_id=1, source_target_pairs={{0,2},{1,3},{2,0},{3,1},{4,6},{5,7},{6,4},{7,5},{8,10},{9,11},{10,... | collective-permute-start | bytes 835592 | tf_op jit(solution)/shard_map/ppermute | solution.py:145
  33.1 7.0 %collective-permute-done.2 = f32[136,512]{1,0:T(8,128)S(1)} collective-permute-done((f32[136,512]{1,0:T(8,128)S(1)}, f32[136,512]{1,0:T(8,128)S(1)}, u32[]{:S(2)}, u32[]{:S(2)}) %collective-permute-start.2) | collective-permute-done | bytes 278560 | tf_op jit(solution)/shard_map/ppermute | solution.py:145
  40.1 4.0 %collective-permute-start.3 = (f32[136,512]{1,0:T(8,128)S(1)}, f32[136,512]{1,0:T(8,128)S(1)}, u32[]{:S(2)}, u32[]{:S(2)}) collective-permute-start(f32[136,512]{1,0:T(8,128)S(1)} %fusion.25), channel_id=1, source_target_pairs={{0,4},{1,5},{2,6},{3,7},{4,0},{5,1},{6,2},{7,3},{8,12},{9,13},{10,... | collective-permute-start | bytes 835592 | tf_op jit(solution)/shard_map/ppermute | solution.py:145
  44.1 3.5 %collective-permute-start.10 = (bf16[256,256]{1,0:T(8,128)(2,1)S(1)}, bf16[256,256]{1,0:T(8,128)(2,1)}, u32[]{:S(2)}, u32[]{:S(2)}) collective-permute-start(bf16[256,256]{1,0:T(8,128)(2,1)S(1)} %constant_dynamic-update-slice_fusion), channel_id=1, source_target_pairs={{0,64},{8,72},{16,80},{24,88},{32,96},{40,104},{48,112},{56,120},{... | collective-permute-start | bytes 393224 | tf_op jit(solution)/shard_map/ppermute | solution.py:22
  47.8 8.7 %collective-permute-done.3 = f32[136,512]{1,0:T(8,128)S(1)} collective-permute-done((f32[136,512]{1,0:T(8,128)S(1)}, f32[136,512]{1,0:T(8,128)S(1)}, u32[]{:S(2)}, u32[]{:S(2)}) %collective-permute-start.3) | collective-permute-done | bytes 278560 | tf_op jit(solution)/shard_map/ppermute | solution.py:145
  56.6 1.9 %bitcast_multiply_fusion.rest_2_ = f32[256,8,256]{2,1,0:T(8,128)} fusion(f32[32,8,8,256]{3,2,1,0:T(8,128)S(1)} %copy.21), kind=kLoop, calls=%fused_computation.1 | loop fusion | flops 2097152 | bytes 4194304 | tf_op jit(solution)/shard_map/jit(silu)/mul | solution.py:248
  58.5 1.3 add.136
  59.8 0.9 neg.27
  60.7 0.7 copy.20
  61.4 1.3 reshape.57.rest_0_
  63.6 0.8 pad_maximum_fusion.2
  64.4 1.9 %collective-permute-start.11 = (bf16[512,256]{1,0:T(8,128)(2,1)}, bf16[512,256]{1,0:T(8,128)(2,1)S(1)}, u32[]{:S(2)}, u32[]{:S(2)}) collective-permute-start(bf16[512,256]{1,0:T(8,128)(2,1)} %pad_maximum_fusion.2), channel_id=1, source_target_pairs={{0,16},{8,24},{16,32},{24,40},{32,48},{40,56},{48,64},{56,72},{64,... | collective-permute-start | bytes 786440 | tf_op jit(solution)/shard_map/ppermute | solution.py:22
  66.3 1.1 maximum_select_fusion
  67.6 0.8 fusion.3
  68.3 1.9 %fusion.18 = (f32[8,256]{1,0:T(8,128)S(1)}, f32[256,8,256]{2,1,0:T(8,128)S(1)}) fusion(f32[8,256]{1,0:T(8,128)S(1)} %copy-done.12, f32[256,8,256]{2,0,1:T(8,128)S(1)} %fusion.3), kind=kLoop, calls=%fused_computation.64 | loop fusion | flops 4192256 | bytes 4210688 | tf_op jit(solution)/shard_map/reduce_sum | solution.py:246
  70.2 1.8 %bitcast_multiply_fusion.1.dr_ref = f32[256,8,256]{2,1,0:T(8,128)} fusion(f32[256,8,256]{2,1,0:T(8,128)S(1)} %get-tuple-element.3.dt_ref, f32[32,8,8,256]{3,2,1,0:T(8,128)S(1)} %copy.19), kind=kLoop, calls=%fused_computation.61 | loop fusion | flops 524288 | bytes 6291456 | tf_op jit(solution)/shard_map/mul | solution.py:241
  73.5 10.3 %shard_map.149 = f32[16,8,256]{2,1,0:T(8,128)} custom-call(f32[32,256]{1,0:T(8,128)} %reshape.55.bc_ref, f32[256,8,256]{2,1,0:T(8,128)} %copy-done.2, f32[256,8,256]{2,1,0:T(8,128)} %bitcast_multiply_fusion.1.dr_ref, f32[16,8,256]{2,1,0:T(8,128)} %bitcast.59, f32[16,8,256]{2,1,0:T(8,128)} %broadcast_in_dim.5.h0_ref), custom_call_target="tpu_custom_call" | custom-call | flops 33554432 | bytes 6553600 | tf_op jit(solution)/shard_map/pallas_call | solution.py:77
  83.8 0.9 pad_maximum_fusion.4
  84.7 6.4 %collective-permute-start.5 = (f32[17,8,256]{2,1,0:T(8,128)S(1)}, f32[17,8,256]{2,1,0:T(8,128)S(1)}, u32[]{:S(2)}, u32[]{:S(2)}) collective-permute-start(f32[17,8,256]{2,1,0:T(8,128)S(1)} %pad_maximum_fusion.4), channel_id=1, source_target_pairs={{0,8},{8,16},{16,24},{24,32},{32,40},{40,48},{48,56},{56,64},{64,7... | collective-permute-start | bytes 417800 | tf_op jit(solution)/shard_map/ppermute | solution.py:22
  91.1 0.9 constant_dynamic-update-slice_fusion.6
  92.1 4.6 %collective-permute-start.12 = (bf16[1024,256]{1,0:T(8,128)(2,1)S(1)}, bf16[1024,256]{1,0:T(8,128)(2,1)S(1)}, u32[]{:S(2)}, u32[]{:S(2)}) collective-permute-start(bf16[1024,256]{1,0:T(8,128)(2,1)S(1)} %pad_maximum_fusion.1), channel_id=1, source_target_pairs={{0,32},{8,40},{16,48},{24,56},{32,64},{40,72},{48,80},{56,88},{64,... | collective-permute-start | bytes 1572872 | tf_op jit(solution)/shard_map/ppermute | solution.py:22
  96.7 5.7 %collective-permute-done.5 = f32[17,8,256]{2,1,0:T(8,128)S(1)} collective-permute-done((f32[17,8,256]{2,1,0:T(8,128)S(1)}, f32[17,8,256]{2,1,0:T(8,128)S(1)}, u32[]{:S(2)}, u32[]{:S(2)}) %collective-permute-start.5) | collective-permute-done | bytes 139296 | tf_op jit(solution)/shard_map/ppermute | solution.py:22
  102.5 1.0 multiply_add_fusion.3
  103.5 1.9 %collective-permute-start.6 = (f32[17,8,256]{2,1,0:T(8,128)S(1)}, f32[17,8,256]{2,1,0:T(8,128)S(1)}, u32[]{:S(2)}, u32[]{:S(2)}) collective-permute-start(f32[17,8,256]{2,1,0:T(8,128)S(1)} %pad_maximum_fusion.5), channel_id=1, source_target_pairs={{0,16},{8,24},{16,32},{24,40},{32,48},{40,56},{48,64},{56,72},{64,... | collective-permute-start | bytes 417800 | tf_op jit(solution)/shard_map/ppermute | solution.py:22
  105.4 8.3 %collective-permute-done.12 = bf16[1024,256]{1,0:T(8,128)(2,1)S(1)} collective-permute-done((bf16[1024,256]{1,0:T(8,128)(2,1)S(1)}, bf16[1024,256]{1,0:T(8,128)(2,1)S(1)}, u32[]{:S(2)}, u32[]{:S(2)}) %collective-permute-start.12) | collective-permute-done | bytes 524320 | tf_op jit(solution)/shard_map/ppermute | solution.py:22
  113.8 2.2 %collective-permute-done.6 = f32[17,8,256]{2,1,0:T(8,128)S(1)} collective-permute-done((f32[17,8,256]{2,1,0:T(8,128)S(1)}, f32[17,8,256]{2,1,0:T(8,128)S(1)}, u32[]{:S(2)}, u32[]{:S(2)}) %collective-permute-start.6) | collective-permute-done | bytes 139296 | tf_op jit(solution)/shard_map/ppermute | solution.py:22
  116.1 2.7 %collective-permute-start.7 = (f32[17,8,256]{2,1,0:T(8,128)S(1)}, f32[17,8,256]{2,1,0:T(8,128)S(1)}, u32[]{:S(2)}, u32[]{:S(2)}) collective-permute-start(f32[17,8,256]{2,1,0:T(8,128)S(1)} %pad_maximum_fusion.6), channel_id=1, source_target_pairs={{0,32},{8,40},{16,48},{24,56},{32,64},{40,72},{48,80},{56,88},{64,... | collective-permute-start | bytes 417800 | tf_op jit(solution)/shard_map/ppermute | solution.py:22
  118.8 7.2 %collective-permute-done.7 = f32[17,8,256]{2,1,0:T(8,128)S(1)} collective-permute-done((f32[17,8,256]{2,1,0:T(8,128)S(1)}, f32[17,8,256]{2,1,0:T(8,128)S(1)}, u32[]{:S(2)}, u32[]{:S(2)}) %collective-permute-start.7) | collective-permute-done | bytes 139296 | tf_op jit(solution)/shard_map/ppermute | solution.py:22
  126.0 3.5 %collective-permute-start.8 = (f32[17,8,256]{2,1,0:T(8,128)S(1)}, f32[17,8,256]{2,1,0:T(8,128)S(1)}, u32[]{:S(2)}, u32[]{:S(2)}) collective-permute-start(f32[17,8,256]{2,1,0:T(8,128)S(1)} %pad_maximum_fusion.7), channel_id=1, source_target_pairs={{0,64},{8,72},{16,80},{24,88},{32,96},{40,104},{48,112},{56,120},{... | collective-permute-start | bytes 417800 | tf_op jit(solution)/shard_map/ppermute | solution.py:22
  129.6 3.4 %collective-permute-done.8 = f32[17,8,256]{2,1,0:T(8,128)S(1)} collective-permute-done((f32[17,8,256]{2,1,0:T(8,128)S(1)}, f32[17,8,256]{2,1,0:T(8,128)S(1)}, u32[]{:S(2)}, u32[]{:S(2)}) %collective-permute-start.8) | collective-permute-done | bytes 139296 | tf_op jit(solution)/shard_map/ppermute | solution.py:22
  133.1 4.2 %collective-permute-start.9 = (f32[17,8,256]{2,1,0:T(8,128)S(1)}, f32[17,8,256]{2,1,0:T(8,128)S(1)}, u32[]{:S(2)}, u32[]{:S(2)}) collective-permute-start(f32[17,8,256]{2,1,0:T(8,128)S(1)} %pad_maximum_fusion.8), channel_id=1, source_target_pairs={{0,128},{8,136},{16,144},{24,152},{32,160},{40,168},{48,176},{56,1... | collective-permute-start | bytes 417800 | tf_op jit(solution)/shard_map/ppermute | solution.py:22
  137.3 13.4 %shard_map.151 = bf16[256,1024]{1,0:T(8,128)(2,1)} custom-call(s32[1]{0:T(128)} %bitcast.14.base_ref, bf16[256,1024]{1,0:T(8,128)(2,1)} %q_ref.1, bf16[2304,256]{1,0:T(8,128)(2,1)} %copy-done.13, bf16[2304,256]{1,0:T(8,128)(2,1)} %copy-done.13), custom_call_target="tpu_custom_call" | custom-call | flops 2415919104 | bytes 3407872 | tf_op jit(solution)/shard_map/pallas_call | solution.py:121
  150.7 0.8 fusion.14.h0_ref
  151.5 15.0 %shard_map.150 = f32[256,8,256]{2,1,0:T(8,128)} custom-call(f32[32,256]{1,0:T(8,128)} %reshape.55.bc_ref, f32[256,8,256]{2,1,0:T(8,128)} %copy-done.2, f32[256,8,256]{2,1,0:T(8,128)} %bitcast_multiply_fusion.1.dr_ref, f32[16,8,256]{2,1,0:T(8,128)} %bitcast.60, f32[16,8,256]{2,1,0:T(8,128)} %fusion.14.h0_ref, f32[8,256]{1,0:T(8,128)} %reshape.57.rest_0_, ...), custom_call_target="tpu_custom_call" | custom-call | flops 50331648 | bytes 6553600 | tf_op jit(solution)/shard_map/pallas_call | solution.py:77
  166.5 1.7 convert_element_type.30
  168.2 1.3 copy.22
  (72 shorter events, 4.5 us)
Async XLA Ops:
  0.6 21.3 %copy-start = (bf16[2048,512]{1,0:T(8,128)(2,1)S(1)}, bf16[2048,512]{1,0:T(8,128)(2,1)}, u32[]{:S(2)}) copy-start(bf16[2048,512]{1,0:T(8,128)(2,1)} %param.21) | copy-start | bytes 6291460
  0.6 19.9 %copy-start.14 = (f32[2048]{0:T(1024)S(1)}, f32[2048]{0:T(1024)}, u32[]{:S(2)}) copy-start(f32[2048]{0:T(1024)} %param.20) | copy-start | bytes 24580
  3.3 15.0 %collective-permute-start = (bf16[280,256]{1,0:T(8,128)(2,1)S(1)}, bf16[280,256]{1,0:T(8,128)(2,1)S(1)}, u32[]{:S(2)}, u32[]{:S(2)}) collective-permute-start(bf16[280,256]{1,0:T(8,128)(2,1)S(1)} %pad_maximum_fusion.3), channel_id=1, source_target_pairs={{0,8},{8,16},{16,24},{24,32},{32,40},{40,48},{48,56},{56,64},{64,7... | collective-permute-start | bytes 430088 | tf_op jit(solution)/shard_map/ppermute | solution.py:22
  18.4 0.7 copy-start.6
  21.9 1.5 copy-start.11
  25.8 2.3 %collective-permute-start.1 = (f32[272,512]{1,0:T(8,128)}, f32[272,512]{1,0:T(8,128)}, u32[]{:S(2)}, u32[]{:S(2)}) collective-permute-start(f32[272,512]{1,0:T(8,128)} %pad_maximum_fusion), channel_id=1, source_target_pairs={{0,1},{1,0},{2,3},{3,2},{4,5},{5,4},{6,7},{7,6},{8,9},{9,8},{10,11... | collective-permute-start | bytes 1671176 | tf_op jit(solution)/shard_map/ppermute | solution.py:145
  25.8 21.8 %copy-start.5 = (bf16[256,2048]{1,0:T(8,128)(2,1)S(1)}, bf16[256,2048]{1,0:T(8,128)(2,1)}, u32[]{:S(2)}) copy-start(bf16[256,2048]{1,0:T(8,128)(2,1)} %param.15) | copy-start | bytes 3145732
  29.4 10.6 %collective-permute-start.2 = (f32[136,512]{1,0:T(8,128)S(1)}, f32[136,512]{1,0:T(8,128)S(1)}, u32[]{:S(2)}, u32[]{:S(2)}) collective-permute-start(f32[136,512]{1,0:T(8,128)S(1)} %slice_select_fusion), channel_id=1, source_target_pairs={{0,2},{1,3},{2,0},{3,1},{4,6},{5,7},{6,4},{7,5},{8,10},{9,11},{10,... | collective-permute-start | bytes 835592 | tf_op jit(solution)/shard_map/ppermute | solution.py:145
  40.1 16.4 %collective-permute-start.3 = (f32[136,512]{1,0:T(8,128)S(1)}, f32[136,512]{1,0:T(8,128)S(1)}, u32[]{:S(2)}, u32[]{:S(2)}) collective-permute-start(f32[136,512]{1,0:T(8,128)S(1)} %fusion.25), channel_id=1, source_target_pairs={{0,4},{1,5},{2,6},{3,7},{4,0},{5,1},{6,2},{7,3},{8,12},{9,13},{10,... | collective-permute-start | bytes 835592 | tf_op jit(solution)/shard_map/ppermute | solution.py:145
  44.1 47.0 %collective-permute-start.10 = (bf16[256,256]{1,0:T(8,128)(2,1)S(1)}, bf16[256,256]{1,0:T(8,128)(2,1)}, u32[]{:S(2)}, u32[]{:S(2)}) collective-permute-start(bf16[256,256]{1,0:T(8,128)(2,1)S(1)} %constant_dynamic-update-slice_fusion), channel_id=1, source_target_pairs={{0,64},{8,72},{16,80},{24,88},{32,96},{40,104},{48,112},{56,120},{... | collective-permute-start | bytes 393224 | tf_op jit(solution)/shard_map/ppermute | solution.py:22
  56.5 9.8 %collective-permute-start.4 = (f32[136,512]{1,0:T(8,128)S(1)}, f32[136,512]{1,0:T(8,128)}, u32[]{:S(2)}, u32[]{:S(2)}) collective-permute-start(f32[136,512]{1,0:T(8,128)S(1)} %add.133), channel_id=1, source_target_pairs={{0,1},{1,0},{2,3},{3,2},{4,5},{5,4},{6,7},{7,6},{8,9},{9,8},{10,11... | collective-permute-start | bytes 835592 | tf_op jit(solution)/shard_map/ppermute | solution.py:157
  62.7 0.9 copy-start.7
  62.7 4.9 %copy-start.4 = (bf16[512,2048]{1,0:T(8,128)(2,1)S(1)}, bf16[512,2048]{1,0:T(8,128)(2,1)}, u32[]{:S(2)}) copy-start(bf16[512,2048]{1,0:T(8,128)(2,1)} %param.24) | copy-start | bytes 6291460
  62.7 4.9 %copy-start.15 = (f32[512]{0:T(512)S(1)}, f32[512]{0:T(512)}, u32[]{:S(2)}) copy-start(f32[512]{0:T(512)} %param.23) | copy-start | bytes 6148
  63.6 6.7 %copy-start.1 = (f32[32,8,8,256]{3,2,1,0:T(8,128)}, f32[32,8,8,256]{3,2,1,0:T(8,128)S(1)}, u32[]{:S(2)}) copy-start(f32[32,8,8,256]{3,2,1,0:T(8,128)S(1)} %copy.19) | copy-start | bytes 6291460
  64.4 27.7 %collective-permute-start.11 = (bf16[512,256]{1,0:T(8,128)(2,1)}, bf16[512,256]{1,0:T(8,128)(2,1)S(1)}, u32[]{:S(2)}, u32[]{:S(2)}) collective-permute-start(bf16[512,256]{1,0:T(8,128)(2,1)} %pad_maximum_fusion.2), channel_id=1, source_target_pairs={{0,16},{8,24},{16,32},{24,40},{32,48},{40,56},{48,64},{56,72},{64,... | collective-permute-start | bytes 786440 | tf_op jit(solution)/shard_map/ppermute | solution.py:22
  67.5 0.8 copy-start.12
  70.2 2.0 %copy-start.2 = (f32[256,8,256]{2,1,0:T(8,128)}, f32[256,8,256]{2,1,0:T(8,128)S(1)}, u32[]{:S(2)}) copy-start(f32[256,8,256]{2,1,0:T(8,128)S(1)} %get-tuple-element.3.dt_ref) | copy-start | bytes 6291460
  73.5 28.9 %copy-start.3 = (f32[2,8,8,256]{3,2,1,0:T(8,128)S(1)}, f32[2,8,8,256]{3,2,1,0:T(8,128)}, u32[]{:S(2)}) copy-start(f32[2,8,8,256]{3,2,1,0:T(8,128)} %copy.20) | copy-start | bytes 393220
  84.7 17.7 %collective-permute-start.5 = (f32[17,8,256]{2,1,0:T(8,128)S(1)}, f32[17,8,256]{2,1,0:T(8,128)S(1)}, u32[]{:S(2)}, u32[]{:S(2)}) collective-permute-start(f32[17,8,256]{2,1,0:T(8,128)S(1)} %pad_maximum_fusion.4), channel_id=1, source_target_pairs={{0,8},{8,16},{16,24},{24,32},{32,40},{40,48},{48,56},{56,64},{64,7... | collective-permute-start | bytes 417800 | tf_op jit(solution)/shard_map/ppermute | solution.py:22
  92.0 26.7 %copy-start.8 = (bf16[280,256]{1,0:T(8,128)(2,1)S(1)}, bf16[280,256]{1,0:T(8,128)(2,1)}, u32[]{:S(2)}) copy-start(bf16[280,256]{1,0:T(8,128)(2,1)} %copy-done.6) | copy-start | bytes 430084
  92.1 21.7 %collective-permute-start.12 = (bf16[1024,256]{1,0:T(8,128)(2,1)S(1)}, bf16[1024,256]{1,0:T(8,128)(2,1)S(1)}, u32[]{:S(2)}, u32[]{:S(2)}) collective-permute-start(bf16[1024,256]{1,0:T(8,128)(2,1)S(1)} %pad_maximum_fusion.1), channel_id=1, source_target_pairs={{0,32},{8,40},{16,48},{24,56},{32,64},{40,72},{48,80},{56,88},{64,... | collective-permute-start | bytes 1572872 | tf_op jit(solution)/shard_map/ppermute | solution.py:22
  102.5 27.1 %copy-start.9 = (bf16[256,128]{1,0:T(8,128)(2,1)S(1)}, bf16[256,128]{1,0:T(8,128)(2,1)}, u32[]{:S(2)}) copy-start(bf16[256,128]{1,0:T(8,128)(2,1)} %param.17) | copy-start | bytes 196612
  102.5 27.1 %copy-start.10 = (bf16[256,128]{1,0:T(8,128)(2,1)S(1)}, bf16[256,128]{1,0:T(8,128)(2,1)}, u32[]{:S(2)}) copy-start(bf16[256,128]{1,0:T(8,128)(2,1)} %param.18) | copy-start | bytes 196612
  103.5 12.5 %collective-permute-start.6 = (f32[17,8,256]{2,1,0:T(8,128)S(1)}, f32[17,8,256]{2,1,0:T(8,128)S(1)}, u32[]{:S(2)}, u32[]{:S(2)}) collective-permute-start(f32[17,8,256]{2,1,0:T(8,128)S(1)} %pad_maximum_fusion.5), channel_id=1, source_target_pairs={{0,16},{8,24},{16,32},{24,40},{32,48},{40,56},{48,64},{56,72},{64,... | collective-permute-start | bytes 417800 | tf_op jit(solution)/shard_map/ppermute | solution.py:22
  116.1 9.9 %collective-permute-start.7 = (f32[17,8,256]{2,1,0:T(8,128)S(1)}, f32[17,8,256]{2,1,0:T(8,128)S(1)}, u32[]{:S(2)}, u32[]{:S(2)}) collective-permute-start(f32[17,8,256]{2,1,0:T(8,128)S(1)} %pad_maximum_fusion.6), channel_id=1, source_target_pairs={{0,32},{8,40},{16,48},{24,56},{32,64},{40,72},{48,80},{56,88},{64,... | collective-permute-start | bytes 417800 | tf_op jit(solution)/shard_map/ppermute | solution.py:22
  126.0 6.9 %collective-permute-start.8 = (f32[17,8,256]{2,1,0:T(8,128)S(1)}, f32[17,8,256]{2,1,0:T(8,128)S(1)}, u32[]{:S(2)}, u32[]{:S(2)}) collective-permute-start(f32[17,8,256]{2,1,0:T(8,128)S(1)} %pad_maximum_fusion.7), channel_id=1, source_target_pairs={{0,64},{8,72},{16,80},{24,88},{32,96},{40,104},{48,112},{56,120},{... | collective-permute-start | bytes 417800 | tf_op jit(solution)/shard_map/ppermute | solution.py:22
  129.6 7.6 %copy-start.13 = (bf16[2304,256]{1,0:T(8,128)(2,1)}, bf16[2304,256]{1,0:T(8,128)(2,1)S(1)}, u32[]{:S(2)}) copy-start(bf16[2304,256]{1,0:T(8,128)(2,1)S(1)} %constant_dynamic-update-slice_fusion.7.k_ref.v_ref) | copy-start | bytes 3538948
  133.1 17.6 %collective-permute-start.9 = (f32[17,8,256]{2,1,0:T(8,128)S(1)}, f32[17,8,256]{2,1,0:T(8,128)S(1)}, u32[]{:S(2)}, u32[]{:S(2)}) collective-permute-start(f32[17,8,256]{2,1,0:T(8,128)S(1)} %pad_maximum_fusion.8), channel_id=1, source_target_pairs={{0,128},{8,136},{16,144},{24,152},{32,160},{40,168},{48,176},{56,1... | collective-permute-start | bytes 417800 | tf_op jit(solution)/shard_map/ppermute | solution.py:22
